TPU v7x, 512 devices: a whole 4x4x16 slice. The times are simulated.
512 devices in a mesh: tile: 32 (over y, x, core), depth: 16 (over z).
Axes of the slice: x: 4, y: 4, z: 16, core: 2. Of those that a mesh axis runs over, the one named last changes fastest.
Arguments:
- grid: float32 [4, 128, 128, 1024], P(None, 'tile', 'depth'), may hold values from -6 to 6
- first_moment: float32 [4, 128, 128, 1024], P(None, 'tile', 'depth'), may hold values from -4 to 4
- second_moment: float32 [4, 128, 128, 1024], P(None, 'tile', 'depth'), may hold values from 0.01 to 1
- ray_offset: int32 [128, 1024], P('tile'), may hold values from 0 to 1
- occupancy: int32 [32, 16, 128], P('tile', 'depth'), may hold values 0 or 1
- target: float32 [3, 128, 1024], P(None, 'tile'), may hold values from 0 to 1
Outputs:
- new_grid: float32 [4, 128, 128, 1024], P(None, 'tile', 'depth')
- new_first: float32 [4, 128, 128, 1024], P(None, 'tile', 'depth')
- new_second: float32 [4, 128, 128, 1024], P(None, 'tile', 'depth')
All inputs are finite; a program needn't handle non-finite values. No bound on the sum of `occupancy` on one device may be relied on, other than what follows from the above.
Results may differ from a plain program's by a relative error of at most 0.00002.
Values sent between devices are 32-bit elements; how exact they have to be, the bound alone decides.
No kernel may reach another device: no remote copies, remote signals or barrier semaphores. Data moves between devices by JAX's collectives and lax.ppermute only.
A program may use at most 64 MiB of HBM per device.

v0:
```python
import jax
import jax.numpy as jnp
from jax import lax
from jax.sharding import PartitionSpec as P

tv_weight = 0.01
beta_one = 0.9
beta_two = 0.95
learn_rate = 0.1
adam_step = 10
epsilon = 1e-08


def carried_in_2(value, axis, join, neutral, backward):
    count, mine = (lax.axis_size(axis), lax.axis_index(axis))
    pieces = jax.tree.map(lambda part: lax.all_gather(part, axis), value)
    if backward:
        pieces = jax.tree.map(lambda part: part[::-1], pieces)
        mine = count - 1 - mine
    total = jax.tree.map(
        lambda part, zero: jnp.full_like(part, 0) + jnp.asarray(zero, part.dtype), value, neutral
    )

    def lap(position, total):
        longer = join(total, jax.tree.map(lambda part: part[position], pieces))
        return jax.tree.map(lambda new, old: jnp.where(position < mine, new, old), longer, total)

    return lax.fori_loop(0, count - 1, lap, total)


def with_halo(cells, sides, width):
    for axis, dim in sides:
        count = lax.axis_size(axis)
        ends = count - 1
        head = lax.slice_in_dim(cells, 0, width, axis=dim)
        tail = lax.slice_in_dim(cells, cells.shape[dim] - width, cells.shape[dim], axis=dim)
        cells = jnp.concatenate(
            [
                lax.ppermute(tail, axis, [(i, (i + 1) % count) for i in range(ends)]),
                cells,
                lax.ppermute(head, axis, [((i + 1) % count, i) for i in range(ends)]),
            ],
            axis=dim,
        )
    return cells


def passed_along(block, axis, distance):
    devices = range(lax.axis_size(axis))
    route = [(i - distance, i) for i in devices if i - distance in devices]
    return lax.ppermute(block, axis, route)


def front_combine(earlier, later):
    return (earlier[0] + earlier[1][None] * later[0], earlier[1] * later[1])


def back_combine(earlier, later):
    return (later[0] + later[1][None] * earlier[0], later[1] * earlier[1])


def render(rows, after_rows, shares, occ, target, total_depth):
    scale = 4.0 / total_depth
    features = (1.0 - shares) * rows + shares * after_rows
    sigma = occ * jax.nn.softplus(features[0]) * scale
    colour = jax.nn.sigmoid(features[1:])
    before = jnp.cumsum(sigma, axis=1) - sigma
    trans = jnp.exp(-before)
    fade = jnp.exp(-sigma)
    weight = trans * -jnp.expm1(-sigma)
    weighted = weight[None] * colour
    seg_colour = jnp.sum(weighted, axis=2)
    seg_trans = jnp.exp(-jnp.sum(sigma, axis=1))
    blank = (jnp.zeros_like(seg_colour), jnp.ones_like(seg_trans))
    front_colour, front_trans = carried_in_2(
        (seg_colour, seg_trans), "depth", front_combine, blank, False
    )
    back_colour, back_trans = carried_in_2(
        (seg_colour, seg_trans), "depth", back_combine, blank, True
    )
    behind = back_colour + back_trans[None]
    pixel = front_colour + front_trans[None] * (seg_colour + seg_trans[None] * behind)
    pixel_grad = 0.5 * total_depth * (pixel - target)
    upto = jnp.cumsum(weighted, axis=2)
    remain = seg_colour[:, :, None, :] - upto + (seg_trans[None] * behind)[:, :, None, :]
    next_trans = trans * fade
    front_wide = front_trans[:, None, :]
    sigma_grad = front_wide * jnp.sum(
        pixel_grad[:, :, None, :] * (next_trans[None] * colour - remain), axis=0
    )
    colour_grad = front_wide[None] * weight[None] * pixel_grad[:, :, None, :]
    density_grad = sigma_grad * occ * scale * jax.nn.sigmoid(features[0])
    return jnp.concatenate([density_grad[None], colour_grad * colour * (1.0 - colour)], axis=0)


def expand_blocks(blocks):
    return jnp.repeat(jnp.repeat(jnp.repeat(blocks, 4, axis=0), 8, axis=1), 8, axis=2)


def body(grid, first_moment, second_moment, ray_offset, occupancy, target):
    depth_count = lax.axis_size("depth")
    planes = grid.shape[2]
    total_depth = planes * depth_count
    padded = with_halo(grid, (("tile", 1), ("depth", 2)), 1)
    shares = (ray_offset.astype(jnp.float32) * 0.5)[None, :, None, :]
    occ = expand_blocks(occupancy.astype(jnp.float32))
    feature_grad = render(grid, padded[:, 2:, 1:-1, :], shares, occ, target, total_depth)
    carried = shares * feature_grad
    incoming = passed_along(carried[:, -1:], "tile", 1)
    carried_in = jnp.concatenate([incoming, carried[:, :-1]], axis=1)
    data_grad = (1.0 - shares) * feature_grad + carried_in
    across_rows = padded[:, 2:, 1:-1, :] + padded[:, :-2, 1:-1, :]
    across_planes = padded[:, 1:-1, 2:, :] + padded[:, 1:-1, :-2, :]
    side_pad = jnp.pad(grid, ((0, 0), (0, 0), (0, 0), (1, 1)))
    across_cols = side_pad[:, :, :, 2:] + side_pad[:, :, :, :-2]
    smooth_grad = 2.0 * tv_weight * (6.0 * grid - across_rows - across_planes - across_cols)
    grad = data_grad + smooth_grad
    new_first = beta_one * first_moment + (1.0 - beta_one) * grad
    new_second = beta_two * second_moment + (1.0 - beta_two) * grad * grad
    corr_one = 1.0 - beta_one**adam_step
    corr_two = 1.0 - beta_two**adam_step
    new_grid = grid - learn_rate * (new_first / corr_one) / (
        jnp.sqrt(new_second / corr_two) + epsilon
    )
    return (new_grid, new_first, new_second)


def solution(mesh):
    in_specs = (
        P(None, "tile", "depth", None),
        P(None, "tile", "depth", None),
        P(None, "tile", "depth", None),
        P("tile", None),
        P("tile", "depth", None),
        P(None, "tile", None),
    )
    out_specs = (
        P(None, "tile", "depth", None),
        P(None, "tile", "depth", None),
        P(None, "tile", "depth", None),
    )
    return jax.shard_map(body, mesh=mesh, in_specs=in_specs, out_specs=out_specs, check_vma=False)
```

profile of v0, /device:TPU:7, one launch (start us, length us, event | category | flops | bytes accessed | tf_op | source)
XLA Modules:
  0.0 128.3 jit_solution(15471579000593413589)
XLA Ops:
  0.6 1.0 fusion.28
  1.7 2.6 %collective-permute-start = (f32[4,1,8,1024]{3,2,1,0:T(8,128)S(1)}, f32[4,1,8,1024]{3,2,1,0:T(8,128)S(1)}, u32[]{:S(2)}, u32[]{:S(2)}) collective-permute-start(f32[4,1,8,1024]{3,2,1,0:T(8,128)S(1)} %get-tuple-element.315), channel_id=1, source_target_pairs={{16,0},{32,16},{48,32},{64,48},{80,64},{96,80},{112,96},{128,112},... | collective-permute-start | bytes 393224 | tf_op jit(solution)/shard_map/ppermute | solution.py:41
  4.3 5.1 %collective-permute-start.2 = (f32[4,1,8,1024]{3,2,1,0:T(8,128)S(1)}, f32[4,1,8,1024]{3,2,1,0:T(8,128)S(1)}, u32[]{:S(2)}, u32[]{:S(2)}) collective-permute-start(f32[4,1,8,1024]{3,2,1,0:T(8,128)S(1)} %get-tuple-element.316), channel_id=1, source_target_pairs={{0,16},{16,32},{32,48},{48,64},{64,80},{80,96},{96,112},{112,128},... | collective-permute-start | bytes 393224 | tf_op jit(solution)/shard_map/ppermute | solution.py:39
  9.4 0.7 broadcast_subtract_fusion
  10.3 0.1 broadcast_in_dim.13
  10.4 0.9 collective-permute-done.2
  11.4 0.6 copy-done.7
  12.0 0.1 fusion.11
  12.1 0.1 fusion.24
  12.2 0.1 reduce_window_sum.22
  12.4 0.6 copy-done.2
  13.0 0.2 fusion.26
  13.2 33.5 %all-gather = f32[48,4,1024]{2,1,0:T(4,128)S(1)} all-gather(f32[3,4,1024]{2,1,0:T(4,128)S(1)} %get-tuple-element.307), channel_id=2, replica_groups=mesh['tile'=32,'depth'=16] {'depth'}, dimensions={0}, use_global_device_ids=true | all-gather | bytes 835584 | tf_op jit(solution)/shard_map/all_gather | solution.py:16
  46.7 0.6 negate_exponential_fusion.1
  47.3 20.7 %all-gather.2 = f32[16,4,1024]{2,1,0:T(4,128)S(1)} all-gather(f32[1,4,1024]{2,1,0:T(4,128)S(1)} %get-tuple-element.320), channel_id=3, replica_groups=mesh['tile'=32,'depth'=16] {'depth'}, dimensions={0}, use_global_device_ids=true | all-gather | bytes 278528 | tf_op jit(solution)/shard_map/all_gather | solution.py:16
  68.0 0.9 rev.6
  68.9 0.7 rev.7
  69.7 1.3 while.32
  70.9 1.0 multiply_bitcast_fusion.1
  71.9 23.9 %while.33 = (s32[]{:T(128)}, f32[3,4,1024]{2,1,0:T(4,128)S(1)}, f32[4,1024]{1,0:T(4,128)S(1)}, s32[]{:T(128)}, f32[16,3,4,1024]{3,2,1,0:T(4,128)}, /*index=5*/f32[16,4,1024]{2,1,0:T(4,128)}, s32[]{:T(128)}, s32[]{:T(128)}) while((s32[]{:T(128)}, f32[3,4,1024]{2,1,0:T(4,128)S(1)}, f32[4,1024]{1,0:T(4,128)S(1)}, s32[]{:T(128)}, ...), condition=%wide.region_6.7_spmd.clone, body=%wide.region_5.6_spmd.clone.sunk | while | flops 61444 | bytes 229491 | solution.py:28
  71.9 0.7 multiply_select_fusion.5
  72.7 0.8 fusion.30
  73.5 0.7 multiply_select_fusion.5
  74.3 0.8 fusion.30
  75.1 0.7 multiply_select_fusion.5
  75.9 0.8 fusion.30
  76.7 0.7 multiply_select_fusion.5
  77.4 0.8 fusion.30
  78.3 0.7 multiply_select_fusion.5
  79.0 0.8 fusion.30
  79.9 0.7 multiply_select_fusion.5
  80.6 0.8 fusion.30
  81.5 0.7 multiply_select_fusion.5
  82.2 0.8 fusion.30
  83.1 0.7 multiply_select_fusion.5
  83.8 0.8 fusion.30
  84.7 0.7 multiply_select_fusion.5
  85.4 0.8 fusion.30
  86.3 0.7 multiply_select_fusion.5
  87.0 0.8 fusion.30
  87.9 0.7 multiply_select_fusion.5
  88.6 0.8 fusion.30
  89.5 0.7 multiply_select_fusion.5
  90.2 0.8 fusion.30
  91.0 0.7 multiply_select_fusion.5
  91.8 0.8 fusion.30
  92.6 0.7 multiply_select_fusion.5
  93.4 0.8 fusion.30
  94.2 0.7 multiply_select_fusion.5
  95.0 0.8 fusion.30
  95.8 0.3 reduce_window_sum.23
  96.2 0.4 copy-done.6
  96.7 0.2 multiply_reduce_fusion
  96.9 0.5 copy-done.16
  97.4 0.7 copy-done.12
  98.2 20.0 %collective-permute-start.1 = (f32[4,1,8,1024]{3,2,1,0:T(8,128)S(1)}, f32[4,1,8,1024]{3,2,1,0:T(8,128)S(1)}, u32[]{:S(2)}, u32[]{:S(2)}) collective-permute-start(f32[4,1,8,1024]{3,2,1,0:T(8,128)S(1)} %slice.64), channel_id=1, source_target_pairs={{0,16},{16,32},{32,48},{48,64},{64,80},{80,96},{96,112},{112,128},... | collective-permute-start | bytes 393224 | tf_op jit(solution)/shard_map/ppermute | solution.py:51
  118.2 0.1 fusion.27
  118.4 1.4 %collective-permute-start.3 = (f32[4,6,1,1024]{3,1,2,0:T(8,128)S(1)}, f32[4,6,1,1024]{3,1,2,0:T(8,128)S(1)}, u32[]{:S(2)}, u32[]{:S(2)}) collective-permute-start(f32[4,6,1,1024]{3,1,2,0:T(8,128)S(1)} %copy.23), channel_id=1, source_target_pairs={{1,0},{2,1},{3,2},{4,3},{5,4},{6,5},{7,6},{8,7},{9,8},{10,9},{11,1... | collective-permute-start | bytes 294920 | tf_op jit(solution)/shard_map/ppermute | solution.py:41
  119.9 4.4 %collective-permute-start.4 = (f32[4,6,1,1024]{3,1,2,0:T(8,128)S(1)}, f32[4,6,1,1024]{3,1,2,0:T(8,128)S(1)}, u32[]{:S(2)}, u32[]{:S(2)}) collective-permute-start(f32[4,6,1,1024]{3,1,2,0:T(8,128)S(1)} %copy.25), channel_id=1, source_target_pairs={{0,1},{1,2},{2,3},{3,4},{4,5},{5,6},{6,7},{7,8},{8,9},{9,10},{10,1... | collective-permute-start | bytes 294920 | tf_op jit(solution)/shard_map/ppermute | solution.py:39
  124.3 0.2 collective-permute-done.3
  124.5 0.1 copy.24
  124.6 1.6 %collective-permute-done.4 = f32[4,6,1,1024]{3,1,2,0:T(8,128)S(1)} collective-permute-done((f32[4,6,1,1024]{3,1,2,0:T(8,128)S(1)}, f32[4,6,1,1024]{3,1,2,0:T(8,128)S(1)}, u32[]{:S(2)}, u32[]{:S(2)}) %collective-permute-start.4) | collective-permute-done | bytes 98336 | tf_op jit(solution)/shard_map/ppermute | solution.py:39
  126.2 0.1 copy.26
  126.4 1.9 %divide_subtract_fusion = (f32[4,4,8,1024]{3,2,1,0:T(8,128)}, f32[4,4,8,1024]{3,2,1,0:T(8,128)}, f32[4,4,8,1024]{3,2,1,0:T(8,128)}) fusion(f32[4,4,8,1024]{3,2,1,0:T(8,128)S(1)} %copy-done, f32[4,4,8,1024]{3,2,1,0:T(8,128)S(1)} %copy-done.9, f32[4,4,8,1024]{3,2,1,0:T(8,128)S(1)} %copy-done.10, f32[4,6,8,1024]{3,2,1,0:T(8,128)S(1)} %constant_dynamic-update-slice_fusion, ...), kind=kLoop, calls=%fused_computation.28 | loop fusion | flops 3801088 | bytes 5455872 | tf_op jit(solution)/shard_map/sub | solution.py:122
  (80 shorter events, 1.4 us)
Async XLA Ops:
  0.6 11.3 %copy-start = (f32[4,4,8,1024]{3,2,1,0:T(8,128)S(1)}, f32[4,4,8,1024]{3,2,1,0:T(8,128)}, u32[]{:S(2)}) copy-start(f32[4,4,8,1024]{3,2,1,0:T(8,128)} %param.10) | copy-start | bytes 1572868
  1.7 9.6 %collective-permute-start = (f32[4,1,8,1024]{3,2,1,0:T(8,128)S(1)}, f32[4,1,8,1024]{3,2,1,0:T(8,128)S(1)}, u32[]{:S(2)}, u32[]{:S(2)}) collective-permute-start(f32[4,1,8,1024]{3,2,1,0:T(8,128)S(1)} %get-tuple-element.315), channel_id=1, source_target_pairs={{16,0},{32,16},{48,32},{64,48},{80,64},{96,80},{112,96},{128,112},... | collective-permute-start | bytes 393224 | tf_op jit(solution)/shard_map/ppermute | solution.py:41
  4.3 5.8 %copy-start.17 = (s32[1,1,128]{2,1,0:T(1,128)S(1)}, s32[1,1,128]{2,1,0:T(1,128)}, u32[]{:S(2)}) copy-start(s32[1,1,128]{2,1,0:T(1,128)} %param.14) | copy-start | bytes 1540
  4.3 7.0 %collective-permute-start.2 = (f32[4,1,8,1024]{3,2,1,0:T(8,128)S(1)}, f32[4,1,8,1024]{3,2,1,0:T(8,128)S(1)}, u32[]{:S(2)}, u32[]{:S(2)}) collective-permute-start(f32[4,1,8,1024]{3,2,1,0:T(8,128)S(1)} %get-tuple-element.316), channel_id=1, source_target_pairs={{0,16},{16,32},{32,48},{48,64},{64,80},{80,96},{96,112},{112,128},... | collective-permute-start | bytes 393224 | tf_op jit(solution)/shard_map/ppermute | solution.py:39
  10.1 1.9 %copy-start.11 = (f32[4,1024]{1,0:T(4,128)}, f32[4,1024]{1,0:T(4,128)S(1)}, u32[]{:S(2)}) copy-start(f32[4,1024]{1,0:T(4,128)S(1)} %get-tuple-element.322) | copy-start | bytes 49156
  10.4 1.7 %copy-start.15 = (f32[1024]{0:T(1024)}, f32[1024]{0:T(1024)S(1)}, u32[]{:S(2)}) copy-start(f32[1024]{0:T(1024)S(1)} %broadcast_in_dim.13) | copy-start | bytes 12292
  11.3 0.7 copy-start.7
  11.3 0.7 copy-start.3
  12.3 0.7 copy-start.2
  13.2 33.5 %copy-start.5 = (f32[3,4,1024]{2,1,0:T(4,128)}, f32[3,4,1024]{2,1,0:T(4,128)S(1)}, u32[]{:S(2)}) copy-start(f32[3,4,1024]{2,1,0:T(4,128)S(1)} %get-tuple-element.307) | copy-start | bytes 147460
  95.8 0.8 copy-start.6
  95.8 0.8 copy-start.13
  95.8 0.8 copy-start.14
  96.7 0.7 copy-start.16
  97.4 0.7 copy-start.12
  98.2 26.1 %copy-start.1 = (f32[4,4,8,1024]{3,2,1,0:T(8,128)}, f32[4,4,8,1024]{3,2,1,0:T(8,128)S(1)}, u32[]{:S(2)}) copy-start(f32[4,4,8,1024]{3,2,1,0:T(8,128)S(1)} %fusion.12) | copy-start | bytes 1572868
  98.2 20.0 %copy-start.4 = (f32[4,1,8,1024]{3,2,1,0:T(8,128)S(1)}, f32[4,1,8,1024]{3,2,1,0:T(8,128)}, u32[]{:S(2)}) copy-start(f32[4,1,8,1024]{3,2,1,0:T(8,128)} %copy-done.3) | copy-start | bytes 393220
  98.2 28.1 %collective-permute-start.1 = (f32[4,1,8,1024]{3,2,1,0:T(8,128)S(1)}, f32[4,1,8,1024]{3,2,1,0:T(8,128)S(1)}, u32[]{:S(2)}, u32[]{:S(2)}) collective-permute-start(f32[4,1,8,1024]{3,2,1,0:T(8,128)S(1)} %slice.64), channel_id=1, source_target_pairs={{0,16},{16,32},{32,48},{48,64},{64,80},{80,96},{96,112},{112,128},... | collective-permute-start | bytes 393224 | tf_op jit(solution)/shard_map/ppermute | solution.py:51
  118.4 8.0 %copy-start.10 = (f32[4,4,8,1024]{3,2,1,0:T(8,128)S(1)}, f32[4,4,8,1024]{3,2,1,0:T(8,128)}, u32[]{:S(2)}) copy-start(f32[4,4,8,1024]{3,2,1,0:T(8,128)} %param.12) | copy-start | bytes 1572868
  118.4 6.1 %collective-permute-start.3 = (f32[4,6,1,1024]{3,1,2,0:T(8,128)S(1)}, f32[4,6,1,1024]{3,1,2,0:T(8,128)S(1)}, u32[]{:S(2)}, u32[]{:S(2)}) collective-permute-start(f32[4,6,1,1024]{3,1,2,0:T(8,128)S(1)} %copy.23), channel_id=1, source_target_pairs={{1,0},{2,1},{3,2},{4,3},{5,4},{6,5},{7,6},{8,7},{9,8},{10,9},{11,1... | collective-permute-start | bytes 294920 | tf_op jit(solution)/shard_map/ppermute | solution.py:41
  119.9 6.5 %copy-start.9 = (f32[4,4,8,1024]{3,2,1,0:T(8,128)S(1)}, f32[4,4,8,1024]{3,2,1,0:T(8,128)}, u32[]{:S(2)}) copy-start(f32[4,4,8,1024]{3,2,1,0:T(8,128)} %param.11) | copy-start | bytes 1572868
  119.9 6.3 %collective-permute-start.4 = (f32[4,6,1,1024]{3,1,2,0:T(8,128)S(1)}, f32[4,6,1,1024]{3,1,2,0:T(8,128)S(1)}, u32[]{:S(2)}, u32[]{:S(2)}) collective-permute-start(f32[4,6,1,1024]{3,1,2,0:T(8,128)S(1)} %copy.25), channel_id=1, source_target_pairs={{0,1},{1,2},{2,3},{3,4},{4,5},{5,6},{6,7},{7,8},{8,9},{9,10},{10,1... | collective-permute-start | bytes 294920 | tf_op jit(solution)/shard_map/ppermute | solution.py:39
  124.3 2.1 %copy-start.8 = (f32[4,1,8,1024]{3,2,1,0:T(8,128)S(1)}, f32[4,1,8,1024]{3,2,1,0:T(8,128)}, u32[]{:S(2)}) copy-start(f32[4,1,8,1024]{3,2,1,0:T(8,128)} %copy-done.7) | copy-start | bytes 393220
  124.3 2.0 %slice-start = ((f32[4,4,8,1024]{3,2,1,0:T(8,128)}), f32[4,3,8,1024]{3,2,1,0:T(8,128)S(1)}, s32[]{:S(2)}) async-start(f32[4,4,8,1024]{3,2,1,0:T(8,128)} %copy-done.1), calls=%async_computation | async-start | bytes 786432 | tf_op jit(solution)/shard_map/slice | solution.py:110
where the time goes:
time: 131 us; the launch traced here: 128 us
  blocking collectives  54.2 us (41%)
  starting transfers between devices  33.5 us (26%)
  other arithmetic  30 us (23%)
  local copies, waits for them, and re-layouts  6.14 us (5%)
  waiting for transfers between devices  2.72 us (2%)
    all_gather x2, blocking collectives, carried_in_2(): pieces = jax.tree.map(lambda part: lax.all_gather(part, axis), value)  54.2 us
    select_n x60, other arithmetic, lap(): jnp.where(position < mine, new, old)  24.5 us
    ppermute x1, starting transfers between devices, passed_along(): return lax.ppermute(block, axis, route)  20 us
    ppermute x2, starting transfers between devices, with_halo(): lax.ppermute(tail, axis, [(i, (i + 1) % count) for i in range(ends)])  9.49 us
    ppermute x2, starting transfers between devices, with_halo(): lax.ppermute(head, axis, [((i + 1) % count, i) for i in range(ends)])  4.01 us
    unnamed x37, local copies, waits for them, and re-layouts  2.86 us
  transfers between devices with their start and end apart: 5, of which 3 were waited for; matrix products, arithmetic and copies ran while one was open for 1% of the time, Pallas kernels for 0%

commit v1 on v0

--- a/solution.py
+++ b/solution.py
@@ -59,6 +59,27 @@
     return (later[0] + later[1][None] * earlier[0], later[1] * earlier[1])
 
 
+def over(front, back):
+    return jnp.concatenate([front[:-1] + front[-1:] * back[:-1], front[-1:] * back[-1:]], axis=0)
+
+
+def butterfly_scan(seg_colour, seg_trans, axis):
+    count, mine = (lax.axis_size(axis), lax.axis_index(axis))
+    block = jnp.concatenate([seg_colour, seg_trans[None]], axis=0)
+    blank = jnp.concatenate([jnp.zeros_like(seg_colour), jnp.ones_like(seg_trans)[None]], axis=0)
+    prefix, suffix = (blank, blank)
+    step = 1
+    while step < count:
+        other = lax.ppermute(block, axis, [(i, i ^ step) for i in range(count)])
+        upper = (mine & step) != 0
+        joined = over(jnp.where(upper, other, block), jnp.where(upper, block, other))
+        prefix = jnp.where(upper, over(other, prefix), prefix)
+        suffix = jnp.where(upper, suffix, over(suffix, other))
+        block = joined
+        step *= 2
+    return (prefix[:-1], prefix[-1], suffix[:-1], suffix[-1])
+
+
 def render(rows, after_rows, shares, occ, target, total_depth):
     scale = 4.0 / total_depth
     features = (1.0 - shares) * rows + shares * after_rows
@@ -71,13 +92,19 @@
     weighted = weight[None] * colour
     seg_colour = jnp.sum(weighted, axis=2)
     seg_trans = jnp.exp(-jnp.sum(sigma, axis=1))
-    blank = (jnp.zeros_like(seg_colour), jnp.ones_like(seg_trans))
-    front_colour, front_trans = carried_in_2(
-        (seg_colour, seg_trans), "depth", front_combine, blank, False
-    )
-    back_colour, back_trans = carried_in_2(
-        (seg_colour, seg_trans), "depth", back_combine, blank, True
-    )
+    count = lax.axis_size("depth")
+    if count & (count - 1) == 0:
+        front_colour, front_trans, back_colour, back_trans = butterfly_scan(
+            seg_colour, seg_trans, "depth"
+        )
+    else:
+        blank = (jnp.zeros_like(seg_colour), jnp.ones_like(seg_trans))
+        front_colour, front_trans = carried_in_2(
+            (seg_colour, seg_trans), "depth", front_combine, blank, False
+        )
+        back_colour, back_trans = carried_in_2(
+            (seg_colour, seg_trans), "depth", back_combine, blank, True
+        )
     behind = back_colour + back_trans[None]
     pixel = front_colour + front_trans[None] * (seg_colour + seg_trans[None] * behind)
     pixel_grad = 0.5 * total_depth * (pixel - target)

time: 131 us -> 76.8 us (0.59)
  the two profiles are of different devices: /device:TPU:7 before, /device:TPU:239 now
where the time goes in v1:
time: 76.8 us; the launch traced here: 76.3 us
  starting transfers between devices  37.5 us (49%)
  waiting for transfers between devices  30.6 us (40%)
  other arithmetic  4.59 us (6%)
  local copies, waits for them, and re-layouts  2.44 us (3%)
  between operations  1.17 us (2%)
    ppermute x4, waiting for transfers between devices, butterfly_scan(): other = lax.ppermute(block, axis, [(i, i ^ step) for i in range(count)])  24.7 us
    ppermute x4, starting transfers between devices, butterfly_scan(): other = lax.ppermute(block, axis, [(i, i ^ step) for i in range(count)])  14.5 us
    ppermute x2, starting transfers between devices, with_halo(): lax.ppermute(tail, axis, [(i, (i + 1) % count) for i in range(ends)])  12.3 us
    ppermute x1, starting transfers between devices, passed_along(): return lax.ppermute(block, axis, route)  6.24 us
    ppermute x2, waiting for transfers between devices, with_halo(): lax.ppermute(head, axis, [((i + 1) % count, i) for i in range(ends)])  4.85 us
    ppermute x2, starting transfers between devices, with_halo(): lax.ppermute(head, axis, [((i + 1) % count, i) for i in range(ends)])  4.5 us
    sub x1, other arithmetic, body(): grid - learn_rate * (new_first / corr_one) / (jnp.sqrt(new_second / corr_...  1.91 us
  transfers between devices with their start and end apart: 9, of which 6 were waited for; matrix products, arithmetic and copies ran while one was open for 2% of the time, Pallas kernels for 0%

profile of v1, /device:TPU:239, one launch (start us, length us, event | category | flops | bytes accessed | tf_op | source)
XLA Modules:
  0.0 76.3 jit_solution(12795442582267222582)
XLA Ops:
  0.6 0.0 copy-start
  0.6 1.0 %fusion.37 = (f32[4,1,8,1024]{3,2,1,0:T(8,128)S(1)}, f32[4,1,8,1024]{3,2,1,0:T(8,128)S(1)}) fusion(f32[4,4,8,1024]{3,2,1,0:T(8,128)} %param.6), kind=kLoop, calls=%fused_computation.113 | loop fusion | bytes 524288 | tf_op jit(solution)/shard_map/slice | solution.py:35
  1.7 2.6 %collective-permute-start = (f32[4,1,8,1024]{3,2,1,0:T(8,128)S(1)}, f32[4,1,8,1024]{3,2,1,0:T(8,128)S(1)}, u32[]{:S(2)}, u32[]{:S(2)}) collective-permute-start(f32[4,1,8,1024]{3,2,1,0:T(8,128)S(1)} %get-tuple-element.21), channel_id=1, source_target_pairs={{16,0},{32,16},{48,32},{64,48},{80,64},{96,80},{112,96},{128,112},... | collective-permute-start | bytes 393224 | tf_op jit(solution)/shard_map/ppermute | solution.py:41
  4.3 0.0 copy-start.5
  4.3 5.1 %collective-permute-start.6 = (f32[4,1,8,1024]{3,2,1,0:T(8,128)S(1)}, f32[4,1,8,1024]{3,2,1,0:T(8,128)S(1)}, u32[]{:S(2)}, u32[]{:S(2)}) collective-permute-start(f32[4,1,8,1024]{3,2,1,0:T(8,128)S(1)} %get-tuple-element.22), channel_id=1, source_target_pairs={{0,16},{16,32},{32,48},{48,64},{64,80},{80,96},{96,112},{112,128},... | collective-permute-start | bytes 393224 | tf_op jit(solution)/shard_map/ppermute | solution.py:39
  9.4 0.7 broadcast_subtract_fusion
  10.1 0.0 copy-done.5
  10.1 0.1 broadcast_in_dim.8
  10.2 0.1 broadcast_in_dim.9
  10.3 1.0 %collective-permute-done.6 = f32[4,1,8,1024]{3,2,1,0:T(8,128)S(1)} collective-permute-done((f32[4,1,8,1024]{3,2,1,0:T(8,128)S(1)}, f32[4,1,8,1024]{3,2,1,0:T(8,128)S(1)}, u32[]{:S(2)}, u32[]{:S(2)}) %collective-permute-start.6) | collective-permute-done | bytes 131104 | tf_op jit(solution)/shard_map/ppermute | solution.py:39
  11.3 0.0 collective-permute-done
  11.3 0.0 copy-done
  11.3 0.1 fusion.10
  11.4 0.1 fusion.34
  11.6 0.1 reduce_window_sum.22
  11.7 0.1 fusion.29
  11.8 0.2 fusion.33
  12.0 0.3 reduce_window_sum.23
  12.4 1.9 %collective-permute-start.1 = (f32[4,4,1024]{2,1,0:T(4,128)S(1)}, f32[4,4,1024]{2,1,0:T(4,128)S(1)}, u32[]{:S(2)}, u32[]{:S(2)}) collective-permute-start(f32[4,4,1024]{2,1,0:T(4,128)S(1)} %pad_maximum_fusion.5), channel_id=1, source_target_pairs={{0,1},{1,0},{2,3},{3,2},{4,5},{5,4},{6,7},{7,6},{8,9},{9,8},{10,11... | collective-permute-start | bytes 196616 | tf_op jit(solution)/shard_map/ppermute | solution.py:73
  14.3 0.0 copy-start.3
  14.3 4.0 %collective-permute-done.1 = f32[4,4,1024]{2,1,0:T(4,128)S(1)} collective-permute-done((f32[4,4,1024]{2,1,0:T(4,128)S(1)}, f32[4,4,1024]{2,1,0:T(4,128)S(1)}, u32[]{:S(2)}, u32[]{:S(2)}) %collective-permute-start.1) | collective-permute-done | bytes 65568 | tf_op jit(solution)/shard_map/ppermute | solution.py:73
  18.3 0.0 copy-done.3
  18.5 1.9 %collective-permute-start.2 = (f32[4,4,1024]{2,1,0:T(4,128)S(1)}, f32[4,4,1024]{2,1,0:T(4,128)S(1)}, u32[]{:S(2)}, u32[]{:S(2)}) collective-permute-start(f32[4,4,1024]{2,1,0:T(4,128)S(1)} %pad_maximum_fusion.6), channel_id=1, source_target_pairs={{0,2},{1,3},{2,0},{3,1},{4,6},{5,7},{6,4},{7,5},{8,10},{9,11},{10,... | collective-permute-start | bytes 196616 | tf_op jit(solution)/shard_map/ppermute | solution.py:73
  20.5 5.5 %collective-permute-done.2 = f32[4,4,1024]{2,1,0:T(4,128)S(1)} collective-permute-done((f32[4,4,1024]{2,1,0:T(4,128)S(1)}, f32[4,4,1024]{2,1,0:T(4,128)S(1)}, u32[]{:S(2)}, u32[]{:S(2)}) %collective-permute-start.2) | collective-permute-done | bytes 65568 | tf_op jit(solution)/shard_map/ppermute | solution.py:73
  26.1 1.9 %collective-permute-start.3 = (f32[4,4,1024]{2,1,0:T(4,128)S(1)}, f32[4,4,1024]{2,1,0:T(4,128)S(1)}, u32[]{:S(2)}, u32[]{:S(2)}) collective-permute-start(f32[4,4,1024]{2,1,0:T(4,128)S(1)} %pad_maximum_fusion.7), channel_id=1, source_target_pairs={{0,4},{1,5},{2,6},{3,7},{4,0},{5,1},{6,2},{7,3},{8,12},{9,13},{10,... | collective-permute-start | bytes 196616 | tf_op jit(solution)/shard_map/ppermute | solution.py:73
  28.1 9.7 %collective-permute-done.3 = f32[4,4,1024]{2,1,0:T(4,128)S(1)} collective-permute-done((f32[4,4,1024]{2,1,0:T(4,128)S(1)}, f32[4,4,1024]{2,1,0:T(4,128)S(1)}, u32[]{:S(2)}, u32[]{:S(2)}) %collective-permute-start.3) | collective-permute-done | bytes 65568 | tf_op jit(solution)/shard_map/ppermute | solution.py:73
  38.0 8.7 %collective-permute-start.4 = (f32[4,4,1024]{2,1,0:T(4,128)S(1)}, f32[4,4,1024]{2,1,0:T(4,128)S(1)}, u32[]{:S(2)}, u32[]{:S(2)}) collective-permute-start(f32[4,4,1024]{2,1,0:T(4,128)S(1)} %pad_maximum_fusion.8), channel_id=1, source_target_pairs={{0,8},{1,9},{2,10},{3,11},{4,12},{5,13},{6,14},{7,15},{8,0},{9,1},... | collective-permute-start | bytes 196616 | tf_op jit(solution)/shard_map/ppermute | solution.py:73
  46.8 5.4 %collective-permute-done.4 = f32[4,4,1024]{2,1,0:T(4,128)S(1)} collective-permute-done((f32[4,4,1024]{2,1,0:T(4,128)S(1)}, f32[4,4,1024]{2,1,0:T(4,128)S(1)}, u32[]{:S(2)}, u32[]{:S(2)}) %collective-permute-start.4) | collective-permute-done | bytes 65568 | tf_op jit(solution)/shard_map/ppermute | solution.py:73
  52.4 0.1 multiply_bitcast_fusion.1
  52.4 0.0 copy-start.4
  52.5 0.7 copy-done.4
  53.3 0.2 multiply_reduce_fusion
  53.5 0.1 fusion.19
  53.6 0.1 fusion.11
  53.6 6.2 %collective-permute-start.5 = (f32[4,1,8,1024]{3,2,1,0:T(8,128)S(1)}, f32[4,1,8,1024]{3,2,1,0:T(8,128)S(1)}, u32[]{:S(2)}, u32[]{:S(2)}) collective-permute-start(f32[4,1,8,1024]{3,2,1,0:T(8,128)S(1)} %slice.263), channel_id=1, source_target_pairs={{0,16},{16,32},{32,48},{48,64},{64,80},{80,96},{96,112},{112,128},... | collective-permute-start | bytes 393224 | tf_op jit(solution)/shard_map/ppermute | solution.py:51
  59.9 0.1 fusion.36
  60.1 7.2 %collective-permute-start.8 = (f32[4,6,1,1024]{3,1,2,0:T(8,128)S(1)}, f32[4,6,1,1024]{3,1,2,0:T(8,128)S(1)}, u32[]{:S(2)}, u32[]{:S(2)}) collective-permute-start(f32[4,6,1,1024]{3,1,2,0:T(8,128)S(1)} %copy.25), channel_id=1, source_target_pairs={{0,1},{1,2},{2,3},{3,4},{4,5},{5,6},{6,7},{7,8},{8,9},{9,10},{10,1... | collective-permute-start | bytes 294920 | tf_op jit(solution)/shard_map/ppermute | solution.py:39
  67.3 1.9 %collective-permute-start.7 = (f32[4,6,1,1024]{3,1,2,0:T(8,128)S(1)}, f32[4,6,1,1024]{3,1,2,0:T(8,128)S(1)}, u32[]{:S(2)}, u32[]{:S(2)}) collective-permute-start(f32[4,6,1,1024]{3,1,2,0:T(8,128)S(1)} %copy.23), channel_id=1, source_target_pairs={{1,0},{2,1},{3,2},{4,3},{5,4},{6,5},{7,6},{8,7},{9,8},{10,9},{11,1... | collective-permute-start | bytes 294920 | tf_op jit(solution)/shard_map/ppermute | solution.py:41
  69.2 0.0 collective-permute-done.8
  69.3 0.0 copy-start.2
  69.3 0.1 copy.26
  69.4 0.0 copy-start.1
  69.4 4.8 %collective-permute-done.7 = f32[4,6,1,1024]{3,1,2,0:T(8,128)S(1)} collective-permute-done((f32[4,6,1,1024]{3,1,2,0:T(8,128)S(1)}, f32[4,6,1,1024]{3,1,2,0:T(8,128)S(1)}, u32[]{:S(2)}, u32[]{:S(2)}) %collective-permute-start.7) | collective-permute-done | bytes 98336 | tf_op jit(solution)/shard_map/ppermute | solution.py:41
  74.2 0.1 copy.24
  74.4 0.0 collective-permute-done.5
  74.4 0.0 copy-done.2
  74.4 0.0 copy-done.1
  74.4 1.9 %divide_subtract_fusion = (f32[4,4,8,1024]{3,2,1,0:T(8,128)}, f32[4,4,8,1024]{3,2,1,0:T(8,128)}, f32[4,4,8,1024]{3,2,1,0:T(8,128)}) fusion(f32[4,4,8,1024]{3,2,1,0:T(8,128)S(1)} %copy-done, f32[4,4,8,1024]{3,2,1,0:T(8,128)S(1)} %copy-done.1, f32[4,4,8,1024]{3,2,1,0:T(8,128)S(1)} %copy-done.2, f32[4,6,8,1024]{3,2,1,0:T(8,128)S(1)} %constant_dynamic-update-slice_fusion, ...), kind=kLoop, calls=%fused_computation.20 | loop fusion | flops 3801088 | bytes 5455872 | tf_op jit(solution)/shard_map/sub | solution.py:149
  (38 shorter events, 0.8 us)
Async XLA Ops:
  0.6 10.7 %copy-start = (f32[4,4,8,1024]{3,2,1,0:T(8,128)S(1)}, f32[4,4,8,1024]{3,2,1,0:T(8,128)}, u32[]{:S(2)}) copy-start(f32[4,4,8,1024]{3,2,1,0:T(8,128)} %param.6) | copy-start | bytes 1572868
  1.7 9.6 %collective-permute-start = (f32[4,1,8,1024]{3,2,1,0:T(8,128)S(1)}, f32[4,1,8,1024]{3,2,1,0:T(8,128)S(1)}, u32[]{:S(2)}, u32[]{:S(2)}) collective-permute-start(f32[4,1,8,1024]{3,2,1,0:T(8,128)S(1)} %get-tuple-element.21), channel_id=1, source_target_pairs={{16,0},{32,16},{48,32},{64,48},{80,64},{96,80},{112,96},{128,112},... | collective-permute-start | bytes 393224 | tf_op jit(solution)/shard_map/ppermute | solution.py:41
  4.3 5.8 %copy-start.5 = (s32[1,1,128]{2,1,0:T(1,128)S(1)}, s32[1,1,128]{2,1,0:T(1,128)}, u32[]{:S(2)}) copy-start(s32[1,1,128]{2,1,0:T(1,128)} %param.10) | copy-start | bytes 1540
  4.3 7.0 %collective-permute-start.6 = (f32[4,1,8,1024]{3,2,1,0:T(8,128)S(1)}, f32[4,1,8,1024]{3,2,1,0:T(8,128)S(1)}, u32[]{:S(2)}, u32[]{:S(2)}) collective-permute-start(f32[4,1,8,1024]{3,2,1,0:T(8,128)S(1)} %get-tuple-element.22), channel_id=1, source_target_pairs={{0,16},{16,32},{32,48},{48,64},{64,80},{80,96},{96,112},{112,128},... | collective-permute-start | bytes 393224 | tf_op jit(solution)/shard_map/ppermute | solution.py:39
  12.4 6.0 %collective-permute-start.1 = (f32[4,4,1024]{2,1,0:T(4,128)S(1)}, f32[4,4,1024]{2,1,0:T(4,128)S(1)}, u32[]{:S(2)}, u32[]{:S(2)}) collective-permute-start(f32[4,4,1024]{2,1,0:T(4,128)S(1)} %pad_maximum_fusion.5), channel_id=1, source_target_pairs={{0,1},{1,0},{2,3},{3,2},{4,5},{5,4},{6,7},{7,6},{8,9},{9,8},{10,11... | collective-permute-start | bytes 196616 | tf_op jit(solution)/shard_map/ppermute | solution.py:73
  14.3 4.1 %copy-start.3 = (f32[4,4,1024]{2,1,0:T(4,128)S(1)}, f32[4,4,1024]{2,1,0:T(4,128)}, u32[]{:S(2)}) copy-start(f32[4,4,1024]{2,1,0:T(4,128)} %constant.14.clone.1) | copy-start | bytes 196612
  18.5 7.5 %collective-permute-start.2 = (f32[4,4,1024]{2,1,0:T(4,128)S(1)}, f32[4,4,1024]{2,1,0:T(4,128)S(1)}, u32[]{:S(2)}, u32[]{:S(2)}) collective-permute-start(f32[4,4,1024]{2,1,0:T(4,128)S(1)} %pad_maximum_fusion.6), channel_id=1, source_target_pairs={{0,2},{1,3},{2,0},{3,1},{4,6},{5,7},{6,4},{7,5},{8,10},{9,11},{10,... | collective-permute-start | bytes 196616 | tf_op jit(solution)/shard_map/ppermute | solution.py:73
  26.1 11.8 %collective-permute-start.3 = (f32[4,4,1024]{2,1,0:T(4,128)S(1)}, f32[4,4,1024]{2,1,0:T(4,128)S(1)}, u32[]{:S(2)}, u32[]{:S(2)}) collective-permute-start(f32[4,4,1024]{2,1,0:T(4,128)S(1)} %pad_maximum_fusion.7), channel_id=1, source_target_pairs={{0,4},{1,5},{2,6},{3,7},{4,0},{5,1},{6,2},{7,3},{8,12},{9,13},{10,... | collective-permute-start | bytes 196616 | tf_op jit(solution)/shard_map/ppermute | solution.py:73
  38.0 14.3 %collective-permute-start.4 = (f32[4,4,1024]{2,1,0:T(4,128)S(1)}, f32[4,4,1024]{2,1,0:T(4,128)S(1)}, u32[]{:S(2)}, u32[]{:S(2)}) collective-permute-start(f32[4,4,1024]{2,1,0:T(4,128)S(1)} %pad_maximum_fusion.8), channel_id=1, source_target_pairs={{0,8},{1,9},{2,10},{3,11},{4,12},{5,13},{6,14},{7,15},{8,0},{9,1},... | collective-permute-start | bytes 196616 | tf_op jit(solution)/shard_map/ppermute | solution.py:73
  52.4 0.8 %copy-start.4 = (f32[3,4,1024]{2,1,0:T(4,128)S(1)}, f32[3,4,1024]{2,1,0:T(4,128)}, u32[]{:S(2)}) copy-start(f32[3,4,1024]{2,1,0:T(4,128)} %param.11) | copy-start | bytes 147460
  53.6 20.7 %collective-permute-start.5 = (f32[4,1,8,1024]{3,2,1,0:T(8,128)S(1)}, f32[4,1,8,1024]{3,2,1,0:T(8,128)S(1)}, u32[]{:S(2)}, u32[]{:S(2)}) collective-permute-start(f32[4,1,8,1024]{3,2,1,0:T(8,128)S(1)} %slice.263), channel_id=1, source_target_pairs={{0,16},{16,32},{32,48},{48,64},{64,80},{80,96},{96,112},{112,128},... | collective-permute-start | bytes 393224 | tf_op jit(solution)/shard_map/ppermute | solution.py:51
  60.1 9.2 %collective-permute-start.8 = (f32[4,6,1,1024]{3,1,2,0:T(8,128)S(1)}, f32[4,6,1,1024]{3,1,2,0:T(8,128)S(1)}, u32[]{:S(2)}, u32[]{:S(2)}) collective-permute-start(f32[4,6,1,1024]{3,1,2,0:T(8,128)S(1)} %copy.25), channel_id=1, source_target_pairs={{0,1},{1,2},{2,3},{3,4},{4,5},{5,6},{6,7},{7,8},{8,9},{9,10},{10,1... | collective-permute-start | bytes 294920 | tf_op jit(solution)/shard_map/ppermute | solution.py:39
  67.3 6.9 %collective-permute-start.7 = (f32[4,6,1,1024]{3,1,2,0:T(8,128)S(1)}, f32[4,6,1,1024]{3,1,2,0:T(8,128)S(1)}, u32[]{:S(2)}, u32[]{:S(2)}) collective-permute-start(f32[4,6,1,1024]{3,1,2,0:T(8,128)S(1)} %copy.23), channel_id=1, source_target_pairs={{1,0},{2,1},{3,2},{4,3},{5,4},{6,5},{7,6},{8,7},{9,8},{10,9},{11,1... | collective-permute-start | bytes 294920 | tf_op jit(solution)/shard_map/ppermute | solution.py:41
  69.3 5.1 %copy-start.2 = (f32[4,4,8,1024]{3,2,1,0:T(8,128)S(1)}, f32[4,4,8,1024]{3,2,1,0:T(8,128)}, u32[]{:S(2)}) copy-start(f32[4,4,8,1024]{3,2,1,0:T(8,128)} %param.8) | copy-start | bytes 1572868
  69.4 5.0 %copy-start.1 = (f32[4,4,8,1024]{3,2,1,0:T(8,128)S(1)}, f32[4,4,8,1024]{3,2,1,0:T(8,128)}, u32[]{:S(2)}) copy-start(f32[4,4,8,1024]{3,2,1,0:T(8,128)} %param.7) | copy-start | bytes 1572868

commit v2 on v1

--- a/solution.py
+++ b/solution.py
@@ -80,6 +80,27 @@
     return (prefix[:-1], prefix[-1], suffix[:-1], suffix[-1])
 
 
+def exchanged_scan(seg_colour, seg_trans, axis):
+    count = lax.axis_size(axis)
+    shape = seg_trans.shape
+    block = jnp.concatenate([seg_colour, seg_trans[None]], axis=0).reshape(4, count, -1)
+    mine = lax.all_to_all(block, axis, 1, 1, tiled=True)
+    inclusive = lax.associative_scan(over, mine, axis=1)
+    flipped = jnp.flip(mine, axis=1)
+    behind_incl = jnp.flip(lax.associative_scan(lambda a, b: over(b, a), flipped, axis=1), axis=1)
+    blank = jnp.concatenate(
+        [jnp.zeros_like(mine[:-1, :1]), jnp.ones_like(mine[-1:, :1])], axis=0
+    )
+    prefix = jnp.concatenate([blank, inclusive[:, :-1]], axis=1)
+    suffix = jnp.concatenate([behind_incl[:, 1:], blank], axis=1)
+    total = inclusive[:, -1:]
+    pixel = jnp.broadcast_to(total[:-1] + total[-1:], suffix[:-1].shape)
+    behind = suffix[:-1] + suffix[-1:]
+    answer = jnp.concatenate([prefix[-1:], pixel, behind], axis=0)
+    answer = lax.all_to_all(answer, axis, 1, 1, tiled=True).reshape(7, *shape)
+    return (answer[0], answer[1:4], answer[4:7])
+
+
 def render(rows, after_rows, shares, occ, target, total_depth):
     scale = 4.0 / total_depth
     features = (1.0 - shares) * rows + shares * after_rows
@@ -93,7 +114,10 @@
     seg_colour = jnp.sum(weighted, axis=2)
     seg_trans = jnp.exp(-jnp.sum(sigma, axis=1))
     count = lax.axis_size("depth")
-    if count & (count - 1) == 0:
+    pixels = seg_trans.size
+    if pixels % count == 0 and (pixels // count) % 128 == 0:
+        front_trans, pixel, behind = exchanged_scan(seg_colour, seg_trans, "depth")
+    elif count & (count - 1) == 0:
         front_colour, front_trans, back_colour, back_trans = butterfly_scan(
             seg_colour, seg_trans, "depth"
         )
@@ -105,8 +129,9 @@
         back_colour, back_trans = carried_in_2(
             (seg_colour, seg_trans), "depth", back_combine, blank, True
         )
-    behind = back_colour + back_trans[None]
-    pixel = front_colour + front_trans[None] * (seg_colour + seg_trans[None] * behind)
+    if not (pixels % count == 0 and (pixels // count) % 128 == 0):
+        behind = back_colour + back_trans[None]
+        pixel = front_colour + front_trans[None] * (seg_colour + seg_trans[None] * behind)
     pixel_grad = 0.5 * total_depth * (pixel - target)
     upto = jnp.cumsum(weighted, axis=2)
     remain = seg_colour[:, :, None, :] - upto + (seg_trans[None] * behind)[:, :, None, :]

time: 76.8 us -> 79.3 us (1.033)
  the two profiles are of different devices: /device:TPU:239 before, /device:TPU:24 now
where the time goes in v2:
time: 79.3 us; the launch traced here: 78.8 us
  blocking collectives  27.8 us (35%)
  waiting for transfers between devices  23.9 us (30%)
  starting transfers between devices  15.8 us (20%)
  other arithmetic  5.37 us (7%)
  local copies, waits for them, and re-layouts  4.34 us (5%)
  between operations  1.51 us (2%)
    all_to_all x1, blocking collectives, exchanged_scan(): mine = lax.all_to_all(block, axis, 1, 1, tiled=True)  27.8 us
    all_to_all x1, waiting for transfers between devices, exchanged_scan(): answer = lax.all_to_all(answer, axis, 1, 1, tiled=True).reshape(7, *shape)  12.9 us
    ppermute x2, waiting for transfers between devices, with_halo(): lax.ppermute(tail, axis, [(i, (i + 1) % count) for i in range(ends)])  6.71 us
    ppermute x2, starting transfers between devices, with_halo(): lax.ppermute(head, axis, [((i + 1) % count, i) for i in range(ends)])  5.58 us
    ppermute x2, starting transfers between devices, with_halo(): lax.ppermute(tail, axis, [(i, (i + 1) % count) for i in range(ends)])  4.81 us
    ppermute x2, waiting for transfers between devices, with_halo(): lax.ppermute(head, axis, [((i + 1) % count, i) for i in range(ends)])  4.28 us
    all_to_all x1, starting transfers between devices, exchanged_scan(): answer = lax.all_to_all(answer, axis, 1, 1, tiled=True).reshape(7, *shape)  3.51 us
    ppermute x1, starting transfers between devices, passed_along(): return lax.ppermute(block, axis, route)  1.92 us
  transfers between devices with their start and end apart: 6, of which 4 were waited for; matrix products, arithmetic and copies ran while one was open for 2% of the time, Pallas kernels for 0%

profile of v2, /device:TPU:24, one launch (start us, length us, event | category | flops | bytes accessed | tf_op | source)
XLA Modules:
  0.0 78.8 jit_solution(4947608545723568527)
XLA Ops:
  0.6 0.0 copy-start
  0.6 1.0 %fusion.53 = (f32[4,1,8,1024]{3,2,1,0:T(8,128)S(1)}, f32[4,1,8,1024]{3,2,1,0:T(8,128)S(1)}) fusion(f32[4,4,8,1024]{3,2,1,0:T(8,128)} %param.6), kind=kLoop, calls=%fused_computation.151 | loop fusion | bytes 524288 | tf_op jit(solution)/shard_map/slice | solution.py:35
  1.7 4.3 %collective-permute-start = (f32[4,1,8,1024]{3,2,1,0:T(8,128)S(1)}, f32[4,1,8,1024]{3,2,1,0:T(8,128)S(1)}, u32[]{:S(2)}, u32[]{:S(2)}) collective-permute-start(f32[4,1,8,1024]{3,2,1,0:T(8,128)S(1)} %get-tuple-element.26), channel_id=1, source_target_pairs={{16,0},{32,16},{48,32},{64,48},{80,64},{96,80},{112,96},{128,112},... | collective-permute-start | bytes 393224 | tf_op jit(solution)/shard_map/ppermute | solution.py:41
  6.0 0.0 copy-start.5
  6.0 1.9 %collective-permute-start.2 = (f32[4,1,8,1024]{3,2,1,0:T(8,128)S(1)}, f32[4,1,8,1024]{3,2,1,0:T(8,128)S(1)}, u32[]{:S(2)}, u32[]{:S(2)}) collective-permute-start(f32[4,1,8,1024]{3,2,1,0:T(8,128)S(1)} %get-tuple-element.27), channel_id=1, source_target_pairs={{0,16},{16,32},{32,48},{48,64},{64,80},{80,96},{96,112},{112,128},... | collective-permute-start | bytes 393224 | tf_op jit(solution)/shard_map/ppermute | solution.py:39
  7.9 0.7 broadcast_subtract_fusion
  8.6 0.0 copy-done.5
  8.7 0.1 broadcast_in_dim.10
  8.7 0.1 broadcast_in_dim.11
  8.8 5.5 %collective-permute-done.2 = f32[4,1,8,1024]{3,2,1,0:T(8,128)S(1)} collective-permute-done((f32[4,1,8,1024]{3,2,1,0:T(8,128)S(1)}, f32[4,1,8,1024]{3,2,1,0:T(8,128)S(1)}, u32[]{:S(2)}, u32[]{:S(2)}) %collective-permute-start.2) | collective-permute-done | bytes 131104 | tf_op jit(solution)/shard_map/ppermute | solution.py:39
  14.4 0.0 collective-permute-done
  14.4 0.0 copy-done
  14.4 0.1 fusion.10
  14.5 0.1 fusion.50
  14.7 0.1 reduce_window_sum.22
  14.8 0.1 fusion.28
  14.9 0.2 fusion.49
  15.2 27.8 %all_to_all.10 = f32[4,16,256]{2,0,1:T(4,128)S(1)} all-to-all(f32[4,16,256]{2,0,1:T(4,128)S(1)} %copy.40), channel_id=1, replica_groups=mesh['tile'=32,'depth'=16] {'depth'}, dimensions={1} | all-to-all | bytes 131072 | tf_op jit(solution)/shard_map/all_to_all | solution.py:87
  43.7 0.1 pad.66
  43.7 0.1 pad.67
  44.2 0.1 pad.58
  44.2 0.1 pad.59
  44.3 0.1 pad.290
  44.4 0.1 pad.61
  44.7 0.1 pad.60
  44.8 0.1 pad.288
  44.9 0.1 pad.148
  45.0 0.0 copy-start.4
  45.0 0.7 copy-done.4
  45.8 0.7 fusion.18
  46.6 3.5 %all-to-all-start.1 = ((f32[7,16,256]{2,0,1:T(8,128)}), f32[7,16,256]{2,0,1:T(8,128)S(1)}, u32[]{:S(2)}, u32[]{:S(2)}) async-start(f32[7,16,256]{2,0,1:T(8,128)} %fusion.18), calls=%async_computation.1 | async-start | bytes 262144 | tf_op jit(solution)/shard_map/all_to_all | solution.py:100
  50.1 0.3 reduce_window_sum.23
  50.4 12.9 %all-to-all-done.1 = f32[7,16,256]{2,0,1:T(8,128)S(1)} async-done(((f32[7,16,256]{2,0,1:T(8,128)}), f32[7,16,256]{2,0,1:T(8,128)S(1)}, u32[]{:S(2)}, u32[]{:S(2)}) %all-to-all-start.1) | async-done | bytes 114720 | tf_op jit(solution)/shard_map/all_to_all | solution.py:100
  63.4 0.1 multiply_bitcast_fusion.1
  63.6 0.0 copy-start.3
  63.7 0.8 copy-done.3
  64.4 0.2 multiply_reduce_fusion
  64.7 0.1 fusion.21
  64.7 0.1 fusion.11
  64.8 1.9 %collective-permute-start.1 = (f32[4,1,8,1024]{3,2,1,0:T(8,128)S(1)}, f32[4,1,8,1024]{3,2,1,0:T(8,128)S(1)}, u32[]{:S(2)}, u32[]{:S(2)}) collective-permute-start(f32[4,1,8,1024]{3,2,1,0:T(8,128)S(1)} %slice.597), channel_id=1, source_target_pairs={{0,16},{16,32},{32,48},{48,64},{64,80},{80,96},{96,112},{112,128},... | collective-permute-start | bytes 393224 | tf_op jit(solution)/shard_map/ppermute | solution.py:51
  66.7 0.1 fusion.52
  66.9 2.9 %collective-permute-start.4 = (f32[4,6,1,1024]{3,1,2,0:T(8,128)S(1)}, f32[4,6,1,1024]{3,1,2,0:T(8,128)S(1)}, u32[]{:S(2)}, u32[]{:S(2)}) collective-permute-start(f32[4,6,1,1024]{3,1,2,0:T(8,128)S(1)} %copy.45), channel_id=1, source_target_pairs={{0,1},{1,2},{2,3},{3,4},{4,5},{5,6},{6,7},{7,8},{8,9},{9,10},{10,1... | collective-permute-start | bytes 294920 | tf_op jit(solution)/shard_map/ppermute | solution.py:39
  69.8 1.3 %collective-permute-start.3 = (f32[4,6,1,1024]{3,1,2,0:T(8,128)S(1)}, f32[4,6,1,1024]{3,1,2,0:T(8,128)S(1)}, u32[]{:S(2)}, u32[]{:S(2)}) collective-permute-start(f32[4,6,1,1024]{3,1,2,0:T(8,128)S(1)} %copy.43), channel_id=1, source_target_pairs={{1,0},{2,1},{3,2},{4,3},{5,4},{6,5},{7,6},{8,7},{9,8},{10,9},{11,1... | collective-permute-start | bytes 294920 | tf_op jit(solution)/shard_map/ppermute | solution.py:41
  71.1 1.2 %collective-permute-done.4 = f32[4,6,1,1024]{3,1,2,0:T(8,128)S(1)} collective-permute-done((f32[4,6,1,1024]{3,1,2,0:T(8,128)S(1)}, f32[4,6,1,1024]{3,1,2,0:T(8,128)S(1)}, u32[]{:S(2)}, u32[]{:S(2)}) %collective-permute-start.4) | collective-permute-done | bytes 98336 | tf_op jit(solution)/shard_map/ppermute | solution.py:39
  72.3 0.0 copy-start.2
  72.3 0.1 copy.46
  72.4 0.0 copy-start.1
  72.4 4.3 %collective-permute-done.3 = f32[4,6,1,1024]{3,1,2,0:T(8,128)S(1)} collective-permute-done((f32[4,6,1,1024]{3,1,2,0:T(8,128)S(1)}, f32[4,6,1,1024]{3,1,2,0:T(8,128)S(1)}, u32[]{:S(2)}, u32[]{:S(2)}) %collective-permute-start.3) | collective-permute-done | bytes 98336 | tf_op jit(solution)/shard_map/ppermute | solution.py:41
  76.7 0.1 copy.44
  76.8 0.0 collective-permute-done.1
  76.8 0.0 copy-done.2
  76.8 0.0 copy-done.1
  76.9 1.9 %divide_subtract_fusion = (f32[4,4,8,1024]{3,2,1,0:T(8,128)}, f32[4,4,8,1024]{3,2,1,0:T(8,128)}, f32[4,4,8,1024]{3,2,1,0:T(8,128)}) fusion(f32[4,4,8,1024]{3,2,1,0:T(8,128)S(1)} %copy-done, f32[4,4,8,1024]{3,2,1,0:T(8,128)S(1)} %copy-done.1, f32[4,4,8,1024]{3,2,1,0:T(8,128)S(1)} %copy-done.2, f32[4,6,8,1024]{3,2,1,0:T(8,128)S(1)} %constant_dynamic-update-slice_fusion, ...), kind=kLoop, calls=%fused_computation.20 | loop fusion | flops 3801088 | bytes 5455872 | tf_op jit(solution)/shard_map/sub | solution.py:174
  (103 shorter events, 1.3 us)
Async XLA Ops:
  0.6 13.8 %copy-start = (f32[4,4,8,1024]{3,2,1,0:T(8,128)S(1)}, f32[4,4,8,1024]{3,2,1,0:T(8,128)}, u32[]{:S(2)}) copy-start(f32[4,4,8,1024]{3,2,1,0:T(8,128)} %param.6) | copy-start | bytes 1572868
  1.7 12.7 %collective-permute-start = (f32[4,1,8,1024]{3,2,1,0:T(8,128)S(1)}, f32[4,1,8,1024]{3,2,1,0:T(8,128)S(1)}, u32[]{:S(2)}, u32[]{:S(2)}) collective-permute-start(f32[4,1,8,1024]{3,2,1,0:T(8,128)S(1)} %get-tuple-element.26), channel_id=1, source_target_pairs={{16,0},{32,16},{48,32},{64,48},{80,64},{96,80},{112,96},{128,112},... | collective-permute-start | bytes 393224 | tf_op jit(solution)/shard_map/ppermute | solution.py:41
  6.0 2.7 %copy-start.5 = (s32[1,1,128]{2,1,0:T(1,128)S(1)}, s32[1,1,128]{2,1,0:T(1,128)}, u32[]{:S(2)}) copy-start(s32[1,1,128]{2,1,0:T(1,128)} %param.10) | copy-start | bytes 1540
  6.0 8.4 %collective-permute-start.2 = (f32[4,1,8,1024]{3,2,1,0:T(8,128)S(1)}, f32[4,1,8,1024]{3,2,1,0:T(8,128)S(1)}, u32[]{:S(2)}, u32[]{:S(2)}) collective-permute-start(f32[4,1,8,1024]{3,2,1,0:T(8,128)S(1)} %get-tuple-element.27), channel_id=1, source_target_pairs={{0,16},{16,32},{32,48},{48,64},{64,80},{80,96},{96,112},{112,128},... | collective-permute-start | bytes 393224 | tf_op jit(solution)/shard_map/ppermute | solution.py:39
  45.0 0.7 copy-start.4
  46.6 16.8 %all-to-all-start.1 = ((f32[7,16,256]{2,0,1:T(8,128)}), f32[7,16,256]{2,0,1:T(8,128)S(1)}, u32[]{:S(2)}, u32[]{:S(2)}) async-start(f32[7,16,256]{2,0,1:T(8,128)} %fusion.18), calls=%async_computation.1 | async-start | bytes 262144 | tf_op jit(solution)/shard_map/all_to_all | solution.py:100
  63.6 0.8 %copy-start.3 = (f32[3,4,1024]{2,1,0:T(4,128)S(1)}, f32[3,4,1024]{2,1,0:T(4,128)}, u32[]{:S(2)}) copy-start(f32[3,4,1024]{2,1,0:T(4,128)} %param.11) | copy-start | bytes 147460
  64.8 12.0 %collective-permute-start.1 = (f32[4,1,8,1024]{3,2,1,0:T(8,128)S(1)}, f32[4,1,8,1024]{3,2,1,0:T(8,128)S(1)}, u32[]{:S(2)}, u32[]{:S(2)}) collective-permute-start(f32[4,1,8,1024]{3,2,1,0:T(8,128)S(1)} %slice.597), channel_id=1, source_target_pairs={{0,16},{16,32},{32,48},{48,64},{64,80},{80,96},{96,112},{112,128},... | collective-permute-start | bytes 393224 | tf_op jit(solution)/shard_map/ppermute | solution.py:51
  66.9 5.4 %collective-permute-start.4 = (f32[4,6,1,1024]{3,1,2,0:T(8,128)S(1)}, f32[4,6,1,1024]{3,1,2,0:T(8,128)S(1)}, u32[]{:S(2)}, u32[]{:S(2)}) collective-permute-start(f32[4,6,1,1024]{3,1,2,0:T(8,128)S(1)} %copy.45), channel_id=1, source_target_pairs={{0,1},{1,2},{2,3},{3,4},{4,5},{5,6},{6,7},{7,8},{8,9},{9,10},{10,1... | collective-permute-start | bytes 294920 | tf_op jit(solution)/shard_map/ppermute | solution.py:39
  69.8 6.9 %collective-permute-start.3 = (f32[4,6,1,1024]{3,1,2,0:T(8,128)S(1)}, f32[4,6,1,1024]{3,1,2,0:T(8,128)S(1)}, u32[]{:S(2)}, u32[]{:S(2)}) collective-permute-start(f32[4,6,1,1024]{3,1,2,0:T(8,128)S(1)} %copy.43), channel_id=1, source_target_pairs={{1,0},{2,1},{3,2},{4,3},{5,4},{6,5},{7,6},{8,7},{9,8},{10,9},{11,1... | collective-permute-start | bytes 294920 | tf_op jit(solution)/shard_map/ppermute | solution.py:41
  72.3 4.6 %copy-start.2 = (f32[4,4,8,1024]{3,2,1,0:T(8,128)S(1)}, f32[4,4,8,1024]{3,2,1,0:T(8,128)}, u32[]{:S(2)}) copy-start(f32[4,4,8,1024]{3,2,1,0:T(8,128)} %param.8) | copy-start | bytes 1572868
  72.4 4.5 %copy-start.1 = (f32[4,4,8,1024]{3,2,1,0:T(8,128)S(1)}, f32[4,4,8,1024]{3,2,1,0:T(8,128)}, u32[]{:S(2)}) copy-start(f32[4,4,8,1024]{3,2,1,0:T(8,128)} %param.7) | copy-start | bytes 1572868

commit v3 on v1

--- a/solution.py
+++ b/solution.py
@@ -128,16 +128,28 @@
     depth_count = lax.axis_size("depth")
     planes = grid.shape[2]
     total_depth = planes * depth_count
-    padded = with_halo(grid, (("tile", 1), ("depth", 2)), 1)
+    halos = []
+    for axis, dim in (("tile", 1), ("depth", 2)):
+        count = lax.axis_size(axis)
+        head = lax.slice_in_dim(grid, 0, 1, axis=dim)
+        tail = lax.slice_in_dim(grid, grid.shape[dim] - 1, grid.shape[dim], axis=dim)
+        halos.append(lax.ppermute(tail, axis, [(i, i + 1) for i in range(count - 1)]))
+        halos.append(lax.ppermute(head, axis, [(i + 1, i) for i in range(count - 1)]))
+    grid, halos = lax.optimization_barrier((grid, halos))
+    row_before, row_after, plane_before, plane_after = halos
+    rows_after = jnp.concatenate([grid[:, 1:], row_after], axis=1)
+    rows_before = jnp.concatenate([row_before, grid[:, :-1]], axis=1)
+    planes_after = jnp.concatenate([grid[:, :, 1:], plane_after], axis=2)
+    planes_before = jnp.concatenate([plane_before, grid[:, :, :-1]], axis=2)
     shares = (ray_offset.astype(jnp.float32) * 0.5)[None, :, None, :]
     occ = expand_blocks(occupancy.astype(jnp.float32))
-    feature_grad = render(grid, padded[:, 2:, 1:-1, :], shares, occ, target, total_depth)
+    feature_grad = render(grid, rows_after, shares, occ, target, total_depth)
     carried = shares * feature_grad
     incoming = passed_along(carried[:, -1:], "tile", 1)
     carried_in = jnp.concatenate([incoming, carried[:, :-1]], axis=1)
     data_grad = (1.0 - shares) * feature_grad + carried_in
-    across_rows = padded[:, 2:, 1:-1, :] + padded[:, :-2, 1:-1, :]
-    across_planes = padded[:, 1:-1, 2:, :] + padded[:, 1:-1, :-2, :]
+    across_rows = rows_after + rows_before
+    across_planes = planes_after + planes_before
     side_pad = jnp.pad(grid, ((0, 0), (0, 0), (0, 0), (1, 1)))
     across_cols = side_pad[:, :, :, 2:] + side_pad[:, :, :, :-2]
     smooth_grad = 2.0 * tv_weight * (6.0 * grid - across_rows - across_planes - across_cols)

time: 76.8 us -> 79.7 us (1.038)
  the two profiles are of different devices: /device:TPU:239 before, /device:TPU:24 now
where the time goes in v3:
time: 79.7 us; the launch traced here: 79.2 us
  starting transfers between devices  49 us (61%)
  waiting for transfers between devices  21 us (26%)
  other arithmetic  4.53 us (6%)
  local copies, waits for them, and re-layouts  3.53 us (4%)
  between operations  1.14 us (1%)
    ppermute x4, starting transfers between devices, butterfly_scan(): other = lax.ppermute(block, axis, [(i, i ^ step) for i in range(count)])  35.4 us
    ppermute x4, waiting for transfers between devices, butterfly_scan(): other = lax.ppermute(block, axis, [(i, i ^ step) for i in range(count)])  8.53 us
    ppermute x2, starting transfers between devices, body(): lax.ppermute(tail, axis, [(i, i + 1) for i in range(count - 1)])  6.47 us
    ppermute x1, waiting for transfers between devices, passed_along(): return lax.ppermute(block, axis, route)  6.29 us
    ppermute x2, waiting for transfers between devices, body(): lax.ppermute(tail, axis, [(i, i + 1) for i in range(count - 1)])  5.91 us
    ppermute x2, starting transfers between devices, body(): lax.ppermute(head, axis, [(i + 1, i) for i in range(count - 1)])  5.2 us
    slice x2, local copies, waits for them, and re-layouts, body(): head = lax.slice_in_dim(grid, 0, 1, axis=dim)  2.34 us
    sub x1, other arithmetic, body(): grid - learn_rate * (new_first / corr_one) / (jnp.sqrt(new_second / corr_...  1.93 us
  transfers between devices with their start and end apart: 9, of which 7 were waited for; matrix products, arithmetic and copies ran while one was open for 2% of the time, Pallas kernels for 0%

profile of v3, /device:TPU:24, one launch (start us, length us, event | category | flops | bytes accessed | tf_op | source)
XLA Modules:
  0.0 79.2 jit_solution(5448027178745922378)
XLA Ops:
  0.6 0.0 copy-start
  0.6 1.4 %fusion.34 = (f32[4,4,1,1024]{3,2,1,0:T(1,128)S(1)}, f32[4,4,1,1024]{3,2,1,0:T(1,128)S(1)}) fusion(f32[4,4,8,1024]{3,2,1,0:T(8,128)} %param.6), kind=kLoop, calls=%fused_computation.107 | loop fusion | bytes 262144 | tf_op jit(solution)/shard_map/slice | solution.py:134
  2.0 1.3 %collective-permute-start.3 = (f32[4,4,1,1024]{3,2,1,0:T(1,128)S(1)}, f32[4,4,1,1024]{3,2,1,0:T(1,128)S(1)}, u32[]{:S(2)}, u32[]{:S(2)}) collective-permute-start(f32[4,4,1,1024]{3,2,1,0:T(1,128)S(1)} %get-tuple-element.28), channel_id=1, source_target_pairs={{1,0},{2,1},{3,2},{4,3},{5,4},{6,5},{7,6},{8,7},{9,8},{10,9},{11,1... | collective-permute-start | bytes 196616 | tf_op jit(solution)/shard_map/ppermute | solution.py:137
  3.3 0.0 copy-start.5
  3.3 4.5 %collective-permute-start.2 = (f32[4,4,1,1024]{3,2,1,0:T(1,128)S(1)}, f32[4,4,1,1024]{3,2,1,0:T(1,128)S(1)}, u32[]{:S(2)}, u32[]{:S(2)}) collective-permute-start(f32[4,4,1,1024]{3,2,1,0:T(1,128)S(1)} %get-tuple-element.29), channel_id=1, source_target_pairs={{0,1},{1,2},{2,3},{3,4},{4,5},{5,6},{6,7},{7,8},{8,9},{9,10},{10,1... | collective-permute-start | bytes 196616 | tf_op jit(solution)/shard_map/ppermute | solution.py:136
  7.9 1.0 %fusion.35 = (f32[4,1,8,1024]{3,2,1,0:T(8,128)S(1)}, f32[4,1,8,1024]{3,2,1,0:T(8,128)S(1)}) fusion(f32[4,4,8,1024]{3,2,1,0:T(8,128)} %param.6), kind=kLoop, calls=%fused_computation.108 | loop fusion | bytes 524288 | tf_op jit(solution)/shard_map/slice | solution.py:134
  8.9 3.9 %collective-permute-start.1 = (f32[4,1,8,1024]{3,2,1,0:T(8,128)S(1)}, f32[4,1,8,1024]{3,2,1,0:T(8,128)S(1)}, u32[]{:S(2)}, u32[]{:S(2)}) collective-permute-start(f32[4,1,8,1024]{3,2,1,0:T(8,128)S(1)} %get-tuple-element.30), channel_id=1, source_target_pairs={{16,0},{32,16},{48,32},{64,48},{80,64},{96,80},{112,96},{128,112},... | collective-permute-start | bytes 393224 | tf_op jit(solution)/shard_map/ppermute | solution.py:137
  12.8 0.0 copy-start.6
  12.8 1.9 %collective-permute-start = (f32[4,1,8,1024]{3,2,1,0:T(8,128)S(1)}, f32[4,1,8,1024]{3,2,1,0:T(8,128)S(1)}, u32[]{:S(2)}, u32[]{:S(2)}) collective-permute-start(f32[4,1,8,1024]{3,2,1,0:T(8,128)S(1)} %get-tuple-element.31), channel_id=1, source_target_pairs={{0,16},{16,32},{32,48},{48,64},{64,80},{80,96},{96,112},{112,128},... | collective-permute-start | bytes 393224 | tf_op jit(solution)/shard_map/ppermute | solution.py:136
  14.7 0.0 copy-done.5
  14.7 0.0 copy-done.6
  14.8 0.1 broadcast_in_dim.8
  14.8 0.1 broadcast_in_dim.9
  14.9 0.0 collective-permute-done.3
  15.0 0.0 collective-permute-done.2
  15.0 0.3 collective-permute-done.1
  15.3 5.9 %collective-permute-done = f32[4,1,8,1024]{3,2,1,0:T(8,128)S(1)} collective-permute-done((f32[4,1,8,1024]{3,2,1,0:T(8,128)S(1)}, f32[4,1,8,1024]{3,2,1,0:T(8,128)S(1)}, u32[]{:S(2)}, u32[]{:S(2)}) %collective-permute-start) | collective-permute-done | bytes 131104 | tf_op jit(solution)/shard_map/ppermute | solution.py:136
  21.2 0.0 copy-done
  21.2 0.1 fusion.33
  21.3 0.1 multiply_add_fusion.1
  21.4 0.1 fusion.30
  21.5 0.1 reduce_window_sum.22
  21.6 0.1 fusion.25
  21.7 0.2 fusion.29
  21.9 0.6 pad_maximum_fusion.2
  22.5 3.8 %collective-permute-start.4 = (f32[4,4,1024]{2,1,0:T(4,128)}, f32[4,4,1024]{2,1,0:T(4,128)S(1)}, u32[]{:S(2)}, u32[]{:S(2)}) collective-permute-start(f32[4,4,1024]{2,1,0:T(4,128)} %pad_maximum_fusion.2), channel_id=1, source_target_pairs={{0,1},{1,0},{2,3},{3,2},{4,5},{5,4},{6,7},{7,6},{8,9},{9,8},{10,11... | collective-permute-start | bytes 196616 | tf_op jit(solution)/shard_map/ppermute | solution.py:73
  26.4 0.0 copy-start.3
  26.4 0.3 reduce_window_sum.23
  26.7 2.2 %collective-permute-done.4 = f32[4,4,1024]{2,1,0:T(4,128)S(1)} collective-permute-done((f32[4,4,1024]{2,1,0:T(4,128)}, f32[4,4,1024]{2,1,0:T(4,128)S(1)}, u32[]{:S(2)}, u32[]{:S(2)}) %collective-permute-start.4) | collective-permute-done | bytes 65568 | tf_op jit(solution)/shard_map/ppermute | solution.py:73
  28.9 0.0 copy-done.3
  29.0 6.5 %collective-permute-start.5 = (f32[4,4,1024]{2,1,0:T(4,128)S(1)}, f32[4,4,1024]{2,1,0:T(4,128)S(1)}, u32[]{:S(2)}, u32[]{:S(2)}) collective-permute-start(f32[4,4,1024]{2,1,0:T(4,128)S(1)} %pad_maximum_fusion.3), channel_id=1, source_target_pairs={{0,2},{1,3},{2,0},{3,1},{4,6},{5,7},{6,4},{7,5},{8,10},{9,11},{10,... | collective-permute-start | bytes 196616 | tf_op jit(solution)/shard_map/ppermute | solution.py:73
  35.6 2.2 %collective-permute-done.5 = f32[4,4,1024]{2,1,0:T(4,128)S(1)} collective-permute-done((f32[4,4,1024]{2,1,0:T(4,128)S(1)}, f32[4,4,1024]{2,1,0:T(4,128)S(1)}, u32[]{:S(2)}, u32[]{:S(2)}) %collective-permute-start.5) | collective-permute-done | bytes 65568 | tf_op jit(solution)/shard_map/ppermute | solution.py:73
  37.9 9.1 %collective-permute-start.6 = (f32[4,4,1024]{2,1,0:T(4,128)S(1)}, f32[4,4,1024]{2,1,0:T(4,128)S(1)}, u32[]{:S(2)}, u32[]{:S(2)}) collective-permute-start(f32[4,4,1024]{2,1,0:T(4,128)S(1)} %pad_maximum_fusion.4), channel_id=1, source_target_pairs={{0,4},{1,5},{2,6},{3,7},{4,0},{5,1},{6,2},{7,3},{8,12},{9,13},{10,... | collective-permute-start | bytes 196616 | tf_op jit(solution)/shard_map/ppermute | solution.py:73
  47.1 2.1 %collective-permute-done.6 = f32[4,4,1024]{2,1,0:T(4,128)S(1)} collective-permute-done((f32[4,4,1024]{2,1,0:T(4,128)S(1)}, f32[4,4,1024]{2,1,0:T(4,128)S(1)}, u32[]{:S(2)}, u32[]{:S(2)}) %collective-permute-start.6) | collective-permute-done | bytes 65568 | tf_op jit(solution)/shard_map/ppermute | solution.py:73
  49.4 15.9 %collective-permute-start.7 = (f32[4,4,1024]{2,1,0:T(4,128)S(1)}, f32[4,4,1024]{2,1,0:T(4,128)S(1)}, u32[]{:S(2)}, u32[]{:S(2)}) collective-permute-start(f32[4,4,1024]{2,1,0:T(4,128)S(1)} %pad_maximum_fusion.5), channel_id=1, source_target_pairs={{0,8},{1,9},{2,10},{3,11},{4,12},{5,13},{6,14},{7,15},{8,0},{9,1},... | collective-permute-start | bytes 196616 | tf_op jit(solution)/shard_map/ppermute | solution.py:73
  65.4 2.1 %collective-permute-done.7 = f32[4,4,1024]{2,1,0:T(4,128)S(1)} collective-permute-done((f32[4,4,1024]{2,1,0:T(4,128)S(1)}, f32[4,4,1024]{2,1,0:T(4,128)S(1)}, u32[]{:S(2)}, u32[]{:S(2)}) %collective-permute-start.7) | collective-permute-done | bytes 65568 | tf_op jit(solution)/shard_map/ppermute | solution.py:73
  67.6 0.1 multiply_bitcast_fusion.1
  67.7 0.0 copy-start.4
  67.7 0.7 copy-done.4
  68.5 0.2 multiply_reduce_fusion
  68.7 0.1 fusion.15
  68.8 0.1 fusion.7
  68.9 1.9 %collective-permute-start.8 = (f32[4,1,8,1024]{3,2,1,0:T(8,128)S(1)}, f32[4,1,8,1024]{3,2,1,0:T(8,128)S(1)}, u32[]{:S(2)}, u32[]{:S(2)}) collective-permute-start(f32[4,1,8,1024]{3,2,1,0:T(8,128)S(1)} %slice.258), channel_id=1, source_target_pairs={{0,16},{16,32},{32,48},{48,64},{64,80},{80,96},{96,112},{112,128},... | collective-permute-start | bytes 393224 | tf_op jit(solution)/shard_map/ppermute | solution.py:51
  70.8 0.0 copy-start.2
  70.8 0.1 fusion.32
  70.9 0.0 copy-start.1
  71.0 6.3 %collective-permute-done.8 = f32[4,1,8,1024]{3,2,1,0:T(8,128)S(1)} collective-permute-done((f32[4,1,8,1024]{3,2,1,0:T(8,128)S(1)}, f32[4,1,8,1024]{3,2,1,0:T(8,128)S(1)}, u32[]{:S(2)}, u32[]{:S(2)}) %collective-permute-start.8) | collective-permute-done | bytes 131104 | tf_op jit(solution)/shard_map/ppermute | solution.py:51
  77.3 0.0 copy-done.2
  77.3 0.0 copy-done.1
  77.3 1.9 %divide_subtract_fusion = (f32[4,4,8,1024]{3,2,1,0:T(8,128)}, f32[4,4,8,1024]{3,2,1,0:T(8,128)}, f32[4,4,8,1024]{3,2,1,0:T(8,128)}) fusion(f32[4,4,8,1024]{3,2,1,0:T(8,128)S(1)} %copy-done, f32[4,4,8,1024]{3,2,1,0:T(8,128)S(1)} %copy-done.1, f32[4,4,8,1024]{3,2,1,0:T(8,128)S(1)} %copy-done.2, f32[4,4,7,1024]{3,2,1,0:T(8,128)S(1)} %get-tuple-element.24, ...), kind=kLoop, calls=%fused_computation.15 | loop fusion | flops 3801088 | bytes 6307840 | tf_op jit(solution)/shard_map/sub | solution.py:161
  (34 shorter events, 0.7 us)
Async XLA Ops:
  0.6 20.6 %copy-start = (f32[4,4,8,1024]{3,2,1,0:T(8,128)S(1)}, f32[4,4,8,1024]{3,2,1,0:T(8,128)}, u32[]{:S(2)}) copy-start(f32[4,4,8,1024]{3,2,1,0:T(8,128)} %param.6) | copy-start | bytes 1572868
  2.0 12.9 %collective-permute-start.3 = (f32[4,4,1,1024]{3,2,1,0:T(1,128)S(1)}, f32[4,4,1,1024]{3,2,1,0:T(1,128)S(1)}, u32[]{:S(2)}, u32[]{:S(2)}) collective-permute-start(f32[4,4,1,1024]{3,2,1,0:T(1,128)S(1)} %get-tuple-element.28), channel_id=1, source_target_pairs={{1,0},{2,1},{3,2},{4,3},{5,4},{6,5},{7,6},{8,7},{9,8},{10,9},{11,1... | collective-permute-start | bytes 196616 | tf_op jit(solution)/shard_map/ppermute | solution.py:137
  3.3 11.4 %copy-start.5 = (s32[4,1024]{1,0:T(4,128)S(1)}, s32[4,1024]{1,0:T(4,128)}, u32[]{:S(2)}) copy-start(s32[4,1024]{1,0:T(4,128)} %param.9) | copy-start | bytes 49156
  3.3 11.6 %collective-permute-start.2 = (f32[4,4,1,1024]{3,2,1,0:T(1,128)S(1)}, f32[4,4,1,1024]{3,2,1,0:T(1,128)S(1)}, u32[]{:S(2)}, u32[]{:S(2)}) collective-permute-start(f32[4,4,1,1024]{3,2,1,0:T(1,128)S(1)} %get-tuple-element.29), channel_id=1, source_target_pairs={{0,1},{1,2},{2,3},{3,4},{4,5},{5,6},{6,7},{7,8},{8,9},{9,10},{10,1... | collective-permute-start | bytes 196616 | tf_op jit(solution)/shard_map/ppermute | solution.py:136
  8.9 6.4 %collective-permute-start.1 = (f32[4,1,8,1024]{3,2,1,0:T(8,128)S(1)}, f32[4,1,8,1024]{3,2,1,0:T(8,128)S(1)}, u32[]{:S(2)}, u32[]{:S(2)}) collective-permute-start(f32[4,1,8,1024]{3,2,1,0:T(8,128)S(1)} %get-tuple-element.30), channel_id=1, source_target_pairs={{16,0},{32,16},{48,32},{64,48},{80,64},{96,80},{112,96},{128,112},... | collective-permute-start | bytes 393224 | tf_op jit(solution)/shard_map/ppermute | solution.py:137
  12.8 2.0 %copy-start.6 = (s32[1,1,128]{2,1,0:T(1,128)S(1)}, s32[1,1,128]{2,1,0:T(1,128)}, u32[]{:S(2)}) copy-start(s32[1,1,128]{2,1,0:T(1,128)} %param.10) | copy-start | bytes 1540
  12.8 8.4 %collective-permute-start = (f32[4,1,8,1024]{3,2,1,0:T(8,128)S(1)}, f32[4,1,8,1024]{3,2,1,0:T(8,128)S(1)}, u32[]{:S(2)}, u32[]{:S(2)}) collective-permute-start(f32[4,1,8,1024]{3,2,1,0:T(8,128)S(1)} %get-tuple-element.31), channel_id=1, source_target_pairs={{0,16},{16,32},{32,48},{48,64},{64,80},{80,96},{96,112},{112,128},... | collective-permute-start | bytes 393224 | tf_op jit(solution)/shard_map/ppermute | solution.py:136
  22.5 6.4 %collective-permute-start.4 = (f32[4,4,1024]{2,1,0:T(4,128)}, f32[4,4,1024]{2,1,0:T(4,128)S(1)}, u32[]{:S(2)}, u32[]{:S(2)}) collective-permute-start(f32[4,4,1024]{2,1,0:T(4,128)} %pad_maximum_fusion.2), channel_id=1, source_target_pairs={{0,1},{1,0},{2,3},{3,2},{4,5},{5,4},{6,7},{7,6},{8,9},{9,8},{10,11... | collective-permute-start | bytes 196616 | tf_op jit(solution)/shard_map/ppermute | solution.py:73
  26.4 2.5 %copy-start.3 = (f32[4,4,1024]{2,1,0:T(4,128)S(1)}, f32[4,4,1024]{2,1,0:T(4,128)}, u32[]{:S(2)}) copy-start(f32[4,4,1024]{2,1,0:T(4,128)} %constant.14.clone.1) | copy-start | bytes 196612
  29.0 8.7 %collective-permute-start.5 = (f32[4,4,1024]{2,1,0:T(4,128)S(1)}, f32[4,4,1024]{2,1,0:T(4,128)S(1)}, u32[]{:S(2)}, u32[]{:S(2)}) collective-permute-start(f32[4,4,1024]{2,1,0:T(4,128)S(1)} %pad_maximum_fusion.3), channel_id=1, source_target_pairs={{0,2},{1,3},{2,0},{3,1},{4,6},{5,7},{6,4},{7,5},{8,10},{9,11},{10,... | collective-permute-start | bytes 196616 | tf_op jit(solution)/shard_map/ppermute | solution.py:73
  37.9 11.4 %collective-permute-start.6 = (f32[4,4,1024]{2,1,0:T(4,128)S(1)}, f32[4,4,1024]{2,1,0:T(4,128)S(1)}, u32[]{:S(2)}, u32[]{:S(2)}) collective-permute-start(f32[4,4,1024]{2,1,0:T(4,128)S(1)} %pad_maximum_fusion.4), channel_id=1, source_target_pairs={{0,4},{1,5},{2,6},{3,7},{4,0},{5,1},{6,2},{7,3},{8,12},{9,13},{10,... | collective-permute-start | bytes 196616 | tf_op jit(solution)/shard_map/ppermute | solution.py:73
  49.4 18.1 %collective-permute-start.7 = (f32[4,4,1024]{2,1,0:T(4,128)S(1)}, f32[4,4,1024]{2,1,0:T(4,128)S(1)}, u32[]{:S(2)}, u32[]{:S(2)}) collective-permute-start(f32[4,4,1024]{2,1,0:T(4,128)S(1)} %pad_maximum_fusion.5), channel_id=1, source_target_pairs={{0,8},{1,9},{2,10},{3,11},{4,12},{5,13},{6,14},{7,15},{8,0},{9,1},... | collective-permute-start | bytes 196616 | tf_op jit(solution)/shard_map/ppermute | solution.py:73
  67.7 0.8 %copy-start.4 = (f32[3,4,1024]{2,1,0:T(4,128)S(1)}, f32[3,4,1024]{2,1,0:T(4,128)}, u32[]{:S(2)}) copy-start(f32[3,4,1024]{2,1,0:T(4,128)} %param.11) | copy-start | bytes 147460
  68.9 8.4 %collective-permute-start.8 = (f32[4,1,8,1024]{3,2,1,0:T(8,128)S(1)}, f32[4,1,8,1024]{3,2,1,0:T(8,128)S(1)}, u32[]{:S(2)}, u32[]{:S(2)}) collective-permute-start(f32[4,1,8,1024]{3,2,1,0:T(8,128)S(1)} %slice.258), channel_id=1, source_target_pairs={{0,16},{16,32},{32,48},{48,64},{64,80},{80,96},{96,112},{112,128},... | collective-permute-start | bytes 393224 | tf_op jit(solution)/shard_map/ppermute | solution.py:51
  70.8 6.5 %copy-start.2 = (f32[4,4,8,1024]{3,2,1,0:T(8,128)S(1)}, f32[4,4,8,1024]{3,2,1,0:T(8,128)}, u32[]{:S(2)}) copy-start(f32[4,4,8,1024]{3,2,1,0:T(8,128)} %param.8) | copy-start | bytes 1572868
  70.9 6.3 %copy-start.1 = (f32[4,4,8,1024]{3,2,1,0:T(8,128)S(1)}, f32[4,4,8,1024]{3,2,1,0:T(8,128)}, u32[]{:S(2)}) copy-start(f32[4,4,8,1024]{3,2,1,0:T(8,128)} %param.7) | copy-start | bytes 1572868

commit v4 on v1

--- a/solution.py
+++ b/solution.py
@@ -70,8 +70,9 @@
     prefix, suffix = (blank, blank)
     step = 1
     while step < count:
-        other = lax.ppermute(block, axis, [(i, i ^ step) for i in range(count)])
-        upper = (mine & step) != 0
+        route = [(i, i - i % (2 * step) + 2 * step - 1 - i % (2 * step)) for i in range(count)]
+        other = lax.ppermute(block, axis, route)
+        upper = mine % (2 * step) >= step
         joined = over(jnp.where(upper, other, block), jnp.where(upper, block, other))
         prefix = jnp.where(upper, over(other, prefix), prefix)
         suffix = jnp.where(upper, suffix, over(suffix, other))

time: 76.8 us -> 73.6 us (0.958)
  the two profiles are of different devices: /device:TPU:239 before, /device:TPU:24 now
where the time goes in v4:
time: 73.6 us; the launch traced here: 72.6 us
  starting transfers between devices  44.6 us (61%)
  waiting for transfers between devices  19.7 us (27%)
  other arithmetic  4.59 us (6%)
  local copies, waits for them, and re-layouts  2.44 us (3%)
  between operations  1.18 us (2%)
    ppermute x4, starting transfers between devices, butterfly_scan(): other = lax.ppermute(block, axis, route)  33.9 us
    ppermute x4, waiting for transfers between devices, butterfly_scan(): other = lax.ppermute(block, axis, route)  8.77 us
    ppermute x2, waiting for transfers between devices, with_halo(): lax.ppermute(tail, axis, [(i, (i + 1) % count) for i in range(ends)])  6.67 us
    ppermute x2, starting transfers between devices, with_halo(): lax.ppermute(head, axis, [((i + 1) % count, i) for i in range(ends)])  5.58 us
    ppermute x2, waiting for transfers between devices, with_halo(): lax.ppermute(head, axis, [((i + 1) % count, i) for i in range(ends)])  4.28 us
    ppermute x2, starting transfers between devices, with_halo(): lax.ppermute(tail, axis, [(i, (i + 1) % count) for i in range(ends)])  3.22 us
    ppermute x1, starting transfers between devices, passed_along(): return lax.ppermute(block, axis, route)  1.92 us
    sub x1, other arithmetic, body(): grid - learn_rate * (new_first / corr_one) / (jnp.sqrt(new_second / corr_...  1.91 us
  transfers between devices with their start and end apart: 9, of which 7 were waited for; matrix products, arithmetic and copies ran while one was open for 2% of the time, Pallas kernels for 0%

profile of v4, /device:TPU:24, one launch (start us, length us, event | category | flops | bytes accessed | tf_op | source)
XLA Modules:
  0.0 72.6 jit_solution(10720164543358056522)
XLA Ops:
  0.6 0.0 copy-start
  0.6 1.0 %fusion.37 = (f32[4,1,8,1024]{3,2,1,0:T(8,128)S(1)}, f32[4,1,8,1024]{3,2,1,0:T(8,128)S(1)}) fusion(f32[4,4,8,1024]{3,2,1,0:T(8,128)} %param.6), kind=kLoop, calls=%fused_computation.113 | loop fusion | bytes 524288 | tf_op jit(solution)/shard_map/slice | solution.py:35
  1.7 4.3 %collective-permute-start = (f32[4,1,8,1024]{3,2,1,0:T(8,128)S(1)}, f32[4,1,8,1024]{3,2,1,0:T(8,128)S(1)}, u32[]{:S(2)}, u32[]{:S(2)}) collective-permute-start(f32[4,1,8,1024]{3,2,1,0:T(8,128)S(1)} %get-tuple-element.21), channel_id=1, source_target_pairs={{16,0},{32,16},{48,32},{64,48},{80,64},{96,80},{112,96},{128,112},... | collective-permute-start | bytes 393224 | tf_op jit(solution)/shard_map/ppermute | solution.py:41
  6.0 0.0 copy-start.5
  6.0 1.9 %collective-permute-start.6 = (f32[4,1,8,1024]{3,2,1,0:T(8,128)S(1)}, f32[4,1,8,1024]{3,2,1,0:T(8,128)S(1)}, u32[]{:S(2)}, u32[]{:S(2)}) collective-permute-start(f32[4,1,8,1024]{3,2,1,0:T(8,128)S(1)} %get-tuple-element.22), channel_id=1, source_target_pairs={{0,16},{16,32},{32,48},{48,64},{64,80},{80,96},{96,112},{112,128},... | collective-permute-start | bytes 393224 | tf_op jit(solution)/shard_map/ppermute | solution.py:39
  7.9 0.7 %broadcast_subtract_fusion = (f32[4,1024]{1,0:T(4,128)S(1)}, f32[4,1024]{1,0:T(4,128)S(1)}) fusion(s32[4,1024]{1,0:T(4,128)} %param.9), kind=kLoop, calls=%fused_computation.107 | loop fusion | flops 12288 | bytes 49152 | tf_op jit(solution)/shard_map/sub | solution.py:139
  8.6 0.0 copy-done.5
  8.7 0.1 broadcast_in_dim.8
  8.8 0.1 broadcast_in_dim.9
  8.9 5.5 %collective-permute-done.6 = f32[4,1,8,1024]{3,2,1,0:T(8,128)S(1)} collective-permute-done((f32[4,1,8,1024]{3,2,1,0:T(8,128)S(1)}, f32[4,1,8,1024]{3,2,1,0:T(8,128)S(1)}, u32[]{:S(2)}, u32[]{:S(2)}) %collective-permute-start.6) | collective-permute-done | bytes 131104 | tf_op jit(solution)/shard_map/ppermute | solution.py:39
  14.4 0.0 collective-permute-done
  14.4 0.0 copy-done
  14.4 0.1 fusion.10
  14.5 0.1 fusion.34
  14.7 0.1 reduce_window_sum.22
  14.8 0.1 fusion.29
  14.9 0.2 fusion.33
  15.1 0.3 reduce_window_sum.23
  15.4 3.8 %collective-permute-start.1 = (f32[4,4,1024]{2,1,0:T(4,128)S(1)}, f32[4,4,1024]{2,1,0:T(4,128)S(1)}, u32[]{:S(2)}, u32[]{:S(2)}) collective-permute-start(f32[4,4,1024]{2,1,0:T(4,128)S(1)} %pad_maximum_fusion.5), channel_id=1, source_target_pairs={{0,1},{1,0},{2,3},{3,2},{4,5},{5,4},{6,7},{7,6},{8,9},{9,8},{10,11... | collective-permute-start | bytes 196616 | tf_op jit(solution)/shard_map/ppermute | solution.py:74
  19.3 0.0 copy-start.3
  19.3 2.3 %collective-permute-done.1 = f32[4,4,1024]{2,1,0:T(4,128)S(1)} collective-permute-done((f32[4,4,1024]{2,1,0:T(4,128)S(1)}, f32[4,4,1024]{2,1,0:T(4,128)S(1)}, u32[]{:S(2)}, u32[]{:S(2)}) %collective-permute-start.1) | collective-permute-done | bytes 65568 | tf_op jit(solution)/shard_map/ppermute | solution.py:74
  21.6 0.0 copy-done.3
  21.7 6.5 %collective-permute-start.2 = (f32[4,4,1024]{2,1,0:T(4,128)S(1)}, f32[4,4,1024]{2,1,0:T(4,128)S(1)}, u32[]{:S(2)}, u32[]{:S(2)}) collective-permute-start(f32[4,4,1024]{2,1,0:T(4,128)S(1)} %pad_maximum_fusion.6), channel_id=1, source_target_pairs={{0,3},{1,2},{2,1},{3,0},{4,7},{5,6},{6,5},{7,4},{8,11},{9,10},{10,... | collective-permute-start | bytes 196616 | tf_op jit(solution)/shard_map/ppermute | solution.py:74
  28.3 2.2 %collective-permute-done.2 = f32[4,4,1024]{2,1,0:T(4,128)S(1)} collective-permute-done((f32[4,4,1024]{2,1,0:T(4,128)S(1)}, f32[4,4,1024]{2,1,0:T(4,128)S(1)}, u32[]{:S(2)}, u32[]{:S(2)}) %collective-permute-start.2) | collective-permute-done | bytes 65568 | tf_op jit(solution)/shard_map/ppermute | solution.py:74
  30.6 13.0 %collective-permute-start.3 = (f32[4,4,1024]{2,1,0:T(4,128)S(1)}, f32[4,4,1024]{2,1,0:T(4,128)S(1)}, u32[]{:S(2)}, u32[]{:S(2)}) collective-permute-start(f32[4,4,1024]{2,1,0:T(4,128)S(1)} %pad_maximum_fusion.7), channel_id=1, source_target_pairs={{0,7},{1,6},{2,5},{3,4},{4,3},{5,2},{6,1},{7,0},{8,15},{9,14},{10,... | collective-permute-start | bytes 196616 | tf_op jit(solution)/shard_map/ppermute | solution.py:74
  43.8 2.2 %collective-permute-done.3 = f32[4,4,1024]{2,1,0:T(4,128)S(1)} collective-permute-done((f32[4,4,1024]{2,1,0:T(4,128)S(1)}, f32[4,4,1024]{2,1,0:T(4,128)S(1)}, u32[]{:S(2)}, u32[]{:S(2)}) %collective-permute-start.3) | collective-permute-done | bytes 65568 | tf_op jit(solution)/shard_map/ppermute | solution.py:74
  46.1 10.5 %collective-permute-start.4 = (f32[4,4,1024]{2,1,0:T(4,128)S(1)}, f32[4,4,1024]{2,1,0:T(4,128)S(1)}, u32[]{:S(2)}, u32[]{:S(2)}) collective-permute-start(f32[4,4,1024]{2,1,0:T(4,128)S(1)} %pad_maximum_fusion.8), channel_id=1, source_target_pairs={{0,15},{1,14},{2,13},{3,12},{4,11},{5,10},{6,9},{7,8},{8,7},{9,6},... | collective-permute-start | bytes 196616 | tf_op jit(solution)/shard_map/ppermute | solution.py:74
  56.7 2.1 %collective-permute-done.4 = f32[4,4,1024]{2,1,0:T(4,128)S(1)} collective-permute-done((f32[4,4,1024]{2,1,0:T(4,128)S(1)}, f32[4,4,1024]{2,1,0:T(4,128)S(1)}, u32[]{:S(2)}, u32[]{:S(2)}) %collective-permute-start.4) | collective-permute-done | bytes 65568 | tf_op jit(solution)/shard_map/ppermute | solution.py:74
  58.9 0.1 multiply_bitcast_fusion.1
  59.0 0.0 copy-start.4
  59.1 0.7 %copy-done.4 = f32[3,4,1024]{2,1,0:T(4,128)S(1)} copy-done((f32[3,4,1024]{2,1,0:T(4,128)S(1)}, f32[3,4,1024]{2,1,0:T(4,128)}, u32[]{:S(2)}) %copy-start.4) | copy-done | bytes 49176
  59.9 0.2 multiply_reduce_fusion
  60.1 0.1 fusion.19
  60.1 0.1 fusion.11
  60.2 1.9 %collective-permute-start.5 = (f32[4,1,8,1024]{3,2,1,0:T(8,128)S(1)}, f32[4,1,8,1024]{3,2,1,0:T(8,128)S(1)}, u32[]{:S(2)}, u32[]{:S(2)}) collective-permute-start(f32[4,1,8,1024]{3,2,1,0:T(8,128)S(1)} %slice.263), channel_id=1, source_target_pairs={{0,16},{16,32},{32,48},{48,64},{64,80},{80,96},{96,112},{112,128},... | collective-permute-start | bytes 393224 | tf_op jit(solution)/shard_map/ppermute | solution.py:51
  62.1 0.1 fusion.36
  62.3 1.3 %collective-permute-start.8 = (f32[4,6,1,1024]{3,1,2,0:T(8,128)S(1)}, f32[4,6,1,1024]{3,1,2,0:T(8,128)S(1)}, u32[]{:S(2)}, u32[]{:S(2)}) collective-permute-start(f32[4,6,1,1024]{3,1,2,0:T(8,128)S(1)} %copy.25), channel_id=1, source_target_pairs={{0,1},{1,2},{2,3},{3,4},{4,5},{5,6},{6,7},{7,8},{8,9},{9,10},{10,1... | collective-permute-start | bytes 294920 | tf_op jit(solution)/shard_map/ppermute | solution.py:39
  63.6 1.3 %collective-permute-start.7 = (f32[4,6,1,1024]{3,1,2,0:T(8,128)S(1)}, f32[4,6,1,1024]{3,1,2,0:T(8,128)S(1)}, u32[]{:S(2)}, u32[]{:S(2)}) collective-permute-start(f32[4,6,1,1024]{3,1,2,0:T(8,128)S(1)} %copy.23), channel_id=1, source_target_pairs={{1,0},{2,1},{3,2},{4,3},{5,4},{6,5},{7,6},{8,7},{9,8},{10,9},{11,1... | collective-permute-start | bytes 294920 | tf_op jit(solution)/shard_map/ppermute | solution.py:41
  64.9 1.2 %collective-permute-done.8 = f32[4,6,1,1024]{3,1,2,0:T(8,128)S(1)} collective-permute-done((f32[4,6,1,1024]{3,1,2,0:T(8,128)S(1)}, f32[4,6,1,1024]{3,1,2,0:T(8,128)S(1)}, u32[]{:S(2)}, u32[]{:S(2)}) %collective-permute-start.8) | collective-permute-done | bytes 98336 | tf_op jit(solution)/shard_map/ppermute | solution.py:39
  66.1 0.0 copy-start.2
  66.1 0.1 copy.26
  66.2 0.0 copy-start.1
  66.2 4.3 %collective-permute-done.7 = f32[4,6,1,1024]{3,1,2,0:T(8,128)S(1)} collective-permute-done((f32[4,6,1,1024]{3,1,2,0:T(8,128)S(1)}, f32[4,6,1,1024]{3,1,2,0:T(8,128)S(1)}, u32[]{:S(2)}, u32[]{:S(2)}) %collective-permute-start.7) | collective-permute-done | bytes 98336 | tf_op jit(solution)/shard_map/ppermute | solution.py:41
  70.5 0.1 copy.24
  70.6 0.0 collective-permute-done.5
  70.7 0.0 copy-done.2
  70.7 0.0 copy-done.1
  70.7 1.9 %divide_subtract_fusion = (f32[4,4,8,1024]{3,2,1,0:T(8,128)}, f32[4,4,8,1024]{3,2,1,0:T(8,128)}, f32[4,4,8,1024]{3,2,1,0:T(8,128)}) fusion(f32[4,4,8,1024]{3,2,1,0:T(8,128)S(1)} %copy-done, f32[4,4,8,1024]{3,2,1,0:T(8,128)S(1)} %copy-done.1, f32[4,4,8,1024]{3,2,1,0:T(8,128)S(1)} %copy-done.2, f32[4,6,8,1024]{3,2,1,0:T(8,128)S(1)} %constant_dynamic-update-slice_fusion, ...), kind=kLoop, calls=%fused_computation.20 | loop fusion | flops 3801088 | bytes 5455872 | tf_op jit(solution)/shard_map/sub | solution.py:150
  (38 shorter events, 0.8 us)
Async XLA Ops:
  0.6 13.8 %copy-start = (f32[4,4,8,1024]{3,2,1,0:T(8,128)S(1)}, f32[4,4,8,1024]{3,2,1,0:T(8,128)}, u32[]{:S(2)}) copy-start(f32[4,4,8,1024]{3,2,1,0:T(8,128)} %param.6) | copy-start | bytes 1572868
  1.7 12.7 %collective-permute-start = (f32[4,1,8,1024]{3,2,1,0:T(8,128)S(1)}, f32[4,1,8,1024]{3,2,1,0:T(8,128)S(1)}, u32[]{:S(2)}, u32[]{:S(2)}) collective-permute-start(f32[4,1,8,1024]{3,2,1,0:T(8,128)S(1)} %get-tuple-element.21), channel_id=1, source_target_pairs={{16,0},{32,16},{48,32},{64,48},{80,64},{96,80},{112,96},{128,112},... | collective-permute-start | bytes 393224 | tf_op jit(solution)/shard_map/ppermute | solution.py:41
  6.0 2.7 %copy-start.5 = (s32[1,1,128]{2,1,0:T(1,128)S(1)}, s32[1,1,128]{2,1,0:T(1,128)}, u32[]{:S(2)}) copy-start(s32[1,1,128]{2,1,0:T(1,128)} %param.10) | copy-start | bytes 1540
  6.0 8.4 %collective-permute-start.6 = (f32[4,1,8,1024]{3,2,1,0:T(8,128)S(1)}, f32[4,1,8,1024]{3,2,1,0:T(8,128)S(1)}, u32[]{:S(2)}, u32[]{:S(2)}) collective-permute-start(f32[4,1,8,1024]{3,2,1,0:T(8,128)S(1)} %get-tuple-element.22), channel_id=1, source_target_pairs={{0,16},{16,32},{32,48},{48,64},{64,80},{80,96},{96,112},{112,128},... | collective-permute-start | bytes 393224 | tf_op jit(solution)/shard_map/ppermute | solution.py:39
  15.4 6.2 %collective-permute-start.1 = (f32[4,4,1024]{2,1,0:T(4,128)S(1)}, f32[4,4,1024]{2,1,0:T(4,128)S(1)}, u32[]{:S(2)}, u32[]{:S(2)}) collective-permute-start(f32[4,4,1024]{2,1,0:T(4,128)S(1)} %pad_maximum_fusion.5), channel_id=1, source_target_pairs={{0,1},{1,0},{2,3},{3,2},{4,5},{5,4},{6,7},{7,6},{8,9},{9,8},{10,11... | collective-permute-start | bytes 196616 | tf_op jit(solution)/shard_map/ppermute | solution.py:74
  19.3 2.3 %copy-start.3 = (f32[4,4,1024]{2,1,0:T(4,128)S(1)}, f32[4,4,1024]{2,1,0:T(4,128)}, u32[]{:S(2)}) copy-start(f32[4,4,1024]{2,1,0:T(4,128)} %constant.84.clone.1) | copy-start | bytes 196612
  21.7 8.8 %collective-permute-start.2 = (f32[4,4,1024]{2,1,0:T(4,128)S(1)}, f32[4,4,1024]{2,1,0:T(4,128)S(1)}, u32[]{:S(2)}, u32[]{:S(2)}) collective-permute-start(f32[4,4,1024]{2,1,0:T(4,128)S(1)} %pad_maximum_fusion.6), channel_id=1, source_target_pairs={{0,3},{1,2},{2,1},{3,0},{4,7},{5,6},{6,5},{7,4},{8,11},{9,10},{10,... | collective-permute-start | bytes 196616 | tf_op jit(solution)/shard_map/ppermute | solution.py:74
  30.6 15.4 %collective-permute-start.3 = (f32[4,4,1024]{2,1,0:T(4,128)S(1)}, f32[4,4,1024]{2,1,0:T(4,128)S(1)}, u32[]{:S(2)}, u32[]{:S(2)}) collective-permute-start(f32[4,4,1024]{2,1,0:T(4,128)S(1)} %pad_maximum_fusion.7), channel_id=1, source_target_pairs={{0,7},{1,6},{2,5},{3,4},{4,3},{5,2},{6,1},{7,0},{8,15},{9,14},{10,... | collective-permute-start | bytes 196616 | tf_op jit(solution)/shard_map/ppermute | solution.py:74
  46.1 12.8 %collective-permute-start.4 = (f32[4,4,1024]{2,1,0:T(4,128)S(1)}, f32[4,4,1024]{2,1,0:T(4,128)S(1)}, u32[]{:S(2)}, u32[]{:S(2)}) collective-permute-start(f32[4,4,1024]{2,1,0:T(4,128)S(1)} %pad_maximum_fusion.8), channel_id=1, source_target_pairs={{0,15},{1,14},{2,13},{3,12},{4,11},{5,10},{6,9},{7,8},{8,7},{9,6},... | collective-permute-start | bytes 196616 | tf_op jit(solution)/shard_map/ppermute | solution.py:74
  59.0 0.8 %copy-start.4 = (f32[3,4,1024]{2,1,0:T(4,128)S(1)}, f32[3,4,1024]{2,1,0:T(4,128)}, u32[]{:S(2)}) copy-start(f32[3,4,1024]{2,1,0:T(4,128)} %param.11) | copy-start | bytes 147460
  60.2 10.4 %collective-permute-start.5 = (f32[4,1,8,1024]{3,2,1,0:T(8,128)S(1)}, f32[4,1,8,1024]{3,2,1,0:T(8,128)S(1)}, u32[]{:S(2)}, u32[]{:S(2)}) collective-permute-start(f32[4,1,8,1024]{3,2,1,0:T(8,128)S(1)} %slice.263), channel_id=1, source_target_pairs={{0,16},{16,32},{32,48},{48,64},{64,80},{80,96},{96,112},{112,128},... | collective-permute-start | bytes 393224 | tf_op jit(solution)/shard_map/ppermute | solution.py:51
  62.3 3.8 %collective-permute-start.8 = (f32[4,6,1,1024]{3,1,2,0:T(8,128)S(1)}, f32[4,6,1,1024]{3,1,2,0:T(8,128)S(1)}, u32[]{:S(2)}, u32[]{:S(2)}) collective-permute-start(f32[4,6,1,1024]{3,1,2,0:T(8,128)S(1)} %copy.25), channel_id=1, source_target_pairs={{0,1},{1,2},{2,3},{3,4},{4,5},{5,6},{6,7},{7,8},{8,9},{9,10},{10,1... | collective-permute-start | bytes 294920 | tf_op jit(solution)/shard_map/ppermute | solution.py:39
  63.6 6.9 %collective-permute-start.7 = (f32[4,6,1,1024]{3,1,2,0:T(8,128)S(1)}, f32[4,6,1,1024]{3,1,2,0:T(8,128)S(1)}, u32[]{:S(2)}, u32[]{:S(2)}) collective-permute-start(f32[4,6,1,1024]{3,1,2,0:T(8,128)S(1)} %copy.23), channel_id=1, source_target_pairs={{1,0},{2,1},{3,2},{4,3},{5,4},{6,5},{7,6},{8,7},{9,8},{10,9},{11,1... | collective-permute-start | bytes 294920 | tf_op jit(solution)/shard_map/ppermute | solution.py:41
  66.1 4.6 %copy-start.2 = (f32[4,4,8,1024]{3,2,1,0:T(8,128)S(1)}, f32[4,4,8,1024]{3,2,1,0:T(8,128)}, u32[]{:S(2)}) copy-start(f32[4,4,8,1024]{3,2,1,0:T(8,128)} %param.8) | copy-start | bytes 1572868
  66.2 4.5 %copy-start.1 = (f32[4,4,8,1024]{3,2,1,0:T(8,128)S(1)}, f32[4,4,8,1024]{3,2,1,0:T(8,128)}, u32[]{:S(2)}) copy-start(f32[4,4,8,1024]{3,2,1,0:T(8,128)} %param.7) | copy-start | bytes 1572868

commit v5 on v4

--- a/solution.py
+++ b/solution.py
@@ -9,23 +9,6 @@
 learn_rate = 0.1
 adam_step = 10
 epsilon = 1e-08
-
-
-def carried_in_2(value, axis, join, neutral, backward):
-    count, mine = (lax.axis_size(axis), lax.axis_index(axis))
-    pieces = jax.tree.map(lambda part: lax.all_gather(part, axis), value)
-    if backward:
-        pieces = jax.tree.map(lambda part: part[::-1], pieces)
-        mine = count - 1 - mine
-    total = jax.tree.map(
-        lambda part, zero: jnp.full_like(part, 0) + jnp.asarray(zero, part.dtype), value, neutral
-    )
-
-    def lap(position, total):
-        longer = join(total, jax.tree.map(lambda part: part[position], pieces))
-        return jax.tree.map(lambda new, old: jnp.where(position < mine, new, old), longer, total)
-
-    return lax.fori_loop(0, count - 1, lap, total)
 
 
 def with_halo(cells, sides, width):
@@ -51,37 +34,41 @@
     return lax.ppermute(block, axis, route)
 
 
-def front_combine(earlier, later):
-    return (earlier[0] + earlier[1][None] * later[0], earlier[1] * later[1])
-
-
-def back_combine(earlier, later):
-    return (later[0] + later[1][None] * earlier[0], later[1] * earlier[1])
-
-
 def over(front, back):
     return jnp.concatenate([front[:-1] + front[-1:] * back[:-1], front[-1:] * back[-1:]], axis=0)
 
 
-def butterfly_scan(seg_colour, seg_trans, axis):
+def depth_swap(grid, axis):
+    count, mine = (lax.axis_size(axis), lax.axis_index(axis))
+    odd = mine % 2 == 1
+    route = [(i, i + 1) for i in range(1, count - 1, 2)] + [(i, i - 1) for i in range(2, count, 2)]
+    return lax.ppermute(jnp.where(odd, grid[:, :, -1], grid[:, :, 0]), axis, route)
+
+
+def butterfly_scan(seg_colour, seg_trans, axis, plane_out):
     count, mine = (lax.axis_size(axis), lax.axis_index(axis))
     block = jnp.concatenate([seg_colour, seg_trans[None]], axis=0)
+    plane_in = None
     blank = jnp.concatenate([jnp.zeros_like(seg_colour), jnp.ones_like(seg_trans)[None]], axis=0)
     prefix, suffix = (blank, blank)
     step = 1
     while step < count:
         route = [(i, i - i % (2 * step) + 2 * step - 1 - i % (2 * step)) for i in range(count)]
-        other = lax.ppermute(block, axis, route)
+        if step == 1:
+            both = lax.ppermute(jnp.concatenate([block, plane_out], axis=0), axis, route)
+            other, plane_in = (both[: block.shape[0]], both[block.shape[0] :])
+        else:
+            other = lax.ppermute(block, axis, route)
         upper = mine % (2 * step) >= step
         joined = over(jnp.where(upper, other, block), jnp.where(upper, block, other))
         prefix = jnp.where(upper, over(other, prefix), prefix)
         suffix = jnp.where(upper, suffix, over(suffix, other))
         block = joined
         step *= 2
-    return (prefix[:-1], prefix[-1], suffix[:-1], suffix[-1])
+    return (prefix[:-1], prefix[-1], suffix[:-1], suffix[-1], plane_in)
 
 
-def render(rows, after_rows, shares, occ, target, total_depth):
+def render(rows, after_rows, shares, occ, target, total_depth, plane_out):
     scale = 4.0 / total_depth
     features = (1.0 - shares) * rows + shares * after_rows
     sigma = occ * jax.nn.softplus(features[0]) * scale
@@ -93,19 +80,9 @@
     weighted = weight[None] * colour
     seg_colour = jnp.sum(weighted, axis=2)
     seg_trans = jnp.exp(-jnp.sum(sigma, axis=1))
-    count = lax.axis_size("depth")
-    if count & (count - 1) == 0:
-        front_colour, front_trans, back_colour, back_trans = butterfly_scan(
-            seg_colour, seg_trans, "depth"
-        )
-    else:
-        blank = (jnp.zeros_like(seg_colour), jnp.ones_like(seg_trans))
-        front_colour, front_trans = carried_in_2(
-            (seg_colour, seg_trans), "depth", front_combine, blank, False
-        )
-        back_colour, back_trans = carried_in_2(
-            (seg_colour, seg_trans), "depth", back_combine, blank, True
-        )
+    front_colour, front_trans, back_colour, back_trans, plane_in = butterfly_scan(
+        seg_colour, seg_trans, "depth", plane_out
+    )
     behind = back_colour + back_trans[None]
     pixel = front_colour + front_trans[None] * (seg_colour + seg_trans[None] * behind)
     pixel_grad = 0.5 * total_depth * (pixel - target)
@@ -118,7 +95,7 @@
     )
     colour_grad = front_wide[None] * weight[None] * pixel_grad[:, :, None, :]
     density_grad = sigma_grad * occ * scale * jax.nn.sigmoid(features[0])
-    return jnp.concatenate([density_grad[None], colour_grad * colour * (1.0 - colour)], axis=0)
+    return (jnp.concatenate([density_grad[None], colour_grad * colour * (1.0 - colour)], axis=0), plane_in)
 
 
 def expand_blocks(blocks):
@@ -129,16 +106,23 @@
     depth_count = lax.axis_size("depth")
     planes = grid.shape[2]
     total_depth = planes * depth_count
-    padded = with_halo(grid, (("tile", 1), ("depth", 2)), 1)
+    padded = with_halo(grid, (("tile", 1),), 1)
+    odd = lax.axis_index("depth") % 2 == 1
+    swapped = depth_swap(grid, "depth")
     shares = (ray_offset.astype(jnp.float32) * 0.5)[None, :, None, :]
     occ = expand_blocks(occupancy.astype(jnp.float32))
-    feature_grad = render(grid, padded[:, 2:, 1:-1, :], shares, occ, target, total_depth)
+    plane_out = jnp.where(odd, grid[:, :, 0], grid[:, :, -1])
+    feature_grad, plane_in = render(grid, padded[:, 2:], shares, occ, target, total_depth, plane_out)
+    plane_before = jnp.where(odd, plane_in, swapped)[:, :, None]
+    plane_after = jnp.where(odd, swapped, plane_in)[:, :, None]
     carried = shares * feature_grad
     incoming = passed_along(carried[:, -1:], "tile", 1)
     carried_in = jnp.concatenate([incoming, carried[:, :-1]], axis=1)
     data_grad = (1.0 - shares) * feature_grad + carried_in
-    across_rows = padded[:, 2:, 1:-1, :] + padded[:, :-2, 1:-1, :]
-    across_planes = padded[:, 1:-1, 2:, :] + padded[:, 1:-1, :-2, :]
+    across_rows = padded[:, 2:] + padded[:, :-2]
+    across_planes = jnp.concatenate([grid[:, :, 1:], plane_after], axis=2) + jnp.concatenate(
+        [plane_before, grid[:, :, :-1]], axis=2
+    )
     side_pad = jnp.pad(grid, ((0, 0), (0, 0), (0, 0), (1, 1)))
     across_cols = side_pad[:, :, :, 2:] + side_pad[:, :, :, :-2]
     smooth_grad = 2.0 * tv_weight * (6.0 * grid - across_rows - across_planes - across_cols)

time: 73.6 us -> 64.6 us (0.88)
  waiting for transfers between devices: 19.7 us -> 13.5 us
  starting transfers between devices: 44.6 us -> 41 us
  local copies, waits for them, and re-layouts: 2.44 us -> 4.48 us
    ppermute x2 -> x1, waiting for transfers between devices: 6.67 us -> 0.01 us  [with_halo(): lax.ppermute(tail, axis, [(i, (i + 1) % count) for i in range(ends)])]
    ppermute x1, waiting for transfers between devices: 0.01 us -> 6.15 us  [passed_along(): return lax.ppermute(block, axis, route)]
    ppermute x4 -> x3, starting transfers between devices: 33.9 us -> 28.3 us  [butterfly_scan(): other = lax.ppermute(block, axis, route)]
    ppermute x4 -> x3, waiting for transfers between devices: 8.77 us -> 4.22 us  [butterfly_scan(): other = lax.ppermute(block, axis, route)]
    ppermute x0 -> x2, starting transfers between devices: none -> 4.49 us  [the longest x1 3.83 us: butterfly_scan(): lax.ppermute(jnp.concatenate([block, plane_out], axis=0), axis, route)]
    ppermute x2 -> x1, waiting for transfers between devices: 4.28 us -> 0.81 us  [with_halo(): lax.ppermute(head, axis, [((i + 1) % count, i) for i in range(ends)])]
    ppermute x0 -> x2, waiting for transfers between devices: none -> 2.35 us  [the longest x1 2.35 us: butterfly_scan(): lax.ppermute(jnp.concatenate([block, plane_out], axis=0), axis, route)]
    unnamed x13 -> x14, local copies, waits for them, and re-layouts: 0.79 us -> 2.89 us
  transfers between devices with their start and end apart: 9 -> 8, of which waited for: 7 -> 5; matrix products, arithmetic and copies ran while one was open for 2% -> 3% of each run, Pallas kernels for 0% -> 0%
where the time goes in v5:
time: 64.6 us; the launch traced here: 64.1 us
  starting transfers between devices  41 us (63%)
  waiting for transfers between devices  13.5 us (21%)
  local copies, waits for them, and re-layouts  4.48 us (7%)
  other arithmetic  3.96 us (6%)
  between operations  1.17 us (2%)
    ppermute x3, starting transfers between devices, butterfly_scan(): other = lax.ppermute(block, axis, route)  28.3 us
    ppermute x1, waiting for transfers between devices, passed_along(): return lax.ppermute(block, axis, route)  6.15 us
    ppermute x1, starting transfers between devices, with_halo(): lax.ppermute(head, axis, [((i + 1) % count, i) for i in range(ends)])  4.29 us
    ppermute x3, waiting for transfers between devices, butterfly_scan(): other = lax.ppermute(block, axis, route)  4.22 us
    ppermute x1, starting transfers between devices, butterfly_scan(): lax.ppermute(jnp.concatenate([block, plane_out], axis=0), axis, route)  3.83 us
    unnamed x14, local copies, waits for them, and re-layouts  2.89 us
    ppermute x1, waiting for transfers between devices, butterfly_scan(): lax.ppermute(jnp.concatenate([block, plane_out], axis=0), axis, route)  2.35 us
    sub x1, other arithmetic, body(): grid - learn_rate * (new_first / corr_one) / (jnp.sqrt(new_second / corr_...  1.94 us
  transfers between devices with their start and end apart: 8, of which 5 were waited for; matrix products, arithmetic and copies ran while one was open for 3% of the time, Pallas kernels for 0%

profile of v5, /device:TPU:24, one launch (start us, length us, event | category | flops | bytes accessed | tf_op | source)
XLA Modules:
  0.0 64.1 jit_solution(96607049558400743)
XLA Ops:
  0.6 0.0 copy-start
  0.6 1.0 %fusion.37 = (f32[4,1,8,1024]{3,2,1,0:T(8,128)S(1)}, f32[4,1,8,1024]{3,2,1,0:T(8,128)S(1)}) fusion(f32[4,4,8,1024]{3,2,1,0:T(8,128)} %param.6), kind=kLoop, calls=%fused_computation.114 | loop fusion | bytes 524288 | tf_op jit(solution)/shard_map/slice | solution.py:18
  1.7 4.3 %collective-permute-start = (f32[4,1,8,1024]{3,2,1,0:T(8,128)S(1)}, f32[4,1,8,1024]{3,2,1,0:T(8,128)S(1)}, u32[]{:S(2)}, u32[]{:S(2)}) collective-permute-start(f32[4,1,8,1024]{3,2,1,0:T(8,128)S(1)} %get-tuple-element.18), channel_id=1, source_target_pairs={{16,0},{32,16},{48,32},{64,48},{80,64},{96,80},{112,96},{128,112},... | collective-permute-start | bytes 393224 | tf_op jit(solution)/shard_map/ppermute | solution.py:24
  6.0 0.0 copy-done
  6.0 0.1 fusion.36
  6.1 0.0 copy-start.6
  6.1 0.6 %copy-done.6 = s32[1,1,128]{2,1,0:T(1,128)S(1)} copy-done((s32[1,1,128]{2,1,0:T(1,128)S(1)}, s32[1,1,128]{2,1,0:T(1,128)}, u32[]{:S(2)}) %copy-start.6) | copy-done | bytes 536
  6.8 0.1 broadcast_in_dim.12
  6.8 0.1 broadcast_in_dim.13
  6.9 0.0 copy-start.5
  7.0 0.7 %copy-done.5 = s32[4,1024]{1,0:T(4,128)S(1)} copy-done((s32[4,1024]{1,0:T(4,128)S(1)}, s32[4,1024]{1,0:T(4,128)}, u32[]{:S(2)}) %copy-start.5) | copy-done | bytes 16408
  7.7 0.8 %collective-permute-done = f32[4,1,8,1024]{3,2,1,0:T(8,128)S(1)} collective-permute-done((f32[4,1,8,1024]{3,2,1,0:T(8,128)S(1)}, f32[4,1,8,1024]{3,2,1,0:T(8,128)S(1)}, u32[]{:S(2)}, u32[]{:S(2)}) %collective-permute-start) | collective-permute-done | bytes 131104 | tf_op jit(solution)/shard_map/ppermute | solution.py:24
  8.5 0.1 fusion.9
  8.6 0.1 fusion.33
  8.7 0.1 reduce_window_sum.22
  8.8 0.1 fusion.28
  8.9 0.2 fusion.32
  9.1 3.8 %collective-permute-start.1 = (f32[8,4,1024]{2,1,0:T(4,128)S(1)}, f32[8,4,1024]{2,1,0:T(4,128)S(1)}, u32[]{:S(2)}, u32[]{:S(2)}) collective-permute-start(f32[8,4,1024]{2,1,0:T(4,128)S(1)} %pad_maximum_fusion.3), channel_id=1, source_target_pairs={{0,1},{1,0},{2,3},{3,2},{4,5},{5,4},{6,7},{7,6},{8,9},{9,8},{10,11... | collective-permute-start | bytes 393224 | tf_op jit(solution)/shard_map/ppermute | solution.py:58
  13.0 0.7 %collective-permute-start.7 = (f32[4,4,1024]{2,1,0:T(4,128)S(1)}, f32[4,4,1024]{2,1,0:T(4,128)S(1)}, u32[]{:S(2)}, u32[]{:S(2)}) collective-permute-start(f32[4,4,1024]{2,1,0:T(4,128)S(1)} %get-tuple-element.29), channel_id=1, source_target_pairs={{1,2},{3,4},{5,6},{7,8},{9,10},{11,12},{13,14},{2,1},{4,3},{6,5},{... | collective-permute-start | bytes 196616 | tf_op jit(solution)/shard_map/ppermute | solution.py:45
  13.6 2.4 %collective-permute-done.1 = f32[8,4,1024]{2,1,0:T(4,128)S(1)} collective-permute-done((f32[8,4,1024]{2,1,0:T(4,128)S(1)}, f32[8,4,1024]{2,1,0:T(4,128)S(1)}, u32[]{:S(2)}, u32[]{:S(2)}) %collective-permute-start.1) | collective-permute-done | bytes 131104 | tf_op jit(solution)/shard_map/ppermute | solution.py:58
  16.0 0.0 copy-start.3
  16.0 0.0 collective-permute-done.7
  16.0 0.8 %copy-done.3 = f32[4,4,1024]{2,1,0:T(4,128)S(1)} copy-done((f32[4,4,1024]{2,1,0:T(4,128)S(1)}, f32[4,4,1024]{2,1,0:T(4,128)}, u32[]{:S(2)}) %copy-start.3) | copy-done | bytes 65560
  16.8 0.1 select_bitcast_fusion
  17.0 9.9 %collective-permute-start.2 = (f32[4,4,1024]{2,1,0:T(4,128)S(1)}, f32[4,4,1024]{2,1,0:T(4,128)S(1)}, u32[]{:S(2)}, u32[]{:S(2)}) collective-permute-start(f32[4,4,1024]{2,1,0:T(4,128)S(1)} %pad_maximum_fusion.5), channel_id=1, source_target_pairs={{0,3},{1,2},{2,1},{3,0},{4,7},{5,6},{6,5},{7,4},{8,11},{9,10},{10,... | collective-permute-start | bytes 196616 | tf_op jit(solution)/shard_map/ppermute | solution.py:61
  27.0 1.9 %collective-permute-start.6 = (f32[4,1,8,1024]{3,2,1,0:T(8,128)S(1)}, f32[4,1,8,1024]{3,2,1,0:T(8,128)S(1)}, u32[]{:S(2)}, u32[]{:S(2)}) collective-permute-start(f32[4,1,8,1024]{3,2,1,0:T(8,128)S(1)} %get-tuple-element.19), channel_id=1, source_target_pairs={{0,16},{16,32},{32,48},{48,64},{64,80},{80,96},{96,112},{112,128},... | collective-permute-start | bytes 393224 | tf_op jit(solution)/shard_map/ppermute | solution.py:22
  28.9 0.3 reduce_window_sum.23
  29.3 0.0 collective-permute-done.2
  29.4 11.4 %collective-permute-start.3 = (f32[4,4,1024]{2,1,0:T(4,128)S(1)}, f32[4,4,1024]{2,1,0:T(4,128)S(1)}, u32[]{:S(2)}, u32[]{:S(2)}) collective-permute-start(f32[4,4,1024]{2,1,0:T(4,128)S(1)} %pad_maximum_fusion.6), channel_id=1, source_target_pairs={{0,7},{1,6},{2,5},{3,4},{4,3},{5,2},{6,1},{7,0},{8,15},{9,14},{10,... | collective-permute-start | bytes 196616 | tf_op jit(solution)/shard_map/ppermute | solution.py:61
  40.9 2.1 %collective-permute-done.3 = f32[4,4,1024]{2,1,0:T(4,128)S(1)} collective-permute-done((f32[4,4,1024]{2,1,0:T(4,128)S(1)}, f32[4,4,1024]{2,1,0:T(4,128)S(1)}, u32[]{:S(2)}, u32[]{:S(2)}) %collective-permute-start.3) | collective-permute-done | bytes 65568 | tf_op jit(solution)/shard_map/ppermute | solution.py:61
  43.1 7.0 %collective-permute-start.4 = (f32[4,4,1024]{2,1,0:T(4,128)S(1)}, f32[4,4,1024]{2,1,0:T(4,128)S(1)}, u32[]{:S(2)}, u32[]{:S(2)}) collective-permute-start(f32[4,4,1024]{2,1,0:T(4,128)S(1)} %pad_maximum_fusion.7), channel_id=1, source_target_pairs={{0,15},{1,14},{2,13},{3,12},{4,11},{5,10},{6,9},{7,8},{8,7},{9,6},... | collective-permute-start | bytes 196616 | tf_op jit(solution)/shard_map/ppermute | solution.py:61
  50.3 2.1 %collective-permute-done.4 = f32[4,4,1024]{2,1,0:T(4,128)S(1)} collective-permute-done((f32[4,4,1024]{2,1,0:T(4,128)S(1)}, f32[4,4,1024]{2,1,0:T(4,128)S(1)}, u32[]{:S(2)}, u32[]{:S(2)}) %collective-permute-start.4) | collective-permute-done | bytes 65568 | tf_op jit(solution)/shard_map/ppermute | solution.py:61
  52.5 0.1 multiply_bitcast_fusion.1
  52.5 0.0 copy-start.4
  52.6 0.7 %copy-done.4 = f32[3,4,1024]{2,1,0:T(4,128)S(1)} copy-done((f32[3,4,1024]{2,1,0:T(4,128)S(1)}, f32[3,4,1024]{2,1,0:T(4,128)}, u32[]{:S(2)}) %copy-start.4) | copy-done | bytes 49176
  53.4 0.2 multiply_reduce_fusion
  53.6 0.1 fusion.18
  53.7 0.1 fusion.10
  53.7 1.9 %collective-permute-start.5 = (f32[4,1,8,1024]{3,2,1,0:T(8,128)S(1)}, f32[4,1,8,1024]{3,2,1,0:T(8,128)S(1)}, u32[]{:S(2)}, u32[]{:S(2)}) collective-permute-start(f32[4,1,8,1024]{3,2,1,0:T(8,128)S(1)} %slice.274), channel_id=1, source_target_pairs={{0,16},{16,32},{32,48},{48,64},{64,80},{80,96},{96,112},{112,128},... | collective-permute-start | bytes 393224 | tf_op jit(solution)/shard_map/ppermute | solution.py:34
  55.7 0.1 fusion.35
  55.8 0.0 copy-start.1
  55.8 0.0 copy-start.2
  55.8 0.1 copy.18
  55.9 0.1 copy.17
  56.0 0.0 collective-permute-done.6
  56.0 6.1 %collective-permute-done.5 = f32[4,1,8,1024]{3,2,1,0:T(8,128)S(1)} collective-permute-done((f32[4,1,8,1024]{3,2,1,0:T(8,128)S(1)}, f32[4,1,8,1024]{3,2,1,0:T(8,128)S(1)}, u32[]{:S(2)}, u32[]{:S(2)}) %collective-permute-start.5) | collective-permute-done | bytes 131104 | tf_op jit(solution)/shard_map/ppermute | solution.py:34
  62.2 0.0 copy-done.1
  62.2 0.0 copy-done.2
  62.2 1.9 %divide_subtract_fusion = (f32[4,4,8,1024]{3,2,1,0:T(8,128)}, f32[4,4,8,1024]{3,2,1,0:T(8,128)}, f32[4,4,8,1024]{3,2,1,0:T(8,128)}) fusion(f32[4,4,8,1024]{3,2,1,0:T(8,128)S(1)} %copy-done, f32[4,4,8,1024]{3,2,1,0:T(8,128)S(1)} %copy-done.1, f32[4,4,8,1024]{3,2,1,0:T(8,128)S(1)} %copy-done.2, f32[4,4,7,1024]{3,2,1,0:T(8,128)S(1)} %get-tuple-element.14, ...), kind=kLoop, calls=%fused_computation.18 | loop fusion | flops 3801088 | bytes 5521408 | tf_op jit(solution)/shard_map/sub | solution.py:134
  (34 shorter events, 0.7 us)
Async XLA Ops:
  0.6 5.4 %copy-start = (f32[4,4,8,1024]{3,2,1,0:T(8,128)S(1)}, f32[4,4,8,1024]{3,2,1,0:T(8,128)}, u32[]{:S(2)}) copy-start(f32[4,4,8,1024]{3,2,1,0:T(8,128)} %param.6) | copy-start | bytes 1572868
  1.7 6.8 %collective-permute-start = (f32[4,1,8,1024]{3,2,1,0:T(8,128)S(1)}, f32[4,1,8,1024]{3,2,1,0:T(8,128)S(1)}, u32[]{:S(2)}, u32[]{:S(2)}) collective-permute-start(f32[4,1,8,1024]{3,2,1,0:T(8,128)S(1)} %get-tuple-element.18), channel_id=1, source_target_pairs={{16,0},{32,16},{48,32},{64,48},{80,64},{96,80},{112,96},{128,112},... | collective-permute-start | bytes 393224 | tf_op jit(solution)/shard_map/ppermute | solution.py:24
  6.1 0.7 %copy-start.6 = (s32[1,1,128]{2,1,0:T(1,128)S(1)}, s32[1,1,128]{2,1,0:T(1,128)}, u32[]{:S(2)}) copy-start(s32[1,1,128]{2,1,0:T(1,128)} %param.10) | copy-start | bytes 1540
  6.9 0.7 %copy-start.5 = (s32[4,1024]{1,0:T(4,128)S(1)}, s32[4,1024]{1,0:T(4,128)}, u32[]{:S(2)}) copy-start(s32[4,1024]{1,0:T(4,128)} %param.9) | copy-start | bytes 49156
  9.1 6.9 %collective-permute-start.1 = (f32[8,4,1024]{2,1,0:T(4,128)S(1)}, f32[8,4,1024]{2,1,0:T(4,128)S(1)}, u32[]{:S(2)}, u32[]{:S(2)}) collective-permute-start(f32[8,4,1024]{2,1,0:T(4,128)S(1)} %pad_maximum_fusion.3), channel_id=1, source_target_pairs={{0,1},{1,0},{2,3},{3,2},{4,5},{5,4},{6,7},{7,6},{8,9},{9,8},{10,11... | collective-permute-start | bytes 393224 | tf_op jit(solution)/shard_map/ppermute | solution.py:58
  13.0 3.1 %collective-permute-start.7 = (f32[4,4,1024]{2,1,0:T(4,128)S(1)}, f32[4,4,1024]{2,1,0:T(4,128)S(1)}, u32[]{:S(2)}, u32[]{:S(2)}) collective-permute-start(f32[4,4,1024]{2,1,0:T(4,128)S(1)} %get-tuple-element.29), channel_id=1, source_target_pairs={{1,2},{3,4},{5,6},{7,8},{9,10},{11,12},{13,14},{2,1},{4,3},{6,5},{... | collective-permute-start | bytes 196616 | tf_op jit(solution)/shard_map/ppermute | solution.py:45
  16.0 0.8 %copy-start.3 = (f32[4,4,1024]{2,1,0:T(4,128)S(1)}, f32[4,4,1024]{2,1,0:T(4,128)}, u32[]{:S(2)}) copy-start(f32[4,4,1024]{2,1,0:T(4,128)} %constant.88.clone.1) | copy-start | bytes 196612
  17.0 12.3 %collective-permute-start.2 = (f32[4,4,1024]{2,1,0:T(4,128)S(1)}, f32[4,4,1024]{2,1,0:T(4,128)S(1)}, u32[]{:S(2)}, u32[]{:S(2)}) collective-permute-start(f32[4,4,1024]{2,1,0:T(4,128)S(1)} %pad_maximum_fusion.5), channel_id=1, source_target_pairs={{0,3},{1,2},{2,1},{3,0},{4,7},{5,6},{6,5},{7,4},{8,11},{9,10},{10,... | collective-permute-start | bytes 196616 | tf_op jit(solution)/shard_map/ppermute | solution.py:61
  27.0 29.0 %collective-permute-start.6 = (f32[4,1,8,1024]{3,2,1,0:T(8,128)S(1)}, f32[4,1,8,1024]{3,2,1,0:T(8,128)S(1)}, u32[]{:S(2)}, u32[]{:S(2)}) collective-permute-start(f32[4,1,8,1024]{3,2,1,0:T(8,128)S(1)} %get-tuple-element.19), channel_id=1, source_target_pairs={{0,16},{16,32},{32,48},{48,64},{64,80},{80,96},{96,112},{112,128},... | collective-permute-start | bytes 393224 | tf_op jit(solution)/shard_map/ppermute | solution.py:22
  29.4 13.6 %collective-permute-start.3 = (f32[4,4,1024]{2,1,0:T(4,128)S(1)}, f32[4,4,1024]{2,1,0:T(4,128)S(1)}, u32[]{:S(2)}, u32[]{:S(2)}) collective-permute-start(f32[4,4,1024]{2,1,0:T(4,128)S(1)} %pad_maximum_fusion.6), channel_id=1, source_target_pairs={{0,7},{1,6},{2,5},{3,4},{4,3},{5,2},{6,1},{7,0},{8,15},{9,14},{10,... | collective-permute-start | bytes 196616 | tf_op jit(solution)/shard_map/ppermute | solution.py:61
  43.1 9.3 %collective-permute-start.4 = (f32[4,4,1024]{2,1,0:T(4,128)S(1)}, f32[4,4,1024]{2,1,0:T(4,128)S(1)}, u32[]{:S(2)}, u32[]{:S(2)}) collective-permute-start(f32[4,4,1024]{2,1,0:T(4,128)S(1)} %pad_maximum_fusion.7), channel_id=1, source_target_pairs={{0,15},{1,14},{2,13},{3,12},{4,11},{5,10},{6,9},{7,8},{8,7},{9,6},... | collective-permute-start | bytes 196616 | tf_op jit(solution)/shard_map/ppermute | solution.py:61
  52.5 0.8 %copy-start.4 = (f32[3,4,1024]{2,1,0:T(4,128)S(1)}, f32[3,4,1024]{2,1,0:T(4,128)}, u32[]{:S(2)}) copy-start(f32[3,4,1024]{2,1,0:T(4,128)} %param.11) | copy-start | bytes 147460
  53.7 8.4 %collective-permute-start.5 = (f32[4,1,8,1024]{3,2,1,0:T(8,128)S(1)}, f32[4,1,8,1024]{3,2,1,0:T(8,128)S(1)}, u32[]{:S(2)}, u32[]{:S(2)}) collective-permute-start(f32[4,1,8,1024]{3,2,1,0:T(8,128)S(1)} %slice.274), channel_id=1, source_target_pairs={{0,16},{16,32},{32,48},{48,64},{64,80},{80,96},{96,112},{112,128},... | collective-permute-start | bytes 393224 | tf_op jit(solution)/shard_map/ppermute | solution.py:34
  55.8 6.4 %copy-start.1 = (f32[4,4,8,1024]{3,2,1,0:T(8,128)S(1)}, f32[4,4,8,1024]{3,2,1,0:T(8,128)}, u32[]{:S(2)}) copy-start(f32[4,4,8,1024]{3,2,1,0:T(8,128)} %param.7) | copy-start | bytes 1572868
  55.8 6.4 %copy-start.2 = (f32[4,4,8,1024]{3,2,1,0:T(8,128)S(1)}, f32[4,4,8,1024]{3,2,1,0:T(8,128)}, u32[]{:S(2)}) copy-start(f32[4,4,8,1024]{3,2,1,0:T(8,128)} %param.8) | copy-start | bytes 1572868

commit v6 on v5

--- a/solution.py
+++ b/solution.py
@@ -85,17 +85,25 @@
     )
     behind = back_colour + back_trans[None]
     pixel = front_colour + front_trans[None] * (seg_colour + seg_trans[None] * behind)
-    pixel_grad = 0.5 * total_depth * (pixel - target)
-    upto = jnp.cumsum(weighted, axis=2)
-    remain = seg_colour[:, :, None, :] - upto + (seg_trans[None] * behind)[:, :, None, :]
-    next_trans = trans * fade
-    front_wide = front_trans[:, None, :]
-    sigma_grad = front_wide * jnp.sum(
-        pixel_grad[:, :, None, :] * (next_trans[None] * colour - remain), axis=0
-    )
-    colour_grad = front_wide[None] * weight[None] * pixel_grad[:, :, None, :]
-    density_grad = sigma_grad * occ * scale * jax.nn.sigmoid(features[0])
-    return (jnp.concatenate([density_grad[None], colour_grad * colour * (1.0 - colour)], axis=0), plane_in)
+
+    def backward(rows):
+        pixel_grad = 0.5 * total_depth * (pixel[:, rows] - target[:, rows])
+        part = weighted[:, rows]
+        upto = jnp.cumsum(part, axis=2)
+        seg_c = seg_colour[:, rows]
+        remain = seg_c[:, :, None, :] - upto + (seg_trans[None, rows] * behind[:, rows])[:, :, None, :]
+        next_trans = trans[rows] * fade[rows]
+        front_wide = front_trans[rows][:, None, :]
+        col = colour[:, rows]
+        sigma_grad = front_wide * jnp.sum(
+            pixel_grad[:, :, None, :] * (next_trans[None] * col - remain), axis=0
+        )
+        colour_grad = front_wide[None] * weight[None, rows] * pixel_grad[:, :, None, :]
+        density_grad = sigma_grad * occ[rows] * scale * jax.nn.sigmoid(features[0, rows])
+        return jnp.concatenate([density_grad[None], colour_grad * col * (1.0 - col)], axis=0)
+
+    last = slice(rows.shape[1] - 1, rows.shape[1])
+    return (backward(last), backward(slice(None)), plane_in)
 
 
 def expand_blocks(blocks):
@@ -112,13 +120,14 @@
     shares = (ray_offset.astype(jnp.float32) * 0.5)[None, :, None, :]
     occ = expand_blocks(occupancy.astype(jnp.float32))
     plane_out = jnp.where(odd, grid[:, :, 0], grid[:, :, -1])
-    feature_grad, plane_in = render(grid, padded[:, 2:], shares, occ, target, total_depth, plane_out)
+    last_grad, feature_grad, plane_in = render(
+        grid, padded[:, 2:], shares, occ, target, total_depth, plane_out
+    )
     plane_before = jnp.where(odd, plane_in, swapped)[:, :, None]
     plane_after = jnp.where(odd, swapped, plane_in)[:, :, None]
     carried = shares * feature_grad
-    incoming = passed_along(carried[:, -1:], "tile", 1)
-    carried_in = jnp.concatenate([incoming, carried[:, :-1]], axis=1)
-    data_grad = (1.0 - shares) * feature_grad + carried_in
+    incoming = passed_along(shares[:, -1:] * last_grad, "tile", 1)
+    data_grad = (1.0 - shares) * feature_grad
     across_rows = padded[:, 2:] + padded[:, :-2]
     across_planes = jnp.concatenate([grid[:, :, 1:], plane_after], axis=2) + jnp.concatenate(
         [plane_before, grid[:, :, :-1]], axis=2
@@ -126,7 +135,14 @@
     side_pad = jnp.pad(grid, ((0, 0), (0, 0), (0, 0), (1, 1)))
     across_cols = side_pad[:, :, :, 2:] + side_pad[:, :, :, :-2]
     smooth_grad = 2.0 * tv_weight * (6.0 * grid - across_rows - across_planes - across_cols)
-    grad = data_grad + smooth_grad
+    grad = data_grad + jnp.concatenate([jnp.zeros_like(incoming), carried[:, :-1]], axis=1) + smooth_grad
+    outs = adam(grid, first_moment, second_moment, grad)
+    head_grad = data_grad[:, :1] + incoming + smooth_grad[:, :1]
+    heads = adam(grid[:, :1], first_moment[:, :1], second_moment[:, :1], head_grad)
+    return tuple(lax.dynamic_update_slice_in_dim(out, head, 0, axis=1) for out, head in zip(outs, heads))
+
+
+def adam(grid, first_moment, second_moment, grad):
     new_first = beta_one * first_moment + (1.0 - beta_one) * grad
     new_second = beta_two * second_moment + (1.0 - beta_two) * grad * grad
     corr_one = 1.0 - beta_one**adam_step

time: 64.6 us -> 83.9 us (1.30)
  local copies, waits for them, and re-layouts: 4.48 us -> 14.6 us
  other arithmetic: 3.96 us -> 13 us
  waiting for transfers between devices: 13.5 us -> 12.5 us
    unnamed x14 -> x57, local copies, waits for them, and re-layouts: 2.89 us -> 9.47 us
    ppermute x3, starting transfers between devices: 28.3 us -> 24 us  [butterfly_scan(): other = lax.ppermute(block, axis, route)]
    ppermute x1, starting transfers between devices: 3.83 us -> 6.37 us  [butterfly_scan(): lax.ppermute(jnp.concatenate([block, plane_out], axis=0), axis, route)]
    ppermute x1, waiting for transfers between devices: 6.15 us -> 3.85 us  [passed_along(): return lax.ppermute(block, axis, route)]
    slice x4 -> x7, local copies, waits for them, and re-layouts: 1.19 us -> 3.35 us  [the longest x1 0.72 us: backward(): seg_trans[None, rows] * behind[:, rows]]
    another operation x1 -> x2, other arithmetic: 0.34 us -> 1.98 us  [backward(): upto = jnp.cumsum(part, axis=2)]
    mul x3 -> x9, other arithmetic: 0.17 us -> 1.76 us  [the longest x1 0.8 us: backward(): front_wide[None] * weight[None, rows] * pixel_grad[:, :, None, :]]
    broadcast_in_dim x1 -> x2, other arithmetic: 0.1 us -> 1.6 us  [the longest x1 1.59 us: body(): plane_after = jnp.where(odd, swapped, plane_in)[:, :, None]]
  transfers between devices with their start and end apart: 8 -> 8, of which waited for: 5 -> 5; matrix products, arithmetic and copies ran while one was open for 3% -> 20% of each run, Pallas kernels for 0% -> 0%
where the time goes in v6:
time: 83.9 us; the launch traced here: 82.7 us
  starting transfers between devices  41.3 us (49%)
  local copies, waits for them, and re-layouts  14.6 us (17%)
  other arithmetic  13 us (15%)
  waiting for transfers between devices  12.5 us (15%)
  between operations  1.31 us (2%)
    ppermute x3, starting transfers between devices, butterfly_scan(): other = lax.ppermute(block, axis, route)  24 us
    unnamed x57, local copies, waits for them, and re-layouts  9.47 us
    ppermute x1, starting transfers between devices, butterfly_scan(): lax.ppermute(jnp.concatenate([block, plane_out], axis=0), axis, route)  6.37 us
    ppermute x1, starting transfers between devices, with_halo(): lax.ppermute(head, axis, [((i + 1) % count, i) for i in range(ends)])  5.75 us
    ppermute x3, waiting for transfers between devices, butterfly_scan(): other = lax.ppermute(block, axis, route)  4.7 us
    ppermute x1, waiting for transfers between devices, passed_along(): return lax.ppermute(block, axis, route)  3.85 us
    ppermute x1, waiting for transfers between devices, butterfly_scan(): lax.ppermute(jnp.concatenate([block, plane_out], axis=0), axis, route)  3.22 us
    ppermute x1, starting transfers between devices, passed_along(): return lax.ppermute(block, axis, route)  2.05 us
  transfers between devices with their start and end apart: 8, of which 5 were waited for; matrix products, arithmetic and copies ran while one was open for 20% of the time, Pallas kernels for 0%

profile of v6, /device:TPU:24, one launch (start us, length us, event | category | flops | bytes accessed | tf_op | source)
XLA Modules:
  0.0 82.7 jit_solution(1421811142815123397)
XLA Ops:
  0.7 1.4 %fusion.56 = (f32[4,4,1,1024]{3,2,1,0:T(1,128)S(1)}, f32[4,4,1,1024]{3,2,1,0:T(1,128)S(1)}) fusion(f32[4,4,8,1024]{3,2,1,0:T(8,128)} %param.6), kind=kLoop, calls=%fused_computation.157 | loop fusion | bytes 262144 | tf_op jit(solution)/shard_map/slice | solution.py:122
  2.1 0.7 select_bitcast_fusion.2
  2.8 1.3 %collective-permute-start.6 = (f32[4,4,1024]{2,1,0:T(4,128)}, f32[4,4,1024]{2,1,0:T(4,128)}, u32[]{:S(2)}, u32[]{:S(2)}) collective-permute-start(f32[4,4,1024]{2,1,0:T(4,128)} %get-tuple-element.42), channel_id=1, source_target_pairs={{1,2},{3,4},{5,6},{7,8},{9,10},{11,12},{13,14},{2,1},{4,3},{6,5},{... | collective-permute-start | bytes 196616 | tf_op jit(solution)/shard_map/ppermute | solution.py:45
  4.1 0.7 fusion.54
  4.7 1.9 %collective-permute-start.5 = (f32[4,1,8,1024]{3,2,1,0:T(8,128)}, f32[4,1,8,1024]{3,2,1,0:T(8,128)}, u32[]{:S(2)}, u32[]{:S(2)}) collective-permute-start(f32[4,1,8,1024]{3,2,1,0:T(8,128)} %get-tuple-element.27), channel_id=1, source_target_pairs={{0,16},{16,32},{32,48},{48,64},{64,80},{80,96},{96,112},{112,128},... | collective-permute-start | bytes 393224 | tf_op jit(solution)/shard_map/ppermute | solution.py:22
  6.6 5.8 %collective-permute-start = (f32[4,1,8,1024]{3,2,1,0:T(8,128)S(1)}, f32[4,1,8,1024]{3,2,1,0:T(8,128)S(1)}, u32[]{:S(2)}, u32[]{:S(2)}) collective-permute-start(f32[4,1,8,1024]{3,2,1,0:T(8,128)S(1)} %get-tuple-element.28), channel_id=1, source_target_pairs={{16,0},{32,16},{48,32},{64,48},{80,64},{96,80},{112,96},{128,112},... | collective-permute-start | bytes 393224 | tf_op jit(solution)/shard_map/ppermute | solution.py:24
  12.4 0.1 fusion.55
  12.5 0.0 copy-start.25
  12.6 0.7 copy-done.25
  13.3 0.0 copy-start.26
  13.3 0.6 slice.351
  13.9 0.1 copy-done.26
  13.9 0.1 broadcast_in_dim.18
  14.0 0.1 broadcast_in_dim.19
  14.1 0.8 collective-permute-done
  14.9 0.1 fusion.9
  15.0 0.6 copy-done.7
  15.6 0.1 fusion.48
  15.7 0.1 reduce_window_sum.35
  15.8 0.2 fusion.44
  16.0 0.6 negate_exponential_fusion.1
  16.6 0.2 fusion.53
  16.8 6.4 %collective-permute-start.1 = (f32[8,4,1024]{2,1,0:T(4,128)S(1)}, f32[8,4,1024]{2,1,0:T(4,128)S(1)}, u32[]{:S(2)}, u32[]{:S(2)}) collective-permute-start(f32[8,4,1024]{2,1,0:T(4,128)S(1)} %pad_maximum_fusion.3), channel_id=1, source_target_pairs={{0,1},{1,0},{2,3},{3,2},{4,5},{5,4},{6,7},{7,6},{8,9},{9,8},{10,11... | collective-permute-start | bytes 393224 | tf_op jit(solution)/shard_map/ppermute | solution.py:58
  23.3 3.2 %collective-permute-done.1 = f32[8,4,1024]{2,1,0:T(4,128)S(1)} collective-permute-done((f32[8,4,1024]{2,1,0:T(4,128)S(1)}, f32[8,4,1024]{2,1,0:T(4,128)S(1)}, u32[]{:S(2)}, u32[]{:S(2)}) %collective-permute-start.1) | collective-permute-done | bytes 131104 | tf_op jit(solution)/shard_map/ppermute | solution.py:58
  26.5 0.8 copy-done.23
  27.3 1.6 %select_bitcast_fusion.1 = (f32[4,4,1,1024]{3,1,0,2:T(4,128)}, f32[4,4,1,1024]{3,1,0,2:T(4,128)}, f32[4,4,1024]{2,1,0:T(4,128)S(1)}, f32[4,4,1024]{2,1,0:T(4,128...) fusion(f32[4,4,1024]{2,1,0:T(4,128)} %collective-permute-done.6, f32[8,4,1024]{2,1,0:T(4,128)S(1)} %collective-permute-done.1, ...), kind=kLoop, calls=%fused_computation.76 | loop fusion | flops 131072 | bytes 786434 | tf_op jit(solution)/shard_map/broadcast_in_dim | solution.py:127
  29.0 0.6 copy-done.18
  29.5 0.6 pad_maximum_fusion.5
  30.2 7.5 %collective-permute-start.2 = (f32[4,4,1024]{2,1,0:T(4,128)}, f32[4,4,1024]{2,1,0:T(4,128)}, u32[]{:S(2)}, u32[]{:S(2)}) collective-permute-start(f32[4,4,1024]{2,1,0:T(4,128)} %pad_maximum_fusion.5), channel_id=1, source_target_pairs={{0,3},{1,2},{2,1},{3,0},{4,7},{5,6},{6,5},{7,4},{8,11},{9,10},{10,... | collective-permute-start | bytes 196616 | tf_op jit(solution)/shard_map/ppermute | solution.py:61
  37.8 0.6 multiply_bitcast_fusion.2
  38.4 0.6 slice.357
  39.0 0.6 slice.358
  39.6 0.3 reduce_window_sum.37
  40.0 0.7 slice.359
  40.7 0.7 copy.36
  41.4 1.6 %reduce_window_sum.38 = f32[3,1,8,1024]{3,2,1,0:T(8,128)} reduce-window(f32[3,1,8,1024]{3,2,1,0:T(8,128)} %slice.358, f32[]{:T(128)} %constant.104.clone.1), window={size=1x1x8x1 pad=0_0x0_0x7_0x0_0}, to_apply=%region_5.6 | reduce-window | flops 172032 | bytes 196612 | tf_op jit(solution)/shard_map/jit(cumsum)/reduce_window_sum | solution.py:92
  43.0 0.1 copy.21
  43.1 0.8 copy-done.14
  43.9 0.1 copy.22
  44.0 0.7 copy-done.10
  44.7 0.9 %broadcast_select_fusion.1 = (f32[4,4,1024]{2,1,0:T(4,128)S(1)}, f32[4,4,1024]{2,1,0:T(4,128)S(1)}) fusion(f32[4,4,1024]{2,1,0:T(4,128)} %collective-permute-done.2, pred[]{:T(512)S(6)} %ge.14, f32[1,4,1024]{2,1,0:T(4,128)S(1)} %copy-done.19, f32[3,4,1024]{2,1,0:T(4,128)S(1)} %copy-done.10), kind=kLoop, calls=%fused_computation.113 | loop fusion | flops 49152 | bytes 262145 | tf_op jit(solution)/shard_map/jit(_where)/select_n | solution.py:63
  45.6 8.5 %collective-permute-start.3 = (f32[4,4,1024]{2,1,0:T(4,128)S(1)}, f32[4,4,1024]{2,1,0:T(4,128)S(1)}, u32[]{:S(2)}, u32[]{:S(2)}) collective-permute-start(f32[4,4,1024]{2,1,0:T(4,128)S(1)} %pad_maximum_fusion.6), channel_id=1, source_target_pairs={{0,7},{1,6},{2,5},{3,4},{4,3},{5,2},{6,1},{7,0},{8,15},{9,14},{10,... | collective-permute-start | bytes 196616 | tf_op jit(solution)/shard_map/ppermute | solution.py:61
  54.2 0.7 slice_bitcast_fusion.4
  54.9 0.8 %slice_add_fusion.5 = (f32[3,4,1024]{2,1,0:T(4,128)S(1)}, f32[3,4,1024]{2,1,0:T(4,128)S(1)}) fusion(f32[4,4,1024]{2,1,0:T(4,128)S(1)} %get-tuple-element.39, f32[4,4,1024]{2,1,0:T(4,128)} %collective-permute-done.2, f32[4,1024]{1,0:T(4,128)S(1)} %get-tuple-element.65, f32[4,4,1024]{2,1,0:T(4,128)S(1)} %copy-done.3, f32[4,1024]{1,0:T(4,128)S(1)} %get-tuple-element.68), kind=kLoop, calls=%fused_computation.85 | loop fusion | flops 49152 | bytes 278528 | tf_op jit(solution)/shard_map/add | solution.py:38
  55.8 2.6 %collective-permute-done.3 = f32[4,4,1024]{2,1,0:T(4,128)S(1)} collective-permute-done((f32[4,4,1024]{2,1,0:T(4,128)S(1)}, f32[4,4,1024]{2,1,0:T(4,128)S(1)}, u32[]{:S(2)}, u32[]{:S(2)}) %collective-permute-start.3) | collective-permute-done | bytes 65568 | tf_op jit(solution)/shard_map/ppermute | solution.py:61
  58.5 7.9 %collective-permute-start.4 = (f32[4,4,1024]{2,1,0:T(4,128)S(1)}, f32[4,4,1024]{2,1,0:T(4,128)S(1)}, u32[]{:S(2)}, u32[]{:S(2)}) collective-permute-start(f32[4,4,1024]{2,1,0:T(4,128)S(1)} %pad_maximum_fusion.7), channel_id=1, source_target_pairs={{0,15},{1,14},{2,13},{3,12},{4,11},{5,10},{6,9},{7,8},{8,7},{9,6},... | collective-permute-start | bytes 196616 | tf_op jit(solution)/shard_map/ppermute | solution.py:61
  66.5 2.1 %collective-permute-done.4 = f32[4,4,1024]{2,1,0:T(4,128)S(1)} collective-permute-done((f32[4,4,1024]{2,1,0:T(4,128)S(1)}, f32[4,4,1024]{2,1,0:T(4,128)S(1)}, u32[]{:S(2)}, u32[]{:S(2)}) %collective-permute-start.4) | collective-permute-done | bytes 65568 | tf_op jit(solution)/shard_map/ppermute | solution.py:61
  68.7 0.8 bitcast_multiply_fusion.1
  69.6 0.7 copy-done.17
  70.2 0.2 multiply_bitcast_fusion.1
  70.4 0.5 copy-done.21
  71.0 0.1 copy-done.22
  71.2 0.8 copy-done.11
  72.1 0.2 multiply_reduce_fusion
  72.3 0.1 fusion.22
  72.4 0.6 copy-done.24
  73.0 2.1 %collective-permute-start.7 = (f32[4,1,8,1024]{3,2,1,0:T(8,128)S(1)}, f32[4,1,8,1024]{3,2,1,0:T(8,128)S(1)}, u32[]{:S(2)}, u32[]{:S(2)}) collective-permute-start(f32[4,1,8,1024]{3,2,1,0:T(8,128)S(1)} %maximum_multiply_fusion), channel_id=1, source_target_pairs={{0,16},{16,32},{32,48},{48,64},{64,80},{80,96},{96,112},{112,128},... | collective-permute-start | bytes 393224 | tf_op jit(solution)/shard_map/ppermute | solution.py:34
  75.1 0.8 copy-done.8
  76.0 1.7 %divide_subtract_fusion = (f32[4,4,8,1024]{3,2,1,0:T(8,128)S(1)}, f32[4,4,8,1024]{3,2,1,0:T(8,128)S(1)}, f32[4,4,8,1024]{3,2,1,0:T(8,128)S(1)}, f32[4,4,8,1024]{3,2,1,0:T(8,128)S(1)}, f32[4,4,8,1024]{3,2,1,0:T(8,128)S(1)}) fusion(f32[4,4,8,1024]{3,2,1,0:T(8,128)S(1)} %copy-done, f32[4,3,8,1024]{3,2,1,0:T(8,128)S(1)} %fusion.11, ...), kind=kLoop, calls=%fused_computation.19 | loop fusion | flops 3670016 | bytes 6438912 | tf_op jit(solution)/shard_map/sub | solution.py:150
  77.7 3.9 %collective-permute-done.7 = f32[4,1,8,1024]{3,2,1,0:T(8,128)S(1)} collective-permute-done((f32[4,1,8,1024]{3,2,1,0:T(8,128)S(1)}, f32[4,1,8,1024]{3,2,1,0:T(8,128)S(1)}, u32[]{:S(2)}, u32[]{:S(2)}) %collective-permute-start.7) | collective-permute-done | bytes 131104 | tf_op jit(solution)/shard_map/ppermute | solution.py:34
  81.6 0.1 fusion.35
  81.7 0.7 copy-done.6
  82.4 0.2 copy-done.4
  82.5 0.2 copy-done.5
  (76 shorter events, 0.8 us)
Async XLA Ops:
  0.6 3.4 %copy-start = (f32[4,4,8,1024]{3,2,1,0:T(8,128)S(1)}, f32[4,4,8,1024]{3,2,1,0:T(8,128)}, u32[]{:S(2)}) copy-start(f32[4,4,8,1024]{3,2,1,0:T(8,128)} %param.6) | copy-start | bytes 1572868
  2.8 23.8 %collective-permute-start.6 = (f32[4,4,1024]{2,1,0:T(4,128)}, f32[4,4,1024]{2,1,0:T(4,128)}, u32[]{:S(2)}, u32[]{:S(2)}) collective-permute-start(f32[4,4,1024]{2,1,0:T(4,128)} %get-tuple-element.42), channel_id=1, source_target_pairs={{1,2},{3,4},{5,6},{7,8},{9,10},{11,12},{13,14},{2,1},{4,3},{6,5},{... | collective-permute-start | bytes 196616 | tf_op jit(solution)/shard_map/ppermute | solution.py:45
  4.7 70.4 %collective-permute-start.5 = (f32[4,1,8,1024]{3,2,1,0:T(8,128)}, f32[4,1,8,1024]{3,2,1,0:T(8,128)}, u32[]{:S(2)}, u32[]{:S(2)}) collective-permute-start(f32[4,1,8,1024]{3,2,1,0:T(8,128)} %get-tuple-element.27), channel_id=1, source_target_pairs={{0,16},{16,32},{32,48},{48,64},{64,80},{80,96},{96,112},{112,128},... | collective-permute-start | bytes 393224 | tf_op jit(solution)/shard_map/ppermute | solution.py:22
  6.6 8.3 %collective-permute-start = (f32[4,1,8,1024]{3,2,1,0:T(8,128)S(1)}, f32[4,1,8,1024]{3,2,1,0:T(8,128)S(1)}, u32[]{:S(2)}, u32[]{:S(2)}) collective-permute-start(f32[4,1,8,1024]{3,2,1,0:T(8,128)S(1)} %get-tuple-element.28), channel_id=1, source_target_pairs={{16,0},{32,16},{48,32},{64,48},{80,64},{96,80},{112,96},{128,112},... | collective-permute-start | bytes 393224 | tf_op jit(solution)/shard_map/ppermute | solution.py:24
  12.5 0.7 copy-start.25
  13.3 0.7 copy-start.26
  14.1 1.7 %copy-start.16 = (f32[1024]{0:T(1024)}, f32[1024]{0:T(1024)S(1)}, u32[]{:S(2)}) copy-start(f32[1024]{0:T(1024)S(1)} %broadcast_in_dim.19) | copy-start | bytes 12292
  14.9 0.7 copy-start.7
  15.7 22.1 %copy-start.12 = (f32[4,8,1024]{2,1,0:T(8,128)}, f32[4,8,1024]{2,1,0:T(8,128)S(1)}, u32[]{:S(2)}) copy-start(f32[4,8,1024]{2,1,0:T(8,128)S(1)} %get-tuple-element.5) | copy-start | bytes 393220
  16.8 9.6 %collective-permute-start.1 = (f32[8,4,1024]{2,1,0:T(4,128)S(1)}, f32[8,4,1024]{2,1,0:T(4,128)S(1)}, u32[]{:S(2)}, u32[]{:S(2)}) collective-permute-start(f32[8,4,1024]{2,1,0:T(4,128)S(1)} %pad_maximum_fusion.3), channel_id=1, source_target_pairs={{0,1},{1,0},{2,3},{3,2},{4,5},{5,4},{6,7},{7,6},{8,9},{9,8},{10,11... | collective-permute-start | bytes 393224 | tf_op jit(solution)/shard_map/ppermute | solution.py:58
  23.3 14.5 %copy-start.13 = (f32[4,8,1024]{2,1,0:T(8,128)}, f32[4,8,1024]{2,1,0:T(8,128)S(1)}, u32[]{:S(2)}) copy-start(f32[4,8,1024]{2,1,0:T(8,128)S(1)} %negate_exponential_fusion) | copy-start | bytes 393220
  26.5 0.8 %copy-start.23 = (f32[4,4,1024]{2,1,0:T(4,128)S(1)}, f32[4,4,1024]{2,1,0:T(4,128)}, u32[]{:S(2)}) copy-start(f32[4,4,1024]{2,1,0:T(4,128)} %constant.106.clone.1) | copy-start | bytes 196612
  28.9 0.6 copy-start.18
  29.0 1.2 %copy-start.9 = (f32[3,4,1024]{2,1,0:T(4,128)}, f32[3,4,1024]{2,1,0:T(4,128)S(1)}, u32[]{:S(2)}) copy-start(f32[3,4,1024]{2,1,0:T(4,128)S(1)} %fusion.34) | copy-start | bytes 147460
  30.2 13.8 %collective-permute-start.2 = (f32[4,4,1024]{2,1,0:T(4,128)}, f32[4,4,1024]{2,1,0:T(4,128)}, u32[]{:S(2)}, u32[]{:S(2)}) collective-permute-start(f32[4,4,1024]{2,1,0:T(4,128)} %pad_maximum_fusion.5), channel_id=1, source_target_pairs={{0,3},{1,2},{2,1},{3,0},{4,7},{5,6},{6,5},{7,4},{8,11},{9,10},{10,... | collective-permute-start | bytes 196616 | tf_op jit(solution)/shard_map/ppermute | solution.py:61
  41.4 1.6 %copy-start.15 = (f32[4,4,1,1024]{3,1,0,2:T(4,128)S(1)}, f32[4,4,1,1024]{3,1,0,2:T(4,128)}, u32[]{:S(2)}) copy-start(f32[4,4,1,1024]{3,1,0,2:T(4,128)} %get-tuple-element.35) | copy-start | bytes 196612
  43.0 0.8 %copy-start.14 = (f32[4,4,1,1024]{3,1,0,2:T(4,128)S(1)}, f32[4,4,1,1024]{3,1,0,2:T(4,128)}, u32[]{:S(2)}) copy-start(f32[4,4,1,1024]{3,1,0,2:T(4,128)} %get-tuple-element.36) | copy-start | bytes 196612
  43.9 0.8 copy-start.10
  43.9 0.8 copy-start.19
  45.6 8.6 %copy-start.3 = (f32[4,4,1024]{2,1,0:T(4,128)S(1)}, f32[4,4,1024]{2,1,0:T(4,128)}, u32[]{:S(2)}) copy-start(f32[4,4,1024]{2,1,0:T(4,128)} %get-tuple-element.50) | copy-start | bytes 196612
  45.6 12.8 %collective-permute-start.3 = (f32[4,4,1024]{2,1,0:T(4,128)S(1)}, f32[4,4,1024]{2,1,0:T(4,128)S(1)}, u32[]{:S(2)}, u32[]{:S(2)}) collective-permute-start(f32[4,4,1024]{2,1,0:T(4,128)S(1)} %pad_maximum_fusion.6), channel_id=1, source_target_pairs={{0,7},{1,6},{2,5},{3,4},{4,3},{5,2},{6,1},{7,0},{8,15},{9,14},{10,... | collective-permute-start | bytes 196616 | tf_op jit(solution)/shard_map/ppermute | solution.py:61
  58.5 10.1 %collective-permute-start.4 = (f32[4,4,1024]{2,1,0:T(4,128)S(1)}, f32[4,4,1024]{2,1,0:T(4,128)S(1)}, u32[]{:S(2)}, u32[]{:S(2)}) collective-permute-start(f32[4,4,1024]{2,1,0:T(4,128)S(1)} %pad_maximum_fusion.7), channel_id=1, source_target_pairs={{0,15},{1,14},{2,13},{3,12},{4,11},{5,10},{6,9},{7,8},{8,7},{9,6},... | collective-permute-start | bytes 196616 | tf_op jit(solution)/shard_map/ppermute | solution.py:61
  69.6 0.7 copy-start.17
  70.2 0.7 copy-start.21
  70.2 0.8 copy-start.22
  71.1 0.9 %copy-start.11 = (f32[3,1,8,1024]{3,2,1,0:T(8,128)S(1)}, f32[3,1,8,1024]{3,2,1,0:T(8,128)}, u32[]{:S(2)}) copy-start(f32[3,1,8,1024]{3,2,1,0:T(8,128)} %reduce_window_sum.38) | copy-start | bytes 294916
  71.2 0.8 %copy-start.20 = (f32[8,1024]{1,0:T(8,128)S(1)}, f32[8,1024]{1,0:T(8,128)}, u32[]{:S(2)}) copy-start(f32[8,1024]{1,0:T(8,128)} %multiply_bitcast_fusion.2) | copy-start | bytes 98308
  72.3 0.7 copy-start.24
  73.0 2.2 %copy-start.2 = (f32[4,4,8,1024]{3,2,1,0:T(8,128)S(1)}, f32[4,4,8,1024]{3,2,1,0:T(8,128)}, u32[]{:S(2)}) copy-start(f32[4,4,8,1024]{3,2,1,0:T(8,128)} %param.7) | copy-start | bytes 1572868
  73.0 2.1 %copy-start.1 = (f32[4,4,8,1024]{3,2,1,0:T(8,128)S(1)}, f32[4,4,8,1024]{3,2,1,0:T(8,128)}, u32[]{:S(2)}) copy-start(f32[4,4,8,1024]{3,2,1,0:T(8,128)} %param.8) | copy-start | bytes 1572868
  73.0 8.5 %collective-permute-start.7 = (f32[4,1,8,1024]{3,2,1,0:T(8,128)S(1)}, f32[4,1,8,1024]{3,2,1,0:T(8,128)S(1)}, u32[]{:S(2)}, u32[]{:S(2)}) collective-permute-start(f32[4,1,8,1024]{3,2,1,0:T(8,128)S(1)} %maximum_multiply_fusion), channel_id=1, source_target_pairs={{0,16},{16,32},{32,48},{48,64},{64,80},{80,96},{96,112},{112,128},... | collective-permute-start | bytes 393224 | tf_op jit(solution)/shard_map/ppermute | solution.py:34
  75.1 0.9 %copy-start.8 = (f32[4,1,8,1024]{3,2,1,0:T(8,128)S(1)}, f32[4,1,8,1024]{3,2,1,0:T(8,128)}, u32[]{:S(2)}) copy-start(f32[4,1,8,1024]{3,2,1,0:T(8,128)} %copy-done.7) | copy-start | bytes 393220
  81.6 0.8 copy-start.6
  81.7 0.8 %copy-start.4 = (f32[4,4,8,1024]{3,2,1,0:T(8,128)}, f32[4,4,8,1024]{3,2,1,0:T(8,128)S(1)}, u32[]{:S(2)}) copy-start(f32[4,4,8,1024]{3,2,1,0:T(8,128)S(1)} %get-tuple-element.21) | copy-start | bytes 1572868
  81.7 1.0 %copy-start.5 = (f32[4,4,8,1024]{3,2,1,0:T(8,128)}, f32[4,4,8,1024]{3,2,1,0:T(8,128)S(1)}, u32[]{:S(2)}) copy-start(f32[4,4,8,1024]{3,2,1,0:T(8,128)S(1)} %get-tuple-element.20) | copy-start | bytes 1572868

commit v7 on v5

--- a/solution.py
+++ b/solution.py
@@ -9,29 +9,6 @@
 learn_rate = 0.1
 adam_step = 10
 epsilon = 1e-08
-
-
-def with_halo(cells, sides, width):
-    for axis, dim in sides:
-        count = lax.axis_size(axis)
-        ends = count - 1
-        head = lax.slice_in_dim(cells, 0, width, axis=dim)
-        tail = lax.slice_in_dim(cells, cells.shape[dim] - width, cells.shape[dim], axis=dim)
-        cells = jnp.concatenate(
-            [
-                lax.ppermute(tail, axis, [(i, (i + 1) % count) for i in range(ends)]),
-                cells,
-                lax.ppermute(head, axis, [((i + 1) % count, i) for i in range(ends)]),
-            ],
-            axis=dim,
-        )
-    return cells
-
-
-def passed_along(block, axis, distance):
-    devices = range(lax.axis_size(axis))
-    route = [(i - distance, i) for i in devices if i - distance in devices]
-    return lax.ppermute(block, axis, route)
 
 
 def over(front, back):
@@ -55,8 +32,10 @@
     while step < count:
         route = [(i, i - i % (2 * step) + 2 * step - 1 - i % (2 * step)) for i in range(count)]
         if step == 1:
-            both = lax.ppermute(jnp.concatenate([block, plane_out], axis=0), axis, route)
-            other, plane_in = (both[: block.shape[0]], both[block.shape[0] :])
+            flat = jnp.concatenate([block.reshape(4, -1), plane_out.reshape(4, -1)], axis=1)
+            both = lax.ppermute(flat, axis, route)
+            other = both[:, : block[0].size].reshape(block.shape)
+            plane_in = both[:, block[0].size :].reshape(plane_out.shape)
         else:
             other = lax.ppermute(block, axis, route)
         upper = mine % (2 * step) >= step
@@ -104,22 +83,41 @@
 
 def body(grid, first_moment, second_moment, ray_offset, occupancy, target):
     depth_count = lax.axis_size("depth")
+    tiles = lax.axis_size("tile")
     planes = grid.shape[2]
     total_depth = planes * depth_count
-    padded = with_halo(grid, (("tile", 1),), 1)
+    packed = jnp.concatenate(
+        [
+            grid[:, -1].reshape(-1),
+            ray_offset[-1].astype(jnp.float32),
+            target[:, -1].reshape(-1),
+            occupancy.astype(jnp.float32).reshape(-1),
+        ]
+    )
+    prev = lax.ppermute(packed, "tile", [(i, i + 1) for i in range(tiles - 1)])
+    row_after = lax.ppermute(grid[:, :1], "tile", [(i + 1, i) for i in range(tiles - 1)])
+    sizes = [grid[:, -1].size, ray_offset.shape[1], target[:, -1].size]
+    row_before = prev[: sizes[0]].reshape(grid.shape[0], 1, *grid.shape[2:])
+    offset_before = prev[sizes[0] : sizes[0] + sizes[1]].reshape(1, -1)
+    target_before = prev[sizes[0] + sizes[1] : sum(sizes)].reshape(target.shape[0], 1, -1)
+    occupancy_before = prev[sum(sizes) :].reshape(occupancy.shape)
     odd = lax.axis_index("depth") % 2 == 1
     swapped = depth_swap(grid, "depth")
-    shares = (ray_offset.astype(jnp.float32) * 0.5)[None, :, None, :]
+    ext_rows = jnp.concatenate([row_before, grid], axis=1)
+    after_rows = jnp.concatenate([grid, row_after], axis=1)
+    shares = (jnp.concatenate([offset_before, ray_offset.astype(jnp.float32)]) * 0.5)[None, :, None, :]
     occ = expand_blocks(occupancy.astype(jnp.float32))
+    occ_before = expand_blocks(occupancy_before)[-1:]
+    occ_ext = jnp.concatenate([occ_before, occ], axis=0)
+    target_ext = jnp.concatenate([target_before, target], axis=1)
     plane_out = jnp.where(odd, grid[:, :, 0], grid[:, :, -1])
-    feature_grad, plane_in = render(grid, padded[:, 2:], shares, occ, target, total_depth, plane_out)
+    feature_grad, plane_in = render(
+        ext_rows, after_rows, shares, occ_ext, target_ext, total_depth, plane_out
+    )
     plane_before = jnp.where(odd, plane_in, swapped)[:, :, None]
     plane_after = jnp.where(odd, swapped, plane_in)[:, :, None]
-    carried = shares * feature_grad
-    incoming = passed_along(carried[:, -1:], "tile", 1)
-    carried_in = jnp.concatenate([incoming, carried[:, :-1]], axis=1)
-    data_grad = (1.0 - shares) * feature_grad + carried_in
-    across_rows = padded[:, 2:] + padded[:, :-2]
+    data_grad = (1.0 - shares[:, 1:]) * feature_grad[:, 1:] + shares[:, :-1] * feature_grad[:, :-1]
+    across_rows = after_rows[:, 1:] + ext_rows[:, :-1]
     across_planes = jnp.concatenate([grid[:, :, 1:], plane_after], axis=2) + jnp.concatenate(
         [plane_before, grid[:, :, :-1]], axis=2
     )

time: 64.6 us -> 97.8 us (1.51)
  the two profiles are of different devices: /device:TPU:24 before, /device:TPU:6 now
where the time goes in v7:
time: 97.8 us; the launch traced here: 96.6 us
  starting transfers between devices  37.5 us (38%)
  local copies, waits for them, and re-layouts  19.7 us (20%)
  other arithmetic  19.3 us (20%)
  waiting for transfers between devices  18.7 us (19%)
  between operations  1.34 us (1%)
    ppermute x3, starting transfers between devices, butterfly_scan(): other = lax.ppermute(block, axis, route)  25.7 us
    ppermute x3, waiting for transfers between devices, butterfly_scan(): other = lax.ppermute(block, axis, route)  12.4 us
    ppermute x1, starting transfers between devices, butterfly_scan(): both = lax.ppermute(flat, axis, route)  6.13 us
    unnamed x62, local copies, waits for them, and re-layouts  5.44 us
    ppermute x1, waiting for transfers between devices, butterfly_scan(): both = lax.ppermute(flat, axis, route)  3.79 us
    ppermute x1, waiting for transfers between devices, body(): prev = lax.ppermute(packed, 'tile', [(i, i + 1) for i in range(tiles - 1)])  2.57 us
    another operation x1, other arithmetic, render(): upto = jnp.cumsum(weighted, axis=2)  2.21 us
    ppermute x1, starting transfers between devices, body(): lax.ppermute(grid[:, :1], 'tile', [(i + 1, i) for i in range(tiles - 1)])  2.18 us
  transfers between devices with their start and end apart: 7, of which 4 were waited for; matrix products, arithmetic and copies ran while one was open for 29% of the time, Pallas kernels for 0%

profile of v7, /device:TPU:6, one launch (start us, length us, event | category | flops | bytes accessed | tf_op | source)
XLA Modules:
  0.0 96.6 jit_solution(9655898383298009674)
XLA Ops:
  0.6 1.6 %broadcast_select_fusion = (f32[4,4,1,1024]{3,2,1,0:T(1,128)S(1)}, f32[4,4,1024]{2,1,0:T(4,128)S(1)}) fusion(pred[]{:T(512)S(6)} %eq.11, f32[4,4,8,1024]{3,2,1,0:T(8,128)} %param.6), kind=kLoop, calls=%fused_computation.68 | loop fusion | flops 32768 | bytes 262145 | tf_op jit(solution)/shard_map/jit(_where)/select_n | solution.py:22
  2.2 0.6 copy.25
  2.9 1.4 %collective-permute-start.6 = (f32[4,4,1024]{2,1,0:T(4,128)}, f32[4,4,1024]{2,1,0:T(4,128)}, u32[]{:S(2)}, u32[]{:S(2)}) collective-permute-start(f32[4,4,1024]{2,1,0:T(4,128)} %bitcast.80), channel_id=1, source_target_pairs={{1,2},{3,4},{5,6},{7,8},{9,10},{11,12},{13,14},{2,1},{4,3},{6,5},{... | collective-permute-start | bytes 196616 | tf_op jit(solution)/shard_map/ppermute | solution.py:22
  4.3 1.0 %fusion.48 = (f32[4,1,8,1024]{3,2,1,0:T(8,128)S(1)}, f32[4,8,8,128]{3,2,1,0:T(8,128)S(1)}) fusion(f32[4,4,8,1024]{3,2,1,0:T(8,128)} %param.6), kind=kLoop, calls=%fused_computation.142 | loop fusion | bytes 524288 | tf_op jit(solution)/shard_map/slice | solution.py:98
  5.3 2.2 %collective-permute-start.1 = (f32[4,1,8,1024]{3,2,1,0:T(8,128)S(1)}, f32[4,1,8,1024]{3,2,1,0:T(8,128)S(1)}, u32[]{:S(2)}, u32[]{:S(2)}) collective-permute-start(f32[4,1,8,1024]{3,2,1,0:T(8,128)S(1)} %get-tuple-element.22), channel_id=1, source_target_pairs={{16,0},{32,16},{48,32},{64,48},{80,64},{96,80},{112,96},{128,112},... | collective-permute-start | bytes 393224 | tf_op jit(solution)/shard_map/ppermute | solution.py:98
  7.5 0.8 slice.221
  8.4 2.2 %collective-permute-start = (f32[36992]{0:T(1024)S(1)}, f32[36992]{0:T(1024)S(1)}, u32[]{:S(2)}, u32[]{:S(2)}) collective-permute-start(f32[36992]{0:T(1024)S(1)} %pad_maximum_fusion.4), channel_id=1, source_target_pairs={{0,16},{16,32},{32,48},{48,64},{64,80},{80,96},{96,112},{112,128},... | collective-permute-start | bytes 443912 | tf_op jit(solution)/shard_map/ppermute | solution.py:97
  10.6 0.9 fusion.47
  11.5 0.1 broadcast_in_dim.14
  11.5 0.1 broadcast_in_dim.15
  11.7 0.6 convert_bitcast_fusion.1
  12.3 2.6 %collective-permute-done = f32[36992]{0:T(1024)S(1)} collective-permute-done((f32[36992]{0:T(1024)S(1)}, f32[36992]{0:T(1024)S(1)}, u32[]{:S(2)}, u32[]{:S(2)}) %collective-permute-start) | collective-permute-done | bytes 148000 | tf_op jit(solution)/shard_map/ppermute | solution.py:97
  14.9 0.1 slice.225
  15.0 0.1 slice.226
  15.1 0.4 copy-done.14
  15.6 0.6 copy-done.24
  16.1 0.1 constant_dynamic-update-slice_fusion
  16.3 0.1 multiply_add_fusion
  16.5 0.1 fusion.18
  16.6 0.6 negate_exponential_fusion.1
  17.3 0.8 fusion.15
  18.1 1.1 %reduce_window_sum.22 = f32[1,5,8,1024]{3,2,1,0:T(8,128)S(1)} reduce-window(f32[1,5,8,1024]{3,2,1,0:T(8,128)} %fusion.15, f32[]{:T(128)} %constant.87.clone.1), window={size=1x1x8x1 pad=0_0x0_0x7_0x0_0}, to_apply=%region_0.1 | reduce-window | flops 286720 | bytes 327684 | tf_op jit(solution)/shard_map/jit(cumsum)/reduce_window_sum | solution.py:55
  19.1 0.2 fusion.41
  19.3 0.9 fusion.46
  20.3 2.2 %reduce_window_sum.23 = f32[3,5,8,1024]{3,2,1,0:T(8,128)} reduce-window(f32[3,5,8,1024]{3,2,1,0:T(8,128)} %get-tuple-element.11, f32[]{:T(128)} %constant.87.clone.1), window={size=1x1x8x1 pad=0_0x0_0x7_0x0_0}, to_apply=%region_3.4 | reduce-window | flops 860160 | bytes 983044 | tf_op jit(solution)/shard_map/jit(cumsum)/reduce_window_sum | solution.py:68
  22.6 6.1 %collective-permute-start.2 = (f32[4,9216]{1,0:T(4,128)S(1)}, f32[4,9216]{1,0:T(4,128)S(1)}, u32[]{:S(2)}, u32[]{:S(2)}) collective-permute-start(f32[4,9216]{1,0:T(4,128)S(1)} %pad_maximum_fusion.5), channel_id=1, source_target_pairs={{0,1},{1,0},{2,3},{3,2},{4,5},{5,4},{6,7},{7,6},{8,9},{9,8},{10,11... | collective-permute-start | bytes 442376 | tf_op jit(solution)/shard_map/ppermute | solution.py:36
  28.8 0.6 fusion.40
  29.4 3.8 %collective-permute-done.2 = f32[4,9216]{1,0:T(4,128)S(1)} collective-permute-done((f32[4,9216]{1,0:T(4,128)S(1)}, f32[4,9216]{1,0:T(4,128)S(1)}, u32[]{:S(2)}, u32[]{:S(2)}) %collective-permute-start.2) | collective-permute-done | bytes 147488 | tf_op jit(solution)/shard_map/ppermute | solution.py:36
  33.2 0.7 multiply_reduce_fusion.1
  33.9 1.3 %mul.415 = f32[5,1024]{1,0:T(8,128)} reshape(f32[5120]{0:T(1024)} %get-tuple-element.3) | data formatting | bytes 40960 | tf_op jit(solution)/shard_map/mul | solution.py:15
  35.2 1.3 %slice.257 = f32[1,5,1024]{2,1,0:T(8,128)} reshape(f32[5120]{0:T(1024)} %get-tuple-element.4) | data formatting | bytes 40960 | tf_op jit(solution)/shard_map/slice | solution.py:15
  36.6 0.6 slice.310
  37.2 0.9 slice.255
  38.2 1.6 %slice.291 = f32[4,5120]{1,0:T(4,128)} slice(f32[4,9216]{1,0:T(4,128)} %copy-done.11), slice={[0:4], [0:5120]} | slice | bytes 163840 | tf_op jit(solution)/shard_map/slice | solution.py:37
  39.7 1.6 %reshape.176 = f32[4,5,1024]{2,1,0:T(8,128)} reshape(f32[4,5120]{1,0:T(4,128)} %slice.291) | data formatting | bytes 163840 | tf_op jit(solution)/shard_map/reshape | solution.py:37
  41.3 0.9 fusion.29
  42.3 0.6 copy-done.12
  42.9 0.7 pad_maximum_fusion.7
  43.5 8.2 %collective-permute-start.3 = (f32[4,5,1024]{2,1,0:T(8,128)}, f32[4,5,1024]{2,1,0:T(8,128)}, u32[]{:S(2)}, u32[]{:S(2)}) collective-permute-start(f32[4,5,1024]{2,1,0:T(8,128)} %pad_maximum_fusion.7), channel_id=1, source_target_pairs={{0,3},{1,2},{2,1},{3,0},{4,7},{5,6},{6,5},{7,4},{8,11},{9,10},{10,... | collective-permute-start | bytes 245768 | tf_op jit(solution)/shard_map/ppermute | solution.py:40
  51.8 1.6 %fusion.27 = (f32[4,5,1024]{2,1,0:T(8,128)S(1)}, f32[4,5,1024]{2,1,0:T(8,128)}) fusion(f32[4,5,1024]{2,1,0:T(8,128)S(1)} %copy-done.19, f32[1,5,1024]{2,1,0:T(8,128)S(1)} %copy-done.15, f32[3,5,1024]{2,1,0:T(8,128)} %copy-done.6, pred[]{:T(512)S(6)} %ge.15, f32[3,5,1024]{2,1,0:T(8,128)S(1)} %broadcast_add_fusion), kind=kLoop, calls=%fused_computation.56 | loop fusion | flops 81920 | bytes 389121 | tf_op jit(solution)/shard_map/jit(_where)/select_n | solution.py:44
  53.3 1.5 %slice.334 = f32[4,4096]{1,0:T(4,128)} slice(f32[4,9216]{1,0:T(4,128)} %copy-done.11), slice={[0:4], [5120:9216]} | slice | bytes 131072 | tf_op jit(solution)/shard_map/slice | solution.py:38
  54.8 1.5 %reshape.178 = f32[4,4,1024]{2,1,0:T(4,128)} reshape(f32[4,4096]{1,0:T(4,128)} %slice.334) | data formatting | bytes 131072 | tf_op jit(solution)/shard_map/reshape | solution.py:38
  56.3 0.9 select_bitcast_fusion
  57.2 0.1 copy.18
  57.3 0.1 copy.17
  57.4 0.8 copy-done.5
  58.2 0.9 broadcast_select_fusion.3
  59.2 9.8 %collective-permute-start.4 = (f32[4,5,1024]{2,1,0:T(8,128)S(1)}, f32[4,5,1024]{2,1,0:T(8,128)S(1)}, u32[]{:S(2)}, u32[]{:S(2)}) collective-permute-start(f32[4,5,1024]{2,1,0:T(8,128)S(1)} %pad_maximum_fusion.8), channel_id=1, source_target_pairs={{0,7},{1,6},{2,5},{3,4},{4,3},{5,2},{6,1},{7,0},{8,15},{9,14},{10,... | collective-permute-start | bytes 245768 | tf_op jit(solution)/shard_map/ppermute | solution.py:40
  69.1 0.8 slice_bitcast_fusion.5
  69.8 0.9 slice_add_fusion.4
  70.8 2.5 %collective-permute-done.4 = f32[4,5,1024]{2,1,0:T(8,128)S(1)} collective-permute-done((f32[4,5,1024]{2,1,0:T(8,128)S(1)}, f32[4,5,1024]{2,1,0:T(8,128)S(1)}, u32[]{:S(2)}, u32[]{:S(2)}) %collective-permute-start.4) | collective-permute-done | bytes 81952 | tf_op jit(solution)/shard_map/ppermute | solution.py:40
  73.4 7.7 %collective-permute-start.5 = (f32[4,5,1024]{2,1,0:T(8,128)S(1)}, f32[4,5,1024]{2,1,0:T(8,128)S(1)}, u32[]{:S(2)}, u32[]{:S(2)}) collective-permute-start(f32[4,5,1024]{2,1,0:T(8,128)S(1)} %pad_maximum_fusion.9), channel_id=1, source_target_pairs={{0,15},{1,14},{2,13},{3,12},{4,11},{5,10},{6,9},{7,8},{8,7},{9,6},... | collective-permute-start | bytes 245768 | tf_op jit(solution)/shard_map/ppermute | solution.py:40
  81.2 9.8 %collective-permute-done.5 = f32[4,5,1024]{2,1,0:T(8,128)S(1)} collective-permute-done((f32[4,5,1024]{2,1,0:T(8,128)S(1)}, f32[4,5,1024]{2,1,0:T(8,128)S(1)}, u32[]{:S(2)}, u32[]{:S(2)}) %collective-permute-start.5) | collective-permute-done | bytes 81952 | tf_op jit(solution)/shard_map/ppermute | solution.py:40
  91.2 0.7 copy-done.8
  91.9 0.2 multiply_bitcast_fusion
  92.1 0.5 slice-done
  92.6 0.1 copy-done.17
  92.8 0.4 copy-done.2
  93.2 0.3 subtract_multiply_fusion
  93.5 0.1 fusion.21
  93.6 0.6 copy-done.9
  94.2 0.2 copy-done.10
  94.4 0.2 copy-done.1
  94.6 2.0 %divide_subtract_fusion = (f32[4,4,8,1024]{3,2,1,0:T(8,128)}, f32[4,4,8,1024]{3,2,1,0:T(8,128)}, f32[4,4,8,1024]{3,2,1,0:T(8,128)}) fusion(f32[4,4,8,1024]{3,2,1,0:T(8,128)S(1)} %copy-done, f32[4,4,8,1024]{3,2,1,0:T(8,128)S(1)} %copy-done.9, f32[4,4,8,1024]{3,2,1,0:T(8,128)S(1)} %copy-done.10, f32[4,4,7,1024]{3,2,1,0:T(8,128)S(1)} %get-tuple-element.16, ...), kind=kLoop, calls=%fused_computation.20 | loop fusion | flops 3670016 | bytes 5931008 | tf_op jit(solution)/shard_map/sub | solution.py:132
  (92 shorter events, 0.9 us)
Async XLA Ops:
  2.2 5.2 %copy-start.27 = (s32[1,1,128]{2,1,0:T(1,128)S(1)}, s32[1,1,128]{2,1,0:T(1,128)}, u32[]{:S(2)}) copy-start(s32[1,1,128]{2,1,0:T(1,128)} %param.10) | copy-start | bytes 1540
  2.9 4.6 %copy-start.26 = (s32[4,1024]{1,0:T(4,128)S(1)}, s32[4,1024]{1,0:T(4,128)}, u32[]{:S(2)}) copy-start(s32[4,1024]{1,0:T(4,128)} %param.9) | copy-start | bytes 49156
  2.9 7.7 %copy-start = (f32[4,4,8,1024]{3,2,1,0:T(8,128)S(1)}, f32[4,4,8,1024]{3,2,1,0:T(8,128)}, u32[]{:S(2)}) copy-start(f32[4,4,8,1024]{3,2,1,0:T(8,128)} %param.6) | copy-start | bytes 1572868
  2.9 53.5 %collective-permute-start.6 = (f32[4,4,1024]{2,1,0:T(4,128)}, f32[4,4,1024]{2,1,0:T(4,128)}, u32[]{:S(2)}, u32[]{:S(2)}) collective-permute-start(f32[4,4,1024]{2,1,0:T(4,128)} %bitcast.80), channel_id=1, source_target_pairs={{1,2},{3,4},{5,6},{7,8},{9,10},{11,12},{13,14},{2,1},{4,3},{6,5},{... | collective-permute-start | bytes 196616 | tf_op jit(solution)/shard_map/ppermute | solution.py:22
  5.3 11.0 %collective-permute-start.1 = (f32[4,1,8,1024]{3,2,1,0:T(8,128)S(1)}, f32[4,1,8,1024]{3,2,1,0:T(8,128)S(1)}, u32[]{:S(2)}, u32[]{:S(2)}) collective-permute-start(f32[4,1,8,1024]{3,2,1,0:T(8,128)S(1)} %get-tuple-element.22), channel_id=1, source_target_pairs={{16,0},{32,16},{48,32},{64,48},{80,64},{96,80},{112,96},{128,112},... | collective-permute-start | bytes 393224 | tf_op jit(solution)/shard_map/ppermute | solution.py:98
  8.4 6.5 %collective-permute-start = (f32[36992]{0:T(1024)S(1)}, f32[36992]{0:T(1024)S(1)}, u32[]{:S(2)}, u32[]{:S(2)}) collective-permute-start(f32[36992]{0:T(1024)S(1)} %pad_maximum_fusion.4), channel_id=1, source_target_pairs={{0,16},{16,32},{32,48},{48,64},{64,80},{80,96},{96,112},{112,128},... | collective-permute-start | bytes 443912 | tf_op jit(solution)/shard_map/ppermute | solution.py:97
  14.9 0.7 copy-start.14
  15.5 0.6 copy-start.24
  17.3 1.8 %copy-start.7 = (f32[1,1,8,1024]{3,2,1,0:T(8,128)}, f32[1,1,8,1024]{3,2,1,0:T(8,128)S(1)}, u32[]{:S(2)}) copy-start(f32[1,1,8,1024]{3,2,1,0:T(8,128)S(1)} %slice.227) | copy-start | bytes 98308
  22.5 6.2 %copy-start.23 = (f32[1,4,1,1024]{3,1,2,0:T(4,128)S(1)}, f32[1,4,1,1024]{3,1,2,0:T(4,128)}, u32[]{:S(2)}) copy-start(f32[1,4,1,1024]{3,1,2,0:T(4,128)} %get-tuple-element.65) | copy-start | bytes 49156
  22.5 6.2 %copy-start.25 = (f32[1024]{0:T(1024)S(1)}, f32[1024]{0:T(1024)}, u32[]{:S(2)}) copy-start(f32[1024]{0:T(1024)} %copy-done.24) | copy-start | bytes 12292
  22.6 10.6 %collective-permute-start.2 = (f32[4,9216]{1,0:T(4,128)S(1)}, f32[4,9216]{1,0:T(4,128)S(1)}, u32[]{:S(2)}, u32[]{:S(2)}) collective-permute-start(f32[4,9216]{1,0:T(4,128)S(1)} %pad_maximum_fusion.5), channel_id=1, source_target_pairs={{0,1},{1,0},{2,3},{3,2},{4,5},{5,4},{6,7},{7,6},{8,9},{9,8},{10,11... | collective-permute-start | bytes 442376 | tf_op jit(solution)/shard_map/ppermute | solution.py:36
  33.2 3.4 %copy-start.11 = (f32[4,9216]{1,0:T(4,128)}, f32[4,9216]{1,0:T(4,128)S(1)}, u32[]{:S(2)}) copy-start(f32[4,9216]{1,0:T(4,128)S(1)} %collective-permute-done.2) | copy-start | bytes 442372
  38.2 13.6 %copy-start.6 = (f32[3,5,1024]{2,1,0:T(8,128)}, f32[3,5,1024]{2,1,0:T(8,128)S(1)}, u32[]{:S(2)}) copy-start(f32[3,5,1024]{2,1,0:T(8,128)S(1)} %slice.255) | copy-start | bytes 184324
  39.7 1.6 %copy-start.18 = (f32[1,5,1024]{2,1,0:T(8,128)S(1)}, f32[1,5,1024]{2,1,0:T(8,128)}, u32[]{:S(2)}) copy-start(f32[1,5,1024]{2,1,0:T(8,128)} %get-tuple-element.62) | copy-start | bytes 61444
  42.3 0.6 copy-start.12
  42.3 1.2 %copy-start.4 = (f32[3,5,1024]{2,1,0:T(8,128)}, f32[3,5,1024]{2,1,0:T(8,128)S(1)}, u32[]{:S(2)}) copy-start(f32[3,5,1024]{2,1,0:T(8,128)S(1)} %fusion.38) | copy-start | bytes 184324
  42.9 8.8 %copy-start.16 = (f32[5,1024]{1,0:T(8,128)S(1)}, f32[5,1024]{1,0:T(8,128)}, u32[]{:S(2)}) copy-start(f32[5,1024]{1,0:T(8,128)} %mul.415) | copy-start | bytes 61444
  43.5 8.2 %copy-start.15 = (f32[1,5,1024]{2,1,0:T(8,128)S(1)}, f32[1,5,1024]{2,1,0:T(8,128)}, u32[]{:S(2)}) copy-start(f32[1,5,1024]{2,1,0:T(8,128)} %slice.257) | copy-start | bytes 61444
  43.5 8.2 %copy-start.19 = (f32[4,5,1024]{2,1,0:T(8,128)S(1)}, f32[4,5,1024]{2,1,0:T(8,128)}, u32[]{:S(2)}) copy-start(f32[4,5,1024]{2,1,0:T(8,128)} %constant.89.clone.1) | copy-start | bytes 245764
  43.5 13.9 %collective-permute-start.3 = (f32[4,5,1024]{2,1,0:T(8,128)}, f32[4,5,1024]{2,1,0:T(8,128)}, u32[]{:S(2)}, u32[]{:S(2)}) collective-permute-start(f32[4,5,1024]{2,1,0:T(8,128)} %pad_maximum_fusion.7), channel_id=1, source_target_pairs={{0,3},{1,2},{2,1},{3,0},{4,7},{5,6},{6,5},{7,4},{8,11},{9,10},{10,... | collective-permute-start | bytes 245768 | tf_op jit(solution)/shard_map/ppermute | solution.py:40
  57.3 0.9 copy-start.5
  57.3 0.9 copy-start.13
  59.2 9.9 %copy-start.3 = (f32[4,5,1024]{2,1,0:T(8,128)S(1)}, f32[4,5,1024]{2,1,0:T(8,128)}, u32[]{:S(2)}) copy-start(f32[4,5,1024]{2,1,0:T(8,128)} %get-tuple-element.31) | copy-start | bytes 245764
  59.2 14.1 %collective-permute-start.4 = (f32[4,5,1024]{2,1,0:T(8,128)S(1)}, f32[4,5,1024]{2,1,0:T(8,128)S(1)}, u32[]{:S(2)}, u32[]{:S(2)}) collective-permute-start(f32[4,5,1024]{2,1,0:T(8,128)S(1)} %pad_maximum_fusion.8), channel_id=1, source_target_pairs={{0,7},{1,6},{2,5},{3,4},{4,3},{5,2},{6,1},{7,0},{8,15},{9,14},{10,... | collective-permute-start | bytes 245768 | tf_op jit(solution)/shard_map/ppermute | solution.py:40
  73.4 17.6 %collective-permute-start.5 = (f32[4,5,1024]{2,1,0:T(8,128)S(1)}, f32[4,5,1024]{2,1,0:T(8,128)S(1)}, u32[]{:S(2)}, u32[]{:S(2)}) collective-permute-start(f32[4,5,1024]{2,1,0:T(8,128)S(1)} %pad_maximum_fusion.9), channel_id=1, source_target_pairs={{0,15},{1,14},{2,13},{3,12},{4,11},{5,10},{6,9},{7,8},{8,7},{9,6},... | collective-permute-start | bytes 245768 | tf_op jit(solution)/shard_map/ppermute | solution.py:40
  91.2 0.8 copy-start.8
  91.9 0.7 slice-start
  91.9 0.8 copy-start.17
  91.9 0.8 copy-start.20
  92.1 1.0 %copy-start.2 = (f32[3,5,8,1024]{3,2,1,0:T(8,128)S(1)}, f32[3,5,8,1024]{3,2,1,0:T(8,128)}, u32[]{:S(2)}) copy-start(f32[3,5,8,1024]{3,2,1,0:T(8,128)} %reduce_window_sum.23) | copy-start | bytes 1474564
  93.2 1.0 %copy-start.9 = (f32[4,4,8,1024]{3,2,1,0:T(8,128)S(1)}, f32[4,4,8,1024]{3,2,1,0:T(8,128)}, u32[]{:S(2)}) copy-start(f32[4,4,8,1024]{3,2,1,0:T(8,128)} %param.7) | copy-start | bytes 1572868
  93.2 1.2 %copy-start.10 = (f32[4,4,8,1024]{3,2,1,0:T(8,128)S(1)}, f32[4,4,8,1024]{3,2,1,0:T(8,128)}, u32[]{:S(2)}) copy-start(f32[4,4,8,1024]{3,2,1,0:T(8,128)} %param.8) | copy-start | bytes 1572868
  93.5 1.1 %copy-start.1 = (f32[4,4,7,1024]{3,2,1,0:T(8,128)S(1)}, f32[4,4,7,1024]{3,2,1,0:T(8,128)}, u32[]{:S(2)}) copy-start(f32[4,4,7,1024]{3,2,1,0:T(8,128)} %get-tuple-element.17) | copy-start | bytes 1376260
  93.5 1.1 %copy-start.21 = (f32[4,1024]{1,0:T(4,128)S(1)}, f32[4,1024]{1,0:T(4,128)}, u32[]{:S(2)}) copy-start(f32[4,1024]{1,0:T(4,128)} %get-tuple-element.58) | copy-start | bytes 49156
  93.5 1.1 %copy-start.22 = (f32[4,1024]{1,0:T(4,128)S(1)}, f32[4,1024]{1,0:T(4,128)}, u32[]{:S(2)}) copy-start(f32[4,1024]{1,0:T(4,128)} %get-tuple-element.59) | copy-start | bytes 49156

commit v8 on v5

--- a/solution.py
+++ b/solution.py
@@ -9,23 +9,6 @@
 learn_rate = 0.1
 adam_step = 10
 epsilon = 1e-08
-
-
-def with_halo(cells, sides, width):
-    for axis, dim in sides:
-        count = lax.axis_size(axis)
-        ends = count - 1
-        head = lax.slice_in_dim(cells, 0, width, axis=dim)
-        tail = lax.slice_in_dim(cells, cells.shape[dim] - width, cells.shape[dim], axis=dim)
-        cells = jnp.concatenate(
-            [
-                lax.ppermute(tail, axis, [(i, (i + 1) % count) for i in range(ends)]),
-                cells,
-                lax.ppermute(head, axis, [((i + 1) % count, i) for i in range(ends)]),
-            ],
-            axis=dim,
-        )
-    return cells
 
 
 def passed_along(block, axis, distance):
@@ -106,20 +89,23 @@
     depth_count = lax.axis_size("depth")
     planes = grid.shape[2]
     total_depth = planes * depth_count
-    padded = with_halo(grid, (("tile", 1),), 1)
+    tiles = lax.axis_size("tile")
+    row_after = lax.ppermute(grid[:, :1], "tile", [(i + 1, i) for i in range(tiles - 1)])
+    rows_after = jnp.concatenate([grid[:, 1:], row_after], axis=1)
     odd = lax.axis_index("depth") % 2 == 1
     swapped = depth_swap(grid, "depth")
     shares = (ray_offset.astype(jnp.float32) * 0.5)[None, :, None, :]
     occ = expand_blocks(occupancy.astype(jnp.float32))
     plane_out = jnp.where(odd, grid[:, :, 0], grid[:, :, -1])
-    feature_grad, plane_in = render(grid, padded[:, 2:], shares, occ, target, total_depth, plane_out)
+    feature_grad, plane_in = render(grid, rows_after, shares, occ, target, total_depth, plane_out)
     plane_before = jnp.where(odd, plane_in, swapped)[:, :, None]
     plane_after = jnp.where(odd, swapped, plane_in)[:, :, None]
     carried = shares * feature_grad
-    incoming = passed_along(carried[:, -1:], "tile", 1)
+    both = passed_along(jnp.concatenate([carried[:, -1:], grid[:, -1:]], axis=0), "tile", 1)
+    incoming, row_before = (both[: grid.shape[0]], both[grid.shape[0] :])
     carried_in = jnp.concatenate([incoming, carried[:, :-1]], axis=1)
     data_grad = (1.0 - shares) * feature_grad + carried_in
-    across_rows = padded[:, 2:] + padded[:, :-2]
+    across_rows = rows_after + jnp.concatenate([row_before, grid[:, :-1]], axis=1)
     across_planes = jnp.concatenate([grid[:, :, 1:], plane_after], axis=2) + jnp.concatenate(
         [plane_before, grid[:, :, :-1]], axis=2
     )

time: 64.6 us -> 70.8 us (1.096)
  other arithmetic: 3.96 us -> 9.04 us
  waiting for transfers between devices: 13.5 us -> 15.5 us
  starting transfers between devices: 41 us -> 39.9 us
    ppermute x2 -> x1, starting transfers between devices: 6.21 us -> 4.29 us  [body(): lax.ppermute(grid[:, :1], 'tile', [(i + 1, i) for i in range(tiles - 1)])]
    ppermute x1, waiting for transfers between devices: 6.15 us -> 7.55 us  [passed_along(): return lax.ppermute(block, axis, route)]
    ppermute x3, starting transfers between devices: 28.3 us -> 29.2 us  [butterfly_scan(): other = lax.ppermute(block, axis, route)]
    select_n x2, other arithmetic: 0.06 us -> 0.9 us  [butterfly_scan(): jnp.where(upper, other, block)]
    broadcast_in_dim x1, other arithmetic: 0.1 us -> 0.94 us  [body(): plane_before = jnp.where(odd, plane_in, swapped)[:, :, None]]
    add x7, other arithmetic: 0.16 us -> 0.96 us  [over(): front[:-1] + front[-1:] * back[:-1]]
    mul x7, other arithmetic: 0.07 us -> 0.79 us  [over(): front[-1:] * back[:-1]]
    unnamed x14 -> x24, local copies, waits for them, and re-layouts: 2.89 us -> 2.73 us
  transfers between devices with their start and end apart: 8 -> 7, of which waited for: 5 -> 6; matrix products, arithmetic and copies ran while one was open for 3% -> 5% of each run, Pallas kernels for 0% -> 0%
where the time goes in v8:
time: 70.8 us; the launch traced here: 70.1 us
  starting transfers between devices  39.9 us (56%)
  waiting for transfers between devices  15.5 us (22%)
  other arithmetic  9.04 us (13%)
  local copies, waits for them, and re-layouts  4.4 us (6%)
  between operations  1.21 us (2%)
    ppermute x3, starting transfers between devices, butterfly_scan(): other = lax.ppermute(block, axis, route)  29.2 us
    ppermute x1, waiting for transfers between devices, passed_along(): return lax.ppermute(block, axis, route)  7.55 us
    ppermute x3, waiting for transfers between devices, butterfly_scan(): other = lax.ppermute(block, axis, route)  4.88 us
    ppermute x1, starting transfers between devices, body(): lax.ppermute(grid[:, :1], 'tile', [(i + 1, i) for i in range(tiles - 1)])  4.29 us
    ppermute x1, starting transfers between devices, butterfly_scan(): lax.ppermute(jnp.concatenate([block, plane_out], axis=0), axis, route)  3.83 us
    unnamed x24, local copies, waits for them, and re-layouts  2.73 us
    ppermute x1, waiting for transfers between devices, butterfly_scan(): lax.ppermute(jnp.concatenate([block, plane_out], axis=0), axis, route)  2.35 us
    sub x1, other arithmetic, body(): grid - learn_rate * (new_first / corr_one) / (jnp.sqrt(new_second / corr_...  1.94 us
  transfers between devices with their start and end apart: 7, of which 6 were waited for; matrix products, arithmetic and copies ran while one was open for 5% of the time, Pallas kernels for 0%

profile of v8, /device:TPU:24, one launch (start us, length us, event | category | flops | bytes accessed | tf_op | source)
XLA Modules:
  0.0 70.1 jit_solution(3689145880960987262)
XLA Ops:
  0.6 0.0 copy-start
  0.6 1.0 %fusion.34 = (f32[4,1,8,1024]{3,2,1,0:T(8,128)S(1)}, f32[4,1,8,1024]{3,2,1,0:T(8,128)S(1)}) fusion(f32[4,4,8,1024]{3,2,1,0:T(8,128)} %param.6), kind=kLoop, calls=%fused_computation.113 | loop fusion | bytes 524288 | tf_op jit(solution)/shard_map/slice | solution.py:104
  1.7 4.3 %collective-permute-start = (f32[4,1,8,1024]{3,2,1,0:T(8,128)S(1)}, f32[4,1,8,1024]{3,2,1,0:T(8,128)S(1)}, u32[]{:S(2)}, u32[]{:S(2)}) collective-permute-start(f32[4,1,8,1024]{3,2,1,0:T(8,128)S(1)} %get-tuple-element.19), channel_id=1, source_target_pairs={{16,0},{32,16},{48,32},{64,48},{80,64},{96,80},{112,96},{128,112},... | collective-permute-start | bytes 393224 | tf_op jit(solution)/shard_map/ppermute | solution.py:93
  6.0 0.0 copy-done
  6.0 0.1 fusion.35
  6.1 0.1 fusion.33
  6.2 0.0 copy-start.11
  6.2 0.6 copy-done.11
  6.8 0.1 broadcast_in_dim.12
  6.9 0.1 broadcast_in_dim.13
  7.0 0.0 copy-start.8
  7.0 0.0 copy-start.10
  7.1 0.7 select_bitcast_fusion.2
  7.7 0.0 copy-done.10
  7.8 0.7 %collective-permute-done = f32[4,1,8,1024]{3,2,1,0:T(8,128)S(1)} collective-permute-done((f32[4,1,8,1024]{3,2,1,0:T(8,128)S(1)}, f32[4,1,8,1024]{3,2,1,0:T(8,128)S(1)}, u32[]{:S(2)}, u32[]{:S(2)}) %collective-permute-start) | collective-permute-done | bytes 131104 | tf_op jit(solution)/shard_map/ppermute | solution.py:93
  8.5 0.1 multiply_add_fusion.1
  8.6 0.0 copy-done.8
  8.6 0.1 fusion.30
  8.7 0.6 negate_exponential_fusion.1
  9.3 0.1 reduce_window_sum.22
  9.4 0.1 fusion.25
  9.5 0.2 fusion.29
  9.7 3.8 %collective-permute-start.1 = (f32[8,4,1024]{2,1,0:T(4,128)S(1)}, f32[8,4,1024]{2,1,0:T(4,128)S(1)}, u32[]{:S(2)}, u32[]{:S(2)}) collective-permute-start(f32[8,4,1024]{2,1,0:T(4,128)S(1)} %pad_maximum_fusion.3), channel_id=1, source_target_pairs={{0,1},{1,0},{2,3},{3,2},{4,5},{5,4},{6,7},{7,6},{8,9},{9,8},{10,11... | collective-permute-start | bytes 393224 | tf_op jit(solution)/shard_map/ppermute | solution.py:41
  13.6 0.7 collective-permute-start.6
  14.3 2.4 %collective-permute-done.1 = f32[8,4,1024]{2,1,0:T(4,128)S(1)} collective-permute-done((f32[8,4,1024]{2,1,0:T(4,128)S(1)}, f32[8,4,1024]{2,1,0:T(4,128)S(1)}, u32[]{:S(2)}, u32[]{:S(2)}) %collective-permute-start.1) | collective-permute-done | bytes 131104 | tf_op jit(solution)/shard_map/ppermute | solution.py:41
  16.6 0.0 collective-permute-done.6
  16.7 0.0 copy-start.5
  16.7 0.6 copy-done.5
  17.3 0.2 copy-done.4
  17.5 0.9 %select_bitcast_fusion = (f32[4,4,1,1024]{3,1,0,2:T(4,128)S(1)}, f32[4,4,1,1024]{3,1,0,2:T(4,128)S(1)}, f32[4,4,1024]{2,1,0:T(4,128)S(1)}, f32[4,4,1024]{2,1,0:T...) fusion(f32[4,4,1024]{2,1,0:T(4,128)} %copy-done.5, f32[8,4,1024]{2,1,0:T(4,128)S(1)} %collective-permute-done.1, ...), kind=kLoop, calls=%fused_computation.50 | loop fusion | flops 131072 | bytes 786434 | tf_op jit(solution)/shard_map/broadcast_in_dim | solution.py:101
  18.4 0.6 pad_maximum_fusion.5
  19.1 10.8 %collective-permute-start.2 = (f32[4,4,1024]{2,1,0:T(4,128)}, f32[4,4,1024]{2,1,0:T(4,128)}, u32[]{:S(2)}, u32[]{:S(2)}) collective-permute-start(f32[4,4,1024]{2,1,0:T(4,128)} %pad_maximum_fusion.5), channel_id=1, source_target_pairs={{0,3},{1,2},{2,1},{3,0},{4,7},{5,6},{6,5},{7,4},{8,11},{9,10},{10,... | collective-permute-start | bytes 196616 | tf_op jit(solution)/shard_map/ppermute | solution.py:44
  29.9 0.3 reduce_window_sum.23
  30.2 2.2 %collective-permute-done.2 = f32[4,4,1024]{2,1,0:T(4,128)} collective-permute-done((f32[4,4,1024]{2,1,0:T(4,128)}, f32[4,4,1024]{2,1,0:T(4,128)}, u32[]{:S(2)}, u32[]{:S(2)}) %collective-permute-start.2) | collective-permute-done | bytes 65568 | tf_op jit(solution)/shard_map/ppermute | solution.py:44
  32.4 0.9 %broadcast_select_fusion.1 = (f32[4,4,1024]{2,1,0:T(4,128)S(1)}, f32[4,4,1024]{2,1,0:T(4,128)S(1)}) fusion(f32[4,4,1024]{2,1,0:T(4,128)} %collective-permute-done.2, pred[]{:T(512)S(6)} %ge.14, f32[1,4,1024]{2,1,0:T(4,128)S(1)} %get-tuple-element.65, f32[3,4,1024]{2,1,0:T(4,128)S(1)} %fusion.24), kind=kLoop, calls=%fused_computation.79 | loop fusion | flops 49152 | bytes 262145 | tf_op jit(solution)/shard_map/jit(_where)/select_n | solution.py:46
  33.3 11.4 %collective-permute-start.3 = (f32[4,4,1024]{2,1,0:T(4,128)S(1)}, f32[4,4,1024]{2,1,0:T(4,128)S(1)}, u32[]{:S(2)}, u32[]{:S(2)}) collective-permute-start(f32[4,4,1024]{2,1,0:T(4,128)S(1)} %pad_maximum_fusion.6), channel_id=1, source_target_pairs={{0,7},{1,6},{2,5},{3,4},{4,3},{5,2},{6,1},{7,0},{8,15},{9,14},{10,... | collective-permute-start | bytes 196616 | tf_op jit(solution)/shard_map/ppermute | solution.py:44
  44.8 0.7 %slice_bitcast_fusion.4 = (f32[4,1024]{1,0:T(4,128)S(1)}, f32[1,4,1024]{2,1,0:T(4,128)S(1)}, f32[1,4,1024]{2,1,0:T(4,128)S(1)}, f32[4,1024]{1,0:T(4,128)S(1)}) fusion(f32[4,4,1024]{2,1,0:T(4,128)S(1)} %get-tuple-element.30, f32[4,4,1024]{2,1,0:T(4,128)} %collective-permute-done.2, f32[4,4,1024]{2,1,0:T(4,128)S(1)} %get-tuple-element.41), kind=kLoop, calls=%fused_computation.98 | loop fusion | flops 8192 | bytes 114688 | tf_op jit(solution)/shard_map/mul | solution.py:21
  45.5 0.8 %slice_add_fusion.3 = (f32[3,4,1024]{2,1,0:T(4,128)S(1)}, f32[3,4,1024]{2,1,0:T(4,128)S(1)}) fusion(f32[4,4,1024]{2,1,0:T(4,128)S(1)} %get-tuple-element.30, f32[4,4,1024]{2,1,0:T(4,128)} %collective-permute-done.2, f32[4,1024]{1,0:T(4,128)S(1)} %get-tuple-element.56, f32[4,4,1024]{2,1,0:T(4,128)S(1)} %get-tuple-element.41, f32[4,1024]{1,0:T(4,128)S(1)} %get-tuple-element.59), kind=kLoop, calls=%fused_computation.61 | loop fusion | flops 49152 | bytes 278528 | tf_op jit(solution)/shard_map/add | solution.py:21
  46.4 0.6 collective-permute-done.3
  47.1 7.0 %collective-permute-start.4 = (f32[4,4,1024]{2,1,0:T(4,128)S(1)}, f32[4,4,1024]{2,1,0:T(4,128)S(1)}, u32[]{:S(2)}, u32[]{:S(2)}) collective-permute-start(f32[4,4,1024]{2,1,0:T(4,128)S(1)} %pad_maximum_fusion.7), channel_id=1, source_target_pairs={{0,15},{1,14},{2,13},{3,12},{4,11},{5,10},{6,9},{7,8},{8,7},{9,6},... | collective-permute-start | bytes 196616 | tf_op jit(solution)/shard_map/ppermute | solution.py:44
  54.3 2.1 %collective-permute-done.4 = f32[4,4,1024]{2,1,0:T(4,128)S(1)} collective-permute-done((f32[4,4,1024]{2,1,0:T(4,128)S(1)}, f32[4,4,1024]{2,1,0:T(4,128)S(1)}, u32[]{:S(2)}, u32[]{:S(2)}) %collective-permute-start.4) | collective-permute-done | bytes 65568 | tf_op jit(solution)/shard_map/ppermute | solution.py:44
  56.5 0.1 multiply_bitcast_fusion.1
  56.6 0.0 copy-start.7
  56.6 0.0 copy-start.6
  56.6 0.7 %copy-done.7 = f32[3,4,1024]{2,1,0:T(4,128)S(1)} copy-done((f32[3,4,1024]{2,1,0:T(4,128)S(1)}, f32[3,4,1024]{2,1,0:T(4,128)}, u32[]{:S(2)}) %copy-start.7) | copy-done | bytes 49176
  57.4 0.0 copy-done.6
  57.4 0.0 copy-start.9
  57.4 0.2 multiply_reduce_fusion
  57.6 0.5 copy-done.9
  58.1 0.1 fusion.15
  58.1 0.1 fusion.7
  58.2 0.0 copy-start.1
  58.3 1.9 %collective-permute-start.5 = (f32[8,1,8,1024]{3,2,1,0:T(8,128)S(1)}, f32[8,1,8,1024]{3,2,1,0:T(8,128)S(1)}, u32[]{:S(2)}, u32[]{:S(2)}) collective-permute-start(f32[8,1,8,1024]{3,2,1,0:T(8,128)S(1)} %pad_maximum_fusion.2), channel_id=1, source_target_pairs={{0,16},{16,32},{32,48},{48,64},{64,80},{80,96},{96,112},{112,128},... | collective-permute-start | bytes 786440 | tf_op jit(solution)/shard_map/ppermute | solution.py:17
  60.2 0.1 fusion.32
  60.3 0.1 copy.18
  60.4 0.0 copy-start.3
  60.4 0.1 copy.17
  60.5 0.0 copy-done.1
  60.5 0.0 copy-start.2
  60.5 0.0 slice-start
  60.5 7.6 %collective-permute-done.5 = f32[8,1,8,1024]{3,2,1,0:T(8,128)S(1)} collective-permute-done((f32[8,1,8,1024]{3,2,1,0:T(8,128)S(1)}, f32[8,1,8,1024]{3,2,1,0:T(8,128)S(1)}, u32[]{:S(2)}, u32[]{:S(2)}) %collective-permute-start.5) | collective-permute-done | bytes 262176 | tf_op jit(solution)/shard_map/ppermute | solution.py:17
  68.1 0.0 copy-done.3
  68.1 0.0 copy-done.2
  68.1 1.9 %divide_subtract_fusion = (f32[4,4,8,1024]{3,2,1,0:T(8,128)}, f32[4,4,8,1024]{3,2,1,0:T(8,128)}, f32[4,4,8,1024]{3,2,1,0:T(8,128)}) fusion(f32[4,4,8,1024]{3,2,1,0:T(8,128)S(1)} %copy-done, f32[4,4,8,1024]{3,2,1,0:T(8,128)S(1)} %copy-done.2, f32[4,4,8,1024]{3,2,1,0:T(8,128)S(1)} %copy-done.3, f32[4,4,7,1024]{3,2,1,0:T(8,128)S(1)} %get-tuple-element.14, ...), kind=kLoop, calls=%fused_computation.15 | loop fusion | flops 3801088 | bytes 6307840 | tf_op jit(solution)/shard_map/sub | solution.py:120
  (31 shorter events, 0.5 us)
Async XLA Ops:
  0.6 5.4 %copy-start = (f32[4,4,8,1024]{3,2,1,0:T(8,128)S(1)}, f32[4,4,8,1024]{3,2,1,0:T(8,128)}, u32[]{:S(2)}) copy-start(f32[4,4,8,1024]{3,2,1,0:T(8,128)} %param.6) | copy-start | bytes 1572868
  1.7 6.8 %collective-permute-start = (f32[4,1,8,1024]{3,2,1,0:T(8,128)S(1)}, f32[4,1,8,1024]{3,2,1,0:T(8,128)S(1)}, u32[]{:S(2)}, u32[]{:S(2)}) collective-permute-start(f32[4,1,8,1024]{3,2,1,0:T(8,128)S(1)} %get-tuple-element.19), channel_id=1, source_target_pairs={{16,0},{32,16},{48,32},{64,48},{80,64},{96,80},{112,96},{128,112},... | collective-permute-start | bytes 393224 | tf_op jit(solution)/shard_map/ppermute | solution.py:93
  6.2 0.7 copy-start.11
  7.0 1.5 %copy-start.8 = (f32[1024]{0:T(1024)}, f32[1024]{0:T(1024)S(1)}, u32[]{:S(2)}) copy-start(f32[1024]{0:T(1024)S(1)} %broadcast_in_dim.13) | copy-start | bytes 12292
  7.0 0.7 %copy-start.10 = (s32[4,1024]{1,0:T(4,128)S(1)}, s32[4,1024]{1,0:T(4,128)}, u32[]{:S(2)}) copy-start(s32[4,1024]{1,0:T(4,128)} %param.9) | copy-start | bytes 49156
  9.7 6.9 %collective-permute-start.1 = (f32[8,4,1024]{2,1,0:T(4,128)S(1)}, f32[8,4,1024]{2,1,0:T(4,128)S(1)}, u32[]{:S(2)}, u32[]{:S(2)}) collective-permute-start(f32[8,4,1024]{2,1,0:T(4,128)S(1)} %pad_maximum_fusion.3), channel_id=1, source_target_pairs={{0,1},{1,0},{2,3},{3,2},{4,5},{5,4},{6,7},{7,6},{8,9},{9,8},{10,11... | collective-permute-start | bytes 393224 | tf_op jit(solution)/shard_map/ppermute | solution.py:41
  13.6 3.1 %collective-permute-start.6 = (f32[4,4,1024]{2,1,0:T(4,128)}, f32[4,4,1024]{2,1,0:T(4,128)S(1)}, u32[]{:S(2)}, u32[]{:S(2)}) collective-permute-start(f32[4,4,1024]{2,1,0:T(4,128)} %get-tuple-element.33), channel_id=1, source_target_pairs={{1,2},{3,4},{5,6},{7,8},{9,10},{11,12},{13,14},{2,1},{4,3},{6,5},{... | collective-permute-start | bytes 196616 | tf_op jit(solution)/shard_map/ppermute | solution.py:28
  16.6 0.8 %copy-start.4 = (f32[4,4,1024]{2,1,0:T(4,128)S(1)}, f32[4,4,1024]{2,1,0:T(4,128)}, u32[]{:S(2)}) copy-start(f32[4,4,1024]{2,1,0:T(4,128)} %constant.88.clone.1) | copy-start | bytes 196612
  16.7 0.6 copy-start.5
  19.1 13.3 %collective-permute-start.2 = (f32[4,4,1024]{2,1,0:T(4,128)}, f32[4,4,1024]{2,1,0:T(4,128)}, u32[]{:S(2)}, u32[]{:S(2)}) collective-permute-start(f32[4,4,1024]{2,1,0:T(4,128)} %pad_maximum_fusion.5), channel_id=1, source_target_pairs={{0,3},{1,2},{2,1},{3,0},{4,7},{5,6},{6,5},{7,4},{8,11},{9,10},{10,... | collective-permute-start | bytes 196616 | tf_op jit(solution)/shard_map/ppermute | solution.py:44
  33.3 13.7 %collective-permute-start.3 = (f32[4,4,1024]{2,1,0:T(4,128)S(1)}, f32[4,4,1024]{2,1,0:T(4,128)S(1)}, u32[]{:S(2)}, u32[]{:S(2)}) collective-permute-start(f32[4,4,1024]{2,1,0:T(4,128)S(1)} %pad_maximum_fusion.6), channel_id=1, source_target_pairs={{0,7},{1,6},{2,5},{3,4},{4,3},{5,2},{6,1},{7,0},{8,15},{9,14},{10,... | collective-permute-start | bytes 196616 | tf_op jit(solution)/shard_map/ppermute | solution.py:44
  47.1 9.2 %collective-permute-start.4 = (f32[4,4,1024]{2,1,0:T(4,128)S(1)}, f32[4,4,1024]{2,1,0:T(4,128)S(1)}, u32[]{:S(2)}, u32[]{:S(2)}) collective-permute-start(f32[4,4,1024]{2,1,0:T(4,128)S(1)} %pad_maximum_fusion.7), channel_id=1, source_target_pairs={{0,15},{1,14},{2,13},{3,12},{4,11},{5,10},{6,9},{7,8},{8,7},{9,6},... | collective-permute-start | bytes 196616 | tf_op jit(solution)/shard_map/ppermute | solution.py:44
  56.6 0.8 %copy-start.7 = (f32[3,4,1024]{2,1,0:T(4,128)S(1)}, f32[3,4,1024]{2,1,0:T(4,128)}, u32[]{:S(2)}) copy-start(f32[3,4,1024]{2,1,0:T(4,128)} %param.11) | copy-start | bytes 147460
  56.6 0.8 %copy-start.6 = (f32[4,1024]{1,0:T(4,128)S(1)}, f32[4,1024]{1,0:T(4,128)}, u32[]{:S(2)}) copy-start(f32[4,1024]{1,0:T(4,128)} %get-tuple-element.66) | copy-start | bytes 49156
  57.4 0.7 copy-start.9
  58.2 2.3 %copy-start.1 = (f32[4,4,8,1024]{3,2,1,0:T(8,128)}, f32[4,4,8,1024]{3,2,1,0:T(8,128)S(1)}, u32[]{:S(2)}) copy-start(f32[4,4,8,1024]{3,2,1,0:T(8,128)S(1)} %fusion.7) | copy-start | bytes 1572868
  58.3 9.8 %collective-permute-start.5 = (f32[8,1,8,1024]{3,2,1,0:T(8,128)S(1)}, f32[8,1,8,1024]{3,2,1,0:T(8,128)S(1)}, u32[]{:S(2)}, u32[]{:S(2)}) collective-permute-start(f32[8,1,8,1024]{3,2,1,0:T(8,128)S(1)} %pad_maximum_fusion.2), channel_id=1, source_target_pairs={{0,16},{16,32},{32,48},{48,64},{64,80},{80,96},{96,112},{112,128},... | collective-permute-start | bytes 786440 | tf_op jit(solution)/shard_map/ppermute | solution.py:17
  60.4 7.7 %copy-start.3 = (f32[4,4,8,1024]{3,2,1,0:T(8,128)S(1)}, f32[4,4,8,1024]{3,2,1,0:T(8,128)}, u32[]{:S(2)}) copy-start(f32[4,4,8,1024]{3,2,1,0:T(8,128)} %param.8) | copy-start | bytes 1572868
  60.5 7.6 %copy-start.2 = (f32[4,4,8,1024]{3,2,1,0:T(8,128)S(1)}, f32[4,4,8,1024]{3,2,1,0:T(8,128)}, u32[]{:S(2)}) copy-start(f32[4,4,8,1024]{3,2,1,0:T(8,128)} %param.7) | copy-start | bytes 1572868
  60.5 7.6 %slice-start = ((f32[4,4,8,1024]{3,2,1,0:T(8,128)}), f32[4,3,8,1024]{3,2,1,0:T(8,128)S(1)}, s32[]{:S(2)}) async-start(f32[4,4,8,1024]{3,2,1,0:T(8,128)} %copy-done.1), calls=%async_computation | async-start | bytes 786432 | tf_op jit(solution)/shard_map/slice | solution.py:106

commit v9 on v5

--- a/solution.py
+++ b/solution.py
@@ -48,11 +48,11 @@
 def butterfly_scan(seg_colour, seg_trans, axis, plane_out):
     count, mine = (lax.axis_size(axis), lax.axis_index(axis))
     block = jnp.concatenate([seg_colour, seg_trans[None]], axis=0)
-    plane_in = None
     blank = jnp.concatenate([jnp.zeros_like(seg_colour), jnp.ones_like(seg_trans)[None]], axis=0)
     prefix, suffix = (blank, blank)
+    plane_in = None
     step = 1
-    while step < count:
+    while step < count and (count // step != 4 or step == 1):
         route = [(i, i - i % (2 * step) + 2 * step - 1 - i % (2 * step)) for i in range(count)]
         if step == 1:
             both = lax.ppermute(jnp.concatenate([block, plane_out], axis=0), axis, route)
@@ -65,6 +65,27 @@
         suffix = jnp.where(upper, suffix, over(suffix, other))
         block = joined
         step *= 2
+    if step < count:
+        group, spot = (mine // step, mine % step)
+        routes = (
+            [(i, (i // step - 1) % 4 * step + i % step) for i in range(count)],
+            [(i, (i // step + 2) % 4 * step + step - 1 - i % step) for i in range(count)],
+            [(i, (i // step + 1) % 4 * step + i % step) for i in range(count)],
+        )
+        got = [lax.ppermute(block, axis, route) for route in routes]
+        parts = []
+        for j in range(4):
+            rel = (j - group) % 4
+            parts.append(
+                jnp.where(rel == 0, block, jnp.where(rel == 1, got[0], jnp.where(rel == 2, got[1], got[2])))
+            )
+        front, back = (blank, blank)
+        for j in range(4):
+            front = jnp.where(j < group, over(front, parts[j]), front)
+        for j in reversed(range(4)):
+            back = jnp.where(j > group, over(parts[j], back), back)
+        prefix = over(front, prefix)
+        suffix = over(suffix, back)
     return (prefix[:-1], prefix[-1], suffix[:-1], suffix[-1], plane_in)
 
 

time: 64.6 us -> 69.9 us (1.082)
  starting transfers between devices: 41 us -> 44.9 us
  waiting for transfers between devices: 13.5 us -> 14.5 us
    ppermute x0 -> x3, starting transfers between devices: none -> 22.3 us  [butterfly_scan(): got = [lax.ppermute(block, axis, route) for route in routes]]
    ppermute x3 -> x1, starting transfers between devices: 28.3 us -> 9.94 us  [butterfly_scan(): other = lax.ppermute(block, axis, route)]
    ppermute x0 -> x3, waiting for transfers between devices: none -> 4.82 us  [butterfly_scan(): got = [lax.ppermute(block, axis, route) for route in routes]]
    ppermute x3 -> x1, waiting for transfers between devices: 4.22 us -> 0.01 us  [butterfly_scan(): other = lax.ppermute(block, axis, route)]
  transfers between devices with their start and end apart: 8 -> 9, of which waited for: 5 -> 5; matrix products, arithmetic and copies ran while one was open for 3% -> 3% of each run, Pallas kernels for 0% -> 0%
where the time goes in v9:
time: 69.9 us; the launch traced here: 69.4 us
  starting transfers between devices  44.9 us (64%)
  waiting for transfers between devices  14.5 us (21%)
  local copies, waits for them, and re-layouts  4.5 us (6%)
  other arithmetic  4.19 us (6%)
  between operations  1.34 us (2%)
    ppermute x3, starting transfers between devices, butterfly_scan(): got = [lax.ppermute(block, axis, route) for route in routes]  22.3 us
    ppermute x1, starting transfers between devices, butterfly_scan(): other = lax.ppermute(block, axis, route)  9.94 us
    ppermute x1, waiting for transfers between devices, passed_along(): return lax.ppermute(block, axis, route)  6.51 us
    ppermute x3, waiting for transfers between devices, butterfly_scan(): got = [lax.ppermute(block, axis, route) for route in routes]  4.82 us
    ppermute x1, starting transfers between devices, with_halo(): lax.ppermute(head, axis, [((i + 1) % count, i) for i in range(ends)])  4.29 us
    ppermute x1, starting transfers between devices, butterfly_scan(): lax.ppermute(jnp.concatenate([block, plane_out], axis=0), axis, route)  3.83 us
    unnamed x14, local copies, waits for them, and re-layouts  2.92 us
    ppermute x1, waiting for transfers between devices, butterfly_scan(): lax.ppermute(jnp.concatenate([block, plane_out], axis=0), axis, route)  2.35 us
  transfers between devices with their start and end apart: 9, of which 5 were waited for; matrix products, arithmetic and copies ran while one was open for 3% of the time, Pallas kernels for 0%

profile of v9, /device:TPU:24, one launch (start us, length us, event | category | flops | bytes accessed | tf_op | source)
XLA Modules:
  0.0 69.4 jit_solution(8168858695163551545)
XLA Ops:
  0.6 0.0 copy-start
  0.6 1.0 %fusion.43 = (f32[4,1,8,1024]{3,2,1,0:T(8,128)S(1)}, f32[4,1,8,1024]{3,2,1,0:T(8,128)S(1)}) fusion(f32[4,4,8,1024]{3,2,1,0:T(8,128)} %param.6), kind=kLoop, calls=%fused_computation.132 | loop fusion | bytes 524288 | tf_op jit(solution)/shard_map/slice | solution.py:18
  1.7 4.3 %collective-permute-start = (f32[4,1,8,1024]{3,2,1,0:T(8,128)S(1)}, f32[4,1,8,1024]{3,2,1,0:T(8,128)S(1)}, u32[]{:S(2)}, u32[]{:S(2)}) collective-permute-start(f32[4,1,8,1024]{3,2,1,0:T(8,128)S(1)} %get-tuple-element.20), channel_id=1, source_target_pairs={{16,0},{32,16},{48,32},{64,48},{80,64},{96,80},{112,96},{128,112},... | collective-permute-start | bytes 393224 | tf_op jit(solution)/shard_map/ppermute | solution.py:24
  6.0 0.0 copy-done
  6.0 0.1 fusion.42
  6.1 0.0 copy-start.6
  6.1 0.6 copy-done.6
  6.8 0.1 broadcast_in_dim.12
  6.8 0.1 broadcast_in_dim.13
  6.9 0.0 copy-start.5
  7.0 0.7 copy-done.5
  7.7 0.8 %collective-permute-done = f32[4,1,8,1024]{3,2,1,0:T(8,128)S(1)} collective-permute-done((f32[4,1,8,1024]{3,2,1,0:T(8,128)S(1)}, f32[4,1,8,1024]{3,2,1,0:T(8,128)S(1)}, u32[]{:S(2)}, u32[]{:S(2)}) %collective-permute-start) | collective-permute-done | bytes 131104 | tf_op jit(solution)/shard_map/ppermute | solution.py:24
  8.5 0.1 fusion.9
  8.6 0.1 fusion.39
  8.7 0.1 reduce_window_sum.22
  8.8 0.1 fusion.34
  8.9 0.2 fusion.38
  9.1 3.8 %collective-permute-start.1 = (f32[8,4,1024]{2,1,0:T(4,128)S(1)}, f32[8,4,1024]{2,1,0:T(4,128)S(1)}, u32[]{:S(2)}, u32[]{:S(2)}) collective-permute-start(f32[8,4,1024]{2,1,0:T(4,128)S(1)} %pad_maximum_fusion.3), channel_id=1, source_target_pairs={{0,1},{1,0},{2,3},{3,2},{4,5},{5,4},{6,7},{7,6},{8,9},{9,8},{10,11... | collective-permute-start | bytes 393224 | tf_op jit(solution)/shard_map/ppermute | solution.py:58
  13.0 0.7 collective-permute-start.8
  13.6 2.4 %collective-permute-done.1 = f32[8,4,1024]{2,1,0:T(4,128)S(1)} collective-permute-done((f32[8,4,1024]{2,1,0:T(4,128)S(1)}, f32[8,4,1024]{2,1,0:T(4,128)S(1)}, u32[]{:S(2)}, u32[]{:S(2)}) %collective-permute-start.1) | collective-permute-done | bytes 131104 | tf_op jit(solution)/shard_map/ppermute | solution.py:58
  16.0 0.0 copy-start.3
  16.0 0.0 collective-permute-done.8
  16.0 0.8 %copy-done.3 = f32[4,4,1024]{2,1,0:T(4,128)S(1)} copy-done((f32[4,4,1024]{2,1,0:T(4,128)S(1)}, f32[4,4,1024]{2,1,0:T(4,128)}, u32[]{:S(2)}) %copy-start.3) | copy-done | bytes 65560
  16.8 0.1 select_bitcast_fusion
  17.0 9.9 %collective-permute-start.2 = (f32[4,4,1024]{2,1,0:T(4,128)S(1)}, f32[4,4,1024]{2,1,0:T(4,128)S(1)}, u32[]{:S(2)}, u32[]{:S(2)}) collective-permute-start(f32[4,4,1024]{2,1,0:T(4,128)S(1)} %pad_maximum_fusion.5), channel_id=1, source_target_pairs={{0,3},{1,2},{2,1},{3,0},{4,7},{5,6},{6,5},{7,4},{8,11},{9,10},{10,... | collective-permute-start | bytes 196616 | tf_op jit(solution)/shard_map/ppermute | solution.py:61
  27.0 1.9 %collective-permute-start.7 = (f32[4,1,8,1024]{3,2,1,0:T(8,128)S(1)}, f32[4,1,8,1024]{3,2,1,0:T(8,128)S(1)}, u32[]{:S(2)}, u32[]{:S(2)}) collective-permute-start(f32[4,1,8,1024]{3,2,1,0:T(8,128)S(1)} %get-tuple-element.21), channel_id=1, source_target_pairs={{0,16},{16,32},{32,48},{48,64},{64,80},{80,96},{96,112},{112,128},... | collective-permute-start | bytes 393224 | tf_op jit(solution)/shard_map/ppermute | solution.py:22
  29.0 0.3 reduce_window_sum.23
  29.4 0.0 collective-permute-done.2
  29.5 8.2 %collective-permute-start.5 = (f32[4,4,1024]{2,1,0:T(4,128)S(1)}, f32[4,4,1024]{2,1,0:T(4,128)S(1)}, u32[]{:S(2)}, u32[]{:S(2)}) collective-permute-start(f32[4,4,1024]{2,1,0:T(4,128)S(1)} %pad_maximum_fusion.6), channel_id=1, source_target_pairs={{0,4},{1,5},{2,6},{3,7},{4,8},{5,9},{6,10},{7,11},{8,12},{9,13},{1... | collective-permute-start | bytes 196616 | tf_op jit(solution)/shard_map/ppermute | solution.py:75
  37.7 7.0 %collective-permute-start.4 = (f32[4,4,1024]{2,1,0:T(4,128)S(1)}, f32[4,4,1024]{2,1,0:T(4,128)S(1)}, u32[]{:S(2)}, u32[]{:S(2)}) collective-permute-start(f32[4,4,1024]{2,1,0:T(4,128)S(1)} %pad_maximum_fusion.6), channel_id=1, source_target_pairs={{0,11},{1,10},{2,9},{3,8},{4,15},{5,14},{6,13},{7,12},{8,3},{9,2},... | collective-permute-start | bytes 196616 | tf_op jit(solution)/shard_map/ppermute | solution.py:75
  44.6 7.2 %collective-permute-start.3 = (f32[4,4,1024]{2,1,0:T(4,128)S(1)}, f32[4,4,1024]{2,1,0:T(4,128)S(1)}, u32[]{:S(2)}, u32[]{:S(2)}) collective-permute-start(f32[4,4,1024]{2,1,0:T(4,128)S(1)} %pad_maximum_fusion.6), channel_id=1, source_target_pairs={{0,12},{1,13},{2,14},{3,15},{4,0},{5,1},{6,2},{7,3},{8,4},{9,5},{1... | collective-permute-start | bytes 196616 | tf_op jit(solution)/shard_map/ppermute | solution.py:75
  51.9 0.0 collective-permute-done.5
  52.0 0.3 collective-permute-done.4
  52.3 4.5 %collective-permute-done.3 = f32[4,4,1024]{2,1,0:T(4,128)S(1)} collective-permute-done((f32[4,4,1024]{2,1,0:T(4,128)S(1)}, f32[4,4,1024]{2,1,0:T(4,128)S(1)}, u32[]{:S(2)}, u32[]{:S(2)}) %collective-permute-start.3) | collective-permute-done | bytes 65568 | tf_op jit(solution)/shard_map/ppermute | solution.py:75
  56.8 0.1 select_select_fusion
  56.9 0.1 broadcast_select_fusion.2
  57.3 0.1 multiply_bitcast_fusion.1
  57.5 0.0 copy-start.4
  57.5 0.8 %copy-done.4 = f32[3,4,1024]{2,1,0:T(4,128)S(1)} copy-done((f32[3,4,1024]{2,1,0:T(4,128)S(1)}, f32[3,4,1024]{2,1,0:T(4,128)}, u32[]{:S(2)}) %copy-start.4) | copy-done | bytes 49176
  58.3 0.1 fusion.28
  58.3 0.2 multiply_reduce_fusion
  58.5 0.1 fusion.18
  58.6 0.1 fusion.10
  58.7 1.9 %collective-permute-start.6 = (f32[4,1,8,1024]{3,2,1,0:T(8,128)S(1)}, f32[4,1,8,1024]{3,2,1,0:T(8,128)S(1)}, u32[]{:S(2)}, u32[]{:S(2)}) collective-permute-start(f32[4,1,8,1024]{3,2,1,0:T(8,128)S(1)} %slice.323), channel_id=1, source_target_pairs={{0,16},{16,32},{32,48},{48,64},{64,80},{80,96},{96,112},{112,128},... | collective-permute-start | bytes 393224 | tf_op jit(solution)/shard_map/ppermute | solution.py:34
  60.6 0.1 fusion.41
  60.7 0.0 copy-start.1
  60.7 0.0 copy-start.2
  60.7 0.1 copy.18
  60.8 0.1 copy.17
  60.9 0.0 collective-permute-done.7
  60.9 6.5 %collective-permute-done.6 = f32[4,1,8,1024]{3,2,1,0:T(8,128)S(1)} collective-permute-done((f32[4,1,8,1024]{3,2,1,0:T(8,128)S(1)}, f32[4,1,8,1024]{3,2,1,0:T(8,128)S(1)}, u32[]{:S(2)}, u32[]{:S(2)}) %collective-permute-start.6) | collective-permute-done | bytes 131104 | tf_op jit(solution)/shard_map/ppermute | solution.py:34
  67.5 0.0 copy-done.1
  67.5 0.0 copy-done.2
  67.5 1.9 %divide_subtract_fusion = (f32[4,4,8,1024]{3,2,1,0:T(8,128)}, f32[4,4,8,1024]{3,2,1,0:T(8,128)}, f32[4,4,8,1024]{3,2,1,0:T(8,128)}) fusion(f32[4,4,8,1024]{3,2,1,0:T(8,128)S(1)} %copy-done, f32[4,4,8,1024]{3,2,1,0:T(8,128)S(1)} %copy-done.1, f32[4,4,8,1024]{3,2,1,0:T(8,128)S(1)} %copy-done.2, f32[4,4,7,1024]{3,2,1,0:T(8,128)S(1)} %get-tuple-element.16, ...), kind=kLoop, calls=%fused_computation.18 | loop fusion | flops 3801088 | bytes 5521408 | tf_op jit(solution)/shard_map/sub | solution.py:155
  (38 shorter events, 0.7 us)
Async XLA Ops:
  0.6 5.4 %copy-start = (f32[4,4,8,1024]{3,2,1,0:T(8,128)S(1)}, f32[4,4,8,1024]{3,2,1,0:T(8,128)}, u32[]{:S(2)}) copy-start(f32[4,4,8,1024]{3,2,1,0:T(8,128)} %param.6) | copy-start | bytes 1572868
  1.7 6.8 %collective-permute-start = (f32[4,1,8,1024]{3,2,1,0:T(8,128)S(1)}, f32[4,1,8,1024]{3,2,1,0:T(8,128)S(1)}, u32[]{:S(2)}, u32[]{:S(2)}) collective-permute-start(f32[4,1,8,1024]{3,2,1,0:T(8,128)S(1)} %get-tuple-element.20), channel_id=1, source_target_pairs={{16,0},{32,16},{48,32},{64,48},{80,64},{96,80},{112,96},{128,112},... | collective-permute-start | bytes 393224 | tf_op jit(solution)/shard_map/ppermute | solution.py:24
  6.1 0.7 copy-start.6
  6.9 0.7 %copy-start.5 = (s32[4,1024]{1,0:T(4,128)S(1)}, s32[4,1024]{1,0:T(4,128)}, u32[]{:S(2)}) copy-start(s32[4,1024]{1,0:T(4,128)} %param.9) | copy-start | bytes 49156
  9.1 6.9 %collective-permute-start.1 = (f32[8,4,1024]{2,1,0:T(4,128)S(1)}, f32[8,4,1024]{2,1,0:T(4,128)S(1)}, u32[]{:S(2)}, u32[]{:S(2)}) collective-permute-start(f32[8,4,1024]{2,1,0:T(4,128)S(1)} %pad_maximum_fusion.3), channel_id=1, source_target_pairs={{0,1},{1,0},{2,3},{3,2},{4,5},{5,4},{6,7},{7,6},{8,9},{9,8},{10,11... | collective-permute-start | bytes 393224 | tf_op jit(solution)/shard_map/ppermute | solution.py:58
  13.0 3.1 %collective-permute-start.8 = (f32[4,4,1024]{2,1,0:T(4,128)S(1)}, f32[4,4,1024]{2,1,0:T(4,128)S(1)}, u32[]{:S(2)}, u32[]{:S(2)}) collective-permute-start(f32[4,4,1024]{2,1,0:T(4,128)S(1)} %get-tuple-element.34), channel_id=1, source_target_pairs={{1,2},{3,4},{5,6},{7,8},{9,10},{11,12},{13,14},{2,1},{4,3},{6,5},{... | collective-permute-start | bytes 196616 | tf_op jit(solution)/shard_map/ppermute | solution.py:45
  16.0 0.8 %copy-start.3 = (f32[4,4,1024]{2,1,0:T(4,128)S(1)}, f32[4,4,1024]{2,1,0:T(4,128)}, u32[]{:S(2)}) copy-start(f32[4,4,1024]{2,1,0:T(4,128)} %constant.96.clone.1) | copy-start | bytes 196612
  17.0 12.3 %collective-permute-start.2 = (f32[4,4,1024]{2,1,0:T(4,128)S(1)}, f32[4,4,1024]{2,1,0:T(4,128)S(1)}, u32[]{:S(2)}, u32[]{:S(2)}) collective-permute-start(f32[4,4,1024]{2,1,0:T(4,128)S(1)} %pad_maximum_fusion.5), channel_id=1, source_target_pairs={{0,3},{1,2},{2,1},{3,0},{4,7},{5,6},{6,5},{7,4},{8,11},{9,10},{10,... | collective-permute-start | bytes 196616 | tf_op jit(solution)/shard_map/ppermute | solution.py:61
  27.0 34.0 %collective-permute-start.7 = (f32[4,1,8,1024]{3,2,1,0:T(8,128)S(1)}, f32[4,1,8,1024]{3,2,1,0:T(8,128)S(1)}, u32[]{:S(2)}, u32[]{:S(2)}) collective-permute-start(f32[4,1,8,1024]{3,2,1,0:T(8,128)S(1)} %get-tuple-element.21), channel_id=1, source_target_pairs={{0,16},{16,32},{32,48},{48,64},{64,80},{80,96},{96,112},{112,128},... | collective-permute-start | bytes 393224 | tf_op jit(solution)/shard_map/ppermute | solution.py:22
  29.5 22.5 %collective-permute-start.5 = (f32[4,4,1024]{2,1,0:T(4,128)S(1)}, f32[4,4,1024]{2,1,0:T(4,128)S(1)}, u32[]{:S(2)}, u32[]{:S(2)}) collective-permute-start(f32[4,4,1024]{2,1,0:T(4,128)S(1)} %pad_maximum_fusion.6), channel_id=1, source_target_pairs={{0,4},{1,5},{2,6},{3,7},{4,8},{5,9},{6,10},{7,11},{8,12},{9,13},{1... | collective-permute-start | bytes 196616 | tf_op jit(solution)/shard_map/ppermute | solution.py:75
  37.7 14.6 %collective-permute-start.4 = (f32[4,4,1024]{2,1,0:T(4,128)S(1)}, f32[4,4,1024]{2,1,0:T(4,128)S(1)}, u32[]{:S(2)}, u32[]{:S(2)}) collective-permute-start(f32[4,4,1024]{2,1,0:T(4,128)S(1)} %pad_maximum_fusion.6), channel_id=1, source_target_pairs={{0,11},{1,10},{2,9},{3,8},{4,15},{5,14},{6,13},{7,12},{8,3},{9,2},... | collective-permute-start | bytes 196616 | tf_op jit(solution)/shard_map/ppermute | solution.py:75
  44.6 12.1 %collective-permute-start.3 = (f32[4,4,1024]{2,1,0:T(4,128)S(1)}, f32[4,4,1024]{2,1,0:T(4,128)S(1)}, u32[]{:S(2)}, u32[]{:S(2)}) collective-permute-start(f32[4,4,1024]{2,1,0:T(4,128)S(1)} %pad_maximum_fusion.6), channel_id=1, source_target_pairs={{0,12},{1,13},{2,14},{3,15},{4,0},{5,1},{6,2},{7,3},{8,4},{9,5},{1... | collective-permute-start | bytes 196616 | tf_op jit(solution)/shard_map/ppermute | solution.py:75
  57.5 0.8 %copy-start.4 = (f32[3,4,1024]{2,1,0:T(4,128)S(1)}, f32[3,4,1024]{2,1,0:T(4,128)}, u32[]{:S(2)}) copy-start(f32[3,4,1024]{2,1,0:T(4,128)} %param.11) | copy-start | bytes 147460
  58.7 8.8 %collective-permute-start.6 = (f32[4,1,8,1024]{3,2,1,0:T(8,128)S(1)}, f32[4,1,8,1024]{3,2,1,0:T(8,128)S(1)}, u32[]{:S(2)}, u32[]{:S(2)}) collective-permute-start(f32[4,1,8,1024]{3,2,1,0:T(8,128)S(1)} %slice.323), channel_id=1, source_target_pairs={{0,16},{16,32},{32,48},{48,64},{64,80},{80,96},{96,112},{112,128},... | collective-permute-start | bytes 393224 | tf_op jit(solution)/shard_map/ppermute | solution.py:34
  60.7 6.7 %copy-start.1 = (f32[4,4,8,1024]{3,2,1,0:T(8,128)S(1)}, f32[4,4,8,1024]{3,2,1,0:T(8,128)}, u32[]{:S(2)}) copy-start(f32[4,4,8,1024]{3,2,1,0:T(8,128)} %param.7) | copy-start | bytes 1572868
  60.7 6.7 %copy-start.2 = (f32[4,4,8,1024]{3,2,1,0:T(8,128)S(1)}, f32[4,4,8,1024]{3,2,1,0:T(8,128)}, u32[]{:S(2)}) copy-start(f32[4,4,8,1024]{3,2,1,0:T(8,128)} %param.8) | copy-start | bytes 1572868

commit v10 on v5

--- a/solution.py
+++ b/solution.py
@@ -85,17 +85,27 @@
     )
     behind = back_colour + back_trans[None]
     pixel = front_colour + front_trans[None] * (seg_colour + seg_trans[None] * behind)
-    pixel_grad = 0.5 * total_depth * (pixel - target)
-    upto = jnp.cumsum(weighted, axis=2)
-    remain = seg_colour[:, :, None, :] - upto + (seg_trans[None] * behind)[:, :, None, :]
-    next_trans = trans * fade
-    front_wide = front_trans[:, None, :]
-    sigma_grad = front_wide * jnp.sum(
-        pixel_grad[:, :, None, :] * (next_trans[None] * colour - remain), axis=0
-    )
-    colour_grad = front_wide[None] * weight[None] * pixel_grad[:, :, None, :]
-    density_grad = sigma_grad * occ * scale * jax.nn.sigmoid(features[0])
-    return (jnp.concatenate([density_grad[None], colour_grad * colour * (1.0 - colour)], axis=0), plane_in)
+
+    def backward(pixel, target, weighted, seg_colour, seg_trans, behind, trans, fade, front_trans, colour, weight, occ, density):
+        pixel_grad = 0.5 * total_depth * (pixel - target)
+        upto = jnp.cumsum(weighted, axis=2)
+        remain = seg_colour[:, :, None, :] - upto + (seg_trans[None] * behind)[:, :, None, :]
+        next_trans = trans * fade
+        front_wide = front_trans[:, None, :]
+        sigma_grad = front_wide * jnp.sum(
+            pixel_grad[:, :, None, :] * (next_trans[None] * colour - remain), axis=0
+        )
+        colour_grad = front_wide[None] * weight[None] * pixel_grad[:, :, None, :]
+        density_grad = sigma_grad * occ * scale * jax.nn.sigmoid(density)
+        return jnp.concatenate([density_grad[None], colour_grad * colour * (1.0 - colour)], axis=0)
+
+    last = rows.shape[1] - 1
+    ins = (pixel, target, weighted, seg_colour, seg_trans, behind, trans, fade, front_trans, colour, weight, occ, features[0])
+    axes = (1, 1, 1, 1, 0, 1, 0, 0, 0, 1, 0, 0, 0)
+    tail = lax.optimization_barrier(tuple(lax.slice_in_dim(x, last, last + 1, axis=k) for x, k in zip(ins, axes)))
+    last_grad = backward(*tail)
+    full_grad = backward(*ins)
+    return (last_grad, full_grad, plane_in)
 
 
 def expand_blocks(blocks):
@@ -112,11 +122,13 @@
     shares = (ray_offset.astype(jnp.float32) * 0.5)[None, :, None, :]
     occ = expand_blocks(occupancy.astype(jnp.float32))
     plane_out = jnp.where(odd, grid[:, :, 0], grid[:, :, -1])
-    feature_grad, plane_in = render(grid, padded[:, 2:], shares, occ, target, total_depth, plane_out)
+    last_grad, feature_grad, plane_in = render(
+        grid, padded[:, 2:], shares, occ, target, total_depth, plane_out
+    )
     plane_before = jnp.where(odd, plane_in, swapped)[:, :, None]
     plane_after = jnp.where(odd, swapped, plane_in)[:, :, None]
     carried = shares * feature_grad
-    incoming = passed_along(carried[:, -1:], "tile", 1)
+    incoming = passed_along(shares[:, -1:] * last_grad, "tile", 1)
     carried_in = jnp.concatenate([incoming, carried[:, :-1]], axis=1)
     data_grad = (1.0 - shares) * feature_grad + carried_in
     across_rows = padded[:, 2:] + padded[:, :-2]

time: 64.6 us -> 84.4 us (1.31)
  local copies, waits for them, and re-layouts: 4.48 us -> 15.3 us
  other arithmetic: 3.96 us -> 11 us
  starting transfers between devices: 41 us -> 42.8 us
    slice x3 -> x12, local copies, waits for them, and re-layouts: 1.08 us -> 5.95 us  [the longest x10 4.68 us: render(): lax.slice_in_dim(x, last, last + 1, axis=k)]
    unnamed x14 -> x59, local copies, waits for them, and re-layouts: 2.89 us -> 7.44 us
    ppermute x3, starting transfers between devices: 28.3 us -> 25.5 us  [butterfly_scan(): other = lax.ppermute(block, axis, route)]
    ppermute x1, starting transfers between devices: 3.83 us -> 6.39 us  [butterfly_scan(): lax.ppermute(jnp.concatenate([block, plane_out], axis=0), axis, route)]
    broadcast_in_dim x1, other arithmetic: 0.1 us -> 1.59 us  [body(): plane_before = jnp.where(odd, plane_in, swapped)[:, :, None]]
    ppermute x1, starting transfers between devices: 4.29 us -> 5.75 us  [with_halo(): lax.ppermute(head, axis, [((i + 1) % count, i) for i in range(ends)])]
    slice x1, local copies, waits for them, and re-layouts: 0.08 us -> 1.44 us  [body(): plane_out = jnp.where(odd, grid[:, :, 0], grid[:, :, -1])]
    sub x1, other arithmetic: 1.94 us -> 2.84 us  [body(): grid - learn_rate * (new_first / corr_one) / (jnp.sqrt(new_second / corr_...]
  transfers between devices with their start and end apart: 8 -> 8, of which waited for: 5 -> 4; matrix products, arithmetic and copies ran while one was open for 3% -> 17% of each run, Pallas kernels for 0% -> 0%
where the time goes in v10:
time: 84.4 us; the launch traced here: 83.3 us
  starting transfers between devices  42.8 us (51%)
  local copies, waits for them, and re-layouts  15.3 us (18%)
  waiting for transfers between devices  12.9 us (15%)
  other arithmetic  11 us (13%)
  between operations  1.3 us (2%)
    ppermute x3, starting transfers between devices, butterfly_scan(): other = lax.ppermute(block, axis, route)  25.5 us
    unnamed x59, local copies, waits for them, and re-layouts  7.44 us
    ppermute x1, waiting for transfers between devices, passed_along(): return lax.ppermute(block, axis, route)  6.39 us
    ppermute x1, starting transfers between devices, butterfly_scan(): lax.ppermute(jnp.concatenate([block, plane_out], axis=0), axis, route)  6.39 us
    ppermute x1, starting transfers between devices, with_halo(): lax.ppermute(head, axis, [((i + 1) % count, i) for i in range(ends)])  5.75 us
    slice x10, local copies, waits for them, and re-layouts, render(): lax.slice_in_dim(x, last, last + 1, axis=k)  4.68 us
    ppermute x3, waiting for transfers between devices, butterfly_scan(): other = lax.ppermute(block, axis, route)  3.89 us
    sub x1, other arithmetic, body(): grid - learn_rate * (new_first / corr_one) / (jnp.sqrt(new_second / corr_...  2.84 us
  transfers between devices with their start and end apart: 8, of which 4 were waited for; matrix products, arithmetic and copies ran while one was open for 17% of the time, Pallas kernels for 0%

profile of v10, /device:TPU:24, one launch (start us, length us, event | category | flops | bytes accessed | tf_op | source)
XLA Modules:
  0.0 83.3 jit_solution(11629195787101715991)
XLA Ops:
  0.7 1.4 %fusion.50 = (f32[4,4,1,1024]{3,2,1,0:T(1,128)S(1)}, f32[4,4,1,1024]{3,2,1,0:T(1,128)S(1)}) fusion(f32[4,4,8,1024]{3,2,1,0:T(8,128)} %param.6), kind=kLoop, calls=%fused_computation.150 | loop fusion | bytes 262144 | tf_op jit(solution)/shard_map/slice | solution.py:124
  2.1 1.3 %collective-permute-start.7 = (f32[4,4,1024]{2,1,0:T(4,128)S(1)}, f32[4,4,1024]{2,1,0:T(4,128)}, u32[]{:S(2)}, u32[]{:S(2)}) collective-permute-start(f32[4,4,1024]{2,1,0:T(4,128)S(1)} %get-tuple-element.60), channel_id=1, source_target_pairs={{1,2},{3,4},{5,6},{7,8},{9,10},{11,12},{13,14},{2,1},{4,3},{6,5},{... | collective-permute-start | bytes 196616 | tf_op jit(solution)/shard_map/ppermute | solution.py:45
  3.4 0.7 fusion.49
  4.1 1.9 %collective-permute-start.6 = (f32[4,1,8,1024]{3,2,1,0:T(8,128)}, f32[4,1,8,1024]{3,2,1,0:T(8,128)}, u32[]{:S(2)}, u32[]{:S(2)}) collective-permute-start(f32[4,1,8,1024]{3,2,1,0:T(8,128)} %get-tuple-element.49), channel_id=1, source_target_pairs={{0,16},{16,32},{32,48},{48,64},{64,80},{80,96},{96,112},{112,128},... | collective-permute-start | bytes 393224 | tf_op jit(solution)/shard_map/ppermute | solution.py:22
  6.0 5.8 %collective-permute-start = (f32[4,1,8,1024]{3,2,1,0:T(8,128)S(1)}, f32[4,1,8,1024]{3,2,1,0:T(8,128)S(1)}, u32[]{:S(2)}, u32[]{:S(2)}) collective-permute-start(f32[4,1,8,1024]{3,2,1,0:T(8,128)S(1)} %get-tuple-element.50), channel_id=1, source_target_pairs={{16,0},{32,16},{48,32},{64,48},{80,64},{96,80},{112,96},{128,112},... | collective-permute-start | bytes 393224 | tf_op jit(solution)/shard_map/ppermute | solution.py:24
  11.8 0.1 fusion.48
  12.0 1.4 %slice.276 = f32[3,1,1024]{2,1,0:T(1,128)} slice(f32[3,4,1024]{2,1,0:T(4,128)} %param.11), slice={[0:3], [3:4], [0:1024]} | slice | bytes 24576 | tf_op jit(solution)/shard_map/slice | solution.py:105
  13.4 0.0 copy-start.27
  13.4 0.6 slice.337
  14.0 0.1 copy-done.27
  14.1 0.1 broadcast_in_dim.18
  14.1 0.1 broadcast_in_dim.19
  14.3 0.0 collective-permute-done
  14.3 0.1 fusion.11
  14.4 0.6 copy-done.2
  14.9 0.1 fusion.45
  15.0 0.1 reduce_window_sum.35
  15.2 0.2 fusion.40
  15.4 0.6 negate_exponential_fusion.1
  16.0 0.2 fusion.47
  16.2 6.4 %collective-permute-start.1 = (f32[8,4,1024]{2,1,0:T(4,128)S(1)}, f32[8,4,1024]{2,1,0:T(4,128)S(1)}, u32[]{:S(2)}, u32[]{:S(2)}) collective-permute-start(f32[8,4,1024]{2,1,0:T(4,128)S(1)} %pad_maximum_fusion.3), channel_id=1, source_target_pairs={{0,1},{1,0},{2,3},{3,2},{4,5},{5,4},{6,7},{7,6},{8,9},{9,8},{10,11... | collective-permute-start | bytes 393224 | tf_op jit(solution)/shard_map/ppermute | solution.py:58
  22.6 0.7 negate_multiply_fusion.1
  23.3 2.6 %collective-permute-done.1 = f32[8,4,1024]{2,1,0:T(4,128)S(1)} collective-permute-done((f32[8,4,1024]{2,1,0:T(4,128)S(1)}, f32[8,4,1024]{2,1,0:T(4,128)S(1)}, u32[]{:S(2)}, u32[]{:S(2)}) %collective-permute-start.1) | collective-permute-done | bytes 131104 | tf_op jit(solution)/shard_map/ppermute | solution.py:58
  25.9 0.8 copy-done.22
  26.7 1.6 %select_bitcast_fusion = (f32[4,4,1,1024]{3,1,0,2:T(4,128)}, f32[4,4,1,1024]{3,1,0,2:T(4,128)}, f32[4,4,1024]{2,1,0:T(4,128)S(1)}, f32[4,4,1024]{2,1,0:T(4,128)S...) fusion(f32[4,4,1024]{2,1,0:T(4,128)} %collective-permute-done.7, f32[8,4,1024]{2,1,0:T(4,128)S(1)} %collective-permute-done.1, ...), kind=kLoop, calls=%fused_computation.70 | loop fusion | flops 131072 | bytes 786434 | tf_op jit(solution)/shard_map/broadcast_in_dim | solution.py:128
  28.4 0.6 copy-done.14
  29.0 0.6 pad_maximum_fusion.5
  29.6 7.5 %collective-permute-start.2 = (f32[4,4,1024]{2,1,0:T(4,128)}, f32[4,4,1024]{2,1,0:T(4,128)}, u32[]{:S(2)}, u32[]{:S(2)}) collective-permute-start(f32[4,4,1024]{2,1,0:T(4,128)} %pad_maximum_fusion.5), channel_id=1, source_target_pairs={{0,3},{1,2},{2,1},{3,0},{4,7},{5,6},{6,5},{7,4},{8,11},{9,10},{10,... | collective-permute-start | bytes 196616 | tf_op jit(solution)/shard_map/ppermute | solution.py:61
  37.1 0.6 slice_bitcast_fusion
  37.8 0.6 slice.339
  38.4 0.3 reduce_window_sum.37
  38.8 0.7 slice.341
  39.5 0.6 slice.346
  40.1 0.2 copy-done.11
  40.4 0.1 copy.22
  40.4 0.8 copy-done.10
  41.2 0.1 copy.21
  41.3 0.7 copy-done.7
  42.0 0.9 %broadcast_select_fusion.1 = (f32[4,4,1024]{2,1,0:T(4,128)S(1)}, f32[4,4,1024]{2,1,0:T(4,128)S(1)}) fusion(f32[4,4,1024]{2,1,0:T(4,128)} %collective-permute-done.2, pred[]{:T(512)S(6)} %ge.14, f32[1,4,1024]{2,1,0:T(4,128)S(1)} %copy-done.15, f32[3,4,1024]{2,1,0:T(4,128)S(1)} %copy-done.7), kind=kLoop, calls=%fused_computation.106 | loop fusion | flops 49152 | bytes 262145 | tf_op jit(solution)/shard_map/jit(_where)/select_n | solution.py:63
  43.0 10.0 %collective-permute-start.3 = (f32[4,4,1024]{2,1,0:T(4,128)S(1)}, f32[4,4,1024]{2,1,0:T(4,128)S(1)}, u32[]{:S(2)}, u32[]{:S(2)}) collective-permute-start(f32[4,4,1024]{2,1,0:T(4,128)S(1)} %pad_maximum_fusion.6), channel_id=1, source_target_pairs={{0,7},{1,6},{2,5},{3,4},{4,3},{5,2},{6,1},{7,0},{8,15},{9,14},{10,... | collective-permute-start | bytes 196616 | tf_op jit(solution)/shard_map/ppermute | solution.py:61
  53.0 0.7 slice_bitcast_fusion.5
  53.7 0.8 slice_add_fusion.3
  54.6 1.1 %collective-permute-done.3 = f32[4,4,1024]{2,1,0:T(4,128)S(1)} collective-permute-done((f32[4,4,1024]{2,1,0:T(4,128)S(1)}, f32[4,4,1024]{2,1,0:T(4,128)S(1)}, u32[]{:S(2)}, u32[]{:S(2)}) %collective-permute-start.3) | collective-permute-done | bytes 65568 | tf_op jit(solution)/shard_map/ppermute | solution.py:61
  55.8 7.9 %collective-permute-start.4 = (f32[4,4,1024]{2,1,0:T(4,128)S(1)}, f32[4,4,1024]{2,1,0:T(4,128)S(1)}, u32[]{:S(2)}, u32[]{:S(2)}) collective-permute-start(f32[4,4,1024]{2,1,0:T(4,128)S(1)} %pad_maximum_fusion.7), channel_id=1, source_target_pairs={{0,15},{1,14},{2,13},{3,12},{4,11},{5,10},{6,9},{7,8},{8,7},{9,6},... | collective-permute-start | bytes 196616 | tf_op jit(solution)/shard_map/ppermute | solution.py:61
  63.8 2.8 %collective-permute-done.4 = f32[4,4,1024]{2,1,0:T(4,128)S(1)} collective-permute-done((f32[4,4,1024]{2,1,0:T(4,128)S(1)}, f32[4,4,1024]{2,1,0:T(4,128)S(1)}, u32[]{:S(2)}, u32[]{:S(2)}) %collective-permute-start.4) | collective-permute-done | bytes 65568 | tf_op jit(solution)/shard_map/ppermute | solution.py:61
  66.7 0.6 slice_bitcast_fusion.12
  67.4 0.2 multiply_bitcast_fusion.1
  67.5 0.5 copy-done.20
  68.1 0.1 copy-done.21
  68.3 0.0 copy-start.9
  68.3 0.7 copy-done.23
  69.0 0.1 copy-done.9
  69.2 0.1 reduce_window_sum.38
  69.3 0.2 multiply_reduce_fusion
  69.5 0.1 fusion.23
  69.6 0.6 copy-done.18
  70.2 0.0 copy-done.16
  70.2 0.0 copy-done.17
  70.3 0.2 copy-done.8
  70.5 0.7 copy-done.19
  71.3 0.6 copy-done.25
  71.9 2.1 %collective-permute-start.5 = (f32[4,1,8,1024]{3,2,1,0:T(8,128)S(1)}, f32[4,1,8,1024]{3,2,1,0:T(8,128)S(1)}, u32[]{:S(2)}, u32[]{:S(2)}) collective-permute-start(f32[4,1,8,1024]{3,2,1,0:T(8,128)S(1)} %maximum_multiply_fusion), channel_id=1, source_target_pairs={{0,16},{16,32},{32,48},{48,64},{64,80},{80,96},{96,112},{112,128},... | collective-permute-start | bytes 393224 | tf_op jit(solution)/shard_map/ppermute | solution.py:34
  74.1 6.4 %collective-permute-done.5 = f32[4,1,8,1024]{3,2,1,0:T(8,128)S(1)} collective-permute-done((f32[4,1,8,1024]{3,2,1,0:T(8,128)S(1)}, f32[4,1,8,1024]{3,2,1,0:T(8,128)S(1)}, u32[]{:S(2)}, u32[]{:S(2)}) %collective-permute-start.5) | collective-permute-done | bytes 131104 | tf_op jit(solution)/shard_map/ppermute | solution.py:34
  80.5 2.8 %divide_subtract_fusion = (f32[4,4,8,1024]{3,2,1,0:T(8,128)}, f32[4,4,8,1024]{3,2,1,0:T(8,128)}, f32[4,4,8,1024]{3,2,1,0:T(8,128)}) fusion(f32[4,4,8,1024]{3,2,1,0:T(8,128)S(1)} %copy-done, f32[4,4,8,1024]{3,2,1,0:T(8,128)S(1)} %copy-done.4, f32[4,4,8,1024]{3,2,1,0:T(8,128)S(1)} %copy-done.5, f32[4,4,7,1024]{3,2,1,0:T(8,128)S(1)} %get-tuple-element.46, ...), kind=kLoop, calls=%fused_computation.21 | loop fusion | flops 3801088 | bytes 5521408 | tf_op jit(solution)/shard_map/sub | solution.py:146
  (83 shorter events, 0.9 us)
Async XLA Ops:
  0.6 2.8 %copy-start = (f32[4,4,8,1024]{3,2,1,0:T(8,128)S(1)}, f32[4,4,8,1024]{3,2,1,0:T(8,128)}, u32[]{:S(2)}) copy-start(f32[4,4,8,1024]{3,2,1,0:T(8,128)} %param.6) | copy-start | bytes 1572868
  2.1 23.8 %collective-permute-start.7 = (f32[4,4,1024]{2,1,0:T(4,128)S(1)}, f32[4,4,1024]{2,1,0:T(4,128)}, u32[]{:S(2)}, u32[]{:S(2)}) collective-permute-start(f32[4,4,1024]{2,1,0:T(4,128)S(1)} %get-tuple-element.60), channel_id=1, source_target_pairs={{1,2},{3,4},{5,6},{7,8},{9,10},{11,12},{13,14},{2,1},{4,3},{6,5},{... | collective-permute-start | bytes 196616 | tf_op jit(solution)/shard_map/ppermute | solution.py:45
  4.1 70.0 %collective-permute-start.6 = (f32[4,1,8,1024]{3,2,1,0:T(8,128)}, f32[4,1,8,1024]{3,2,1,0:T(8,128)}, u32[]{:S(2)}, u32[]{:S(2)}) collective-permute-start(f32[4,1,8,1024]{3,2,1,0:T(8,128)} %get-tuple-element.49), channel_id=1, source_target_pairs={{0,16},{16,32},{32,48},{48,64},{64,80},{80,96},{96,112},{112,128},... | collective-permute-start | bytes 393224 | tf_op jit(solution)/shard_map/ppermute | solution.py:22
  6.0 8.3 %collective-permute-start = (f32[4,1,8,1024]{3,2,1,0:T(8,128)S(1)}, f32[4,1,8,1024]{3,2,1,0:T(8,128)S(1)}, u32[]{:S(2)}, u32[]{:S(2)}) collective-permute-start(f32[4,1,8,1024]{3,2,1,0:T(8,128)S(1)} %get-tuple-element.50), channel_id=1, source_target_pairs={{16,0},{32,16},{48,32},{64,48},{80,64},{96,80},{112,96},{128,112},... | collective-permute-start | bytes 393224 | tf_op jit(solution)/shard_map/ppermute | solution.py:24
  11.9 1.4 %copy-start.26 = (s32[4,1024]{1,0:T(4,128)S(1)}, s32[4,1024]{1,0:T(4,128)}, u32[]{:S(2)}) copy-start(s32[4,1024]{1,0:T(4,128)} %param.9) | copy-start | bytes 49156
  13.4 0.9 %copy-start.12 = (f32[4,1024]{1,0:T(4,128)}, f32[4,1024]{1,0:T(4,128)S(1)}, u32[]{:S(2)}) copy-start(f32[4,1024]{1,0:T(4,128)S(1)} %get-tuple-element.100) | copy-start | bytes 49156
  13.4 0.7 copy-start.27
  14.3 0.7 copy-start.2
  16.2 9.7 %collective-permute-start.1 = (f32[8,4,1024]{2,1,0:T(4,128)S(1)}, f32[8,4,1024]{2,1,0:T(4,128)S(1)}, u32[]{:S(2)}, u32[]{:S(2)}) collective-permute-start(f32[8,4,1024]{2,1,0:T(4,128)S(1)} %pad_maximum_fusion.3), channel_id=1, source_target_pairs={{0,1},{1,0},{2,3},{3,2},{4,5},{5,4},{6,7},{7,6},{8,9},{9,8},{10,11... | collective-permute-start | bytes 393224 | tf_op jit(solution)/shard_map/ppermute | solution.py:58
  25.9 0.8 %copy-start.22 = (f32[4,4,1024]{2,1,0:T(4,128)S(1)}, f32[4,4,1024]{2,1,0:T(4,128)}, u32[]{:S(2)}) copy-start(f32[4,4,1024]{2,1,0:T(4,128)} %constant.95.clone.1) | copy-start | bytes 196612
  28.3 0.6 copy-start.14
  28.4 1.2 %copy-start.6 = (f32[3,4,1024]{2,1,0:T(4,128)}, f32[3,4,1024]{2,1,0:T(4,128)S(1)}, u32[]{:S(2)}) copy-start(f32[3,4,1024]{2,1,0:T(4,128)S(1)} %fusion.35) | copy-start | bytes 147460
  29.6 11.7 %collective-permute-start.2 = (f32[4,4,1024]{2,1,0:T(4,128)}, f32[4,4,1024]{2,1,0:T(4,128)}, u32[]{:S(2)}, u32[]{:S(2)}) collective-permute-start(f32[4,4,1024]{2,1,0:T(4,128)} %pad_maximum_fusion.5), channel_id=1, source_target_pairs={{0,3},{1,2},{2,1},{3,0},{4,7},{5,6},{6,5},{7,4},{8,11},{9,10},{10,... | collective-permute-start | bytes 196616 | tf_op jit(solution)/shard_map/ppermute | solution.py:61
  39.5 0.9 %copy-start.11 = (f32[4,4,1,1024]{3,1,0,2:T(4,128)S(1)}, f32[4,4,1,1024]{3,1,0,2:T(4,128)}, u32[]{:S(2)}) copy-start(f32[4,4,1,1024]{3,1,0,2:T(4,128)} %get-tuple-element.53) | copy-start | bytes 196612
  40.4 0.8 %copy-start.10 = (f32[4,4,1,1024]{3,1,0,2:T(4,128)S(1)}, f32[4,4,1,1024]{3,1,0,2:T(4,128)}, u32[]{:S(2)}) copy-start(f32[4,4,1,1024]{3,1,0,2:T(4,128)} %get-tuple-element.54) | copy-start | bytes 196612
  41.2 0.8 copy-start.7
  41.2 0.8 copy-start.15
  42.9 10.1 %copy-start.1 = (f32[4,4,1024]{2,1,0:T(4,128)S(1)}, f32[4,4,1024]{2,1,0:T(4,128)}, u32[]{:S(2)}) copy-start(f32[4,4,1024]{2,1,0:T(4,128)} %get-tuple-element.73) | copy-start | bytes 196612
  43.0 12.8 %collective-permute-start.3 = (f32[4,4,1024]{2,1,0:T(4,128)S(1)}, f32[4,4,1024]{2,1,0:T(4,128)S(1)}, u32[]{:S(2)}, u32[]{:S(2)}) collective-permute-start(f32[4,4,1024]{2,1,0:T(4,128)S(1)} %pad_maximum_fusion.6), channel_id=1, source_target_pairs={{0,7},{1,6},{2,5},{3,4},{4,3},{5,2},{6,1},{7,0},{8,15},{9,14},{10,... | collective-permute-start | bytes 196616 | tf_op jit(solution)/shard_map/ppermute | solution.py:61
  55.8 10.8 %collective-permute-start.4 = (f32[4,4,1024]{2,1,0:T(4,128)S(1)}, f32[4,4,1024]{2,1,0:T(4,128)S(1)}, u32[]{:S(2)}, u32[]{:S(2)}) collective-permute-start(f32[4,4,1024]{2,1,0:T(4,128)S(1)} %pad_maximum_fusion.7), channel_id=1, source_target_pairs={{0,15},{1,14},{2,13},{3,12},{4,11},{5,10},{6,9},{7,8},{8,7},{9,6},... | collective-permute-start | bytes 196616 | tf_op jit(solution)/shard_map/ppermute | solution.py:61
  67.3 0.7 copy-start.20
  67.3 0.8 copy-start.21
  68.2 0.7 copy-start.23
  68.3 0.9 %copy-start.9 = (f32[3,1,8,1024]{3,2,1,0:T(8,128)S(1)}, f32[3,1,8,1024]{3,2,1,0:T(8,128)}, u32[]{:S(2)}) copy-start(f32[3,1,8,1024]{3,2,1,0:T(8,128)} %slice.339) | copy-start | bytes 294916
  69.5 0.8 copy-start.18
  69.5 0.8 copy-start.24
  69.5 0.8 copy-start.16
  69.5 0.8 copy-start.17
  69.6 0.9 %copy-start.8 = (f32[3,1,8,1024]{3,2,1,0:T(8,128)S(1)}, f32[3,1,8,1024]{3,2,1,0:T(8,128)}, u32[]{:S(2)}) copy-start(f32[3,1,8,1024]{3,2,1,0:T(8,128)} %slice.346) | copy-start | bytes 294916
  70.5 0.8 copy-start.19
  71.2 0.7 copy-start.25
  71.2 2.8 %copy-start.13 = (f32[4,1024]{1,0:T(4,128)S(1)}, f32[4,1024]{1,0:T(4,128)}, u32[]{:S(2)}) copy-start(f32[4,1024]{1,0:T(4,128)} %copy-done.12) | copy-start | bytes 49156
  71.9 8.6 %copy-start.5 = (f32[4,4,8,1024]{3,2,1,0:T(8,128)S(1)}, f32[4,4,8,1024]{3,2,1,0:T(8,128)}, u32[]{:S(2)}) copy-start(f32[4,4,8,1024]{3,2,1,0:T(8,128)} %param.8) | copy-start | bytes 1572868
  71.9 8.5 %copy-start.4 = (f32[4,4,8,1024]{3,2,1,0:T(8,128)S(1)}, f32[4,4,8,1024]{3,2,1,0:T(8,128)}, u32[]{:S(2)}) copy-start(f32[4,4,8,1024]{3,2,1,0:T(8,128)} %param.7) | copy-start | bytes 1572868
  71.9 8.5 %collective-permute-start.5 = (f32[4,1,8,1024]{3,2,1,0:T(8,128)S(1)}, f32[4,1,8,1024]{3,2,1,0:T(8,128)S(1)}, u32[]{:S(2)}, u32[]{:S(2)}) collective-permute-start(f32[4,1,8,1024]{3,2,1,0:T(8,128)S(1)} %maximum_multiply_fusion), channel_id=1, source_target_pairs={{0,16},{16,32},{32,48},{48,64},{64,80},{80,96},{96,112},{112,128},... | collective-permute-start | bytes 393224 | tf_op jit(solution)/shard_map/ppermute | solution.py:34
  74.0 6.5 %copy-start.3 = (f32[4,1,8,1024]{3,2,1,0:T(8,128)S(1)}, f32[4,1,8,1024]{3,2,1,0:T(8,128)}, u32[]{:S(2)}) copy-start(f32[4,1,8,1024]{3,2,1,0:T(8,128)} %copy-done.2) | copy-start | bytes 393220

commit v11 on v5

--- a/solution.py
+++ b/solution.py
@@ -53,7 +53,10 @@
     prefix, suffix = (blank, blank)
     step = 1
     while step < count:
-        route = [(i, i - i % (2 * step) + 2 * step - 1 - i % (2 * step)) for i in range(count)]
+        if 2 * step == count:
+            route = [(i, count - 1 - i) for i in range(count)]
+        else:
+            route = [(i, i ^ step) for i in range(count)]
         if step == 1:
             both = lax.ppermute(jnp.concatenate([block, plane_out], axis=0), axis, route)
             other, plane_in = (both[: block.shape[0]], both[block.shape[0] :])

time: 64.6 us -> 66 us (1.022)
  waiting for transfers between devices: 13.5 us -> 19.4 us
  starting transfers between devices: 41 us -> 36.5 us
    ppermute x3, starting transfers between devices: 28.3 us -> 23.9 us  [butterfly_scan(): other = lax.ppermute(block, axis, route)]
    ppermute x3, waiting for transfers between devices: 4.22 us -> 8.27 us  [butterfly_scan(): other = lax.ppermute(block, axis, route)]
    ppermute x1, waiting for transfers between devices: 6.15 us -> 7.96 us  [passed_along(): return lax.ppermute(block, axis, route)]
  transfers between devices with their start and end apart: 8 -> 8, of which waited for: 5 -> 6; matrix products, arithmetic and copies ran while one was open for 3% -> 3% of each run, Pallas kernels for 0% -> 0%
where the time goes in v11:
time: 66 us; the launch traced here: 65.5 us
  starting transfers between devices  36.5 us (55%)
  waiting for transfers between devices  19.4 us (29%)
  local copies, waits for them, and re-layouts  4.48 us (7%)
  other arithmetic  3.96 us (6%)
  between operations  1.16 us (2%)
    ppermute x3, starting transfers between devices, butterfly_scan(): other = lax.ppermute(block, axis, route)  23.9 us
    ppermute x3, waiting for transfers between devices, butterfly_scan(): other = lax.ppermute(block, axis, route)  8.27 us
    ppermute x1, waiting for transfers between devices, passed_along(): return lax.ppermute(block, axis, route)  7.96 us
    ppermute x1, starting transfers between devices, with_halo(): lax.ppermute(head, axis, [((i + 1) % count, i) for i in range(ends)])  4.29 us
    ppermute x1, starting transfers between devices, butterfly_scan(): lax.ppermute(jnp.concatenate([block, plane_out], axis=0), axis, route)  3.83 us
    unnamed x14, local copies, waits for them, and re-layouts  2.89 us
    ppermute x1, waiting for transfers between devices, butterfly_scan(): lax.ppermute(jnp.concatenate([block, plane_out], axis=0), axis, route)  2.35 us
    sub x1, other arithmetic, body(): grid - learn_rate * (new_first / corr_one) / (jnp.sqrt(new_second / corr_...  1.94 us
  transfers between devices with their start and end apart: 8, of which 6 were waited for; matrix products, arithmetic and copies ran while one was open for 3% of the time, Pallas kernels for 0%

profile of v11, /device:TPU:24, one launch (start us, length us, event | category | flops | bytes accessed | tf_op | source)
XLA Modules:
  0.0 65.5 jit_solution(10219100560009284916)
XLA Ops:
  0.6 0.0 copy-start
  0.6 1.0 %fusion.37 = (f32[4,1,8,1024]{3,2,1,0:T(8,128)S(1)}, f32[4,1,8,1024]{3,2,1,0:T(8,128)S(1)}) fusion(f32[4,4,8,1024]{3,2,1,0:T(8,128)} %param.6), kind=kLoop, calls=%fused_computation.114 | loop fusion | bytes 524288 | tf_op jit(solution)/shard_map/slice | solution.py:18
  1.7 4.3 %collective-permute-start = (f32[4,1,8,1024]{3,2,1,0:T(8,128)S(1)}, f32[4,1,8,1024]{3,2,1,0:T(8,128)S(1)}, u32[]{:S(2)}, u32[]{:S(2)}) collective-permute-start(f32[4,1,8,1024]{3,2,1,0:T(8,128)S(1)} %get-tuple-element.18), channel_id=1, source_target_pairs={{16,0},{32,16},{48,32},{64,48},{80,64},{96,80},{112,96},{128,112},... | collective-permute-start | bytes 393224 | tf_op jit(solution)/shard_map/ppermute | solution.py:24
  6.0 0.0 copy-done
  6.0 0.1 fusion.36
  6.1 0.0 copy-start.6
  6.1 0.6 copy-done.6
  6.8 0.1 broadcast_in_dim.12
  6.8 0.1 broadcast_in_dim.13
  6.9 0.0 copy-start.5
  7.0 0.7 %copy-done.5 = s32[4,1024]{1,0:T(4,128)S(1)} copy-done((s32[4,1024]{1,0:T(4,128)S(1)}, s32[4,1024]{1,0:T(4,128)}, u32[]{:S(2)}) %copy-start.5) | copy-done | bytes 16408
  7.7 0.8 %collective-permute-done = f32[4,1,8,1024]{3,2,1,0:T(8,128)S(1)} collective-permute-done((f32[4,1,8,1024]{3,2,1,0:T(8,128)S(1)}, f32[4,1,8,1024]{3,2,1,0:T(8,128)S(1)}, u32[]{:S(2)}, u32[]{:S(2)}) %collective-permute-start) | collective-permute-done | bytes 131104 | tf_op jit(solution)/shard_map/ppermute | solution.py:24
  8.5 0.1 fusion.9
  8.6 0.1 fusion.33
  8.7 0.1 reduce_window_sum.22
  8.8 0.1 fusion.28
  8.9 0.2 fusion.32
  9.1 3.8 %collective-permute-start.1 = (f32[8,4,1024]{2,1,0:T(4,128)S(1)}, f32[8,4,1024]{2,1,0:T(4,128)S(1)}, u32[]{:S(2)}, u32[]{:S(2)}) collective-permute-start(f32[8,4,1024]{2,1,0:T(4,128)S(1)} %pad_maximum_fusion.3), channel_id=1, source_target_pairs={{0,1},{1,0},{2,3},{3,2},{4,5},{5,4},{6,7},{7,6},{8,9},{9,8},{10,11... | collective-permute-start | bytes 393224 | tf_op jit(solution)/shard_map/ppermute | solution.py:61
  13.0 0.7 %collective-permute-start.7 = (f32[4,4,1024]{2,1,0:T(4,128)S(1)}, f32[4,4,1024]{2,1,0:T(4,128)S(1)}, u32[]{:S(2)}, u32[]{:S(2)}) collective-permute-start(f32[4,4,1024]{2,1,0:T(4,128)S(1)} %get-tuple-element.29), channel_id=1, source_target_pairs={{1,2},{3,4},{5,6},{7,8},{9,10},{11,12},{13,14},{2,1},{4,3},{6,5},{... | collective-permute-start | bytes 196616 | tf_op jit(solution)/shard_map/ppermute | solution.py:45
  13.6 2.4 %collective-permute-done.1 = f32[8,4,1024]{2,1,0:T(4,128)S(1)} collective-permute-done((f32[8,4,1024]{2,1,0:T(4,128)S(1)}, f32[8,4,1024]{2,1,0:T(4,128)S(1)}, u32[]{:S(2)}, u32[]{:S(2)}) %collective-permute-start.1) | collective-permute-done | bytes 131104 | tf_op jit(solution)/shard_map/ppermute | solution.py:61
  16.0 0.0 copy-start.3
  16.0 0.0 collective-permute-done.7
  16.0 0.8 %copy-done.3 = f32[4,4,1024]{2,1,0:T(4,128)S(1)} copy-done((f32[4,4,1024]{2,1,0:T(4,128)S(1)}, f32[4,4,1024]{2,1,0:T(4,128)}, u32[]{:S(2)}) %copy-start.3) | copy-done | bytes 65560
  16.8 0.1 select_bitcast_fusion
  17.0 7.5 %collective-permute-start.2 = (f32[4,4,1024]{2,1,0:T(4,128)S(1)}, f32[4,4,1024]{2,1,0:T(4,128)S(1)}, u32[]{:S(2)}, u32[]{:S(2)}) collective-permute-start(f32[4,4,1024]{2,1,0:T(4,128)S(1)} %pad_maximum_fusion.5), channel_id=1, source_target_pairs={{0,2},{1,3},{2,0},{3,1},{4,6},{5,7},{6,4},{7,5},{8,10},{9,11},{10,... | collective-permute-start | bytes 196616 | tf_op jit(solution)/shard_map/ppermute | solution.py:64
  24.5 1.9 %collective-permute-start.6 = (f32[4,1,8,1024]{3,2,1,0:T(8,128)S(1)}, f32[4,1,8,1024]{3,2,1,0:T(8,128)S(1)}, u32[]{:S(2)}, u32[]{:S(2)}) collective-permute-start(f32[4,1,8,1024]{3,2,1,0:T(8,128)S(1)} %get-tuple-element.19), channel_id=1, source_target_pairs={{0,16},{16,32},{32,48},{48,64},{64,80},{80,96},{96,112},{112,128},... | collective-permute-start | bytes 393224 | tf_op jit(solution)/shard_map/ppermute | solution.py:22
  26.5 0.3 reduce_window_sum.23
  26.8 0.6 collective-permute-done.2
  27.5 9.3 %collective-permute-start.3 = (f32[4,4,1024]{2,1,0:T(4,128)S(1)}, f32[4,4,1024]{2,1,0:T(4,128)S(1)}, u32[]{:S(2)}, u32[]{:S(2)}) collective-permute-start(f32[4,4,1024]{2,1,0:T(4,128)S(1)} %pad_maximum_fusion.6), channel_id=1, source_target_pairs={{0,4},{1,5},{2,6},{3,7},{4,0},{5,1},{6,2},{7,3},{8,12},{9,13},{10,... | collective-permute-start | bytes 196616 | tf_op jit(solution)/shard_map/ppermute | solution.py:64
  36.9 4.3 %collective-permute-done.3 = f32[4,4,1024]{2,1,0:T(4,128)S(1)} collective-permute-done((f32[4,4,1024]{2,1,0:T(4,128)S(1)}, f32[4,4,1024]{2,1,0:T(4,128)S(1)}, u32[]{:S(2)}, u32[]{:S(2)}) %collective-permute-start.3) | collective-permute-done | bytes 65568 | tf_op jit(solution)/shard_map/ppermute | solution.py:64
  41.3 7.2 %collective-permute-start.4 = (f32[4,4,1024]{2,1,0:T(4,128)S(1)}, f32[4,4,1024]{2,1,0:T(4,128)S(1)}, u32[]{:S(2)}, u32[]{:S(2)}) collective-permute-start(f32[4,4,1024]{2,1,0:T(4,128)S(1)} %pad_maximum_fusion.7), channel_id=1, source_target_pairs={{0,15},{1,14},{2,13},{3,12},{4,11},{5,10},{6,9},{7,8},{8,7},{9,6},... | collective-permute-start | bytes 196616 | tf_op jit(solution)/shard_map/ppermute | solution.py:64
  48.6 3.3 %collective-permute-done.4 = f32[4,4,1024]{2,1,0:T(4,128)S(1)} collective-permute-done((f32[4,4,1024]{2,1,0:T(4,128)S(1)}, f32[4,4,1024]{2,1,0:T(4,128)S(1)}, u32[]{:S(2)}, u32[]{:S(2)}) %collective-permute-start.4) | collective-permute-done | bytes 65568 | tf_op jit(solution)/shard_map/ppermute | solution.py:64
  52.0 0.1 multiply_bitcast_fusion.1
  52.1 0.0 copy-start.4
  52.2 0.7 %copy-done.4 = f32[3,4,1024]{2,1,0:T(4,128)S(1)} copy-done((f32[3,4,1024]{2,1,0:T(4,128)S(1)}, f32[3,4,1024]{2,1,0:T(4,128)}, u32[]{:S(2)}) %copy-start.4) | copy-done | bytes 49176
  53.0 0.2 multiply_reduce_fusion
  53.2 0.1 fusion.18
  53.2 0.1 fusion.10
  53.3 1.9 %collective-permute-start.5 = (f32[4,1,8,1024]{3,2,1,0:T(8,128)S(1)}, f32[4,1,8,1024]{3,2,1,0:T(8,128)S(1)}, u32[]{:S(2)}, u32[]{:S(2)}) collective-permute-start(f32[4,1,8,1024]{3,2,1,0:T(8,128)S(1)} %slice.274), channel_id=1, source_target_pairs={{0,16},{16,32},{32,48},{48,64},{64,80},{80,96},{96,112},{112,128},... | collective-permute-start | bytes 393224 | tf_op jit(solution)/shard_map/ppermute | solution.py:34
  55.2 0.1 fusion.35
  55.4 0.0 copy-start.1
  55.4 0.0 copy-start.2
  55.4 0.1 copy.18
  55.5 0.1 copy.17
  55.6 0.0 collective-permute-done.6
  55.6 8.0 %collective-permute-done.5 = f32[4,1,8,1024]{3,2,1,0:T(8,128)S(1)} collective-permute-done((f32[4,1,8,1024]{3,2,1,0:T(8,128)S(1)}, f32[4,1,8,1024]{3,2,1,0:T(8,128)S(1)}, u32[]{:S(2)}, u32[]{:S(2)}) %collective-permute-start.5) | collective-permute-done | bytes 131104 | tf_op jit(solution)/shard_map/ppermute | solution.py:34
  63.6 0.0 copy-done.1
  63.6 0.0 copy-done.2
  63.6 1.9 %divide_subtract_fusion = (f32[4,4,8,1024]{3,2,1,0:T(8,128)}, f32[4,4,8,1024]{3,2,1,0:T(8,128)}, f32[4,4,8,1024]{3,2,1,0:T(8,128)}) fusion(f32[4,4,8,1024]{3,2,1,0:T(8,128)S(1)} %copy-done, f32[4,4,8,1024]{3,2,1,0:T(8,128)S(1)} %copy-done.1, f32[4,4,8,1024]{3,2,1,0:T(8,128)S(1)} %copy-done.2, f32[4,4,7,1024]{3,2,1,0:T(8,128)S(1)} %get-tuple-element.14, ...), kind=kLoop, calls=%fused_computation.18 | loop fusion | flops 3801088 | bytes 5521408 | tf_op jit(solution)/shard_map/sub | solution.py:137
  (34 shorter events, 0.7 us)
Async XLA Ops:
  0.6 5.4 %copy-start = (f32[4,4,8,1024]{3,2,1,0:T(8,128)S(1)}, f32[4,4,8,1024]{3,2,1,0:T(8,128)}, u32[]{:S(2)}) copy-start(f32[4,4,8,1024]{3,2,1,0:T(8,128)} %param.6) | copy-start | bytes 1572868
  1.7 6.8 %collective-permute-start = (f32[4,1,8,1024]{3,2,1,0:T(8,128)S(1)}, f32[4,1,8,1024]{3,2,1,0:T(8,128)S(1)}, u32[]{:S(2)}, u32[]{:S(2)}) collective-permute-start(f32[4,1,8,1024]{3,2,1,0:T(8,128)S(1)} %get-tuple-element.18), channel_id=1, source_target_pairs={{16,0},{32,16},{48,32},{64,48},{80,64},{96,80},{112,96},{128,112},... | collective-permute-start | bytes 393224 | tf_op jit(solution)/shard_map/ppermute | solution.py:24
  6.1 0.7 %copy-start.6 = (s32[1,1,128]{2,1,0:T(1,128)S(1)}, s32[1,1,128]{2,1,0:T(1,128)}, u32[]{:S(2)}) copy-start(s32[1,1,128]{2,1,0:T(1,128)} %param.10) | copy-start | bytes 1540
  6.9 0.7 %copy-start.5 = (s32[4,1024]{1,0:T(4,128)S(1)}, s32[4,1024]{1,0:T(4,128)}, u32[]{:S(2)}) copy-start(s32[4,1024]{1,0:T(4,128)} %param.9) | copy-start | bytes 49156
  9.1 6.9 %collective-permute-start.1 = (f32[8,4,1024]{2,1,0:T(4,128)S(1)}, f32[8,4,1024]{2,1,0:T(4,128)S(1)}, u32[]{:S(2)}, u32[]{:S(2)}) collective-permute-start(f32[8,4,1024]{2,1,0:T(4,128)S(1)} %pad_maximum_fusion.3), channel_id=1, source_target_pairs={{0,1},{1,0},{2,3},{3,2},{4,5},{5,4},{6,7},{7,6},{8,9},{9,8},{10,11... | collective-permute-start | bytes 393224 | tf_op jit(solution)/shard_map/ppermute | solution.py:61
  13.0 3.1 %collective-permute-start.7 = (f32[4,4,1024]{2,1,0:T(4,128)S(1)}, f32[4,4,1024]{2,1,0:T(4,128)S(1)}, u32[]{:S(2)}, u32[]{:S(2)}) collective-permute-start(f32[4,4,1024]{2,1,0:T(4,128)S(1)} %get-tuple-element.29), channel_id=1, source_target_pairs={{1,2},{3,4},{5,6},{7,8},{9,10},{11,12},{13,14},{2,1},{4,3},{6,5},{... | collective-permute-start | bytes 196616 | tf_op jit(solution)/shard_map/ppermute | solution.py:45
  16.0 0.8 %copy-start.3 = (f32[4,4,1024]{2,1,0:T(4,128)S(1)}, f32[4,4,1024]{2,1,0:T(4,128)}, u32[]{:S(2)}) copy-start(f32[4,4,1024]{2,1,0:T(4,128)} %constant.88.clone.1) | copy-start | bytes 196612
  17.0 10.4 %collective-permute-start.2 = (f32[4,4,1024]{2,1,0:T(4,128)S(1)}, f32[4,4,1024]{2,1,0:T(4,128)S(1)}, u32[]{:S(2)}, u32[]{:S(2)}) collective-permute-start(f32[4,4,1024]{2,1,0:T(4,128)S(1)} %pad_maximum_fusion.5), channel_id=1, source_target_pairs={{0,2},{1,3},{2,0},{3,1},{4,6},{5,7},{6,4},{7,5},{8,10},{9,11},{10,... | collective-permute-start | bytes 196616 | tf_op jit(solution)/shard_map/ppermute | solution.py:64
  24.5 31.1 %collective-permute-start.6 = (f32[4,1,8,1024]{3,2,1,0:T(8,128)S(1)}, f32[4,1,8,1024]{3,2,1,0:T(8,128)S(1)}, u32[]{:S(2)}, u32[]{:S(2)}) collective-permute-start(f32[4,1,8,1024]{3,2,1,0:T(8,128)S(1)} %get-tuple-element.19), channel_id=1, source_target_pairs={{0,16},{16,32},{32,48},{48,64},{64,80},{80,96},{96,112},{112,128},... | collective-permute-start | bytes 393224 | tf_op jit(solution)/shard_map/ppermute | solution.py:22
  27.5 13.7 %collective-permute-start.3 = (f32[4,4,1024]{2,1,0:T(4,128)S(1)}, f32[4,4,1024]{2,1,0:T(4,128)S(1)}, u32[]{:S(2)}, u32[]{:S(2)}) collective-permute-start(f32[4,4,1024]{2,1,0:T(4,128)S(1)} %pad_maximum_fusion.6), channel_id=1, source_target_pairs={{0,4},{1,5},{2,6},{3,7},{4,0},{5,1},{6,2},{7,3},{8,12},{9,13},{10,... | collective-permute-start | bytes 196616 | tf_op jit(solution)/shard_map/ppermute | solution.py:64
  41.3 10.6 %collective-permute-start.4 = (f32[4,4,1024]{2,1,0:T(4,128)S(1)}, f32[4,4,1024]{2,1,0:T(4,128)S(1)}, u32[]{:S(2)}, u32[]{:S(2)}) collective-permute-start(f32[4,4,1024]{2,1,0:T(4,128)S(1)} %pad_maximum_fusion.7), channel_id=1, source_target_pairs={{0,15},{1,14},{2,13},{3,12},{4,11},{5,10},{6,9},{7,8},{8,7},{9,6},... | collective-permute-start | bytes 196616 | tf_op jit(solution)/shard_map/ppermute | solution.py:64
  52.1 0.8 %copy-start.4 = (f32[3,4,1024]{2,1,0:T(4,128)S(1)}, f32[3,4,1024]{2,1,0:T(4,128)}, u32[]{:S(2)}) copy-start(f32[3,4,1024]{2,1,0:T(4,128)} %param.11) | copy-start | bytes 147460
  53.3 10.2 %collective-permute-start.5 = (f32[4,1,8,1024]{3,2,1,0:T(8,128)S(1)}, f32[4,1,8,1024]{3,2,1,0:T(8,128)S(1)}, u32[]{:S(2)}, u32[]{:S(2)}) collective-permute-start(f32[4,1,8,1024]{3,2,1,0:T(8,128)S(1)} %slice.274), channel_id=1, source_target_pairs={{0,16},{16,32},{32,48},{48,64},{64,80},{80,96},{96,112},{112,128},... | collective-permute-start | bytes 393224 | tf_op jit(solution)/shard_map/ppermute | solution.py:34
  55.4 8.2 %copy-start.1 = (f32[4,4,8,1024]{3,2,1,0:T(8,128)S(1)}, f32[4,4,8,1024]{3,2,1,0:T(8,128)}, u32[]{:S(2)}) copy-start(f32[4,4,8,1024]{3,2,1,0:T(8,128)} %param.7) | copy-start | bytes 1572868
  55.4 8.2 %copy-start.2 = (f32[4,4,8,1024]{3,2,1,0:T(8,128)S(1)}, f32[4,4,8,1024]{3,2,1,0:T(8,128)}, u32[]{:S(2)}) copy-start(f32[4,4,8,1024]{3,2,1,0:T(8,128)} %param.8) | copy-start | bytes 1572868

commit v12 on v5

--- a/solution.py
+++ b/solution.py
@@ -49,7 +49,7 @@
     count, mine = (lax.axis_size(axis), lax.axis_index(axis))
     block = jnp.concatenate([seg_colour, seg_trans[None]], axis=0)
     plane_in = None
-    blank = jnp.concatenate([jnp.zeros_like(seg_colour), jnp.ones_like(seg_trans)[None]], axis=0)
+    blank = jnp.concatenate([block[:-1] * 0.0, block[-1:] * 0.0 + 1.0], axis=0)
     prefix, suffix = (blank, blank)
     step = 1
     while step < count:

time: 64.6 us -> 64.5 us (level)
  starting transfers between devices: 41 us -> 41.9 us
  local copies, waits for them, and re-layouts: 4.48 us -> 3.68 us
    ppermute x1, waiting for transfers between devices: 2.35 us -> 0.03 us  [butterfly_scan(): lax.ppermute(jnp.concatenate([block, plane_out], axis=0), axis, route)]
    ppermute x3, waiting for transfers between devices: 4.22 us -> 6.33 us  [butterfly_scan(): other = lax.ppermute(block, axis, route)]
    ppermute x3, starting transfers between devices: 28.3 us -> 29.3 us  [butterfly_scan(): other = lax.ppermute(block, axis, route)]
    unnamed x14 -> x12, local copies, waits for them, and re-layouts: 2.89 us -> 2.08 us
where the time goes in v12:
time: 64.5 us; the launch traced here: 64.1 us
  starting transfers between devices  41.9 us (65%)
  waiting for transfers between devices  13.3 us (21%)
  other arithmetic  4 us (6%)
  local copies, waits for them, and re-layouts  3.68 us (6%)
  between operations  1.18 us (2%)
    ppermute x3, starting transfers between devices, butterfly_scan(): other = lax.ppermute(block, axis, route)  29.3 us
    ppermute x3, waiting for transfers between devices, butterfly_scan(): other = lax.ppermute(block, axis, route)  6.33 us
    ppermute x1, waiting for transfers between devices, passed_along(): return lax.ppermute(block, axis, route)  6.13 us
    ppermute x1, starting transfers between devices, with_halo(): lax.ppermute(head, axis, [((i + 1) % count, i) for i in range(ends)])  4.29 us
    ppermute x1, starting transfers between devices, butterfly_scan(): lax.ppermute(jnp.concatenate([block, plane_out], axis=0), axis, route)  3.83 us
    unnamed x12, local copies, waits for them, and re-layouts  2.08 us
    sub x1, other arithmetic, body(): grid - learn_rate * (new_first / corr_one) / (jnp.sqrt(new_second / corr_...  1.94 us
    ppermute x1, starting transfers between devices, with_halo(): lax.ppermute(tail, axis, [(i, (i + 1) % count) for i in range(ends)])  1.92 us
  transfers between devices with their start and end apart: 8, of which 5 were waited for; matrix products, arithmetic and copies ran while one was open for 3% of the time, Pallas kernels for 0%

profile of v12, /device:TPU:24, one launch (start us, length us, event | category | flops | bytes accessed | tf_op | source)
XLA Modules:
  0.0 64.1 jit_solution(3611566716579778812)
XLA Ops:
  0.6 0.0 copy-start
  0.6 1.0 %fusion.39 = (f32[4,1,8,1024]{3,2,1,0:T(8,128)S(1)}, f32[4,1,8,1024]{3,2,1,0:T(8,128)S(1)}) fusion(f32[4,4,8,1024]{3,2,1,0:T(8,128)} %param.6), kind=kLoop, calls=%fused_computation.122 | loop fusion | bytes 524288 | tf_op jit(solution)/shard_map/slice | solution.py:18
  1.7 4.3 %collective-permute-start = (f32[4,1,8,1024]{3,2,1,0:T(8,128)S(1)}, f32[4,1,8,1024]{3,2,1,0:T(8,128)S(1)}, u32[]{:S(2)}, u32[]{:S(2)}) collective-permute-start(f32[4,1,8,1024]{3,2,1,0:T(8,128)S(1)} %get-tuple-element.18), channel_id=1, source_target_pairs={{16,0},{32,16},{48,32},{64,48},{80,64},{96,80},{112,96},{128,112},... | collective-permute-start | bytes 393224 | tf_op jit(solution)/shard_map/ppermute | solution.py:24
  6.0 0.0 copy-done
  6.0 0.1 fusion.38
  6.1 0.0 copy-start.5
  6.1 0.6 %copy-done.5 = s32[1,1,128]{2,1,0:T(1,128)S(1)} copy-done((s32[1,1,128]{2,1,0:T(1,128)S(1)}, s32[1,1,128]{2,1,0:T(1,128)}, u32[]{:S(2)}) %copy-start.5) | copy-done | bytes 536
  6.8 0.1 broadcast_in_dim.10
  6.8 0.1 broadcast_in_dim.11
  6.9 0.0 copy-start.4
  7.0 0.7 %copy-done.4 = s32[4,1024]{1,0:T(4,128)S(1)} copy-done((s32[4,1024]{1,0:T(4,128)S(1)}, s32[4,1024]{1,0:T(4,128)}, u32[]{:S(2)}) %copy-start.4) | copy-done | bytes 16408
  7.7 0.8 %collective-permute-done = f32[4,1,8,1024]{3,2,1,0:T(8,128)S(1)} collective-permute-done((f32[4,1,8,1024]{3,2,1,0:T(8,128)S(1)}, f32[4,1,8,1024]{3,2,1,0:T(8,128)S(1)}, u32[]{:S(2)}, u32[]{:S(2)}) %collective-permute-start) | collective-permute-done | bytes 131104 | tf_op jit(solution)/shard_map/ppermute | solution.py:24
  8.5 0.1 fusion.9
  8.6 0.1 fusion.35
  8.7 0.1 reduce_window_sum.22
  8.8 0.1 fusion.30
  8.9 0.2 fusion.34
  9.1 3.8 %collective-permute-start.1 = (f32[8,4,1024]{2,1,0:T(4,128)S(1)}, f32[8,4,1024]{2,1,0:T(4,128)S(1)}, u32[]{:S(2)}, u32[]{:S(2)}) collective-permute-start(f32[8,4,1024]{2,1,0:T(4,128)S(1)} %pad_maximum_fusion.3), channel_id=1, source_target_pairs={{0,1},{1,0},{2,3},{3,2},{4,5},{5,4},{6,7},{7,6},{8,9},{9,8},{10,11... | collective-permute-start | bytes 393224 | tf_op jit(solution)/shard_map/ppermute | solution.py:58
  13.0 0.7 %collective-permute-start.7 = (f32[4,4,1024]{2,1,0:T(4,128)S(1)}, f32[4,4,1024]{2,1,0:T(4,128)S(1)}, u32[]{:S(2)}, u32[]{:S(2)}) collective-permute-start(f32[4,4,1024]{2,1,0:T(4,128)S(1)} %get-tuple-element.30), channel_id=1, source_target_pairs={{1,2},{3,4},{5,6},{7,8},{9,10},{11,12},{13,14},{2,1},{4,3},{6,5},{... | collective-permute-start | bytes 196616 | tf_op jit(solution)/shard_map/ppermute | solution.py:45
  13.6 1.9 %collective-permute-start.6 = (f32[4,1,8,1024]{3,2,1,0:T(8,128)S(1)}, f32[4,1,8,1024]{3,2,1,0:T(8,128)S(1)}, u32[]{:S(2)}, u32[]{:S(2)}) collective-permute-start(f32[4,1,8,1024]{3,2,1,0:T(8,128)S(1)} %get-tuple-element.19), channel_id=1, source_target_pairs={{0,16},{16,32},{32,48},{48,64},{64,80},{80,96},{96,112},{112,128},... | collective-permute-start | bytes 393224 | tf_op jit(solution)/shard_map/ppermute | solution.py:22
  15.6 0.3 reduce_window_sum.23
  16.0 0.0 collective-permute-done.7
  16.0 0.0 collective-permute-done.1
  16.0 0.1 select_bitcast_fusion
  16.1 10.9 %collective-permute-start.2 = (f32[4,4,1024]{2,1,0:T(4,128)S(1)}, f32[4,4,1024]{2,1,0:T(4,128)S(1)}, u32[]{:S(2)}, u32[]{:S(2)}) collective-permute-start(f32[4,4,1024]{2,1,0:T(4,128)S(1)} %pad_maximum_fusion.7), channel_id=1, source_target_pairs={{0,3},{1,2},{2,1},{3,0},{4,7},{5,6},{6,5},{7,4},{8,11},{9,10},{10,... | collective-permute-start | bytes 196616 | tf_op jit(solution)/shard_map/ppermute | solution.py:61
  27.1 2.1 %collective-permute-done.2 = f32[4,4,1024]{2,1,0:T(4,128)S(1)} collective-permute-done((f32[4,4,1024]{2,1,0:T(4,128)S(1)}, f32[4,4,1024]{2,1,0:T(4,128)S(1)}, u32[]{:S(2)}, u32[]{:S(2)}) %collective-permute-start.2) | collective-permute-done | bytes 65568 | tf_op jit(solution)/shard_map/ppermute | solution.py:61
  29.4 11.4 %collective-permute-start.3 = (f32[4,4,1024]{2,1,0:T(4,128)S(1)}, f32[4,4,1024]{2,1,0:T(4,128)S(1)}, u32[]{:S(2)}, u32[]{:S(2)}) collective-permute-start(f32[4,4,1024]{2,1,0:T(4,128)S(1)} %pad_maximum_fusion.8), channel_id=1, source_target_pairs={{0,7},{1,6},{2,5},{3,4},{4,3},{5,2},{6,1},{7,0},{8,15},{9,14},{10,... | collective-permute-start | bytes 196616 | tf_op jit(solution)/shard_map/ppermute | solution.py:61
  40.9 2.1 %collective-permute-done.3 = f32[4,4,1024]{2,1,0:T(4,128)S(1)} collective-permute-done((f32[4,4,1024]{2,1,0:T(4,128)S(1)}, f32[4,4,1024]{2,1,0:T(4,128)S(1)}, u32[]{:S(2)}, u32[]{:S(2)}) %collective-permute-start.3) | collective-permute-done | bytes 65568 | tf_op jit(solution)/shard_map/ppermute | solution.py:61
  43.1 7.0 %collective-permute-start.4 = (f32[4,4,1024]{2,1,0:T(4,128)S(1)}, f32[4,4,1024]{2,1,0:T(4,128)S(1)}, u32[]{:S(2)}, u32[]{:S(2)}) collective-permute-start(f32[4,4,1024]{2,1,0:T(4,128)S(1)} %pad_maximum_fusion.9), channel_id=1, source_target_pairs={{0,15},{1,14},{2,13},{3,12},{4,11},{5,10},{6,9},{7,8},{8,7},{9,6},... | collective-permute-start | bytes 196616 | tf_op jit(solution)/shard_map/ppermute | solution.py:61
  50.2 2.1 %collective-permute-done.4 = f32[4,4,1024]{2,1,0:T(4,128)S(1)} collective-permute-done((f32[4,4,1024]{2,1,0:T(4,128)S(1)}, f32[4,4,1024]{2,1,0:T(4,128)S(1)}, u32[]{:S(2)}, u32[]{:S(2)}) %collective-permute-start.4) | collective-permute-done | bytes 65568 | tf_op jit(solution)/shard_map/ppermute | solution.py:61
  52.4 0.1 multiply_bitcast_fusion.1
  52.5 0.0 copy-start.3
  52.6 0.7 %copy-done.3 = f32[3,4,1024]{2,1,0:T(4,128)S(1)} copy-done((f32[3,4,1024]{2,1,0:T(4,128)S(1)}, f32[3,4,1024]{2,1,0:T(4,128)}, u32[]{:S(2)}) %copy-start.3) | copy-done | bytes 49176
  53.4 0.2 multiply_reduce_fusion
  53.6 0.1 fusion.18
  53.6 0.1 fusion.10
  53.7 1.9 %collective-permute-start.5 = (f32[4,1,8,1024]{3,2,1,0:T(8,128)S(1)}, f32[4,1,8,1024]{3,2,1,0:T(8,128)S(1)}, u32[]{:S(2)}, u32[]{:S(2)}) collective-permute-start(f32[4,1,8,1024]{3,2,1,0:T(8,128)S(1)} %slice.273), channel_id=1, source_target_pairs={{0,16},{16,32},{32,48},{48,64},{64,80},{80,96},{96,112},{112,128},... | collective-permute-start | bytes 393224 | tf_op jit(solution)/shard_map/ppermute | solution.py:34
  55.7 0.1 fusion.37
  55.8 0.0 copy-start.1
  55.8 0.0 copy-start.2
  55.8 0.1 copy.18
  55.9 0.1 copy.17
  56.0 0.0 collective-permute-done.6
  56.0 6.1 %collective-permute-done.5 = f32[4,1,8,1024]{3,2,1,0:T(8,128)S(1)} collective-permute-done((f32[4,1,8,1024]{3,2,1,0:T(8,128)S(1)}, f32[4,1,8,1024]{3,2,1,0:T(8,128)S(1)}, u32[]{:S(2)}, u32[]{:S(2)}) %collective-permute-start.5) | collective-permute-done | bytes 131104 | tf_op jit(solution)/shard_map/ppermute | solution.py:34
  62.1 0.0 copy-done.1
  62.1 0.0 copy-done.2
  62.1 1.9 %divide_subtract_fusion = (f32[4,4,8,1024]{3,2,1,0:T(8,128)}, f32[4,4,8,1024]{3,2,1,0:T(8,128)}, f32[4,4,8,1024]{3,2,1,0:T(8,128)}) fusion(f32[4,4,8,1024]{3,2,1,0:T(8,128)S(1)} %copy-done, f32[4,4,8,1024]{3,2,1,0:T(8,128)S(1)} %copy-done.1, f32[4,4,8,1024]{3,2,1,0:T(8,128)S(1)} %copy-done.2, f32[4,4,7,1024]{3,2,1,0:T(8,128)S(1)} %get-tuple-element.14, ...), kind=kLoop, calls=%fused_computation.18 | loop fusion | flops 3801088 | bytes 5521408 | tf_op jit(solution)/shard_map/sub | solution.py:134
  (35 shorter events, 0.7 us)
Async XLA Ops:
  0.6 5.4 %copy-start = (f32[4,4,8,1024]{3,2,1,0:T(8,128)S(1)}, f32[4,4,8,1024]{3,2,1,0:T(8,128)}, u32[]{:S(2)}) copy-start(f32[4,4,8,1024]{3,2,1,0:T(8,128)} %param.6) | copy-start | bytes 1572868
  1.7 6.8 %collective-permute-start = (f32[4,1,8,1024]{3,2,1,0:T(8,128)S(1)}, f32[4,1,8,1024]{3,2,1,0:T(8,128)S(1)}, u32[]{:S(2)}, u32[]{:S(2)}) collective-permute-start(f32[4,1,8,1024]{3,2,1,0:T(8,128)S(1)} %get-tuple-element.18), channel_id=1, source_target_pairs={{16,0},{32,16},{48,32},{64,48},{80,64},{96,80},{112,96},{128,112},... | collective-permute-start | bytes 393224 | tf_op jit(solution)/shard_map/ppermute | solution.py:24
  6.1 0.7 %copy-start.5 = (s32[1,1,128]{2,1,0:T(1,128)S(1)}, s32[1,1,128]{2,1,0:T(1,128)}, u32[]{:S(2)}) copy-start(s32[1,1,128]{2,1,0:T(1,128)} %param.10) | copy-start | bytes 1540
  6.9 0.7 %copy-start.4 = (s32[4,1024]{1,0:T(4,128)S(1)}, s32[4,1024]{1,0:T(4,128)}, u32[]{:S(2)}) copy-start(s32[4,1024]{1,0:T(4,128)} %param.9) | copy-start | bytes 49156
  9.1 6.9 %collective-permute-start.1 = (f32[8,4,1024]{2,1,0:T(4,128)S(1)}, f32[8,4,1024]{2,1,0:T(4,128)S(1)}, u32[]{:S(2)}, u32[]{:S(2)}) collective-permute-start(f32[8,4,1024]{2,1,0:T(4,128)S(1)} %pad_maximum_fusion.3), channel_id=1, source_target_pairs={{0,1},{1,0},{2,3},{3,2},{4,5},{5,4},{6,7},{7,6},{8,9},{9,8},{10,11... | collective-permute-start | bytes 393224 | tf_op jit(solution)/shard_map/ppermute | solution.py:58
  13.0 3.0 %collective-permute-start.7 = (f32[4,4,1024]{2,1,0:T(4,128)S(1)}, f32[4,4,1024]{2,1,0:T(4,128)S(1)}, u32[]{:S(2)}, u32[]{:S(2)}) collective-permute-start(f32[4,4,1024]{2,1,0:T(4,128)S(1)} %get-tuple-element.30), channel_id=1, source_target_pairs={{1,2},{3,4},{5,6},{7,8},{9,10},{11,12},{13,14},{2,1},{4,3},{6,5},{... | collective-permute-start | bytes 196616 | tf_op jit(solution)/shard_map/ppermute | solution.py:45
  13.6 42.3 %collective-permute-start.6 = (f32[4,1,8,1024]{3,2,1,0:T(8,128)S(1)}, f32[4,1,8,1024]{3,2,1,0:T(8,128)S(1)}, u32[]{:S(2)}, u32[]{:S(2)}) collective-permute-start(f32[4,1,8,1024]{3,2,1,0:T(8,128)S(1)} %get-tuple-element.19), channel_id=1, source_target_pairs={{0,16},{16,32},{32,48},{48,64},{64,80},{80,96},{96,112},{112,128},... | collective-permute-start | bytes 393224 | tf_op jit(solution)/shard_map/ppermute | solution.py:22
  16.1 13.1 %collective-permute-start.2 = (f32[4,4,1024]{2,1,0:T(4,128)S(1)}, f32[4,4,1024]{2,1,0:T(4,128)S(1)}, u32[]{:S(2)}, u32[]{:S(2)}) collective-permute-start(f32[4,4,1024]{2,1,0:T(4,128)S(1)} %pad_maximum_fusion.7), channel_id=1, source_target_pairs={{0,3},{1,2},{2,1},{3,0},{4,7},{5,6},{6,5},{7,4},{8,11},{9,10},{10,... | collective-permute-start | bytes 196616 | tf_op jit(solution)/shard_map/ppermute | solution.py:61
  29.4 13.7 %collective-permute-start.3 = (f32[4,4,1024]{2,1,0:T(4,128)S(1)}, f32[4,4,1024]{2,1,0:T(4,128)S(1)}, u32[]{:S(2)}, u32[]{:S(2)}) collective-permute-start(f32[4,4,1024]{2,1,0:T(4,128)S(1)} %pad_maximum_fusion.8), channel_id=1, source_target_pairs={{0,7},{1,6},{2,5},{3,4},{4,3},{5,2},{6,1},{7,0},{8,15},{9,14},{10,... | collective-permute-start | bytes 196616 | tf_op jit(solution)/shard_map/ppermute | solution.py:61
  43.1 9.2 %collective-permute-start.4 = (f32[4,4,1024]{2,1,0:T(4,128)S(1)}, f32[4,4,1024]{2,1,0:T(4,128)S(1)}, u32[]{:S(2)}, u32[]{:S(2)}) collective-permute-start(f32[4,4,1024]{2,1,0:T(4,128)S(1)} %pad_maximum_fusion.9), channel_id=1, source_target_pairs={{0,15},{1,14},{2,13},{3,12},{4,11},{5,10},{6,9},{7,8},{8,7},{9,6},... | collective-permute-start | bytes 196616 | tf_op jit(solution)/shard_map/ppermute | solution.py:61
  52.5 0.8 %copy-start.3 = (f32[3,4,1024]{2,1,0:T(4,128)S(1)}, f32[3,4,1024]{2,1,0:T(4,128)}, u32[]{:S(2)}) copy-start(f32[3,4,1024]{2,1,0:T(4,128)} %param.11) | copy-start | bytes 147460
  53.7 8.4 %collective-permute-start.5 = (f32[4,1,8,1024]{3,2,1,0:T(8,128)S(1)}, f32[4,1,8,1024]{3,2,1,0:T(8,128)S(1)}, u32[]{:S(2)}, u32[]{:S(2)}) collective-permute-start(f32[4,1,8,1024]{3,2,1,0:T(8,128)S(1)} %slice.273), channel_id=1, source_target_pairs={{0,16},{16,32},{32,48},{48,64},{64,80},{80,96},{96,112},{112,128},... | collective-permute-start | bytes 393224 | tf_op jit(solution)/shard_map/ppermute | solution.py:34
  55.8 6.4 %copy-start.1 = (f32[4,4,8,1024]{3,2,1,0:T(8,128)S(1)}, f32[4,4,8,1024]{3,2,1,0:T(8,128)}, u32[]{:S(2)}) copy-start(f32[4,4,8,1024]{3,2,1,0:T(8,128)} %param.7) | copy-start | bytes 1572868
  55.8 6.3 %copy-start.2 = (f32[4,4,8,1024]{3,2,1,0:T(8,128)S(1)}, f32[4,4,8,1024]{3,2,1,0:T(8,128)}, u32[]{:S(2)}) copy-start(f32[4,4,8,1024]{3,2,1,0:T(8,128)} %param.8) | copy-start | bytes 1572868

commit v13 on v8

--- a/solution.py
+++ b/solution.py
@@ -32,7 +32,7 @@
     count, mine = (lax.axis_size(axis), lax.axis_index(axis))
     block = jnp.concatenate([seg_colour, seg_trans[None]], axis=0)
     plane_in = None
-    blank = jnp.concatenate([jnp.zeros_like(seg_colour), jnp.ones_like(seg_trans)[None]], axis=0)
+    blank = jnp.concatenate([block[:-1] * 0.0, block[-1:] * 0.0 + 1.0], axis=0)
     prefix, suffix = (blank, blank)
     step = 1
     while step < count:
@@ -101,11 +101,10 @@
     plane_before = jnp.where(odd, plane_in, swapped)[:, :, None]
     plane_after = jnp.where(odd, swapped, plane_in)[:, :, None]
     carried = shares * feature_grad
-    both = passed_along(jnp.concatenate([carried[:, -1:], grid[:, -1:]], axis=0), "tile", 1)
-    incoming, row_before = (both[: grid.shape[0]], both[grid.shape[0] :])
+    incoming = passed_along(carried[:, -1:] - 2.0 * tv_weight * grid[:, -1:], "tile", 1)
     carried_in = jnp.concatenate([incoming, carried[:, :-1]], axis=1)
     data_grad = (1.0 - shares) * feature_grad + carried_in
-    across_rows = rows_after + jnp.concatenate([row_before, grid[:, :-1]], axis=1)
+    across_rows = rows_after + jnp.concatenate([jnp.zeros_like(grid[:, :1]), grid[:, :-1]], axis=1)
     across_planes = jnp.concatenate([grid[:, :, 1:], plane_after], axis=2) + jnp.concatenate(
         [plane_before, grid[:, :, :-1]], axis=2
     )

time: 70.8 us -> 65.4 us (0.924)
  other arithmetic: 9.04 us -> 4.03 us
  waiting for transfers between devices: 15.5 us -> 14.4 us
  local copies, waits for them, and re-layouts: 4.4 us -> 5.36 us
    ppermute x3, waiting for transfers between devices: 4.88 us -> 6.33 us  [butterfly_scan(): other = lax.ppermute(block, axis, route)]
    ppermute x1, waiting for transfers between devices: 7.55 us -> 6.14 us  [passed_along(): return lax.ppermute(block, axis, route)]
    slice x1, local copies, waits for them, and re-layouts: 0.08 us -> 1.3 us  [body(): plane_out = jnp.where(odd, grid[:, :, 0], grid[:, :, -1])]
    broadcast_in_dim x1, other arithmetic: 0.94 us -> 0.06 us  [body(): plane_before = jnp.where(odd, plane_in, swapped)[:, :, None]]
    select_n x2, other arithmetic: 0.9 us -> 0.06 us  [butterfly_scan(): jnp.where(upper, other, block)]
    add x7, other arithmetic: 0.96 us -> 0.18 us  [over(): front[:-1] + front[-1:] * back[:-1]]
    ppermute x1, waiting for transfers between devices: 0.71 us -> 0.01 us  [body(): lax.ppermute(grid[:, :1], 'tile', [(i + 1, i) for i in range(tiles - 1)])]
    unnamed x24 -> x16, local copies, waits for them, and re-layouts: 2.73 us -> 2.56 us
  transfers between devices with their start and end apart: 7 -> 7, of which waited for: 6 -> 5; matrix products, arithmetic and copies ran while one was open for 5% -> 4% of each run, Pallas kernels for 0% -> 0%
where the time goes in v13:
time: 65.4 us; the launch traced here: 64.9 us
  starting transfers between devices  39.9 us (61%)
  waiting for transfers between devices  14.4 us (22%)
  local copies, waits for them, and re-layouts  5.36 us (8%)
  other arithmetic  4.03 us (6%)
  between operations  1.18 us (2%)
    ppermute x3, starting transfers between devices, butterfly_scan(): other = lax.ppermute(block, axis, route)  29.2 us
    ppermute x3, waiting for transfers between devices, butterfly_scan(): other = lax.ppermute(block, axis, route)  6.33 us
    ppermute x1, waiting for transfers between devices, passed_along(): return lax.ppermute(block, axis, route)  6.14 us
    ppermute x1, starting transfers between devices, body(): lax.ppermute(grid[:, :1], 'tile', [(i + 1, i) for i in range(tiles - 1)])  4.29 us
    ppermute x1, starting transfers between devices, butterfly_scan(): lax.ppermute(jnp.concatenate([block, plane_out], axis=0), axis, route)  3.83 us
    unnamed x16, local copies, waits for them, and re-layouts  2.56 us
    ppermute x1, waiting for transfers between devices, butterfly_scan(): lax.ppermute(jnp.concatenate([block, plane_out], axis=0), axis, route)  1.96 us
    sub x1, other arithmetic, body(): grid - learn_rate * (new_first / corr_one) / (jnp.sqrt(new_second / corr_...  1.93 us
  transfers between devices with their start and end apart: 7, of which 5 were waited for; matrix products, arithmetic and copies ran while one was open for 4% of the time, Pallas kernels for 0%

profile of v13, /device:TPU:24, one launch (start us, length us, event | category | flops | bytes accessed | tf_op | source)
XLA Modules:
  0.0 64.9 jit_solution(10314538157945656023)
XLA Ops:
  0.6 0.0 copy-start
  0.6 1.0 %slice.180 = f32[4,1,8,1024]{3,2,1,0:T(8,128)S(1)} slice(f32[4,4,8,1024]{3,2,1,0:T(8,128)} %param.6), slice={[0:4], [0:1], [0:8], [0:1024]} | slice | bytes 262144 | tf_op jit(solution)/shard_map/slice | solution.py:93
  1.6 4.3 %collective-permute-start = (f32[4,1,8,1024]{3,2,1,0:T(8,128)S(1)}, f32[4,1,8,1024]{3,2,1,0:T(8,128)S(1)}, u32[]{:S(2)}, u32[]{:S(2)}) collective-permute-start(f32[4,1,8,1024]{3,2,1,0:T(8,128)S(1)} %slice.180), channel_id=1, source_target_pairs={{16,0},{32,16},{48,32},{64,48},{80,64},{96,80},{112,96},{128,112},... | collective-permute-start | bytes 393224 | tf_op jit(solution)/shard_map/ppermute | solution.py:93
  5.9 1.3 %fusion.35 = (f32[4,4,1,1024]{3,2,1,0:T(1,128)S(1)}, f32[4,4,1,1024]{3,2,1,0:T(1,128)S(1)}) fusion(f32[4,4,8,1024]{3,2,1,0:T(8,128)} %param.6), kind=kLoop, calls=%fused_computation.119 | loop fusion | bytes 262144 | tf_op jit(solution)/shard_map/slice | solution.py:99
  7.2 0.0 copy-done
  7.2 0.1 fusion.33
  7.3 0.0 copy-start.7
  7.3 0.6 copy-done.7
  8.0 0.1 broadcast_in_dim.10
  8.1 0.1 broadcast_in_dim.11
  8.2 0.0 copy-start.4
  8.2 0.0 copy-start.6
  8.2 0.7 %copy-done.6 = s32[4,1024]{1,0:T(4,128)S(1)} copy-done((s32[4,1024]{1,0:T(4,128)S(1)}, s32[4,1024]{1,0:T(4,128)}, u32[]{:S(2)}) %copy-start.6) | copy-done | bytes 16408
  8.9 0.0 collective-permute-done
  8.9 0.1 multiply_add_fusion.1
  9.0 0.0 copy-done.4
  9.0 0.1 fusion.31
  9.2 0.1 reduce_window_sum.22
  9.3 0.1 fusion.26
  9.4 0.2 fusion.30
  9.6 3.8 %collective-permute-start.1 = (f32[8,4,1024]{2,1,0:T(4,128)S(1)}, f32[8,4,1024]{2,1,0:T(4,128)S(1)}, u32[]{:S(2)}, u32[]{:S(2)}) collective-permute-start(f32[8,4,1024]{2,1,0:T(4,128)S(1)} %pad_maximum_fusion.2), channel_id=1, source_target_pairs={{0,1},{1,0},{2,3},{3,2},{4,5},{5,4},{6,7},{7,6},{8,9},{9,8},{10,11... | collective-permute-start | bytes 393224 | tf_op jit(solution)/shard_map/ppermute | solution.py:41
  13.4 0.7 %collective-permute-start.6 = (f32[4,4,1024]{2,1,0:T(4,128)S(1)}, f32[4,4,1024]{2,1,0:T(4,128)S(1)}, u32[]{:S(2)}, u32[]{:S(2)}) collective-permute-start(f32[4,4,1024]{2,1,0:T(4,128)S(1)} %get-tuple-element.30), channel_id=1, source_target_pairs={{1,2},{3,4},{5,6},{7,8},{9,10},{11,12},{13,14},{2,1},{4,3},{6,5},{... | collective-permute-start | bytes 196616 | tf_op jit(solution)/shard_map/ppermute | solution.py:28
  14.1 0.3 reduce_window_sum.23
  14.5 0.0 collective-permute-done.6
  14.5 2.0 %collective-permute-done.1 = f32[8,4,1024]{2,1,0:T(4,128)S(1)} collective-permute-done((f32[8,4,1024]{2,1,0:T(4,128)S(1)}, f32[8,4,1024]{2,1,0:T(4,128)S(1)}, u32[]{:S(2)}, u32[]{:S(2)}) %collective-permute-start.1) | collective-permute-done | bytes 131104 | tf_op jit(solution)/shard_map/ppermute | solution.py:41
  16.5 0.1 select_bitcast_fusion
  16.6 10.8 %collective-permute-start.2 = (f32[4,4,1024]{2,1,0:T(4,128)S(1)}, f32[4,4,1024]{2,1,0:T(4,128)S(1)}, u32[]{:S(2)}, u32[]{:S(2)}) collective-permute-start(f32[4,4,1024]{2,1,0:T(4,128)S(1)} %pad_maximum_fusion.6), channel_id=1, source_target_pairs={{0,3},{1,2},{2,1},{3,0},{4,7},{5,6},{6,5},{7,4},{8,11},{9,10},{10,... | collective-permute-start | bytes 196616 | tf_op jit(solution)/shard_map/ppermute | solution.py:44
  27.5 2.1 %collective-permute-done.2 = f32[4,4,1024]{2,1,0:T(4,128)S(1)} collective-permute-done((f32[4,4,1024]{2,1,0:T(4,128)S(1)}, f32[4,4,1024]{2,1,0:T(4,128)S(1)}, u32[]{:S(2)}, u32[]{:S(2)}) %collective-permute-start.2) | collective-permute-done | bytes 65568 | tf_op jit(solution)/shard_map/ppermute | solution.py:44
  29.7 11.4 %collective-permute-start.3 = (f32[4,4,1024]{2,1,0:T(4,128)S(1)}, f32[4,4,1024]{2,1,0:T(4,128)S(1)}, u32[]{:S(2)}, u32[]{:S(2)}) collective-permute-start(f32[4,4,1024]{2,1,0:T(4,128)S(1)} %pad_maximum_fusion.7), channel_id=1, source_target_pairs={{0,7},{1,6},{2,5},{3,4},{4,3},{5,2},{6,1},{7,0},{8,15},{9,14},{10,... | collective-permute-start | bytes 196616 | tf_op jit(solution)/shard_map/ppermute | solution.py:44
  41.3 2.1 %collective-permute-done.3 = f32[4,4,1024]{2,1,0:T(4,128)S(1)} collective-permute-done((f32[4,4,1024]{2,1,0:T(4,128)S(1)}, f32[4,4,1024]{2,1,0:T(4,128)S(1)}, u32[]{:S(2)}, u32[]{:S(2)}) %collective-permute-start.3) | collective-permute-done | bytes 65568 | tf_op jit(solution)/shard_map/ppermute | solution.py:44
  43.5 7.0 %collective-permute-start.4 = (f32[4,4,1024]{2,1,0:T(4,128)S(1)}, f32[4,4,1024]{2,1,0:T(4,128)S(1)}, u32[]{:S(2)}, u32[]{:S(2)}) collective-permute-start(f32[4,4,1024]{2,1,0:T(4,128)S(1)} %pad_maximum_fusion.8), channel_id=1, source_target_pairs={{0,15},{1,14},{2,13},{3,12},{4,11},{5,10},{6,9},{7,8},{8,7},{9,6},... | collective-permute-start | bytes 196616 | tf_op jit(solution)/shard_map/ppermute | solution.py:44
  50.6 2.1 %collective-permute-done.4 = f32[4,4,1024]{2,1,0:T(4,128)S(1)} collective-permute-done((f32[4,4,1024]{2,1,0:T(4,128)S(1)}, f32[4,4,1024]{2,1,0:T(4,128)S(1)}, u32[]{:S(2)}, u32[]{:S(2)}) %collective-permute-start.4) | collective-permute-done | bytes 65568 | tf_op jit(solution)/shard_map/ppermute | solution.py:44
  52.8 0.1 multiply_bitcast_fusion.1
  52.9 0.0 copy-start.3
  53.0 0.7 %copy-done.3 = f32[3,4,1024]{2,1,0:T(4,128)S(1)} copy-done((f32[3,4,1024]{2,1,0:T(4,128)S(1)}, f32[3,4,1024]{2,1,0:T(4,128)}, u32[]{:S(2)}) %copy-start.3) | copy-done | bytes 49176
  53.8 0.0 copy-start.5
  53.8 0.2 multiply_reduce_fusion
  54.0 0.5 copy-done.5
  54.5 0.1 fusion.14
  54.5 0.1 fusion.6
  54.6 1.9 %collective-permute-start.5 = (f32[4,1,8,1024]{3,2,1,0:T(8,128)S(1)}, f32[4,1,8,1024]{3,2,1,0:T(8,128)S(1)}, u32[]{:S(2)}, u32[]{:S(2)}) collective-permute-start(f32[4,1,8,1024]{3,2,1,0:T(8,128)S(1)} %slice_subtract_fusion), channel_id=1, source_target_pairs={{0,16},{16,32},{32,48},{48,64},{64,80},{80,96},{96,112},{112,128},... | collective-permute-start | bytes 393224 | tf_op jit(solution)/shard_map/ppermute | solution.py:17
  56.5 0.1 fusion.34
  56.6 0.0 copy-start.1
  56.7 0.0 copy-start.2
  56.7 0.1 copy.18
  56.8 0.1 copy.17
  56.9 6.1 %collective-permute-done.5 = f32[4,1,8,1024]{3,2,1,0:T(8,128)S(1)} collective-permute-done((f32[4,1,8,1024]{3,2,1,0:T(8,128)S(1)}, f32[4,1,8,1024]{3,2,1,0:T(8,128)S(1)}, u32[]{:S(2)}, u32[]{:S(2)}) %collective-permute-start.5) | collective-permute-done | bytes 131104 | tf_op jit(solution)/shard_map/ppermute | solution.py:17
  63.0 0.0 copy-done.1
  63.0 0.0 copy-done.2
  63.0 1.9 %divide_subtract_fusion = (f32[4,4,8,1024]{3,2,1,0:T(8,128)}, f32[4,4,8,1024]{3,2,1,0:T(8,128)}, f32[4,4,8,1024]{3,2,1,0:T(8,128)}) fusion(f32[4,4,8,1024]{3,2,1,0:T(8,128)S(1)} %copy-done, f32[4,4,8,1024]{3,2,1,0:T(8,128)S(1)} %copy-done.1, f32[4,4,8,1024]{3,2,1,0:T(8,128)S(1)} %copy-done.2, f32[4,4,7,1024]{3,2,1,0:T(8,128)S(1)} %get-tuple-element.16, ...), kind=kLoop, calls=%fused_computation.13 | loop fusion | flops 3670016 | bytes 6176768 | tf_op jit(solution)/shard_map/sub | solution.py:119
  (35 shorter events, 0.7 us)
Async XLA Ops:
  0.6 6.6 %copy-start = (f32[4,4,8,1024]{3,2,1,0:T(8,128)S(1)}, f32[4,4,8,1024]{3,2,1,0:T(8,128)}, u32[]{:S(2)}) copy-start(f32[4,4,8,1024]{3,2,1,0:T(8,128)} %param.6) | copy-start | bytes 1572868
  1.6 7.3 %collective-permute-start = (f32[4,1,8,1024]{3,2,1,0:T(8,128)S(1)}, f32[4,1,8,1024]{3,2,1,0:T(8,128)S(1)}, u32[]{:S(2)}, u32[]{:S(2)}) collective-permute-start(f32[4,1,8,1024]{3,2,1,0:T(8,128)S(1)} %slice.180), channel_id=1, source_target_pairs={{16,0},{32,16},{48,32},{64,48},{80,64},{96,80},{112,96},{128,112},... | collective-permute-start | bytes 393224 | tf_op jit(solution)/shard_map/ppermute | solution.py:93
  7.3 0.7 %copy-start.7 = (s32[1,1,128]{2,1,0:T(1,128)S(1)}, s32[1,1,128]{2,1,0:T(1,128)}, u32[]{:S(2)}) copy-start(s32[1,1,128]{2,1,0:T(1,128)} %param.10) | copy-start | bytes 1540
  8.2 0.8 %copy-start.4 = (f32[1024]{0:T(1024)}, f32[1024]{0:T(1024)S(1)}, u32[]{:S(2)}) copy-start(f32[1024]{0:T(1024)S(1)} %broadcast_in_dim.11) | copy-start | bytes 12292
  8.2 0.7 %copy-start.6 = (s32[4,1024]{1,0:T(4,128)S(1)}, s32[4,1024]{1,0:T(4,128)}, u32[]{:S(2)}) copy-start(s32[4,1024]{1,0:T(4,128)} %param.9) | copy-start | bytes 49156
  9.6 6.9 %collective-permute-start.1 = (f32[8,4,1024]{2,1,0:T(4,128)S(1)}, f32[8,4,1024]{2,1,0:T(4,128)S(1)}, u32[]{:S(2)}, u32[]{:S(2)}) collective-permute-start(f32[8,4,1024]{2,1,0:T(4,128)S(1)} %pad_maximum_fusion.2), channel_id=1, source_target_pairs={{0,1},{1,0},{2,3},{3,2},{4,5},{5,4},{6,7},{7,6},{8,9},{9,8},{10,11... | collective-permute-start | bytes 393224 | tf_op jit(solution)/shard_map/ppermute | solution.py:41
  13.4 1.1 %collective-permute-start.6 = (f32[4,4,1024]{2,1,0:T(4,128)S(1)}, f32[4,4,1024]{2,1,0:T(4,128)S(1)}, u32[]{:S(2)}, u32[]{:S(2)}) collective-permute-start(f32[4,4,1024]{2,1,0:T(4,128)S(1)} %get-tuple-element.30), channel_id=1, source_target_pairs={{1,2},{3,4},{5,6},{7,8},{9,10},{11,12},{13,14},{2,1},{4,3},{6,5},{... | collective-permute-start | bytes 196616 | tf_op jit(solution)/shard_map/ppermute | solution.py:28
  16.6 13.0 %collective-permute-start.2 = (f32[4,4,1024]{2,1,0:T(4,128)S(1)}, f32[4,4,1024]{2,1,0:T(4,128)S(1)}, u32[]{:S(2)}, u32[]{:S(2)}) collective-permute-start(f32[4,4,1024]{2,1,0:T(4,128)S(1)} %pad_maximum_fusion.6), channel_id=1, source_target_pairs={{0,3},{1,2},{2,1},{3,0},{4,7},{5,6},{6,5},{7,4},{8,11},{9,10},{10,... | collective-permute-start | bytes 196616 | tf_op jit(solution)/shard_map/ppermute | solution.py:44
  29.7 13.7 %collective-permute-start.3 = (f32[4,4,1024]{2,1,0:T(4,128)S(1)}, f32[4,4,1024]{2,1,0:T(4,128)S(1)}, u32[]{:S(2)}, u32[]{:S(2)}) collective-permute-start(f32[4,4,1024]{2,1,0:T(4,128)S(1)} %pad_maximum_fusion.7), channel_id=1, source_target_pairs={{0,7},{1,6},{2,5},{3,4},{4,3},{5,2},{6,1},{7,0},{8,15},{9,14},{10,... | collective-permute-start | bytes 196616 | tf_op jit(solution)/shard_map/ppermute | solution.py:44
  43.5 9.2 %collective-permute-start.4 = (f32[4,4,1024]{2,1,0:T(4,128)S(1)}, f32[4,4,1024]{2,1,0:T(4,128)S(1)}, u32[]{:S(2)}, u32[]{:S(2)}) collective-permute-start(f32[4,4,1024]{2,1,0:T(4,128)S(1)} %pad_maximum_fusion.8), channel_id=1, source_target_pairs={{0,15},{1,14},{2,13},{3,12},{4,11},{5,10},{6,9},{7,8},{8,7},{9,6},... | collective-permute-start | bytes 196616 | tf_op jit(solution)/shard_map/ppermute | solution.py:44
  52.9 0.8 %copy-start.3 = (f32[3,4,1024]{2,1,0:T(4,128)S(1)}, f32[3,4,1024]{2,1,0:T(4,128)}, u32[]{:S(2)}) copy-start(f32[3,4,1024]{2,1,0:T(4,128)} %param.11) | copy-start | bytes 147460
  53.8 0.7 %copy-start.5 = (f32[1024]{0:T(1024)S(1)}, f32[1024]{0:T(1024)}, u32[]{:S(2)}) copy-start(f32[1024]{0:T(1024)} %copy-done.4) | copy-start | bytes 12292
  54.6 8.4 %collective-permute-start.5 = (f32[4,1,8,1024]{3,2,1,0:T(8,128)S(1)}, f32[4,1,8,1024]{3,2,1,0:T(8,128)S(1)}, u32[]{:S(2)}, u32[]{:S(2)}) collective-permute-start(f32[4,1,8,1024]{3,2,1,0:T(8,128)S(1)} %slice_subtract_fusion), channel_id=1, source_target_pairs={{0,16},{16,32},{32,48},{48,64},{64,80},{80,96},{96,112},{112,128},... | collective-permute-start | bytes 393224 | tf_op jit(solution)/shard_map/ppermute | solution.py:17
  56.6 6.4 %copy-start.1 = (f32[4,4,8,1024]{3,2,1,0:T(8,128)S(1)}, f32[4,4,8,1024]{3,2,1,0:T(8,128)}, u32[]{:S(2)}) copy-start(f32[4,4,8,1024]{3,2,1,0:T(8,128)} %param.7) | copy-start | bytes 1572868
  56.7 6.3 %copy-start.2 = (f32[4,4,8,1024]{3,2,1,0:T(8,128)S(1)}, f32[4,4,8,1024]{3,2,1,0:T(8,128)}, u32[]{:S(2)}) copy-start(f32[4,4,8,1024]{3,2,1,0:T(8,128)} %param.8) | copy-start | bytes 1572868

commit v14 on v12

--- a/solution.py
+++ b/solution.py
@@ -53,7 +53,10 @@
     prefix, suffix = (blank, blank)
     step = 1
     while step < count:
-        route = [(i, i - i % (2 * step) + 2 * step - 1 - i % (2 * step)) for i in range(count)]
+        if step == 2:
+            route = [(i, i ^ step) for i in range(count)]
+        else:
+            route = [(i, i - i % (2 * step) + 2 * step - 1 - i % (2 * step)) for i in range(count)]
         if step == 1:
             both = lax.ppermute(jnp.concatenate([block, plane_out], axis=0), axis, route)
             other, plane_in = (both[: block.shape[0]], both[block.shape[0] :])

time: 64.5 us -> 65.4 us (1.014); the launches traced: 64.1 us -> 64.3 us
  waiting for transfers between devices: 13.3 us -> 15.2 us
  starting transfers between devices: 41.9 us -> 40.2 us
    ppermute x3, waiting for transfers between devices: 6.33 us -> 8.27 us  [butterfly_scan(): other = lax.ppermute(block, axis, route)]
    ppermute x3, starting transfers between devices: 29.3 us -> 27.6 us  [butterfly_scan(): other = lax.ppermute(block, axis, route)]
where the time goes in v14:
time: 65.4 us; the launch traced here: 64.3 us
  starting transfers between devices  40.2 us (61%)
  waiting for transfers between devices  15.2 us (23%)
  other arithmetic  4 us (6%)
  local copies, waits for them, and re-layouts  3.68 us (6%)
  between operations  1.18 us (2%)
    ppermute x3, starting transfers between devices, butterfly_scan(): other = lax.ppermute(block, axis, route)  27.6 us
    ppermute x3, waiting for transfers between devices, butterfly_scan(): other = lax.ppermute(block, axis, route)  8.27 us
    ppermute x1, waiting for transfers between devices, passed_along(): return lax.ppermute(block, axis, route)  6.13 us
    ppermute x1, starting transfers between devices, with_halo(): lax.ppermute(head, axis, [((i + 1) % count, i) for i in range(ends)])  4.29 us
    ppermute x1, starting transfers between devices, butterfly_scan(): lax.ppermute(jnp.concatenate([block, plane_out], axis=0), axis, route)  3.83 us
    unnamed x12, local copies, waits for them, and re-layouts  2.08 us
    sub x1, other arithmetic, body(): grid - learn_rate * (new_first / corr_one) / (jnp.sqrt(new_second / corr_...  1.94 us
    ppermute x1, starting transfers between devices, with_halo(): lax.ppermute(tail, axis, [(i, (i + 1) % count) for i in range(ends)])  1.92 us
  transfers between devices with their start and end apart: 8, of which 5 were waited for; matrix products, arithmetic and copies ran while one was open for 3% of the time, Pallas kernels for 0%

profile of v14, /device:TPU:24, one launch (start us, length us, event | category | flops | bytes accessed | tf_op | source)
XLA Modules:
  0.0 64.3 jit_solution(5945682484927465517)
XLA Ops:
  0.6 0.0 copy-start
  0.6 1.0 %fusion.39 = (f32[4,1,8,1024]{3,2,1,0:T(8,128)S(1)}, f32[4,1,8,1024]{3,2,1,0:T(8,128)S(1)}) fusion(f32[4,4,8,1024]{3,2,1,0:T(8,128)} %param.6), kind=kLoop, calls=%fused_computation.122 | loop fusion | bytes 524288 | tf_op jit(solution)/shard_map/slice | solution.py:18
  1.7 4.3 %collective-permute-start = (f32[4,1,8,1024]{3,2,1,0:T(8,128)S(1)}, f32[4,1,8,1024]{3,2,1,0:T(8,128)S(1)}, u32[]{:S(2)}, u32[]{:S(2)}) collective-permute-start(f32[4,1,8,1024]{3,2,1,0:T(8,128)S(1)} %get-tuple-element.18), channel_id=1, source_target_pairs={{16,0},{32,16},{48,32},{64,48},{80,64},{96,80},{112,96},{128,112},... | collective-permute-start | bytes 393224 | tf_op jit(solution)/shard_map/ppermute | solution.py:24
  6.0 0.0 copy-done
  6.0 0.1 fusion.38
  6.1 0.0 copy-start.5
  6.1 0.6 %copy-done.5 = s32[1,1,128]{2,1,0:T(1,128)S(1)} copy-done((s32[1,1,128]{2,1,0:T(1,128)S(1)}, s32[1,1,128]{2,1,0:T(1,128)}, u32[]{:S(2)}) %copy-start.5) | copy-done | bytes 536
  6.8 0.1 broadcast_in_dim.10
  6.8 0.1 broadcast_in_dim.11
  6.9 0.0 copy-start.4
  7.0 0.7 %copy-done.4 = s32[4,1024]{1,0:T(4,128)S(1)} copy-done((s32[4,1024]{1,0:T(4,128)S(1)}, s32[4,1024]{1,0:T(4,128)}, u32[]{:S(2)}) %copy-start.4) | copy-done | bytes 16408
  7.7 0.8 %collective-permute-done = f32[4,1,8,1024]{3,2,1,0:T(8,128)S(1)} collective-permute-done((f32[4,1,8,1024]{3,2,1,0:T(8,128)S(1)}, f32[4,1,8,1024]{3,2,1,0:T(8,128)S(1)}, u32[]{:S(2)}, u32[]{:S(2)}) %collective-permute-start) | collective-permute-done | bytes 131104 | tf_op jit(solution)/shard_map/ppermute | solution.py:24
  8.5 0.1 fusion.9
  8.6 0.1 fusion.35
  8.7 0.1 reduce_window_sum.22
  8.8 0.1 fusion.30
  8.9 0.2 fusion.34
  9.1 3.8 %collective-permute-start.1 = (f32[8,4,1024]{2,1,0:T(4,128)S(1)}, f32[8,4,1024]{2,1,0:T(4,128)S(1)}, u32[]{:S(2)}, u32[]{:S(2)}) collective-permute-start(f32[8,4,1024]{2,1,0:T(4,128)S(1)} %pad_maximum_fusion.3), channel_id=1, source_target_pairs={{0,1},{1,0},{2,3},{3,2},{4,5},{5,4},{6,7},{7,6},{8,9},{9,8},{10,11... | collective-permute-start | bytes 393224 | tf_op jit(solution)/shard_map/ppermute | solution.py:61
  13.0 0.7 %collective-permute-start.7 = (f32[4,4,1024]{2,1,0:T(4,128)S(1)}, f32[4,4,1024]{2,1,0:T(4,128)S(1)}, u32[]{:S(2)}, u32[]{:S(2)}) collective-permute-start(f32[4,4,1024]{2,1,0:T(4,128)S(1)} %get-tuple-element.30), channel_id=1, source_target_pairs={{1,2},{3,4},{5,6},{7,8},{9,10},{11,12},{13,14},{2,1},{4,3},{6,5},{... | collective-permute-start | bytes 196616 | tf_op jit(solution)/shard_map/ppermute | solution.py:45
  13.6 1.9 %collective-permute-start.6 = (f32[4,1,8,1024]{3,2,1,0:T(8,128)S(1)}, f32[4,1,8,1024]{3,2,1,0:T(8,128)S(1)}, u32[]{:S(2)}, u32[]{:S(2)}) collective-permute-start(f32[4,1,8,1024]{3,2,1,0:T(8,128)S(1)} %get-tuple-element.19), channel_id=1, source_target_pairs={{0,16},{16,32},{32,48},{48,64},{64,80},{80,96},{96,112},{112,128},... | collective-permute-start | bytes 393224 | tf_op jit(solution)/shard_map/ppermute | solution.py:22
  15.6 0.3 reduce_window_sum.23
  16.0 0.0 collective-permute-done.7
  16.0 0.0 collective-permute-done.1
  16.0 0.1 select_bitcast_fusion
  16.1 8.3 %collective-permute-start.2 = (f32[4,4,1024]{2,1,0:T(4,128)S(1)}, f32[4,4,1024]{2,1,0:T(4,128)S(1)}, u32[]{:S(2)}, u32[]{:S(2)}) collective-permute-start(f32[4,4,1024]{2,1,0:T(4,128)S(1)} %pad_maximum_fusion.7), channel_id=1, source_target_pairs={{0,2},{1,3},{2,0},{3,1},{4,6},{5,7},{6,4},{7,5},{8,10},{9,11},{10,... | collective-permute-start | bytes 196616 | tf_op jit(solution)/shard_map/ppermute | solution.py:64
  24.6 2.1 %collective-permute-done.2 = f32[4,4,1024]{2,1,0:T(4,128)S(1)} collective-permute-done((f32[4,4,1024]{2,1,0:T(4,128)S(1)}, f32[4,4,1024]{2,1,0:T(4,128)S(1)}, u32[]{:S(2)}, u32[]{:S(2)}) %collective-permute-start.2) | collective-permute-done | bytes 65568 | tf_op jit(solution)/shard_map/ppermute | solution.py:64
  26.8 13.1 %collective-permute-start.3 = (f32[4,4,1024]{2,1,0:T(4,128)S(1)}, f32[4,4,1024]{2,1,0:T(4,128)S(1)}, u32[]{:S(2)}, u32[]{:S(2)}) collective-permute-start(f32[4,4,1024]{2,1,0:T(4,128)S(1)} %pad_maximum_fusion.8), channel_id=1, source_target_pairs={{0,7},{1,6},{2,5},{3,4},{4,3},{5,2},{6,1},{7,0},{8,15},{9,14},{10,... | collective-permute-start | bytes 196616 | tf_op jit(solution)/shard_map/ppermute | solution.py:64
  40.0 2.1 %collective-permute-done.3 = f32[4,4,1024]{2,1,0:T(4,128)S(1)} collective-permute-done((f32[4,4,1024]{2,1,0:T(4,128)S(1)}, f32[4,4,1024]{2,1,0:T(4,128)S(1)}, u32[]{:S(2)}, u32[]{:S(2)}) %collective-permute-start.3) | collective-permute-done | bytes 65568 | tf_op jit(solution)/shard_map/ppermute | solution.py:64
  42.2 6.2 %collective-permute-start.4 = (f32[4,4,1024]{2,1,0:T(4,128)S(1)}, f32[4,4,1024]{2,1,0:T(4,128)S(1)}, u32[]{:S(2)}, u32[]{:S(2)}) collective-permute-start(f32[4,4,1024]{2,1,0:T(4,128)S(1)} %pad_maximum_fusion.9), channel_id=1, source_target_pairs={{0,15},{1,14},{2,13},{3,12},{4,11},{5,10},{6,9},{7,8},{8,7},{9,6},... | collective-permute-start | bytes 196616 | tf_op jit(solution)/shard_map/ppermute | solution.py:64
  48.5 4.0 %collective-permute-done.4 = f32[4,4,1024]{2,1,0:T(4,128)S(1)} collective-permute-done((f32[4,4,1024]{2,1,0:T(4,128)S(1)}, f32[4,4,1024]{2,1,0:T(4,128)S(1)}, u32[]{:S(2)}, u32[]{:S(2)}) %collective-permute-start.4) | collective-permute-done | bytes 65568 | tf_op jit(solution)/shard_map/ppermute | solution.py:64
  52.7 0.1 multiply_bitcast_fusion.1
  52.8 0.0 copy-start.3
  52.8 0.7 %copy-done.3 = f32[3,4,1024]{2,1,0:T(4,128)S(1)} copy-done((f32[3,4,1024]{2,1,0:T(4,128)S(1)}, f32[3,4,1024]{2,1,0:T(4,128)}, u32[]{:S(2)}) %copy-start.3) | copy-done | bytes 49176
  53.6 0.2 multiply_reduce_fusion
  53.8 0.1 fusion.18
  53.9 0.1 fusion.10
  54.0 1.9 %collective-permute-start.5 = (f32[4,1,8,1024]{3,2,1,0:T(8,128)S(1)}, f32[4,1,8,1024]{3,2,1,0:T(8,128)S(1)}, u32[]{:S(2)}, u32[]{:S(2)}) collective-permute-start(f32[4,1,8,1024]{3,2,1,0:T(8,128)S(1)} %slice.273), channel_id=1, source_target_pairs={{0,16},{16,32},{32,48},{48,64},{64,80},{80,96},{96,112},{112,128},... | collective-permute-start | bytes 393224 | tf_op jit(solution)/shard_map/ppermute | solution.py:34
  55.9 0.1 fusion.37
  56.0 0.0 copy-start.1
  56.0 0.0 copy-start.2
  56.0 0.1 copy.18
  56.1 0.1 copy.17
  56.2 0.0 collective-permute-done.6
  56.2 6.1 %collective-permute-done.5 = f32[4,1,8,1024]{3,2,1,0:T(8,128)S(1)} collective-permute-done((f32[4,1,8,1024]{3,2,1,0:T(8,128)S(1)}, f32[4,1,8,1024]{3,2,1,0:T(8,128)S(1)}, u32[]{:S(2)}, u32[]{:S(2)}) %collective-permute-start.5) | collective-permute-done | bytes 131104 | tf_op jit(solution)/shard_map/ppermute | solution.py:34
  62.3 0.0 copy-done.1
  62.4 0.0 copy-done.2
  62.4 1.9 %divide_subtract_fusion = (f32[4,4,8,1024]{3,2,1,0:T(8,128)}, f32[4,4,8,1024]{3,2,1,0:T(8,128)}, f32[4,4,8,1024]{3,2,1,0:T(8,128)}) fusion(f32[4,4,8,1024]{3,2,1,0:T(8,128)S(1)} %copy-done, f32[4,4,8,1024]{3,2,1,0:T(8,128)S(1)} %copy-done.1, f32[4,4,8,1024]{3,2,1,0:T(8,128)S(1)} %copy-done.2, f32[4,4,7,1024]{3,2,1,0:T(8,128)S(1)} %get-tuple-element.14, ...), kind=kLoop, calls=%fused_computation.18 | loop fusion | flops 3801088 | bytes 5521408 | tf_op jit(solution)/shard_map/sub | solution.py:137
  (35 shorter events, 0.7 us)
Async XLA Ops:
  0.6 5.4 %copy-start = (f32[4,4,8,1024]{3,2,1,0:T(8,128)S(1)}, f32[4,4,8,1024]{3,2,1,0:T(8,128)}, u32[]{:S(2)}) copy-start(f32[4,4,8,1024]{3,2,1,0:T(8,128)} %param.6) | copy-start | bytes 1572868
  1.7 6.8 %collective-permute-start = (f32[4,1,8,1024]{3,2,1,0:T(8,128)S(1)}, f32[4,1,8,1024]{3,2,1,0:T(8,128)S(1)}, u32[]{:S(2)}, u32[]{:S(2)}) collective-permute-start(f32[4,1,8,1024]{3,2,1,0:T(8,128)S(1)} %get-tuple-element.18), channel_id=1, source_target_pairs={{16,0},{32,16},{48,32},{64,48},{80,64},{96,80},{112,96},{128,112},... | collective-permute-start | bytes 393224 | tf_op jit(solution)/shard_map/ppermute | solution.py:24
  6.1 0.7 %copy-start.5 = (s32[1,1,128]{2,1,0:T(1,128)S(1)}, s32[1,1,128]{2,1,0:T(1,128)}, u32[]{:S(2)}) copy-start(s32[1,1,128]{2,1,0:T(1,128)} %param.10) | copy-start | bytes 1540
  6.9 0.7 %copy-start.4 = (s32[4,1024]{1,0:T(4,128)S(1)}, s32[4,1024]{1,0:T(4,128)}, u32[]{:S(2)}) copy-start(s32[4,1024]{1,0:T(4,128)} %param.9) | copy-start | bytes 49156
  9.1 6.9 %collective-permute-start.1 = (f32[8,4,1024]{2,1,0:T(4,128)S(1)}, f32[8,4,1024]{2,1,0:T(4,128)S(1)}, u32[]{:S(2)}, u32[]{:S(2)}) collective-permute-start(f32[8,4,1024]{2,1,0:T(4,128)S(1)} %pad_maximum_fusion.3), channel_id=1, source_target_pairs={{0,1},{1,0},{2,3},{3,2},{4,5},{5,4},{6,7},{7,6},{8,9},{9,8},{10,11... | collective-permute-start | bytes 393224 | tf_op jit(solution)/shard_map/ppermute | solution.py:61
  13.0 3.0 %collective-permute-start.7 = (f32[4,4,1024]{2,1,0:T(4,128)S(1)}, f32[4,4,1024]{2,1,0:T(4,128)S(1)}, u32[]{:S(2)}, u32[]{:S(2)}) collective-permute-start(f32[4,4,1024]{2,1,0:T(4,128)S(1)} %get-tuple-element.30), channel_id=1, source_target_pairs={{1,2},{3,4},{5,6},{7,8},{9,10},{11,12},{13,14},{2,1},{4,3},{6,5},{... | collective-permute-start | bytes 196616 | tf_op jit(solution)/shard_map/ppermute | solution.py:45
  13.6 42.6 %collective-permute-start.6 = (f32[4,1,8,1024]{3,2,1,0:T(8,128)S(1)}, f32[4,1,8,1024]{3,2,1,0:T(8,128)S(1)}, u32[]{:S(2)}, u32[]{:S(2)}) collective-permute-start(f32[4,1,8,1024]{3,2,1,0:T(8,128)S(1)} %get-tuple-element.19), channel_id=1, source_target_pairs={{0,16},{16,32},{32,48},{48,64},{64,80},{80,96},{96,112},{112,128},... | collective-permute-start | bytes 393224 | tf_op jit(solution)/shard_map/ppermute | solution.py:22
  16.1 10.6 %collective-permute-start.2 = (f32[4,4,1024]{2,1,0:T(4,128)S(1)}, f32[4,4,1024]{2,1,0:T(4,128)S(1)}, u32[]{:S(2)}, u32[]{:S(2)}) collective-permute-start(f32[4,4,1024]{2,1,0:T(4,128)S(1)} %pad_maximum_fusion.7), channel_id=1, source_target_pairs={{0,2},{1,3},{2,0},{3,1},{4,6},{5,7},{6,4},{7,5},{8,10},{9,11},{10,... | collective-permute-start | bytes 196616 | tf_op jit(solution)/shard_map/ppermute | solution.py:64
  26.8 15.4 %collective-permute-start.3 = (f32[4,4,1024]{2,1,0:T(4,128)S(1)}, f32[4,4,1024]{2,1,0:T(4,128)S(1)}, u32[]{:S(2)}, u32[]{:S(2)}) collective-permute-start(f32[4,4,1024]{2,1,0:T(4,128)S(1)} %pad_maximum_fusion.8), channel_id=1, source_target_pairs={{0,7},{1,6},{2,5},{3,4},{4,3},{5,2},{6,1},{7,0},{8,15},{9,14},{10,... | collective-permute-start | bytes 196616 | tf_op jit(solution)/shard_map/ppermute | solution.py:64
  42.2 10.3 %collective-permute-start.4 = (f32[4,4,1024]{2,1,0:T(4,128)S(1)}, f32[4,4,1024]{2,1,0:T(4,128)S(1)}, u32[]{:S(2)}, u32[]{:S(2)}) collective-permute-start(f32[4,4,1024]{2,1,0:T(4,128)S(1)} %pad_maximum_fusion.9), channel_id=1, source_target_pairs={{0,15},{1,14},{2,13},{3,12},{4,11},{5,10},{6,9},{7,8},{8,7},{9,6},... | collective-permute-start | bytes 196616 | tf_op jit(solution)/shard_map/ppermute | solution.py:64
  52.8 0.8 %copy-start.3 = (f32[3,4,1024]{2,1,0:T(4,128)S(1)}, f32[3,4,1024]{2,1,0:T(4,128)}, u32[]{:S(2)}) copy-start(f32[3,4,1024]{2,1,0:T(4,128)} %param.11) | copy-start | bytes 147460
  54.0 8.4 %collective-permute-start.5 = (f32[4,1,8,1024]{3,2,1,0:T(8,128)S(1)}, f32[4,1,8,1024]{3,2,1,0:T(8,128)S(1)}, u32[]{:S(2)}, u32[]{:S(2)}) collective-permute-start(f32[4,1,8,1024]{3,2,1,0:T(8,128)S(1)} %slice.273), channel_id=1, source_target_pairs={{0,16},{16,32},{32,48},{48,64},{64,80},{80,96},{96,112},{112,128},... | collective-permute-start | bytes 393224 | tf_op jit(solution)/shard_map/ppermute | solution.py:34
  56.0 6.4 %copy-start.1 = (f32[4,4,8,1024]{3,2,1,0:T(8,128)S(1)}, f32[4,4,8,1024]{3,2,1,0:T(8,128)}, u32[]{:S(2)}) copy-start(f32[4,4,8,1024]{3,2,1,0:T(8,128)} %param.7) | copy-start | bytes 1572868
  56.0 6.3 %copy-start.2 = (f32[4,4,8,1024]{3,2,1,0:T(8,128)S(1)}, f32[4,4,8,1024]{3,2,1,0:T(8,128)}, u32[]{:S(2)}) copy-start(f32[4,4,8,1024]{3,2,1,0:T(8,128)} %param.8) | copy-start | bytes 1572868

commit v15 on v12

--- a/solution.py
+++ b/solution.py
@@ -80,12 +80,13 @@
     weighted = weight[None] * colour
     seg_colour = jnp.sum(weighted, axis=2)
     seg_trans = jnp.exp(-jnp.sum(sigma, axis=1))
+    scaled_target, seg_colour = lax.optimization_barrier((0.5 * total_depth * target, seg_colour))
     front_colour, front_trans, back_colour, back_trans, plane_in = butterfly_scan(
         seg_colour, seg_trans, "depth", plane_out
     )
     behind = back_colour + back_trans[None]
     pixel = front_colour + front_trans[None] * (seg_colour + seg_trans[None] * behind)
-    pixel_grad = 0.5 * total_depth * (pixel - target)
+    pixel_grad = 0.5 * total_depth * pixel - scaled_target
     upto = jnp.cumsum(weighted, axis=2)
     remain = seg_colour[:, :, None, :] - upto + (seg_trans[None] * behind)[:, :, None, :]
     next_trans = trans * fade

time: 64.5 us -> 63.7 us (0.988)
  local copies, waits for them, and re-layouts: 3.68 us -> 2.95 us
    unnamed x12, local copies, waits for them, and re-layouts: 2.08 us -> 1.36 us
where the time goes in v15:
time: 63.7 us; the launch traced here: 63.3 us
  starting transfers between devices  41.9 us (66%)
  waiting for transfers between devices  13.3 us (21%)
  other arithmetic  4.01 us (6%)
  local copies, waits for them, and re-layouts  2.95 us (5%)
  between operations  1.18 us (2%)
    ppermute x3, starting transfers between devices, butterfly_scan(): other = lax.ppermute(block, axis, route)  29.3 us
    ppermute x3, waiting for transfers between devices, butterfly_scan(): other = lax.ppermute(block, axis, route)  6.33 us
    ppermute x1, waiting for transfers between devices, passed_along(): return lax.ppermute(block, axis, route)  6.13 us
    ppermute x1, starting transfers between devices, with_halo(): lax.ppermute(head, axis, [((i + 1) % count, i) for i in range(ends)])  4.29 us
    ppermute x1, starting transfers between devices, butterfly_scan(): lax.ppermute(jnp.concatenate([block, plane_out], axis=0), axis, route)  3.83 us
    sub x1, other arithmetic, body(): grid - learn_rate * (new_first / corr_one) / (jnp.sqrt(new_second / corr_...  1.94 us
    ppermute x1, starting transfers between devices, with_halo(): lax.ppermute(tail, axis, [(i, (i + 1) % count) for i in range(ends)])  1.92 us
    ppermute x1, starting transfers between devices, passed_along(): return lax.ppermute(block, axis, route)  1.92 us
  transfers between devices with their start and end apart: 8, of which 5 were waited for; matrix products, arithmetic and copies ran while one was open for 3% of the time, Pallas kernels for 0%

profile of v15, /device:TPU:24, one launch (start us, length us, event | category | flops | bytes accessed | tf_op | source)
XLA Modules:
  0.0 63.3 jit_solution(258316927999753504)
XLA Ops:
  0.6 0.0 copy-start
  0.6 1.0 %fusion.39 = (f32[4,1,8,1024]{3,2,1,0:T(8,128)S(1)}, f32[4,1,8,1024]{3,2,1,0:T(8,128)S(1)}) fusion(f32[4,4,8,1024]{3,2,1,0:T(8,128)} %param.6), kind=kLoop, calls=%fused_computation.123 | loop fusion | bytes 524288 | tf_op jit(solution)/shard_map/slice | solution.py:18
  1.7 4.3 %collective-permute-start = (f32[4,1,8,1024]{3,2,1,0:T(8,128)S(1)}, f32[4,1,8,1024]{3,2,1,0:T(8,128)S(1)}, u32[]{:S(2)}, u32[]{:S(2)}) collective-permute-start(f32[4,1,8,1024]{3,2,1,0:T(8,128)S(1)} %get-tuple-element.22), channel_id=1, source_target_pairs={{16,0},{32,16},{48,32},{64,48},{80,64},{96,80},{112,96},{128,112},... | collective-permute-start | bytes 393224 | tf_op jit(solution)/shard_map/ppermute | solution.py:24
  6.0 0.0 copy-done
  6.0 0.0 copy-start.3
  6.0 0.1 fusion.38
  6.1 0.0 copy-start.5
  6.1 0.6 %copy-done.5 = s32[1,1,128]{2,1,0:T(1,128)S(1)} copy-done((s32[1,1,128]{2,1,0:T(1,128)S(1)}, s32[1,1,128]{2,1,0:T(1,128)}, u32[]{:S(2)}) %copy-start.5) | copy-done | bytes 536
  6.8 0.0 copy-done.3
  6.8 0.1 broadcast_in_dim.10
  6.9 0.1 broadcast_in_dim.11
  7.0 0.0 copy-start.4
  7.1 0.7 %copy-done.4 = s32[4,1024]{1,0:T(4,128)S(1)} copy-done((s32[4,1024]{1,0:T(4,128)S(1)}, s32[4,1024]{1,0:T(4,128)}, u32[]{:S(2)}) %copy-start.4) | copy-done | bytes 16408
  7.7 0.8 %collective-permute-done = f32[4,1,8,1024]{3,2,1,0:T(8,128)S(1)} collective-permute-done((f32[4,1,8,1024]{3,2,1,0:T(8,128)S(1)}, f32[4,1,8,1024]{3,2,1,0:T(8,128)S(1)}, u32[]{:S(2)}, u32[]{:S(2)}) %collective-permute-start) | collective-permute-done | bytes 131104 | tf_op jit(solution)/shard_map/ppermute | solution.py:24
  8.5 0.1 fusion.9
  8.6 0.1 fusion.35
  8.7 0.1 reduce_window_sum.22
  8.8 0.1 fusion.30
  8.9 0.2 fusion.34
  9.1 3.8 %collective-permute-start.1 = (f32[8,4,1024]{2,1,0:T(4,128)S(1)}, f32[8,4,1024]{2,1,0:T(4,128)S(1)}, u32[]{:S(2)}, u32[]{:S(2)}) collective-permute-start(f32[8,4,1024]{2,1,0:T(4,128)S(1)} %pad_maximum_fusion.3), channel_id=1, source_target_pairs={{0,1},{1,0},{2,3},{3,2},{4,5},{5,4},{6,7},{7,6},{8,9},{9,8},{10,11... | collective-permute-start | bytes 393224 | tf_op jit(solution)/shard_map/ppermute | solution.py:58
  13.0 0.7 %collective-permute-start.7 = (f32[4,4,1024]{2,1,0:T(4,128)S(1)}, f32[4,4,1024]{2,1,0:T(4,128)S(1)}, u32[]{:S(2)}, u32[]{:S(2)}) collective-permute-start(f32[4,4,1024]{2,1,0:T(4,128)S(1)} %get-tuple-element.34), channel_id=1, source_target_pairs={{1,2},{3,4},{5,6},{7,8},{9,10},{11,12},{13,14},{2,1},{4,3},{6,5},{... | collective-permute-start | bytes 196616 | tf_op jit(solution)/shard_map/ppermute | solution.py:45
  13.6 1.9 %collective-permute-start.6 = (f32[4,1,8,1024]{3,2,1,0:T(8,128)S(1)}, f32[4,1,8,1024]{3,2,1,0:T(8,128)S(1)}, u32[]{:S(2)}, u32[]{:S(2)}) collective-permute-start(f32[4,1,8,1024]{3,2,1,0:T(8,128)S(1)} %get-tuple-element.23), channel_id=1, source_target_pairs={{0,16},{16,32},{32,48},{48,64},{64,80},{80,96},{96,112},{112,128},... | collective-permute-start | bytes 393224 | tf_op jit(solution)/shard_map/ppermute | solution.py:22
  15.6 0.3 reduce_window_sum.23
  16.0 0.0 collective-permute-done.7
  16.0 0.0 collective-permute-done.1
  16.0 0.1 select_bitcast_fusion
  16.1 10.9 %collective-permute-start.2 = (f32[4,4,1024]{2,1,0:T(4,128)S(1)}, f32[4,4,1024]{2,1,0:T(4,128)S(1)}, u32[]{:S(2)}, u32[]{:S(2)}) collective-permute-start(f32[4,4,1024]{2,1,0:T(4,128)S(1)} %pad_maximum_fusion.7), channel_id=1, source_target_pairs={{0,3},{1,2},{2,1},{3,0},{4,7},{5,6},{6,5},{7,4},{8,11},{9,10},{10,... | collective-permute-start | bytes 196616 | tf_op jit(solution)/shard_map/ppermute | solution.py:61
  27.1 2.1 %collective-permute-done.2 = f32[4,4,1024]{2,1,0:T(4,128)S(1)} collective-permute-done((f32[4,4,1024]{2,1,0:T(4,128)S(1)}, f32[4,4,1024]{2,1,0:T(4,128)S(1)}, u32[]{:S(2)}, u32[]{:S(2)}) %collective-permute-start.2) | collective-permute-done | bytes 65568 | tf_op jit(solution)/shard_map/ppermute | solution.py:61
  29.4 11.4 %collective-permute-start.3 = (f32[4,4,1024]{2,1,0:T(4,128)S(1)}, f32[4,4,1024]{2,1,0:T(4,128)S(1)}, u32[]{:S(2)}, u32[]{:S(2)}) collective-permute-start(f32[4,4,1024]{2,1,0:T(4,128)S(1)} %pad_maximum_fusion.8), channel_id=1, source_target_pairs={{0,7},{1,6},{2,5},{3,4},{4,3},{5,2},{6,1},{7,0},{8,15},{9,14},{10,... | collective-permute-start | bytes 196616 | tf_op jit(solution)/shard_map/ppermute | solution.py:61
  40.9 2.1 %collective-permute-done.3 = f32[4,4,1024]{2,1,0:T(4,128)S(1)} collective-permute-done((f32[4,4,1024]{2,1,0:T(4,128)S(1)}, f32[4,4,1024]{2,1,0:T(4,128)S(1)}, u32[]{:S(2)}, u32[]{:S(2)}) %collective-permute-start.3) | collective-permute-done | bytes 65568 | tf_op jit(solution)/shard_map/ppermute | solution.py:61
  43.1 7.0 %collective-permute-start.4 = (f32[4,4,1024]{2,1,0:T(4,128)S(1)}, f32[4,4,1024]{2,1,0:T(4,128)S(1)}, u32[]{:S(2)}, u32[]{:S(2)}) collective-permute-start(f32[4,4,1024]{2,1,0:T(4,128)S(1)} %pad_maximum_fusion.9), channel_id=1, source_target_pairs={{0,15},{1,14},{2,13},{3,12},{4,11},{5,10},{6,9},{7,8},{8,7},{9,6},... | collective-permute-start | bytes 196616 | tf_op jit(solution)/shard_map/ppermute | solution.py:61
  50.2 2.1 %collective-permute-done.4 = f32[4,4,1024]{2,1,0:T(4,128)S(1)} collective-permute-done((f32[4,4,1024]{2,1,0:T(4,128)S(1)}, f32[4,4,1024]{2,1,0:T(4,128)S(1)}, u32[]{:S(2)}, u32[]{:S(2)}) %collective-permute-start.4) | collective-permute-done | bytes 65568 | tf_op jit(solution)/shard_map/ppermute | solution.py:61
  52.4 0.1 multiply_bitcast_fusion.1
  52.6 0.2 multiply_reduce_fusion
  52.8 0.1 fusion.18
  52.9 0.1 fusion.10
  53.0 1.9 %collective-permute-start.5 = (f32[4,1,8,1024]{3,2,1,0:T(8,128)S(1)}, f32[4,1,8,1024]{3,2,1,0:T(8,128)S(1)}, u32[]{:S(2)}, u32[]{:S(2)}) collective-permute-start(f32[4,1,8,1024]{3,2,1,0:T(8,128)S(1)} %slice.273), channel_id=1, source_target_pairs={{0,16},{16,32},{32,48},{48,64},{64,80},{80,96},{96,112},{112,128},... | collective-permute-start | bytes 393224 | tf_op jit(solution)/shard_map/ppermute | solution.py:34
  54.9 0.1 fusion.37
  55.0 0.0 copy-start.1
  55.0 0.0 copy-start.2
  55.0 0.1 copy.18
  55.1 0.1 copy.17
  55.2 0.0 collective-permute-done.6
  55.2 6.1 %collective-permute-done.5 = f32[4,1,8,1024]{3,2,1,0:T(8,128)S(1)} collective-permute-done((f32[4,1,8,1024]{3,2,1,0:T(8,128)S(1)}, f32[4,1,8,1024]{3,2,1,0:T(8,128)S(1)}, u32[]{:S(2)}, u32[]{:S(2)}) %collective-permute-start.5) | collective-permute-done | bytes 131104 | tf_op jit(solution)/shard_map/ppermute | solution.py:34
  61.4 0.0 copy-done.1
  61.4 0.0 copy-done.2
  61.4 1.9 %divide_subtract_fusion = (f32[4,4,8,1024]{3,2,1,0:T(8,128)}, f32[4,4,8,1024]{3,2,1,0:T(8,128)}, f32[4,4,8,1024]{3,2,1,0:T(8,128)}) fusion(f32[4,4,8,1024]{3,2,1,0:T(8,128)S(1)} %copy-done, f32[4,4,8,1024]{3,2,1,0:T(8,128)S(1)} %copy-done.1, f32[4,4,8,1024]{3,2,1,0:T(8,128)S(1)} %copy-done.2, f32[4,4,7,1024]{3,2,1,0:T(8,128)S(1)} %get-tuple-element.18, ...), kind=kLoop, calls=%fused_computation.18 | loop fusion | flops 3801088 | bytes 5521408 | tf_op jit(solution)/shard_map/sub | solution.py:135
  (36 shorter events, 0.8 us)
Async XLA Ops:
  0.6 5.4 %copy-start = (f32[4,4,8,1024]{3,2,1,0:T(8,128)S(1)}, f32[4,4,8,1024]{3,2,1,0:T(8,128)}, u32[]{:S(2)}) copy-start(f32[4,4,8,1024]{3,2,1,0:T(8,128)} %param.6) | copy-start | bytes 1572868
  1.7 6.8 %collective-permute-start = (f32[4,1,8,1024]{3,2,1,0:T(8,128)S(1)}, f32[4,1,8,1024]{3,2,1,0:T(8,128)S(1)}, u32[]{:S(2)}, u32[]{:S(2)}) collective-permute-start(f32[4,1,8,1024]{3,2,1,0:T(8,128)S(1)} %get-tuple-element.22), channel_id=1, source_target_pairs={{16,0},{32,16},{48,32},{64,48},{80,64},{96,80},{112,96},{128,112},... | collective-permute-start | bytes 393224 | tf_op jit(solution)/shard_map/ppermute | solution.py:24
  6.0 0.8 %copy-start.3 = (f32[3,4,1024]{2,1,0:T(4,128)S(1)}, f32[3,4,1024]{2,1,0:T(4,128)}, u32[]{:S(2)}) copy-start(f32[3,4,1024]{2,1,0:T(4,128)} %param.11) | copy-start | bytes 147460
  6.1 0.7 %copy-start.5 = (s32[1,1,128]{2,1,0:T(1,128)S(1)}, s32[1,1,128]{2,1,0:T(1,128)}, u32[]{:S(2)}) copy-start(s32[1,1,128]{2,1,0:T(1,128)} %param.10) | copy-start | bytes 1540
  7.0 0.7 %copy-start.4 = (s32[4,1024]{1,0:T(4,128)S(1)}, s32[4,1024]{1,0:T(4,128)}, u32[]{:S(2)}) copy-start(s32[4,1024]{1,0:T(4,128)} %param.9) | copy-start | bytes 49156
  9.1 6.9 %collective-permute-start.1 = (f32[8,4,1024]{2,1,0:T(4,128)S(1)}, f32[8,4,1024]{2,1,0:T(4,128)S(1)}, u32[]{:S(2)}, u32[]{:S(2)}) collective-permute-start(f32[8,4,1024]{2,1,0:T(4,128)S(1)} %pad_maximum_fusion.3), channel_id=1, source_target_pairs={{0,1},{1,0},{2,3},{3,2},{4,5},{5,4},{6,7},{7,6},{8,9},{9,8},{10,11... | collective-permute-start | bytes 393224 | tf_op jit(solution)/shard_map/ppermute | solution.py:58
  13.0 3.0 %collective-permute-start.7 = (f32[4,4,1024]{2,1,0:T(4,128)S(1)}, f32[4,4,1024]{2,1,0:T(4,128)S(1)}, u32[]{:S(2)}, u32[]{:S(2)}) collective-permute-start(f32[4,4,1024]{2,1,0:T(4,128)S(1)} %get-tuple-element.34), channel_id=1, source_target_pairs={{1,2},{3,4},{5,6},{7,8},{9,10},{11,12},{13,14},{2,1},{4,3},{6,5},{... | collective-permute-start | bytes 196616 | tf_op jit(solution)/shard_map/ppermute | solution.py:45
  13.6 41.6 %collective-permute-start.6 = (f32[4,1,8,1024]{3,2,1,0:T(8,128)S(1)}, f32[4,1,8,1024]{3,2,1,0:T(8,128)S(1)}, u32[]{:S(2)}, u32[]{:S(2)}) collective-permute-start(f32[4,1,8,1024]{3,2,1,0:T(8,128)S(1)} %get-tuple-element.23), channel_id=1, source_target_pairs={{0,16},{16,32},{32,48},{48,64},{64,80},{80,96},{96,112},{112,128},... | collective-permute-start | bytes 393224 | tf_op jit(solution)/shard_map/ppermute | solution.py:22
  16.1 13.1 %collective-permute-start.2 = (f32[4,4,1024]{2,1,0:T(4,128)S(1)}, f32[4,4,1024]{2,1,0:T(4,128)S(1)}, u32[]{:S(2)}, u32[]{:S(2)}) collective-permute-start(f32[4,4,1024]{2,1,0:T(4,128)S(1)} %pad_maximum_fusion.7), channel_id=1, source_target_pairs={{0,3},{1,2},{2,1},{3,0},{4,7},{5,6},{6,5},{7,4},{8,11},{9,10},{10,... | collective-permute-start | bytes 196616 | tf_op jit(solution)/shard_map/ppermute | solution.py:61
  29.4 13.7 %collective-permute-start.3 = (f32[4,4,1024]{2,1,0:T(4,128)S(1)}, f32[4,4,1024]{2,1,0:T(4,128)S(1)}, u32[]{:S(2)}, u32[]{:S(2)}) collective-permute-start(f32[4,4,1024]{2,1,0:T(4,128)S(1)} %pad_maximum_fusion.8), channel_id=1, source_target_pairs={{0,7},{1,6},{2,5},{3,4},{4,3},{5,2},{6,1},{7,0},{8,15},{9,14},{10,... | collective-permute-start | bytes 196616 | tf_op jit(solution)/shard_map/ppermute | solution.py:61
  43.1 9.2 %collective-permute-start.4 = (f32[4,4,1024]{2,1,0:T(4,128)S(1)}, f32[4,4,1024]{2,1,0:T(4,128)S(1)}, u32[]{:S(2)}, u32[]{:S(2)}) collective-permute-start(f32[4,4,1024]{2,1,0:T(4,128)S(1)} %pad_maximum_fusion.9), channel_id=1, source_target_pairs={{0,15},{1,14},{2,13},{3,12},{4,11},{5,10},{6,9},{7,8},{8,7},{9,6},... | collective-permute-start | bytes 196616 | tf_op jit(solution)/shard_map/ppermute | solution.py:61
  53.0 8.4 %collective-permute-start.5 = (f32[4,1,8,1024]{3,2,1,0:T(8,128)S(1)}, f32[4,1,8,1024]{3,2,1,0:T(8,128)S(1)}, u32[]{:S(2)}, u32[]{:S(2)}) collective-permute-start(f32[4,1,8,1024]{3,2,1,0:T(8,128)S(1)} %slice.273), channel_id=1, source_target_pairs={{0,16},{16,32},{32,48},{48,64},{64,80},{80,96},{96,112},{112,128},... | collective-permute-start | bytes 393224 | tf_op jit(solution)/shard_map/ppermute | solution.py:34
  55.0 6.4 %copy-start.1 = (f32[4,4,8,1024]{3,2,1,0:T(8,128)S(1)}, f32[4,4,8,1024]{3,2,1,0:T(8,128)}, u32[]{:S(2)}) copy-start(f32[4,4,8,1024]{3,2,1,0:T(8,128)} %param.7) | copy-start | bytes 1572868
  55.0 6.3 %copy-start.2 = (f32[4,4,8,1024]{3,2,1,0:T(8,128)S(1)}, f32[4,4,8,1024]{3,2,1,0:T(8,128)}, u32[]{:S(2)}) copy-start(f32[4,4,8,1024]{3,2,1,0:T(8,128)} %param.8) | copy-start | bytes 1572868

commit v16 on v15

--- a/solution.py
+++ b/solution.py
@@ -107,7 +107,11 @@
     depth_count = lax.axis_size("depth")
     planes = grid.shape[2]
     total_depth = planes * depth_count
-    padded = with_halo(grid, (("tile", 1),), 1)
+    tiles = lax.axis_size("tile")
+    row_after = lax.ppermute(grid[:, :1], "tile", [(i + 1, i) for i in range(tiles - 1)])
+    last_row, row_after = lax.optimization_barrier((grid[:, -1:], row_after))
+    row_before = lax.ppermute(last_row, "tile", [(i, i + 1) for i in range(tiles - 1)])
+    padded = jnp.concatenate([row_before, grid, row_after], axis=1)
     odd = lax.axis_index("depth") % 2 == 1
     swapped = depth_swap(grid, "depth")
     shares = (ray_offset.astype(jnp.float32) * 0.5)[None, :, None, :]

time: 63.7 us -> 63.7 us (level)
  no operation moved by 1% of the time
where the time goes in v16:
time: 63.7 us; the launch traced here: 63.3 us
  starting transfers between devices  41.9 us (66%)
  waiting for transfers between devices  13.2 us (21%)
  other arithmetic  4.01 us (6%)
  local copies, waits for them, and re-layouts  2.95 us (5%)
  between operations  1.18 us (2%)
    ppermute x3, starting transfers between devices, butterfly_scan(): other = lax.ppermute(block, axis, route)  29.3 us
    ppermute x3, waiting for transfers between devices, butterfly_scan(): other = lax.ppermute(block, axis, route)  6.33 us
    ppermute x1, waiting for transfers between devices, passed_along(): return lax.ppermute(block, axis, route)  6.13 us
    ppermute x1, starting transfers between devices, body(): lax.ppermute(grid[:, :1], 'tile', [(i + 1, i) for i in range(tiles - 1)])  4.29 us
    ppermute x1, starting transfers between devices, butterfly_scan(): lax.ppermute(jnp.concatenate([block, plane_out], axis=0), axis, route)  3.83 us
    sub x1, other arithmetic, body(): grid - learn_rate * (new_first / corr_one) / (jnp.sqrt(new_second / corr_...  1.94 us
    ppermute x1, starting transfers between devices, body(): lax.ppermute(last_row, 'tile', [(i, i + 1) for i in range(tiles - 1)])  1.92 us
    ppermute x1, starting transfers between devices, passed_along(): return lax.ppermute(block, axis, route)  1.92 us
  transfers between devices with their start and end apart: 8, of which 5 were waited for; matrix products, arithmetic and copies ran while one was open for 3% of the time, Pallas kernels for 0%

profile of v16, /device:TPU:24, one launch (start us, length us, event | category | flops | bytes accessed | tf_op | source)
XLA Modules:
  0.0 63.3 jit_solution(12027178950551532922)
XLA Ops:
  0.6 0.0 copy-start
  0.6 1.0 %fusion.39 = (f32[4,1,8,1024]{3,2,1,0:T(8,128)S(1)}, f32[4,1,8,1024]{3,2,1,0:T(8,128)S(1)}) fusion(f32[4,4,8,1024]{3,2,1,0:T(8,128)} %param.6), kind=kLoop, calls=%fused_computation.123 | loop fusion | bytes 524288 | tf_op jit(solution)/shard_map/slice | solution.py:111
  1.7 4.3 %collective-permute-start = (f32[4,1,8,1024]{3,2,1,0:T(8,128)S(1)}, f32[4,1,8,1024]{3,2,1,0:T(8,128)S(1)}, u32[]{:S(2)}, u32[]{:S(2)}) collective-permute-start(f32[4,1,8,1024]{3,2,1,0:T(8,128)S(1)} %get-tuple-element.26), channel_id=1, source_target_pairs={{16,0},{32,16},{48,32},{64,48},{80,64},{96,80},{112,96},{128,112},... | collective-permute-start | bytes 393224 | tf_op jit(solution)/shard_map/ppermute | solution.py:111
  6.0 0.0 copy-done
  6.0 0.0 copy-start.3
  6.0 0.1 fusion.38
  6.1 0.0 copy-start.5
  6.1 0.6 %copy-done.5 = s32[1,1,128]{2,1,0:T(1,128)S(1)} copy-done((s32[1,1,128]{2,1,0:T(1,128)S(1)}, s32[1,1,128]{2,1,0:T(1,128)}, u32[]{:S(2)}) %copy-start.5) | copy-done | bytes 536
  6.8 0.0 copy-done.3
  6.8 0.1 broadcast_in_dim.10
  6.9 0.1 broadcast_in_dim.11
  7.0 0.0 copy-start.4
  7.1 0.7 %copy-done.4 = s32[4,1024]{1,0:T(4,128)S(1)} copy-done((s32[4,1024]{1,0:T(4,128)S(1)}, s32[4,1024]{1,0:T(4,128)}, u32[]{:S(2)}) %copy-start.4) | copy-done | bytes 16408
  7.7 0.8 %collective-permute-done = f32[4,1,8,1024]{3,2,1,0:T(8,128)S(1)} collective-permute-done((f32[4,1,8,1024]{3,2,1,0:T(8,128)S(1)}, f32[4,1,8,1024]{3,2,1,0:T(8,128)S(1)}, u32[]{:S(2)}, u32[]{:S(2)}) %collective-permute-start) | collective-permute-done | bytes 131104 | tf_op jit(solution)/shard_map/ppermute | solution.py:111
  8.5 0.1 fusion.9
  8.6 0.1 fusion.35
  8.7 0.1 reduce_window_sum.22
  8.8 0.1 fusion.30
  8.9 0.2 fusion.34
  9.1 3.8 %collective-permute-start.1 = (f32[8,4,1024]{2,1,0:T(4,128)S(1)}, f32[8,4,1024]{2,1,0:T(4,128)S(1)}, u32[]{:S(2)}, u32[]{:S(2)}) collective-permute-start(f32[8,4,1024]{2,1,0:T(4,128)S(1)} %pad_maximum_fusion.3), channel_id=1, source_target_pairs={{0,1},{1,0},{2,3},{3,2},{4,5},{5,4},{6,7},{7,6},{8,9},{9,8},{10,11... | collective-permute-start | bytes 393224 | tf_op jit(solution)/shard_map/ppermute | solution.py:58
  13.0 0.7 %collective-permute-start.7 = (f32[4,4,1024]{2,1,0:T(4,128)S(1)}, f32[4,4,1024]{2,1,0:T(4,128)S(1)}, u32[]{:S(2)}, u32[]{:S(2)}) collective-permute-start(f32[4,4,1024]{2,1,0:T(4,128)S(1)} %get-tuple-element.38), channel_id=1, source_target_pairs={{1,2},{3,4},{5,6},{7,8},{9,10},{11,12},{13,14},{2,1},{4,3},{6,5},{... | collective-permute-start | bytes 196616 | tf_op jit(solution)/shard_map/ppermute | solution.py:45
  13.7 1.9 %collective-permute-start.6 = (f32[4,1,8,1024]{3,2,1,0:T(8,128)S(1)}, f32[4,1,8,1024]{3,2,1,0:T(8,128)S(1)}, u32[]{:S(2)}, u32[]{:S(2)}) collective-permute-start(f32[4,1,8,1024]{3,2,1,0:T(8,128)S(1)} %get-tuple-element.10), channel_id=1, source_target_pairs={{0,16},{16,32},{32,48},{48,64},{64,80},{80,96},{96,112},{112,128},... | collective-permute-start | bytes 393224 | tf_op jit(solution)/shard_map/ppermute | solution.py:113
  15.6 0.3 reduce_window_sum.23
  16.0 0.0 collective-permute-done.7
  16.0 0.0 collective-permute-done.1
  16.0 0.1 select_bitcast_fusion
  16.1 10.9 %collective-permute-start.2 = (f32[4,4,1024]{2,1,0:T(4,128)S(1)}, f32[4,4,1024]{2,1,0:T(4,128)S(1)}, u32[]{:S(2)}, u32[]{:S(2)}) collective-permute-start(f32[4,4,1024]{2,1,0:T(4,128)S(1)} %pad_maximum_fusion.7), channel_id=1, source_target_pairs={{0,3},{1,2},{2,1},{3,0},{4,7},{5,6},{6,5},{7,4},{8,11},{9,10},{10,... | collective-permute-start | bytes 196616 | tf_op jit(solution)/shard_map/ppermute | solution.py:61
  27.1 2.1 %collective-permute-done.2 = f32[4,4,1024]{2,1,0:T(4,128)S(1)} collective-permute-done((f32[4,4,1024]{2,1,0:T(4,128)S(1)}, f32[4,4,1024]{2,1,0:T(4,128)S(1)}, u32[]{:S(2)}, u32[]{:S(2)}) %collective-permute-start.2) | collective-permute-done | bytes 65568 | tf_op jit(solution)/shard_map/ppermute | solution.py:61
  29.4 11.4 %collective-permute-start.3 = (f32[4,4,1024]{2,1,0:T(4,128)S(1)}, f32[4,4,1024]{2,1,0:T(4,128)S(1)}, u32[]{:S(2)}, u32[]{:S(2)}) collective-permute-start(f32[4,4,1024]{2,1,0:T(4,128)S(1)} %pad_maximum_fusion.8), channel_id=1, source_target_pairs={{0,7},{1,6},{2,5},{3,4},{4,3},{5,2},{6,1},{7,0},{8,15},{9,14},{10,... | collective-permute-start | bytes 196616 | tf_op jit(solution)/shard_map/ppermute | solution.py:61
  40.9 2.1 %collective-permute-done.3 = f32[4,4,1024]{2,1,0:T(4,128)S(1)} collective-permute-done((f32[4,4,1024]{2,1,0:T(4,128)S(1)}, f32[4,4,1024]{2,1,0:T(4,128)S(1)}, u32[]{:S(2)}, u32[]{:S(2)}) %collective-permute-start.3) | collective-permute-done | bytes 65568 | tf_op jit(solution)/shard_map/ppermute | solution.py:61
  43.1 7.0 %collective-permute-start.4 = (f32[4,4,1024]{2,1,0:T(4,128)S(1)}, f32[4,4,1024]{2,1,0:T(4,128)S(1)}, u32[]{:S(2)}, u32[]{:S(2)}) collective-permute-start(f32[4,4,1024]{2,1,0:T(4,128)S(1)} %pad_maximum_fusion.9), channel_id=1, source_target_pairs={{0,15},{1,14},{2,13},{3,12},{4,11},{5,10},{6,9},{7,8},{8,7},{9,6},... | collective-permute-start | bytes 196616 | tf_op jit(solution)/shard_map/ppermute | solution.py:61
  50.2 2.1 %collective-permute-done.4 = f32[4,4,1024]{2,1,0:T(4,128)S(1)} collective-permute-done((f32[4,4,1024]{2,1,0:T(4,128)S(1)}, f32[4,4,1024]{2,1,0:T(4,128)S(1)}, u32[]{:S(2)}, u32[]{:S(2)}) %collective-permute-start.4) | collective-permute-done | bytes 65568 | tf_op jit(solution)/shard_map/ppermute | solution.py:61
  52.4 0.1 multiply_bitcast_fusion.1
  52.6 0.2 multiply_reduce_fusion
  52.8 0.1 fusion.18
  52.9 0.1 fusion.10
  53.0 1.9 %collective-permute-start.5 = (f32[4,1,8,1024]{3,2,1,0:T(8,128)S(1)}, f32[4,1,8,1024]{3,2,1,0:T(8,128)S(1)}, u32[]{:S(2)}, u32[]{:S(2)}) collective-permute-start(f32[4,1,8,1024]{3,2,1,0:T(8,128)S(1)} %slice.273), channel_id=1, source_target_pairs={{0,16},{16,32},{32,48},{48,64},{64,80},{80,96},{96,112},{112,128},... | collective-permute-start | bytes 393224 | tf_op jit(solution)/shard_map/ppermute | solution.py:34
  54.9 0.1 fusion.37
  55.0 0.0 copy-start.1
  55.0 0.0 copy-start.2
  55.0 0.1 copy.18
  55.1 0.1 copy.17
  55.2 0.0 collective-permute-done.6
  55.2 6.1 %collective-permute-done.5 = f32[4,1,8,1024]{3,2,1,0:T(8,128)S(1)} collective-permute-done((f32[4,1,8,1024]{3,2,1,0:T(8,128)S(1)}, f32[4,1,8,1024]{3,2,1,0:T(8,128)S(1)}, u32[]{:S(2)}, u32[]{:S(2)}) %collective-permute-start.5) | collective-permute-done | bytes 131104 | tf_op jit(solution)/shard_map/ppermute | solution.py:34
  61.4 0.0 copy-done.1
  61.4 0.0 copy-done.2
  61.4 1.9 %divide_subtract_fusion = (f32[4,4,8,1024]{3,2,1,0:T(8,128)}, f32[4,4,8,1024]{3,2,1,0:T(8,128)}, f32[4,4,8,1024]{3,2,1,0:T(8,128)}) fusion(f32[4,4,8,1024]{3,2,1,0:T(8,128)S(1)} %copy-done, f32[4,4,8,1024]{3,2,1,0:T(8,128)S(1)} %copy-done.1, f32[4,4,8,1024]{3,2,1,0:T(8,128)S(1)} %copy-done.2, f32[4,4,7,1024]{3,2,1,0:T(8,128)S(1)} %get-tuple-element.22, ...), kind=kLoop, calls=%fused_computation.18 | loop fusion | flops 3801088 | bytes 5521408 | tf_op jit(solution)/shard_map/sub | solution.py:139
  (36 shorter events, 0.8 us)
Async XLA Ops:
  0.6 5.4 %copy-start = (f32[4,4,8,1024]{3,2,1,0:T(8,128)S(1)}, f32[4,4,8,1024]{3,2,1,0:T(8,128)}, u32[]{:S(2)}) copy-start(f32[4,4,8,1024]{3,2,1,0:T(8,128)} %param.6) | copy-start | bytes 1572868
  1.7 6.8 %collective-permute-start = (f32[4,1,8,1024]{3,2,1,0:T(8,128)S(1)}, f32[4,1,8,1024]{3,2,1,0:T(8,128)S(1)}, u32[]{:S(2)}, u32[]{:S(2)}) collective-permute-start(f32[4,1,8,1024]{3,2,1,0:T(8,128)S(1)} %get-tuple-element.26), channel_id=1, source_target_pairs={{16,0},{32,16},{48,32},{64,48},{80,64},{96,80},{112,96},{128,112},... | collective-permute-start | bytes 393224 | tf_op jit(solution)/shard_map/ppermute | solution.py:111
  6.0 0.8 %copy-start.3 = (f32[3,4,1024]{2,1,0:T(4,128)S(1)}, f32[3,4,1024]{2,1,0:T(4,128)}, u32[]{:S(2)}) copy-start(f32[3,4,1024]{2,1,0:T(4,128)} %param.11) | copy-start | bytes 147460
  6.1 0.7 %copy-start.5 = (s32[1,1,128]{2,1,0:T(1,128)S(1)}, s32[1,1,128]{2,1,0:T(1,128)}, u32[]{:S(2)}) copy-start(s32[1,1,128]{2,1,0:T(1,128)} %param.10) | copy-start | bytes 1540
  7.0 0.7 %copy-start.4 = (s32[4,1024]{1,0:T(4,128)S(1)}, s32[4,1024]{1,0:T(4,128)}, u32[]{:S(2)}) copy-start(s32[4,1024]{1,0:T(4,128)} %param.9) | copy-start | bytes 49156
  9.1 6.9 %collective-permute-start.1 = (f32[8,4,1024]{2,1,0:T(4,128)S(1)}, f32[8,4,1024]{2,1,0:T(4,128)S(1)}, u32[]{:S(2)}, u32[]{:S(2)}) collective-permute-start(f32[8,4,1024]{2,1,0:T(4,128)S(1)} %pad_maximum_fusion.3), channel_id=1, source_target_pairs={{0,1},{1,0},{2,3},{3,2},{4,5},{5,4},{6,7},{7,6},{8,9},{9,8},{10,11... | collective-permute-start | bytes 393224 | tf_op jit(solution)/shard_map/ppermute | solution.py:58
  13.0 3.0 %collective-permute-start.7 = (f32[4,4,1024]{2,1,0:T(4,128)S(1)}, f32[4,4,1024]{2,1,0:T(4,128)S(1)}, u32[]{:S(2)}, u32[]{:S(2)}) collective-permute-start(f32[4,4,1024]{2,1,0:T(4,128)S(1)} %get-tuple-element.38), channel_id=1, source_target_pairs={{1,2},{3,4},{5,6},{7,8},{9,10},{11,12},{13,14},{2,1},{4,3},{6,5},{... | collective-permute-start | bytes 196616 | tf_op jit(solution)/shard_map/ppermute | solution.py:45
  13.7 41.6 %collective-permute-start.6 = (f32[4,1,8,1024]{3,2,1,0:T(8,128)S(1)}, f32[4,1,8,1024]{3,2,1,0:T(8,128)S(1)}, u32[]{:S(2)}, u32[]{:S(2)}) collective-permute-start(f32[4,1,8,1024]{3,2,1,0:T(8,128)S(1)} %get-tuple-element.10), channel_id=1, source_target_pairs={{0,16},{16,32},{32,48},{48,64},{64,80},{80,96},{96,112},{112,128},... | collective-permute-start | bytes 393224 | tf_op jit(solution)/shard_map/ppermute | solution.py:113
  16.1 13.1 %collective-permute-start.2 = (f32[4,4,1024]{2,1,0:T(4,128)S(1)}, f32[4,4,1024]{2,1,0:T(4,128)S(1)}, u32[]{:S(2)}, u32[]{:S(2)}) collective-permute-start(f32[4,4,1024]{2,1,0:T(4,128)S(1)} %pad_maximum_fusion.7), channel_id=1, source_target_pairs={{0,3},{1,2},{2,1},{3,0},{4,7},{5,6},{6,5},{7,4},{8,11},{9,10},{10,... | collective-permute-start | bytes 196616 | tf_op jit(solution)/shard_map/ppermute | solution.py:61
  29.4 13.7 %collective-permute-start.3 = (f32[4,4,1024]{2,1,0:T(4,128)S(1)}, f32[4,4,1024]{2,1,0:T(4,128)S(1)}, u32[]{:S(2)}, u32[]{:S(2)}) collective-permute-start(f32[4,4,1024]{2,1,0:T(4,128)S(1)} %pad_maximum_fusion.8), channel_id=1, source_target_pairs={{0,7},{1,6},{2,5},{3,4},{4,3},{5,2},{6,1},{7,0},{8,15},{9,14},{10,... | collective-permute-start | bytes 196616 | tf_op jit(solution)/shard_map/ppermute | solution.py:61
  43.1 9.2 %collective-permute-start.4 = (f32[4,4,1024]{2,1,0:T(4,128)S(1)}, f32[4,4,1024]{2,1,0:T(4,128)S(1)}, u32[]{:S(2)}, u32[]{:S(2)}) collective-permute-start(f32[4,4,1024]{2,1,0:T(4,128)S(1)} %pad_maximum_fusion.9), channel_id=1, source_target_pairs={{0,15},{1,14},{2,13},{3,12},{4,11},{5,10},{6,9},{7,8},{8,7},{9,6},... | collective-permute-start | bytes 196616 | tf_op jit(solution)/shard_map/ppermute | solution.py:61
  53.0 8.4 %collective-permute-start.5 = (f32[4,1,8,1024]{3,2,1,0:T(8,128)S(1)}, f32[4,1,8,1024]{3,2,1,0:T(8,128)S(1)}, u32[]{:S(2)}, u32[]{:S(2)}) collective-permute-start(f32[4,1,8,1024]{3,2,1,0:T(8,128)S(1)} %slice.273), channel_id=1, source_target_pairs={{0,16},{16,32},{32,48},{48,64},{64,80},{80,96},{96,112},{112,128},... | collective-permute-start | bytes 393224 | tf_op jit(solution)/shard_map/ppermute | solution.py:34
  55.0 6.4 %copy-start.1 = (f32[4,4,8,1024]{3,2,1,0:T(8,128)S(1)}, f32[4,4,8,1024]{3,2,1,0:T(8,128)}, u32[]{:S(2)}) copy-start(f32[4,4,8,1024]{3,2,1,0:T(8,128)} %param.7) | copy-start | bytes 1572868
  55.0 6.3 %copy-start.2 = (f32[4,4,8,1024]{3,2,1,0:T(8,128)S(1)}, f32[4,4,8,1024]{3,2,1,0:T(8,128)}, u32[]{:S(2)}) copy-start(f32[4,4,8,1024]{3,2,1,0:T(8,128)} %param.8) | copy-start | bytes 1572868

commit v17 on v15

--- a/solution.py
+++ b/solution.py
@@ -112,6 +112,7 @@
     swapped = depth_swap(grid, "depth")
     shares = (ray_offset.astype(jnp.float32) * 0.5)[None, :, None, :]
     occ = expand_blocks(occupancy.astype(jnp.float32))
+    first_moment, second_moment, occ = lax.optimization_barrier((first_moment, second_moment, occ))
     plane_out = jnp.where(odd, grid[:, :, 0], grid[:, :, -1])
     feature_grad, plane_in = render(grid, padded[:, 2:], shares, occ, target, total_depth, plane_out)
     plane_before = jnp.where(odd, plane_in, swapped)[:, :, None]

time: 63.7 us -> 63.7 us (level)
  no operation moved by 1% of the time
where the time goes in v17:
time: 63.7 us; the launch traced here: 63.3 us
  starting transfers between devices  41.9 us (66%)
  waiting for transfers between devices  13.2 us (21%)
  other arithmetic  3.96 us (6%)
  local copies, waits for them, and re-layouts  2.96 us (5%)
  between operations  1.19 us (2%)
    ppermute x3, starting transfers between devices, butterfly_scan(): other = lax.ppermute(block, axis, route)  29.3 us
    ppermute x3, waiting for transfers between devices, butterfly_scan(): other = lax.ppermute(block, axis, route)  6.33 us
    ppermute x1, waiting for transfers between devices, passed_along(): return lax.ppermute(block, axis, route)  6.13 us
    ppermute x1, starting transfers between devices, with_halo(): lax.ppermute(head, axis, [((i + 1) % count, i) for i in range(ends)])  4.29 us
    ppermute x1, starting transfers between devices, butterfly_scan(): lax.ppermute(jnp.concatenate([block, plane_out], axis=0), axis, route)  3.83 us
    sub x1, other arithmetic, body(): grid - learn_rate * (new_first / corr_one) / (jnp.sqrt(new_second / corr_...  1.94 us
    ppermute x1, starting transfers between devices, with_halo(): lax.ppermute(tail, axis, [(i, (i + 1) % count) for i in range(ends)])  1.92 us
    ppermute x1, starting transfers between devices, passed_along(): return lax.ppermute(block, axis, route)  1.92 us
  transfers between devices with their start and end apart: 8, of which 5 were waited for; matrix products, arithmetic and copies ran while one was open for 3% of the time, Pallas kernels for 0%

profile of v17, /device:TPU:24, one launch (start us, length us, event | category | flops | bytes accessed | tf_op | source)
XLA Modules:
  0.0 63.3 jit_solution(17538840100066663612)
XLA Ops:
  0.6 0.0 copy-start
  0.6 1.0 %fusion.35 = (f32[4,1,8,1024]{3,2,1,0:T(8,128)S(1)}, f32[4,1,8,1024]{3,2,1,0:T(8,128)S(1)}) fusion(f32[4,4,8,1024]{3,2,1,0:T(8,128)} %param.6), kind=kLoop, calls=%fused_computation.120 | loop fusion | bytes 524288 | tf_op jit(solution)/shard_map/slice | solution.py:18
  1.7 4.3 %collective-permute-start = (f32[4,1,8,1024]{3,2,1,0:T(8,128)S(1)}, f32[4,1,8,1024]{3,2,1,0:T(8,128)S(1)}, u32[]{:S(2)}, u32[]{:S(2)}) collective-permute-start(f32[4,1,8,1024]{3,2,1,0:T(8,128)S(1)} %get-tuple-element.28), channel_id=1, source_target_pairs={{16,0},{32,16},{48,32},{64,48},{80,64},{96,80},{112,96},{128,112},... | collective-permute-start | bytes 393224 | tf_op jit(solution)/shard_map/ppermute | solution.py:24
  6.0 0.0 copy-done
  6.0 0.0 copy-start.3
  6.0 0.1 fusion.34
  6.1 0.0 copy-start.5
  6.1 0.6 %copy-done.5 = s32[1,1,128]{2,1,0:T(1,128)S(1)} copy-done((s32[1,1,128]{2,1,0:T(1,128)S(1)}, s32[1,1,128]{2,1,0:T(1,128)}, u32[]{:S(2)}) %copy-start.5) | copy-done | bytes 536
  6.8 0.0 copy-done.3
  6.8 0.1 broadcast_in_dim.12
  6.9 0.1 broadcast_in_dim.13
  7.0 0.0 copy-start.4
  7.1 0.7 %copy-done.4 = s32[4,1024]{1,0:T(4,128)S(1)} copy-done((s32[4,1024]{1,0:T(4,128)S(1)}, s32[4,1024]{1,0:T(4,128)}, u32[]{:S(2)}) %copy-start.4) | copy-done | bytes 16408
  7.7 0.7 %collective-permute-done = f32[4,1,8,1024]{3,2,1,0:T(8,128)S(1)} collective-permute-done((f32[4,1,8,1024]{3,2,1,0:T(8,128)S(1)}, f32[4,1,8,1024]{3,2,1,0:T(8,128)S(1)}, u32[]{:S(2)}, u32[]{:S(2)}) %collective-permute-start) | collective-permute-done | bytes 131104 | tf_op jit(solution)/shard_map/ppermute | solution.py:24
  8.5 0.1 fusion.9
  8.6 0.1 fusion.31
  8.7 0.1 reduce_window_sum.22
  8.8 0.1 exponential_multiply_fusion
  8.9 0.2 fusion.30
  9.1 3.8 %collective-permute-start.1 = (f32[8,4,1024]{2,1,0:T(4,128)S(1)}, f32[8,4,1024]{2,1,0:T(4,128)S(1)}, u32[]{:S(2)}, u32[]{:S(2)}) collective-permute-start(f32[8,4,1024]{2,1,0:T(4,128)S(1)} %pad_maximum_fusion.3), channel_id=1, source_target_pairs={{0,1},{1,0},{2,3},{3,2},{4,5},{5,4},{6,7},{7,6},{8,9},{9,8},{10,11... | collective-permute-start | bytes 393224 | tf_op jit(solution)/shard_map/ppermute | solution.py:58
  13.0 0.7 %collective-permute-start.7 = (f32[4,4,1024]{2,1,0:T(4,128)S(1)}, f32[4,4,1024]{2,1,0:T(4,128)S(1)}, u32[]{:S(2)}, u32[]{:S(2)}) collective-permute-start(f32[4,4,1024]{2,1,0:T(4,128)S(1)} %get-tuple-element.40), channel_id=1, source_target_pairs={{1,2},{3,4},{5,6},{7,8},{9,10},{11,12},{13,14},{2,1},{4,3},{6,5},{... | collective-permute-start | bytes 196616 | tf_op jit(solution)/shard_map/ppermute | solution.py:45
  13.6 1.9 %collective-permute-start.6 = (f32[4,1,8,1024]{3,2,1,0:T(8,128)S(1)}, f32[4,1,8,1024]{3,2,1,0:T(8,128)S(1)}, u32[]{:S(2)}, u32[]{:S(2)}) collective-permute-start(f32[4,1,8,1024]{3,2,1,0:T(8,128)S(1)} %get-tuple-element.29), channel_id=1, source_target_pairs={{0,16},{16,32},{32,48},{48,64},{64,80},{80,96},{96,112},{112,128},... | collective-permute-start | bytes 393224 | tf_op jit(solution)/shard_map/ppermute | solution.py:22
  15.6 0.3 reduce_window_sum.23
  16.0 0.0 collective-permute-done.7
  16.0 0.0 collective-permute-done.1
  16.0 0.1 select_bitcast_fusion
  16.1 10.9 %collective-permute-start.2 = (f32[4,4,1024]{2,1,0:T(4,128)S(1)}, f32[4,4,1024]{2,1,0:T(4,128)S(1)}, u32[]{:S(2)}, u32[]{:S(2)}) collective-permute-start(f32[4,4,1024]{2,1,0:T(4,128)S(1)} %pad_maximum_fusion.7), channel_id=1, source_target_pairs={{0,3},{1,2},{2,1},{3,0},{4,7},{5,6},{6,5},{7,4},{8,11},{9,10},{10,... | collective-permute-start | bytes 196616 | tf_op jit(solution)/shard_map/ppermute | solution.py:61
  27.1 2.1 %collective-permute-done.2 = f32[4,4,1024]{2,1,0:T(4,128)S(1)} collective-permute-done((f32[4,4,1024]{2,1,0:T(4,128)S(1)}, f32[4,4,1024]{2,1,0:T(4,128)S(1)}, u32[]{:S(2)}, u32[]{:S(2)}) %collective-permute-start.2) | collective-permute-done | bytes 65568 | tf_op jit(solution)/shard_map/ppermute | solution.py:61
  29.4 11.4 %collective-permute-start.3 = (f32[4,4,1024]{2,1,0:T(4,128)S(1)}, f32[4,4,1024]{2,1,0:T(4,128)S(1)}, u32[]{:S(2)}, u32[]{:S(2)}) collective-permute-start(f32[4,4,1024]{2,1,0:T(4,128)S(1)} %pad_maximum_fusion.8), channel_id=1, source_target_pairs={{0,7},{1,6},{2,5},{3,4},{4,3},{5,2},{6,1},{7,0},{8,15},{9,14},{10,... | collective-permute-start | bytes 196616 | tf_op jit(solution)/shard_map/ppermute | solution.py:61
  40.9 2.1 %collective-permute-done.3 = f32[4,4,1024]{2,1,0:T(4,128)S(1)} collective-permute-done((f32[4,4,1024]{2,1,0:T(4,128)S(1)}, f32[4,4,1024]{2,1,0:T(4,128)S(1)}, u32[]{:S(2)}, u32[]{:S(2)}) %collective-permute-start.3) | collective-permute-done | bytes 65568 | tf_op jit(solution)/shard_map/ppermute | solution.py:61
  43.1 7.0 %collective-permute-start.4 = (f32[4,4,1024]{2,1,0:T(4,128)S(1)}, f32[4,4,1024]{2,1,0:T(4,128)S(1)}, u32[]{:S(2)}, u32[]{:S(2)}) collective-permute-start(f32[4,4,1024]{2,1,0:T(4,128)S(1)} %pad_maximum_fusion.9), channel_id=1, source_target_pairs={{0,15},{1,14},{2,13},{3,12},{4,11},{5,10},{6,9},{7,8},{8,7},{9,6},... | collective-permute-start | bytes 196616 | tf_op jit(solution)/shard_map/ppermute | solution.py:61
  50.2 2.1 %collective-permute-done.4 = f32[4,4,1024]{2,1,0:T(4,128)S(1)} collective-permute-done((f32[4,4,1024]{2,1,0:T(4,128)S(1)}, f32[4,4,1024]{2,1,0:T(4,128)S(1)}, u32[]{:S(2)}, u32[]{:S(2)}) %collective-permute-start.4) | collective-permute-done | bytes 65568 | tf_op jit(solution)/shard_map/ppermute | solution.py:61
  52.6 0.2 multiply_reduce_fusion
  52.8 0.1 multiply_bitcast_fusion
  52.8 0.1 fusion.10
  52.9 1.9 %collective-permute-start.5 = (f32[4,1,8,1024]{3,2,1,0:T(8,128)S(1)}, f32[4,1,8,1024]{3,2,1,0:T(8,128)S(1)}, u32[]{:S(2)}, u32[]{:S(2)}) collective-permute-start(f32[4,1,8,1024]{3,2,1,0:T(8,128)S(1)} %slice.273), channel_id=1, source_target_pairs={{0,16},{16,32},{32,48},{48,64},{64,80},{80,96},{96,112},{112,128},... | collective-permute-start | bytes 393224 | tf_op jit(solution)/shard_map/ppermute | solution.py:34
  54.8 0.1 fusion.33
  55.0 0.0 copy-start.1
  55.0 0.0 copy-start.2
  55.0 0.1 copy.18
  55.1 0.1 copy.17
  55.2 0.0 collective-permute-done.6
  55.2 6.1 %collective-permute-done.5 = f32[4,1,8,1024]{3,2,1,0:T(8,128)S(1)} collective-permute-done((f32[4,1,8,1024]{3,2,1,0:T(8,128)S(1)}, f32[4,1,8,1024]{3,2,1,0:T(8,128)S(1)}, u32[]{:S(2)}, u32[]{:S(2)}) %collective-permute-start.5) | collective-permute-done | bytes 131104 | tf_op jit(solution)/shard_map/ppermute | solution.py:34
  61.3 0.0 copy-done.1
  61.3 0.0 copy-done.2
  61.3 1.9 %divide_subtract_fusion = (f32[4,4,8,1024]{3,2,1,0:T(8,128)}, f32[4,4,8,1024]{3,2,1,0:T(8,128)}, f32[4,4,8,1024]{3,2,1,0:T(8,128)}) fusion(f32[4,4,8,1024]{3,2,1,0:T(8,128)S(1)} %copy-done, f32[4,4,8,1024]{3,2,1,0:T(8,128)S(1)} %copy-done.1, f32[4,4,8,1024]{3,2,1,0:T(8,128)S(1)} %copy-done.2, f32[4,4,7,1024]{3,2,1,0:T(8,128)S(1)} %get-tuple-element.24, ...), kind=kLoop, calls=%fused_computation.18 | loop fusion | flops 3801088 | bytes 5521408 | tf_op jit(solution)/shard_map/sub | solution.py:136
  (38 shorter events, 0.8 us)
Async XLA Ops:
  0.6 5.4 %copy-start = (f32[4,4,8,1024]{3,2,1,0:T(8,128)S(1)}, f32[4,4,8,1024]{3,2,1,0:T(8,128)}, u32[]{:S(2)}) copy-start(f32[4,4,8,1024]{3,2,1,0:T(8,128)} %param.6) | copy-start | bytes 1572868
  1.7 6.8 %collective-permute-start = (f32[4,1,8,1024]{3,2,1,0:T(8,128)S(1)}, f32[4,1,8,1024]{3,2,1,0:T(8,128)S(1)}, u32[]{:S(2)}, u32[]{:S(2)}) collective-permute-start(f32[4,1,8,1024]{3,2,1,0:T(8,128)S(1)} %get-tuple-element.28), channel_id=1, source_target_pairs={{16,0},{32,16},{48,32},{64,48},{80,64},{96,80},{112,96},{128,112},... | collective-permute-start | bytes 393224 | tf_op jit(solution)/shard_map/ppermute | solution.py:24
  6.0 0.8 %copy-start.3 = (f32[3,4,1024]{2,1,0:T(4,128)S(1)}, f32[3,4,1024]{2,1,0:T(4,128)}, u32[]{:S(2)}) copy-start(f32[3,4,1024]{2,1,0:T(4,128)} %param.11) | copy-start | bytes 147460
  6.1 0.7 %copy-start.5 = (s32[1,1,128]{2,1,0:T(1,128)S(1)}, s32[1,1,128]{2,1,0:T(1,128)}, u32[]{:S(2)}) copy-start(s32[1,1,128]{2,1,0:T(1,128)} %param.10) | copy-start | bytes 1540
  7.0 0.7 %copy-start.4 = (s32[4,1024]{1,0:T(4,128)S(1)}, s32[4,1024]{1,0:T(4,128)}, u32[]{:S(2)}) copy-start(s32[4,1024]{1,0:T(4,128)} %param.9) | copy-start | bytes 49156
  9.1 6.9 %collective-permute-start.1 = (f32[8,4,1024]{2,1,0:T(4,128)S(1)}, f32[8,4,1024]{2,1,0:T(4,128)S(1)}, u32[]{:S(2)}, u32[]{:S(2)}) collective-permute-start(f32[8,4,1024]{2,1,0:T(4,128)S(1)} %pad_maximum_fusion.3), channel_id=1, source_target_pairs={{0,1},{1,0},{2,3},{3,2},{4,5},{5,4},{6,7},{7,6},{8,9},{9,8},{10,11... | collective-permute-start | bytes 393224 | tf_op jit(solution)/shard_map/ppermute | solution.py:58
  13.0 3.0 %collective-permute-start.7 = (f32[4,4,1024]{2,1,0:T(4,128)S(1)}, f32[4,4,1024]{2,1,0:T(4,128)S(1)}, u32[]{:S(2)}, u32[]{:S(2)}) collective-permute-start(f32[4,4,1024]{2,1,0:T(4,128)S(1)} %get-tuple-element.40), channel_id=1, source_target_pairs={{1,2},{3,4},{5,6},{7,8},{9,10},{11,12},{13,14},{2,1},{4,3},{6,5},{... | collective-permute-start | bytes 196616 | tf_op jit(solution)/shard_map/ppermute | solution.py:45
  13.6 41.5 %collective-permute-start.6 = (f32[4,1,8,1024]{3,2,1,0:T(8,128)S(1)}, f32[4,1,8,1024]{3,2,1,0:T(8,128)S(1)}, u32[]{:S(2)}, u32[]{:S(2)}) collective-permute-start(f32[4,1,8,1024]{3,2,1,0:T(8,128)S(1)} %get-tuple-element.29), channel_id=1, source_target_pairs={{0,16},{16,32},{32,48},{48,64},{64,80},{80,96},{96,112},{112,128},... | collective-permute-start | bytes 393224 | tf_op jit(solution)/shard_map/ppermute | solution.py:22
  16.1 13.1 %collective-permute-start.2 = (f32[4,4,1024]{2,1,0:T(4,128)S(1)}, f32[4,4,1024]{2,1,0:T(4,128)S(1)}, u32[]{:S(2)}, u32[]{:S(2)}) collective-permute-start(f32[4,4,1024]{2,1,0:T(4,128)S(1)} %pad_maximum_fusion.7), channel_id=1, source_target_pairs={{0,3},{1,2},{2,1},{3,0},{4,7},{5,6},{6,5},{7,4},{8,11},{9,10},{10,... | collective-permute-start | bytes 196616 | tf_op jit(solution)/shard_map/ppermute | solution.py:61
  29.4 13.7 %collective-permute-start.3 = (f32[4,4,1024]{2,1,0:T(4,128)S(1)}, f32[4,4,1024]{2,1,0:T(4,128)S(1)}, u32[]{:S(2)}, u32[]{:S(2)}) collective-permute-start(f32[4,4,1024]{2,1,0:T(4,128)S(1)} %pad_maximum_fusion.8), channel_id=1, source_target_pairs={{0,7},{1,6},{2,5},{3,4},{4,3},{5,2},{6,1},{7,0},{8,15},{9,14},{10,... | collective-permute-start | bytes 196616 | tf_op jit(solution)/shard_map/ppermute | solution.py:61
  43.1 9.2 %collective-permute-start.4 = (f32[4,4,1024]{2,1,0:T(4,128)S(1)}, f32[4,4,1024]{2,1,0:T(4,128)S(1)}, u32[]{:S(2)}, u32[]{:S(2)}) collective-permute-start(f32[4,4,1024]{2,1,0:T(4,128)S(1)} %pad_maximum_fusion.9), channel_id=1, source_target_pairs={{0,15},{1,14},{2,13},{3,12},{4,11},{5,10},{6,9},{7,8},{8,7},{9,6},... | collective-permute-start | bytes 196616 | tf_op jit(solution)/shard_map/ppermute | solution.py:61
  52.9 8.4 %collective-permute-start.5 = (f32[4,1,8,1024]{3,2,1,0:T(8,128)S(1)}, f32[4,1,8,1024]{3,2,1,0:T(8,128)S(1)}, u32[]{:S(2)}, u32[]{:S(2)}) collective-permute-start(f32[4,1,8,1024]{3,2,1,0:T(8,128)S(1)} %slice.273), channel_id=1, source_target_pairs={{0,16},{16,32},{32,48},{48,64},{64,80},{80,96},{96,112},{112,128},... | collective-permute-start | bytes 393224 | tf_op jit(solution)/shard_map/ppermute | solution.py:34
  55.0 6.4 %copy-start.1 = (f32[4,4,8,1024]{3,2,1,0:T(8,128)S(1)}, f32[4,4,8,1024]{3,2,1,0:T(8,128)}, u32[]{:S(2)}) copy-start(f32[4,4,8,1024]{3,2,1,0:T(8,128)} %param.7) | copy-start | bytes 1572868
  55.0 6.3 %copy-start.2 = (f32[4,4,8,1024]{3,2,1,0:T(8,128)S(1)}, f32[4,4,8,1024]{3,2,1,0:T(8,128)}, u32[]{:S(2)}) copy-start(f32[4,4,8,1024]{3,2,1,0:T(8,128)} %param.8) | copy-start | bytes 1572868

commit v18 on v16

--- a/solution.py
+++ b/solution.py
@@ -116,6 +116,7 @@
     swapped = depth_swap(grid, "depth")
     shares = (ray_offset.astype(jnp.float32) * 0.5)[None, :, None, :]
     occ = expand_blocks(occupancy.astype(jnp.float32))
+    first_moment, second_moment, occ = lax.optimization_barrier((first_moment, second_moment, occ))
     plane_out = jnp.where(odd, grid[:, :, 0], grid[:, :, -1])
     feature_grad, plane_in = render(grid, padded[:, 2:], shares, occ, target, total_depth, plane_out)
     plane_before = jnp.where(odd, plane_in, swapped)[:, :, None]

time: 63.7 us -> 63.7 us (level)
  no operation moved by 1% of the time
where the time goes in v18:
time: 63.7 us; the launch traced here: 63.3 us
  starting transfers between devices  41.9 us (66%)
  waiting for transfers between devices  13.2 us (21%)
  other arithmetic  3.96 us (6%)
  local copies, waits for them, and re-layouts  2.96 us (5%)
  between operations  1.19 us (2%)
    ppermute x3, starting transfers between devices, butterfly_scan(): other = lax.ppermute(block, axis, route)  29.3 us
    ppermute x3, waiting for transfers between devices, butterfly_scan(): other = lax.ppermute(block, axis, route)  6.33 us
    ppermute x1, waiting for transfers between devices, passed_along(): return lax.ppermute(block, axis, route)  6.13 us
    ppermute x1, starting transfers between devices, body(): lax.ppermute(grid[:, :1], 'tile', [(i + 1, i) for i in range(tiles - 1)])  4.29 us
    ppermute x1, starting transfers between devices, butterfly_scan(): lax.ppermute(jnp.concatenate([block, plane_out], axis=0), axis, route)  3.83 us
    sub x1, other arithmetic, body(): grid - learn_rate * (new_first / corr_one) / (jnp.sqrt(new_second / corr_...  1.94 us
    ppermute x1, starting transfers between devices, body(): lax.ppermute(last_row, 'tile', [(i, i + 1) for i in range(tiles - 1)])  1.92 us
    ppermute x1, starting transfers between devices, passed_along(): return lax.ppermute(block, axis, route)  1.92 us
  transfers between devices with their start and end apart: 8, of which 5 were waited for; matrix products, arithmetic and copies ran while one was open for 3% of the time, Pallas kernels for 0%

profile of v18, /device:TPU:24, one launch (start us, length us, event | category | flops | bytes accessed | tf_op | source)
XLA Modules:
  0.0 63.3 jit_solution(6156894691197672385)
XLA Ops:
  0.6 0.0 copy-start
  0.6 1.0 %fusion.35 = (f32[4,1,8,1024]{3,2,1,0:T(8,128)S(1)}, f32[4,1,8,1024]{3,2,1,0:T(8,128)S(1)}) fusion(f32[4,4,8,1024]{3,2,1,0:T(8,128)} %param.6), kind=kLoop, calls=%fused_computation.120 | loop fusion | bytes 524288 | tf_op jit(solution)/shard_map/slice | solution.py:111
  1.7 4.3 %collective-permute-start = (f32[4,1,8,1024]{3,2,1,0:T(8,128)S(1)}, f32[4,1,8,1024]{3,2,1,0:T(8,128)S(1)}, u32[]{:S(2)}, u32[]{:S(2)}) collective-permute-start(f32[4,1,8,1024]{3,2,1,0:T(8,128)S(1)} %get-tuple-element.32), channel_id=1, source_target_pairs={{16,0},{32,16},{48,32},{64,48},{80,64},{96,80},{112,96},{128,112},... | collective-permute-start | bytes 393224 | tf_op jit(solution)/shard_map/ppermute | solution.py:111
  6.0 0.0 copy-done
  6.0 0.0 copy-start.3
  6.0 0.1 fusion.34
  6.1 0.0 copy-start.5
  6.1 0.6 %copy-done.5 = s32[1,1,128]{2,1,0:T(1,128)S(1)} copy-done((s32[1,1,128]{2,1,0:T(1,128)S(1)}, s32[1,1,128]{2,1,0:T(1,128)}, u32[]{:S(2)}) %copy-start.5) | copy-done | bytes 536
  6.8 0.0 copy-done.3
  6.8 0.1 broadcast_in_dim.12
  6.9 0.1 broadcast_in_dim.13
  7.0 0.0 copy-start.4
  7.1 0.7 %copy-done.4 = s32[4,1024]{1,0:T(4,128)S(1)} copy-done((s32[4,1024]{1,0:T(4,128)S(1)}, s32[4,1024]{1,0:T(4,128)}, u32[]{:S(2)}) %copy-start.4) | copy-done | bytes 16408
  7.7 0.7 %collective-permute-done = f32[4,1,8,1024]{3,2,1,0:T(8,128)S(1)} collective-permute-done((f32[4,1,8,1024]{3,2,1,0:T(8,128)S(1)}, f32[4,1,8,1024]{3,2,1,0:T(8,128)S(1)}, u32[]{:S(2)}, u32[]{:S(2)}) %collective-permute-start) | collective-permute-done | bytes 131104 | tf_op jit(solution)/shard_map/ppermute | solution.py:111
  8.5 0.1 fusion.9
  8.6 0.1 fusion.31
  8.7 0.1 reduce_window_sum.22
  8.8 0.1 exponential_multiply_fusion
  8.9 0.2 fusion.30
  9.1 3.8 %collective-permute-start.1 = (f32[8,4,1024]{2,1,0:T(4,128)S(1)}, f32[8,4,1024]{2,1,0:T(4,128)S(1)}, u32[]{:S(2)}, u32[]{:S(2)}) collective-permute-start(f32[8,4,1024]{2,1,0:T(4,128)S(1)} %pad_maximum_fusion.3), channel_id=1, source_target_pairs={{0,1},{1,0},{2,3},{3,2},{4,5},{5,4},{6,7},{7,6},{8,9},{9,8},{10,11... | collective-permute-start | bytes 393224 | tf_op jit(solution)/shard_map/ppermute | solution.py:58
  13.0 0.7 %collective-permute-start.7 = (f32[4,4,1024]{2,1,0:T(4,128)S(1)}, f32[4,4,1024]{2,1,0:T(4,128)S(1)}, u32[]{:S(2)}, u32[]{:S(2)}) collective-permute-start(f32[4,4,1024]{2,1,0:T(4,128)S(1)} %get-tuple-element.44), channel_id=1, source_target_pairs={{1,2},{3,4},{5,6},{7,8},{9,10},{11,12},{13,14},{2,1},{4,3},{6,5},{... | collective-permute-start | bytes 196616 | tf_op jit(solution)/shard_map/ppermute | solution.py:45
  13.7 1.9 %collective-permute-start.6 = (f32[4,1,8,1024]{3,2,1,0:T(8,128)S(1)}, f32[4,1,8,1024]{3,2,1,0:T(8,128)S(1)}, u32[]{:S(2)}, u32[]{:S(2)}) collective-permute-start(f32[4,1,8,1024]{3,2,1,0:T(8,128)S(1)} %get-tuple-element.15), channel_id=1, source_target_pairs={{0,16},{16,32},{32,48},{48,64},{64,80},{80,96},{96,112},{112,128},... | collective-permute-start | bytes 393224 | tf_op jit(solution)/shard_map/ppermute | solution.py:113
  15.6 0.3 reduce_window_sum.23
  16.0 0.0 collective-permute-done.7
  16.0 0.0 collective-permute-done.1
  16.0 0.1 select_bitcast_fusion
  16.1 10.9 %collective-permute-start.2 = (f32[4,4,1024]{2,1,0:T(4,128)S(1)}, f32[4,4,1024]{2,1,0:T(4,128)S(1)}, u32[]{:S(2)}, u32[]{:S(2)}) collective-permute-start(f32[4,4,1024]{2,1,0:T(4,128)S(1)} %pad_maximum_fusion.7), channel_id=1, source_target_pairs={{0,3},{1,2},{2,1},{3,0},{4,7},{5,6},{6,5},{7,4},{8,11},{9,10},{10,... | collective-permute-start | bytes 196616 | tf_op jit(solution)/shard_map/ppermute | solution.py:61
  27.1 2.1 %collective-permute-done.2 = f32[4,4,1024]{2,1,0:T(4,128)S(1)} collective-permute-done((f32[4,4,1024]{2,1,0:T(4,128)S(1)}, f32[4,4,1024]{2,1,0:T(4,128)S(1)}, u32[]{:S(2)}, u32[]{:S(2)}) %collective-permute-start.2) | collective-permute-done | bytes 65568 | tf_op jit(solution)/shard_map/ppermute | solution.py:61
  29.4 11.4 %collective-permute-start.3 = (f32[4,4,1024]{2,1,0:T(4,128)S(1)}, f32[4,4,1024]{2,1,0:T(4,128)S(1)}, u32[]{:S(2)}, u32[]{:S(2)}) collective-permute-start(f32[4,4,1024]{2,1,0:T(4,128)S(1)} %pad_maximum_fusion.8), channel_id=1, source_target_pairs={{0,7},{1,6},{2,5},{3,4},{4,3},{5,2},{6,1},{7,0},{8,15},{9,14},{10,... | collective-permute-start | bytes 196616 | tf_op jit(solution)/shard_map/ppermute | solution.py:61
  40.9 2.1 %collective-permute-done.3 = f32[4,4,1024]{2,1,0:T(4,128)S(1)} collective-permute-done((f32[4,4,1024]{2,1,0:T(4,128)S(1)}, f32[4,4,1024]{2,1,0:T(4,128)S(1)}, u32[]{:S(2)}, u32[]{:S(2)}) %collective-permute-start.3) | collective-permute-done | bytes 65568 | tf_op jit(solution)/shard_map/ppermute | solution.py:61
  43.1 7.0 %collective-permute-start.4 = (f32[4,4,1024]{2,1,0:T(4,128)S(1)}, f32[4,4,1024]{2,1,0:T(4,128)S(1)}, u32[]{:S(2)}, u32[]{:S(2)}) collective-permute-start(f32[4,4,1024]{2,1,0:T(4,128)S(1)} %pad_maximum_fusion.9), channel_id=1, source_target_pairs={{0,15},{1,14},{2,13},{3,12},{4,11},{5,10},{6,9},{7,8},{8,7},{9,6},... | collective-permute-start | bytes 196616 | tf_op jit(solution)/shard_map/ppermute | solution.py:61
  50.2 2.1 %collective-permute-done.4 = f32[4,4,1024]{2,1,0:T(4,128)S(1)} collective-permute-done((f32[4,4,1024]{2,1,0:T(4,128)S(1)}, f32[4,4,1024]{2,1,0:T(4,128)S(1)}, u32[]{:S(2)}, u32[]{:S(2)}) %collective-permute-start.4) | collective-permute-done | bytes 65568 | tf_op jit(solution)/shard_map/ppermute | solution.py:61
  52.6 0.2 multiply_reduce_fusion
  52.8 0.1 multiply_bitcast_fusion
  52.8 0.1 fusion.10
  52.9 1.9 %collective-permute-start.5 = (f32[4,1,8,1024]{3,2,1,0:T(8,128)S(1)}, f32[4,1,8,1024]{3,2,1,0:T(8,128)S(1)}, u32[]{:S(2)}, u32[]{:S(2)}) collective-permute-start(f32[4,1,8,1024]{3,2,1,0:T(8,128)S(1)} %slice.273), channel_id=1, source_target_pairs={{0,16},{16,32},{32,48},{48,64},{64,80},{80,96},{96,112},{112,128},... | collective-permute-start | bytes 393224 | tf_op jit(solution)/shard_map/ppermute | solution.py:34
  54.8 0.1 fusion.33
  55.0 0.0 copy-start.1
  55.0 0.0 copy-start.2
  55.0 0.1 copy.18
  55.1 0.1 copy.17
  55.2 0.0 collective-permute-done.6
  55.2 6.1 %collective-permute-done.5 = f32[4,1,8,1024]{3,2,1,0:T(8,128)S(1)} collective-permute-done((f32[4,1,8,1024]{3,2,1,0:T(8,128)S(1)}, f32[4,1,8,1024]{3,2,1,0:T(8,128)S(1)}, u32[]{:S(2)}, u32[]{:S(2)}) %collective-permute-start.5) | collective-permute-done | bytes 131104 | tf_op jit(solution)/shard_map/ppermute | solution.py:34
  61.3 0.0 copy-done.1
  61.3 0.0 copy-done.2
  61.3 1.9 %divide_subtract_fusion = (f32[4,4,8,1024]{3,2,1,0:T(8,128)}, f32[4,4,8,1024]{3,2,1,0:T(8,128)}, f32[4,4,8,1024]{3,2,1,0:T(8,128)}) fusion(f32[4,4,8,1024]{3,2,1,0:T(8,128)S(1)} %copy-done, f32[4,4,8,1024]{3,2,1,0:T(8,128)S(1)} %copy-done.1, f32[4,4,8,1024]{3,2,1,0:T(8,128)S(1)} %copy-done.2, f32[4,4,7,1024]{3,2,1,0:T(8,128)S(1)} %get-tuple-element.28, ...), kind=kLoop, calls=%fused_computation.18 | loop fusion | flops 3801088 | bytes 5521408 | tf_op jit(solution)/shard_map/sub | solution.py:140
  (38 shorter events, 0.8 us)
Async XLA Ops:
  0.6 5.4 %copy-start = (f32[4,4,8,1024]{3,2,1,0:T(8,128)S(1)}, f32[4,4,8,1024]{3,2,1,0:T(8,128)}, u32[]{:S(2)}) copy-start(f32[4,4,8,1024]{3,2,1,0:T(8,128)} %param.6) | copy-start | bytes 1572868
  1.7 6.8 %collective-permute-start = (f32[4,1,8,1024]{3,2,1,0:T(8,128)S(1)}, f32[4,1,8,1024]{3,2,1,0:T(8,128)S(1)}, u32[]{:S(2)}, u32[]{:S(2)}) collective-permute-start(f32[4,1,8,1024]{3,2,1,0:T(8,128)S(1)} %get-tuple-element.32), channel_id=1, source_target_pairs={{16,0},{32,16},{48,32},{64,48},{80,64},{96,80},{112,96},{128,112},... | collective-permute-start | bytes 393224 | tf_op jit(solution)/shard_map/ppermute | solution.py:111
  6.0 0.8 %copy-start.3 = (f32[3,4,1024]{2,1,0:T(4,128)S(1)}, f32[3,4,1024]{2,1,0:T(4,128)}, u32[]{:S(2)}) copy-start(f32[3,4,1024]{2,1,0:T(4,128)} %param.11) | copy-start | bytes 147460
  6.1 0.7 %copy-start.5 = (s32[1,1,128]{2,1,0:T(1,128)S(1)}, s32[1,1,128]{2,1,0:T(1,128)}, u32[]{:S(2)}) copy-start(s32[1,1,128]{2,1,0:T(1,128)} %param.10) | copy-start | bytes 1540
  7.0 0.7 %copy-start.4 = (s32[4,1024]{1,0:T(4,128)S(1)}, s32[4,1024]{1,0:T(4,128)}, u32[]{:S(2)}) copy-start(s32[4,1024]{1,0:T(4,128)} %param.9) | copy-start | bytes 49156
  9.1 6.9 %collective-permute-start.1 = (f32[8,4,1024]{2,1,0:T(4,128)S(1)}, f32[8,4,1024]{2,1,0:T(4,128)S(1)}, u32[]{:S(2)}, u32[]{:S(2)}) collective-permute-start(f32[8,4,1024]{2,1,0:T(4,128)S(1)} %pad_maximum_fusion.3), channel_id=1, source_target_pairs={{0,1},{1,0},{2,3},{3,2},{4,5},{5,4},{6,7},{7,6},{8,9},{9,8},{10,11... | collective-permute-start | bytes 393224 | tf_op jit(solution)/shard_map/ppermute | solution.py:58
  13.0 3.0 %collective-permute-start.7 = (f32[4,4,1024]{2,1,0:T(4,128)S(1)}, f32[4,4,1024]{2,1,0:T(4,128)S(1)}, u32[]{:S(2)}, u32[]{:S(2)}) collective-permute-start(f32[4,4,1024]{2,1,0:T(4,128)S(1)} %get-tuple-element.44), channel_id=1, source_target_pairs={{1,2},{3,4},{5,6},{7,8},{9,10},{11,12},{13,14},{2,1},{4,3},{6,5},{... | collective-permute-start | bytes 196616 | tf_op jit(solution)/shard_map/ppermute | solution.py:45
  13.7 41.5 %collective-permute-start.6 = (f32[4,1,8,1024]{3,2,1,0:T(8,128)S(1)}, f32[4,1,8,1024]{3,2,1,0:T(8,128)S(1)}, u32[]{:S(2)}, u32[]{:S(2)}) collective-permute-start(f32[4,1,8,1024]{3,2,1,0:T(8,128)S(1)} %get-tuple-element.15), channel_id=1, source_target_pairs={{0,16},{16,32},{32,48},{48,64},{64,80},{80,96},{96,112},{112,128},... | collective-permute-start | bytes 393224 | tf_op jit(solution)/shard_map/ppermute | solution.py:113
  16.1 13.1 %collective-permute-start.2 = (f32[4,4,1024]{2,1,0:T(4,128)S(1)}, f32[4,4,1024]{2,1,0:T(4,128)S(1)}, u32[]{:S(2)}, u32[]{:S(2)}) collective-permute-start(f32[4,4,1024]{2,1,0:T(4,128)S(1)} %pad_maximum_fusion.7), channel_id=1, source_target_pairs={{0,3},{1,2},{2,1},{3,0},{4,7},{5,6},{6,5},{7,4},{8,11},{9,10},{10,... | collective-permute-start | bytes 196616 | tf_op jit(solution)/shard_map/ppermute | solution.py:61
  29.4 13.7 %collective-permute-start.3 = (f32[4,4,1024]{2,1,0:T(4,128)S(1)}, f32[4,4,1024]{2,1,0:T(4,128)S(1)}, u32[]{:S(2)}, u32[]{:S(2)}) collective-permute-start(f32[4,4,1024]{2,1,0:T(4,128)S(1)} %pad_maximum_fusion.8), channel_id=1, source_target_pairs={{0,7},{1,6},{2,5},{3,4},{4,3},{5,2},{6,1},{7,0},{8,15},{9,14},{10,... | collective-permute-start | bytes 196616 | tf_op jit(solution)/shard_map/ppermute | solution.py:61
  43.1 9.2 %collective-permute-start.4 = (f32[4,4,1024]{2,1,0:T(4,128)S(1)}, f32[4,4,1024]{2,1,0:T(4,128)S(1)}, u32[]{:S(2)}, u32[]{:S(2)}) collective-permute-start(f32[4,4,1024]{2,1,0:T(4,128)S(1)} %pad_maximum_fusion.9), channel_id=1, source_target_pairs={{0,15},{1,14},{2,13},{3,12},{4,11},{5,10},{6,9},{7,8},{8,7},{9,6},... | collective-permute-start | bytes 196616 | tf_op jit(solution)/shard_map/ppermute | solution.py:61
  52.9 8.4 %collective-permute-start.5 = (f32[4,1,8,1024]{3,2,1,0:T(8,128)S(1)}, f32[4,1,8,1024]{3,2,1,0:T(8,128)S(1)}, u32[]{:S(2)}, u32[]{:S(2)}) collective-permute-start(f32[4,1,8,1024]{3,2,1,0:T(8,128)S(1)} %slice.273), channel_id=1, source_target_pairs={{0,16},{16,32},{32,48},{48,64},{64,80},{80,96},{96,112},{112,128},... | collective-permute-start | bytes 393224 | tf_op jit(solution)/shard_map/ppermute | solution.py:34
  55.0 6.4 %copy-start.1 = (f32[4,4,8,1024]{3,2,1,0:T(8,128)S(1)}, f32[4,4,8,1024]{3,2,1,0:T(8,128)}, u32[]{:S(2)}) copy-start(f32[4,4,8,1024]{3,2,1,0:T(8,128)} %param.7) | copy-start | bytes 1572868
  55.0 6.3 %copy-start.2 = (f32[4,4,8,1024]{3,2,1,0:T(8,128)S(1)}, f32[4,4,8,1024]{3,2,1,0:T(8,128)}, u32[]{:S(2)}) copy-start(f32[4,4,8,1024]{3,2,1,0:T(8,128)} %param.8) | copy-start | bytes 1572868
